TPU v7x, 512 devices: a whole 4x8x8 slice. The times are simulated.
512 devices in a mesh: dp: 4 (over y_hi, core), context: 16 (over y_lo, x), tensor: 8 (over z).
Axes of the slice: x: 4, y: 8 (y_hi: 2, y_lo: 4; y = y_hi * 4 + y_lo), z: 8, core: 2. Of those that a mesh axis runs over, the one named last changes fastest.
Arguments:
- queries: bfloat16 [8192, 4096], P(('dp', 'context'), 'tensor'), parts along dimension 0, may hold values from -6 to 6
- keys: bfloat16 [8192, 1024], P(('dp', 'context'), 'tensor'), parts along dimension 0, may hold values from -6 to 6
- values: bfloat16 [8192, 1024], P(('dp', 'context'), 'tensor'), parts along dimension 0, may hold values from -6 to 6
- order: int32 [8192], P('dp'), parts along dimension 0, may hold values from 0 to 2047, as said below
- out_weight: bfloat16 [4096, 4096], P('tensor', 'context'), may hold values from -0.125 to 0.125
Outputs:
- output: bfloat16 [8192, 4096], P(('dp', 'context'), 'tensor'), parts along dimension 0
There are 4 independent parts, one for each index of `dp`. A program takes and returns all parts, laid end to end along the dimension named above; an argument that names none is the same for every part. Nothing has to cross between parts.
Inputs may be any that keep to these rules, and one draw needn't show every extreme that they name: A permutation of the positions; each aligned block of 128 rows holds 128 consecutive positions in increasing order, starting at a multiple of 128.
All inputs are finite; a program needn't handle non-finite values.
Results may differ from a plain program's by a relative error of at most 0.019.
Values may be sent and summed in bfloat16 or wider, within the bound.
No kernel may reach another device: no remote copies, remote signals or barrier semaphores. Data moves between devices by JAX's collectives and lax.ppermute only.
A program may use at most 64 MiB of HBM per device.

v0:
```python
import math

import jax
import jax.numpy as jnp
from jax import lax
from jax.sharding import PartitionSpec as P

QUERY_HEADS = 32
KEY_VALUE_HEADS = 8
HEAD_SIZE = 128


def per_device(queries, keys, values, order, out_weight):
    row_count = queries.shape[0]
    local_groups = keys.shape[1] // HEAD_SIZE
    query_head_group = QUERY_HEADS // KEY_VALUE_HEADS
    score_scale = 1.0 / math.sqrt(HEAD_SIZE)
    first_row = lax.axis_index("context") * row_count
    query_pos = lax.dynamic_slice_in_dim(order, first_row, row_count, 0)
    stacked = queries.reshape(row_count, local_groups, query_head_group, HEAD_SIZE)
    stacked = stacked.transpose(1, 2, 0, 3).reshape(
        local_groups, query_head_group * row_count, HEAD_SIZE
    )
    stacked_pos = jnp.tile(query_pos, query_head_group)
    stacked_rows = query_head_group * row_count
    key_part = lax.all_gather(keys, "context", axis=0, tiled=True)
    value_part = lax.all_gather(values, "context", axis=0, tiled=True)
    key_count = key_part.shape[0]
    running_max = jnp.full((local_groups, stacked_rows), -1e30, jnp.float32)
    key_heads = key_part.reshape(key_count, local_groups, HEAD_SIZE)
    value_heads = value_part.reshape(key_count, local_groups, HEAD_SIZE)
    scores = (
        jnp.einsum("grd,kgd->grk", stacked, key_heads, preferred_element_type=jnp.float32)
        * score_scale
    )
    visible = order[None, None, :] <= stacked_pos[None, :, None]
    scores = jnp.where(visible, scores, -1e30)
    new_max = jnp.maximum(running_max, jnp.max(scores, axis=2))
    weights = jnp.where(visible, jnp.exp(scores - new_max[..., None]), 0.0)
    new_sum = jnp.sum(weights, axis=2)
    product = jnp.einsum(
        "grk,kgd->grd",
        weights.astype(jnp.bfloat16),
        value_heads,
        preferred_element_type=jnp.float32,
    )
    attended = (product / new_sum[..., None]).astype(jnp.bfloat16)
    attended = attended.reshape(local_groups, query_head_group, row_count, HEAD_SIZE).transpose(
        2, 0, 1, 3
    )
    attended = attended.reshape(row_count, local_groups * query_head_group * HEAD_SIZE)
    partial_out = jnp.dot(
        attended,
        lax.all_gather(out_weight, "context", axis=1, tiled=True),
        preferred_element_type=jnp.float32,
    )
    summed = lax.psum(partial_out.astype(jnp.bfloat16), "tensor").astype(jnp.float32)
    column_count = summed.shape[1] // lax.axis_size("tensor")
    mine = lax.dynamic_slice_in_dim(
        summed, lax.axis_index("tensor") * column_count, column_count, 1
    )
    return mine.astype(jnp.bfloat16)


def solution(mesh):
    placed = (
        P(("dp", "context"), "tensor"),
        P(("dp", "context"), "tensor"),
        P(("dp", "context"), "tensor"),
        P("dp"),
        P("tensor", "context"),
    )
    return jax.shard_map(
        per_device,
        mesh=mesh,
        in_specs=placed,
        out_specs=P(("dp", "context"), "tensor"),
        check_vma=False,
    )
```

profile of v0, /device:TPU:1, one launch (start us, length us, event | category | flops | bytes accessed | tf_op | source)
XLA Modules:
  0.0 204.6 jit_solution(8475246983671661402)
XLA Ops:
  6.5 0.0 copy-start.1
  6.5 0.0 copy-start
  6.5 0.0 all-gather.2.cloned.1.call-start
  6.5 0.7 all-gather.2.cloned.1.call-update
  7.3 0.0 all-reduce.2.cloned.1.call-start
  7.3 1.0 copy.7
  8.3 0.1 copy.8
  8.5 0.8 dynamic_slice.6
  9.3 40.2 %all_gather.9 = bf16[2048,128]{1,0:T(8,128)(2,1)S(1)} all-gather(bf16[128,128]{1,0:T(8,128)(2,1)} %param.6), channel_id=1, replica_groups=mesh['dp'=4,'context'=16,'tensor'=8] {'context'}, dimensions={0}, use_global_device_ids=true | all-gather | bytes 557056 | tf_op jit(solution)/shard_map/all_gather | solution.py:26
  49.4 1.6 fusion
  51.0 0.0 copy-done
  51.1 37.0 %all_gather.10 = bf16[2048,128]{1,0:T(8,128)(2,1)S(1)} all-gather(bf16[128,128]{1,0:T(8,128)(2,1)S(1)} %copy-done), channel_id=1, replica_groups=mesh['dp'=4,'context'=16,'tensor'=8] {'context'}, dimensions={0}, use_global_device_ids=true | all-gather | bytes 557056 | tf_op jit(solution)/shard_map/all_gather | solution.py:27
  88.1 0.0 copy-done.1
  88.1 1.2 fusion.1
  89.4 1.1 fusion.8
  90.5 0.1 copy.9
  90.6 11.5 %all-gather.2.cloned.1.call-done = bf16[512,4096]{1,0:T(8,128)(2,1)} async-done(((bf16[512,256]{1,0:T(8,128)(2,1)}), bf16[512,4096]{1,0:T(8,128)(2,1)}) %all-gather.2.cloned.1.call-update) | async-done | bytes 4194320 | tf_op jit(solution)/shard_map/all_gather | solution.py:54
  102.1 3.9 %convolution_convert_fusion = bf16[128,4096]{1,0:T(8,128)(2,1)} fusion(bf16[128,512]{0,1:T(8,128)(2,1)S(1)} %bitcast.16, bf16[512,4096]{1,0:T(8,128)(2,1)} %all-gather.2.cloned.1.call-done), kind=kOutput, calls=%fused_computation.2 | convolution fusion | flops 537395200 | bytes 5373952 | tf_op jit(solution)/shard_map/dot_general | solution.py:52
  106.1 0.0 all-reduce.2.cloned.1.call-update
  106.1 90.1 %all-reduce.2.cloned.1.call-done = bf16[128,4096]{1,0:T(8,128)(2,1)} async-done(((bf16[128,4096]{1,0:T(8,128)(2,1)}), bf16[128,4096]{1,0:T(8,128)(2,1)}) %all-reduce.2.cloned.1.call-update) | async-done | bytes 1048592 | tf_op jit(solution)/shard_map/psum | solution.py:57
  196.2 1.6 convert_convert_fusion
  (2 shorter events, 0.0 us)
Async XLA Ops:
  6.5 81.6 %copy-start.1 = (s32[2048]{0:T(1024)S(1)}, s32[2048]{0:T(1024)}, u32[]{:S(2)}) copy-start(s32[2048]{0:T(1024)} %param.8) | copy-start | bytes 24580
  6.5 44.5 %copy-start = (bf16[128,128]{1,0:T(8,128)(2,1)S(1)}, bf16[128,128]{1,0:T(8,128)(2,1)}, u32[]{:S(2)}) copy-start(bf16[128,128]{1,0:T(8,128)(2,1)} %param.7) | copy-start | bytes 98308
  6.5 95.6 %all-gather.2.cloned.1.call-start = ((), (), s32[]{:S(2)}) async-start(), calls=%async_computation | async-start | bytes 4456448 | tf_op jit(solution)/shard_map/all_gather | solution.py:54
  7.3 188.9 %all-reduce.2.cloned.1.call-start = ((), (), s32[]{:S(2)}) async-start(), calls=%async_computation.1 | async-start | bytes 2097152 | tf_op jit(solution)/shard_map/psum | solution.py:57
Sparse Core Ops, SparseCore 0:
  9.3 92.7 all-gather.1
  106.2 89.9 all-reduce.1
where the time goes:
time: 209 us; the launch traced here: 205 us
  waiting for transfers between devices  102 us (49%)
  blocking collectives  77.2 us (37%)
  between operations  13.4 us (6%)
  matrix products  6.63 us (3%)
  other arithmetic  2.82 us (1%)
    psum x1, waiting for transfers between devices, per_device(): lax.psum(partial_out.astype(jnp.bfloat16), 'tensor').astype(jnp.float32)  90.1 us
    all_gather x1, blocking collectives, per_device(): key_part = lax.all_gather(keys, 'context', axis=0, tiled=True)  40.2 us
    all_gather x1, blocking collectives, per_device(): value_part = lax.all_gather(values, 'context', axis=0, tiled=True)  37 us
    all_gather x1, waiting for transfers between devices, per_device(): lax.all_gather(out_weight, 'context', axis=1, tiled=True)  11.5 us
  transfers between devices with their start and end apart: 2, of which 2 were waited for; matrix products, arithmetic and copies ran while one was open for 3% of the time, Pallas kernels for 0%

commit v1 on v0

--- a/solution.py
+++ b/solution.py
@@ -23,8 +23,11 @@
     )
     stacked_pos = jnp.tile(query_pos, query_head_group)
     stacked_rows = query_head_group * row_count
-    key_part = lax.all_gather(keys, "context", axis=0, tiled=True)
-    value_part = lax.all_gather(values, "context", axis=0, tiled=True)
+    kv_part = lax.all_gather(
+        jnp.concatenate([keys, values], axis=1), "context", axis=0, tiled=True
+    )
+    key_part = kv_part[:, : keys.shape[1]]
+    value_part = kv_part[:, keys.shape[1] :]
     key_count = key_part.shape[0]
     running_max = jnp.full((local_groups, stacked_rows), -1e30, jnp.float32)
     key_heads = key_part.reshape(key_count, local_groups, HEAD_SIZE)
@@ -54,12 +57,9 @@
         lax.all_gather(out_weight, "context", axis=1, tiled=True),
         preferred_element_type=jnp.float32,
     )
-    summed = lax.psum(partial_out.astype(jnp.bfloat16), "tensor").astype(jnp.float32)
-    column_count = summed.shape[1] // lax.axis_size("tensor")
-    mine = lax.dynamic_slice_in_dim(
-        summed, lax.axis_index("tensor") * column_count, column_count, 1
+    return lax.psum_scatter(
+        partial_out.astype(jnp.bfloat16), "tensor", scatter_dimension=1, tiled=True
     )
-    return mine.astype(jnp.bfloat16)
 
 
 def solution(mesh):

time: 209 us -> 243 us (1.16)
  waiting for transfers between devices: 102 us -> 214 us
  blocking collectives: 77.2 us -> 0 us
    psum x1 -> x0, waiting for transfers between devices: 90.1 us -> none  [per_device(): lax.psum(partial_out.astype(jnp.bfloat16), 'tensor').astype(jnp.float32)]
    all_gather x2 -> x0, blocking collectives: 77.2 us -> none  [the longest x1 40.2 us: per_device(): key_part = lax.all_gather(keys, 'context', axis=0, tiled=True)]
    all_gather x0 -> x1, waiting for transfers between devices: none -> 76.9 us  [per_device(): lax.all_gather(jnp.concatenate([keys, values], axis=1), 'context', axis=0...]
    all_gather x1, waiting for transfers between devices: 11.5 us -> 88.4 us  [per_device(): lax.all_gather(out_weight, 'context', axis=1, tiled=True)]
    reduce_scatter x0 -> x1, waiting for transfers between devices: none -> 47.6 us  [per_device(): lax.psum_scatter(partial_out.astype(jnp.bfloat16), 'tensor', scatter_dime...]
  transfers between devices with their start and end apart: 2 -> 3, of which waited for: 2 -> 3; matrix products, arithmetic and copies ran while one was open for 3% -> 3% of each run, Pallas kernels for 0% -> 0%
where the time goes in v1:
time: 243 us; the launch traced here: 239 us
  waiting for transfers between devices  214 us (88%)
  between operations  13.2 us (5%)
  matrix products  7.49 us (3%)
  other arithmetic  2.69 us (1%)
    all_gather x1, waiting for transfers between devices, per_device(): lax.all_gather(out_weight, 'context', axis=1, tiled=True)  88.4 us
    all_gather x1, waiting for transfers between devices, per_device(): lax.all_gather(jnp.concatenate([keys, values], axis=1), 'context', axis=0...  76.9 us
    reduce_scatter x1, waiting for transfers between devices, per_device(): lax.psum_scatter(partial_out.astype(jnp.bfloat16), 'tensor', scatter_dime...  47.6 us
  transfers between devices with their start and end apart: 3, of which 3 were waited for; matrix products, arithmetic and copies ran while one was open for 3% of the time, Pallas kernels for 0%

profile of v1, /device:TPU:1, one launch (start us, length us, event | category | flops | bytes accessed | tf_op | source)
XLA Modules:
  0.0 239.1 jit_solution(16070495082497380029)
XLA Ops:
  6.5 0.0 copy-start
  6.5 0.0 all-gather.3.cloned.1.call-start
  6.5 1.4 pad_maximum_fusion
  8.0 0.0 all-gather.3.cloned.1.call-update
  8.0 0.0 all-gather.5.cloned.1.call-start
  8.0 0.7 all-gather.5.cloned.1.call-update
  8.7 0.0 reduce-scatter.2.cloned.1.call-start
  8.8 1.0 copy.7
  9.8 0.1 copy.8
  10.0 0.8 dynamic_slice.3
  10.7 76.9 %all-gather.3.cloned.1.call-done = bf16[2048,256]{1,0:T(8,128)(2,1)} async-done(((bf16[128,256]{1,0:T(8,128)(2,1)}), bf16[2048,256]{1,0:T(8,128)(2,1)}) %all-gather.3.cloned.1.call-update) | async-done | bytes 1048592 | tf_op jit(solution)/shard_map/all_gather | solution.py:26
  87.6 0.0 copy-start.1
  87.6 2.0 fusion
  89.6 0.0 copy-done
  89.6 1.3 fusion.1
  90.9 0.0 copy-done.1
  90.9 1.6 fusion.8
  92.5 0.1 copy.9
  92.7 88.4 %all-gather.5.cloned.1.call-done = bf16[512,4096]{1,0:T(8,128)(2,1)} async-done(((bf16[512,256]{1,0:T(8,128)(2,1)}), bf16[512,4096]{1,0:T(8,128)(2,1)}) %all-gather.5.cloned.1.call-update) | async-done | bytes 4194320 | tf_op jit(solution)/shard_map/all_gather | solution.py:57
  181.0 3.9 %convolution_convert_fusion = bf16[128,4096]{1,0:T(8,128)(2,1)} fusion(bf16[128,512]{0,1:T(8,128)(2,1)S(1)} %bitcast.29, bf16[512,4096]{1,0:T(8,128)(2,1)} %all-gather.5.cloned.1.call-done), kind=kOutput, calls=%fused_computation.2 | convolution fusion | flops 537395200 | bytes 5373952 | tf_op jit(solution)/shard_map/dot_general | solution.py:55
  184.9 0.0 reduce-scatter.2.cloned.1.call-update
  185.0 47.6 %reduce-scatter.2.cloned.1.call-done = bf16[128,512]{1,0:T(8,128)(2,1)} async-done(((bf16[128,4096]{1,0:T(8,128)(2,1)}), bf16[128,512]{1,0:T(8,128)(2,1)}) %reduce-scatter.2.cloned.1.call-update) | async-done | bytes 131088 | tf_op jit(solution)/shard_map/reduce_scatter | solution.py:60
  (2 shorter events, 0.0 us)
Async XLA Ops:
  6.5 83.1 %copy-start = (s32[2048]{0:T(1024)S(1)}, s32[2048]{0:T(1024)}, u32[]{:S(2)}) copy-start(s32[2048]{0:T(1024)} %param.8) | copy-start | bytes 24580
  6.5 81.1 %all-gather.3.cloned.1.call-start = ((), (), s32[]{:S(2)}) async-start(), calls=%async_computation.1 | async-start | bytes 1114112 | tf_op jit(solution)/shard_map/all_gather | solution.py:26
  8.0 173.1 %all-gather.5.cloned.1.call-start = ((), (), s32[]{:S(2)}) async-start(), calls=%async_computation.2 | async-start | bytes 4456448 | tf_op jit(solution)/shard_map/all_gather | solution.py:57
  8.7 223.9 %reduce-scatter.2.cloned.1.call-start = ((), (), s32[]{:S(2)}) async-start(), calls=%async_computation.3 | async-start | bytes 1179648 | tf_op jit(solution)/shard_map/reduce_scatter | solution.py:60
  87.6 3.3 %copy-start.1 = (bf16[2048,256]{1,0:T(8,128)(2,1)S(1)}, bf16[2048,256]{1,0:T(8,128)(2,1)}, u32[]{:S(2)}) copy-start(bf16[2048,256]{1,0:T(8,128)(2,1)} %all-gather.3.cloned.1.call-done) | copy-start | bytes 3145732
Sparse Core Ops, SparseCore 0:
  9.4 78.1 all-gather.2
  89.6 91.3 all-gather.4
  185.1 47.4 reduce-scatter.1

commit v2 on v1

--- a/solution.py
+++ b/solution.py
@@ -10,11 +10,56 @@
 HEAD_SIZE = 128
 
 
+def exchange_gather(block, bits, axis_name, count):
+    index = lax.axis_index(axis_name)
+    stack = block[None]
+    for bit in bits:
+        received = lax.ppermute(stack, axis_name, [(i, i ^ bit) for i in range(count)])
+        upper = (index & bit) != 0
+        stack = jnp.where(
+            upper,
+            jnp.concatenate([received, stack], 0),
+            jnp.concatenate([stack, received], 0),
+        )
+    return stack
+
+
+def context_gather(block, context_size, low_first=True):
+    bit_count = context_size.bit_length() - 1
+    low = [1 << k for k in range(bit_count // 2)]
+    high = [1 << k for k in range(bit_count // 2, bit_count)]
+    if low_first:
+        return exchange_gather(block, low + high, "context", context_size)
+    stack = exchange_gather(block, high + low, "context", context_size)
+    inner = 1 << len(high)
+    stack = stack.reshape((context_size // inner, inner) + stack.shape[1:])
+    stack = jnp.swapaxes(stack, 0, 1)
+    return stack.reshape((context_size,) + stack.shape[2:])
+
+
 def per_device(queries, keys, values, order, out_weight):
     row_count = queries.shape[0]
     local_groups = keys.shape[1] // HEAD_SIZE
     query_head_group = QUERY_HEADS // KEY_VALUE_HEADS
     score_scale = 1.0 / math.sqrt(HEAD_SIZE)
+    context_size = lax.axis_size("context")
+    dp_size = lax.axis_size("dp")
+
+    core = lax.axis_index("dp") % 2
+    weight_rows = out_weight.shape[0]
+    half_rows = weight_rows // 2
+    mine = lax.dynamic_slice_in_dim(out_weight, core * half_rows, half_rows, 0)
+    quarter = half_rows // 2
+    first = context_gather(mine[:quarter], context_size, True)
+    second = context_gather(mine[quarter:], context_size, False)
+    mine_all = jnp.concatenate([first, second], 1)
+    other_all = lax.ppermute(mine_all, "dp", [(i, i ^ 1) for i in range(dp_size)])
+    weight_all = jnp.where(
+        core == 0,
+        jnp.concatenate([mine_all, other_all], 1),
+        jnp.concatenate([other_all, mine_all], 1),
+    )
+
     first_row = lax.axis_index("context") * row_count
     query_pos = lax.dynamic_slice_in_dim(order, first_row, row_count, 0)
     stacked = queries.reshape(row_count, local_groups, query_head_group, HEAD_SIZE)
@@ -23,9 +68,8 @@
     )
     stacked_pos = jnp.tile(query_pos, query_head_group)
     stacked_rows = query_head_group * row_count
-    kv_part = lax.all_gather(
-        jnp.concatenate([keys, values], axis=1), "context", axis=0, tiled=True
-    )
+    kv_part = context_gather(jnp.concatenate([keys, values], axis=1), context_size, True)
+    kv_part = kv_part.reshape(context_size * row_count, keys.shape[1] + values.shape[1])
     key_part = kv_part[:, : keys.shape[1]]
     value_part = kv_part[:, keys.shape[1] :]
     key_count = key_part.shape[0]
@@ -52,11 +96,9 @@
         2, 0, 1, 3
     )
     attended = attended.reshape(row_count, local_groups * query_head_group * HEAD_SIZE)
-    partial_out = jnp.dot(
-        attended,
-        lax.all_gather(out_weight, "context", axis=1, tiled=True),
-        preferred_element_type=jnp.float32,
-    )
+    partial_out = jnp.einsum(
+        "rh,chk->rck", attended, weight_all, preferred_element_type=jnp.float32
+    ).reshape(row_count, -1)
     return lax.psum_scatter(
         partial_out.astype(jnp.bfloat16), "tensor", scatter_dimension=1, tiled=True
     )

time: 243 us -> 167 us (0.69)
  the two profiles are of different devices: /device:TPU:1 before, /device:TPU:6 now
where the time goes in v2:
time: 167 us; the launch traced here: 166 us
  waiting for transfers between devices  85.5 us (51%)
  starting transfers between devices  43.3 us (26%)
  between operations  13.7 us (8%)
  other arithmetic  8.94 us (5%)
  local copies, waits for them, and re-layouts  7.88 us (5%)
  matrix products  6.99 us (4%)
    reduce_scatter x1, waiting for transfers between devices, per_device(): lax.psum_scatter(partial_out.astype(jnp.bfloat16), 'tensor', scatter_dime...  45.6 us
    ppermute x12, starting transfers between devices, exchange_gather(): lax.ppermute(stack, axis_name, [(i, i ^ bit) for i in range(count)])  41.4 us
    ppermute x12, waiting for transfers between devices, exchange_gather(): lax.ppermute(stack, axis_name, [(i, i ^ bit) for i in range(count)])  39.9 us
    dot_general x1, local copies, waits for them, and re-layouts, per_device(): jnp.einsum('rh,chk->rck', attended, weight_all, preferred_element_type=jn...  6.44 us
    dot_general x1, matrix products, per_device(): jnp.einsum('rh,chk->rck', attended, weight_all, preferred_element_type=jn...  4.65 us
    dot_general x1, other arithmetic, per_device(): jnp.einsum('rh,chk->rck', attended, weight_all, preferred_element_type=jn...  4.55 us
  transfers between devices with their start and end apart: 14, of which 7 were waited for; matrix products, arithmetic and copies ran while one was open for 4% of the time, Pallas kernels for 0%

profile of v2, /device:TPU:6, one launch (start us, length us, event | category | flops | bytes accessed | tf_op | source)
XLA Modules:
  0.0 166.3 jit_solution(755529862056330673)
XLA Ops:
  6.5 0.9 dynamic-slice_bitcast_fusion.1
  7.4 3.5 %collective-permute-start.8 = (bf16[1,128,256]{2,1,0:T(8,128)(2,1)S(1)}, bf16[1,128,256]{2,1,0:T(8,128)(2,1)S(1)}, u32[]{:S(2)}, u32[]{:S(2)}) collective-permute-start(bf16[1,128,256]{2,1,0:T(8,128)(2,1)S(1)} %get-tuple-element.6), channel_id=1, source_target_pairs={{0,32},{8,40},{16,48},{24,56},{32,0},{40,8},{48,16},{56,24},{64,96... | collective-permute-start | bytes 196616 | tf_op jit(solution)/shard_map/ppermute | solution.py:17
  10.9 2.7 %collective-permute-start.4 = (bf16[1,128,256]{2,1,0:T(8,128)(2,1)S(1)}, bf16[1,128,256]{2,1,0:T(8,128)(2,1)S(1)}, u32[]{:S(2)}, u32[]{:S(2)}) collective-permute-start(bf16[1,128,256]{2,1,0:T(8,128)(2,1)S(1)} %get-tuple-element.5), channel_id=1, source_target_pairs={{0,8},{8,0},{16,24},{24,16},{32,40},{40,32},{48,56},{56,48},{64,72... | collective-permute-start | bytes 196616 | tf_op jit(solution)/shard_map/ppermute | solution.py:17
  13.7 4.5 %collective-permute-start.9 = (bf16[2,128,256]{2,1,0:T(8,128)(2,1)S(1)}, bf16[2,128,256]{2,1,0:T(8,128)(2,1)S(1)}, u32[]{:S(2)}, u32[]{:S(2)}) collective-permute-start(bf16[2,128,256]{2,1,0:T(8,128)(2,1)S(1)} %maximum_select_fusion.12), channel_id=1, source_target_pairs={{0,64},{8,72},{16,80},{24,88},{32,96},{40,104},{48,112},{56,120},{... | collective-permute-start | bytes 393224 | tf_op jit(solution)/shard_map/ppermute | solution.py:17
  18.2 4.5 %collective-permute-start.5 = (bf16[2,128,256]{2,1,0:T(8,128)(2,1)S(1)}, bf16[2,128,256]{2,1,0:T(8,128)(2,1)S(1)}, u32[]{:S(2)}, u32[]{:S(2)}) collective-permute-start(bf16[2,128,256]{2,1,0:T(8,128)(2,1)S(1)} %maximum_select_fusion.11), channel_id=1, source_target_pairs={{0,16},{8,24},{16,0},{24,8},{32,48},{40,56},{48,32},{56,40},{64,80... | collective-permute-start | bytes 393224 | tf_op jit(solution)/shard_map/ppermute | solution.py:17
  22.7 1.3 collective-permute-done.9
  24.0 3.1 %collective-permute-start.10 = (bf16[4,128,256]{2,1,0:T(8,128)(2,1)S(1)}, bf16[4,128,256]{2,1,0:T(8,128)(2,1)S(1)}, u32[]{:S(2)}, u32[]{:S(2)}) collective-permute-start(bf16[4,128,256]{2,1,0:T(8,128)(2,1)S(1)} %maximum_select_fusion.9), channel_id=1, source_target_pairs={{0,8},{8,0},{16,24},{24,16},{32,40},{40,32},{48,56},{56,48},{64,72... | collective-permute-start | bytes 786440 | tf_op jit(solution)/shard_map/ppermute | solution.py:17
  27.1 0.8 maximum_bitcast_fusion
  27.9 2.8 %collective-permute-start = (bf16[1,128,256]{2,1,0:T(8,128)(2,1)S(1)}, bf16[1,128,256]{2,1,0:T(8,128)(2,1)S(1)}, u32[]{:S(2)}, u32[]{:S(2)}) collective-permute-start(bf16[1,128,256]{2,1,0:T(8,128)(2,1)S(1)} %maximum_bitcast_fusion), channel_id=1, source_target_pairs={{0,8},{8,0},{16,24},{24,16},{32,40},{40,32},{48,56},{56,48},{64,72... | collective-permute-start | bytes 196616 | tf_op jit(solution)/shard_map/ppermute | solution.py:17
  30.7 2.7 %collective-permute-start.6 = (bf16[4,128,256]{2,1,0:T(8,128)(2,1)S(1)}, bf16[4,128,256]{2,1,0:T(8,128)(2,1)S(1)}, u32[]{:S(2)}, u32[]{:S(2)}) collective-permute-start(bf16[4,128,256]{2,1,0:T(8,128)(2,1)S(1)} %maximum_select_fusion.8), channel_id=1, source_target_pairs={{0,32},{8,40},{16,48},{24,56},{32,0},{40,8},{48,16},{56,24},{64,96... | collective-permute-start | bytes 786440 | tf_op jit(solution)/shard_map/ppermute | solution.py:17
  33.4 1.8 %collective-permute-done = bf16[1,128,256]{2,1,0:T(8,128)(2,1)S(1)} collective-permute-done((bf16[1,128,256]{2,1,0:T(8,128)(2,1)S(1)}, bf16[1,128,256]{2,1,0:T(8,128)(2,1)S(1)}, u32[]{:S(2)}, u32[]{:S(2)}) %collective-permute-start) | collective-permute-done | bytes 65568 | tf_op jit(solution)/shard_map/ppermute | solution.py:17
  35.2 5.1 %collective-permute-start.1 = (bf16[2,128,256]{2,1,0:T(8,128)(2,1)S(1)}, bf16[2,128,256]{2,1,0:T(8,128)(2,1)S(1)}, u32[]{:S(2)}, u32[]{:S(2)}) collective-permute-start(bf16[2,128,256]{2,1,0:T(8,128)(2,1)S(1)} %maximum_select_fusion.10), channel_id=1, source_target_pairs={{0,16},{8,24},{16,0},{24,8},{32,48},{40,56},{48,32},{56,40},{64,80... | collective-permute-start | bytes 393224 | tf_op jit(solution)/shard_map/ppermute | solution.py:17
  40.4 2.3 %collective-permute-start.11 = (bf16[8,128,256]{2,1,0:T(8,128)(2,1)S(1)}, bf16[8,128,256]{2,1,0:T(8,128)(2,1)S(1)}, u32[]{:S(2)}, u32[]{:S(2)}) collective-permute-start(bf16[8,128,256]{2,1,0:T(8,128)(2,1)S(1)} %maximum_select_fusion.6), channel_id=1, source_target_pairs={{0,16},{8,24},{16,0},{24,8},{32,48},{40,56},{48,32},{56,40},{64,80... | collective-permute-start | bytes 1572872 | tf_op jit(solution)/shard_map/ppermute | solution.py:17
  42.7 2.3 %collective-permute-done.1 = bf16[2,128,256]{2,1,0:T(8,128)(2,1)S(1)} collective-permute-done((bf16[2,128,256]{2,1,0:T(8,128)(2,1)S(1)}, bf16[2,128,256]{2,1,0:T(8,128)(2,1)S(1)}, u32[]{:S(2)}, u32[]{:S(2)}) %collective-permute-start.1) | collective-permute-done | bytes 131104 | tf_op jit(solution)/shard_map/ppermute | solution.py:17
  45.0 2.8 %collective-permute-start.2 = (bf16[4,128,256]{2,1,0:T(8,128)(2,1)S(1)}, bf16[4,128,256]{2,1,0:T(8,128)(2,1)S(1)}, u32[]{:S(2)}, u32[]{:S(2)}) collective-permute-start(bf16[4,128,256]{2,1,0:T(8,128)(2,1)S(1)} %maximum_select_fusion.7), channel_id=1, source_target_pairs={{0,32},{8,40},{16,48},{24,56},{32,0},{40,8},{48,16},{56,24},{64,96... | collective-permute-start | bytes 786440 | tf_op jit(solution)/shard_map/ppermute | solution.py:17
  47.9 4.1 %collective-permute-start.7 = (bf16[8,128,256]{2,1,0:T(8,128)(2,1)S(1)}, bf16[8,128,256]{2,1,0:T(8,128)(2,1)S(1)}, u32[]{:S(2)}, u32[]{:S(2)}) collective-permute-start(bf16[8,128,256]{2,1,0:T(8,128)(2,1)S(1)} %maximum_select_fusion.5), channel_id=1, source_target_pairs={{0,64},{8,72},{16,80},{24,88},{32,96},{40,104},{48,112},{56,120},{... | collective-permute-start | bytes 1572872 | tf_op jit(solution)/shard_map/ppermute | solution.py:17
  52.0 3.6 %collective-permute-done.2 = bf16[4,128,256]{2,1,0:T(8,128)(2,1)S(1)} collective-permute-done((bf16[4,128,256]{2,1,0:T(8,128)(2,1)S(1)}, bf16[4,128,256]{2,1,0:T(8,128)(2,1)S(1)}, u32[]{:S(2)}, u32[]{:S(2)}) %collective-permute-start.2) | collective-permute-done | bytes 262176 | tf_op jit(solution)/shard_map/ppermute | solution.py:17
  55.6 3.5 %collective-permute-start.3 = (bf16[8,128,256]{2,1,0:T(8,128)(2,1)S(1)}, bf16[8,128,256]{2,1,0:T(8,128)(2,1)S(1)}, u32[]{:S(2)}, u32[]{:S(2)}) collective-permute-start(bf16[8,128,256]{2,1,0:T(8,128)(2,1)S(1)} %maximum_select_fusion.4), channel_id=1, source_target_pairs={{0,64},{8,72},{16,80},{24,88},{32,96},{40,104},{48,112},{56,120},{... | collective-permute-start | bytes 1572872 | tf_op jit(solution)/shard_map/ppermute | solution.py:17
  59.1 0.2 maximum_select_fusion.3
  59.4 25.9 %collective-permute-done.7 = bf16[8,128,256]{2,1,0:T(8,128)(2,1)S(1)} collective-permute-done((bf16[8,128,256]{2,1,0:T(8,128)(2,1)S(1)}, bf16[8,128,256]{2,1,0:T(8,128)(2,1)S(1)}, u32[]{:S(2)}, u32[]{:S(2)}) %collective-permute-start.7) | collective-permute-done | bytes 524320 | tf_op jit(solution)/shard_map/ppermute | solution.py:17
  85.3 0.2 maximum_select_fusion.2
  85.5 1.5 pad_maximum_fusion
  87.0 1.9 %collective-permute-start.12 = (bf16[16,256,256]{2,1,0:T(8,128)(2,1)}, bf16[16,256,256]{2,1,0:T(8,128)(2,1)}, u32[]{:S(2)}, u32[]{:S(2)}) collective-permute-start(bf16[16,256,256]{2,1,0:T(8,128)(2,1)} %pad_maximum_fusion), channel_id=1, source_target_pairs={{0,128},{128,0},{256,384},{384,256},{1,129},{129,1},{257,385},{385... | collective-permute-start | bytes 6291464 | tf_op jit(solution)/shard_map/ppermute | solution.py:56
  89.3 5.0 %collective-permute-done.3 = bf16[8,128,256]{2,1,0:T(8,128)(2,1)S(1)} collective-permute-done((bf16[8,128,256]{2,1,0:T(8,128)(2,1)S(1)}, bf16[8,128,256]{2,1,0:T(8,128)(2,1)S(1)}, u32[]{:S(2)}, u32[]{:S(2)}) %collective-permute-start.3) | collective-permute-done | bytes 524320 | tf_op jit(solution)/shard_map/ppermute | solution.py:17
  94.3 0.2 maximum_select_fusion.1
  94.5 0.8 fusion.1
  95.2 1.3 fusion.2
  96.5 1.6 fusion.9
  98.2 4.5 %fusion = bf16[16,256,512]{1,2,0:T(8,128)(2,1)} fusion(bf16[16,256,256]{2,1,0:T(8,128)(2,1)} %collective-permute-done.12, bf16[16,128,256]{2,1,0:T(8,128)(2,1)S(1)} %bitcast.44, bf16[16,128,256]{2,1,0:T(8,128)(2,1)S(1)} %maximum_select_fusion.2, pred[]{:T(512)S(6)} %eq.5), kind=kLoop, calls=%fused_computation.4 | loop fusion | flops 27262976 | bytes 8388609 | tf_op jit(solution)/shard_map/rh,chk->rck/dot_general | solution.py:99
  102.8 6.4 %copy.16 = bf16[16,256,512]{2,1,0:T(8,128)(2,1)} copy(bf16[16,256,512]{1,2,0:T(8,128)(2,1)} %fusion) | data formatting | bytes 8388608 | tf_op jit(solution)/shard_map/rh,chk->rck/dot_general | solution.py:99
  109.2 4.6 %convolution_convert_fusion = bf16[128,4096]{1,0:T(8,128)(2,1)} fusion(bf16[128,512]{0,1:T(8,128)(2,1)S(1)} %bitcast.49, bf16[4096,512]{1,0:T(8,128)(2,1)} %bitcast.42), kind=kOutput, calls=%fused_computation.2 | convolution fusion | flops 537395200 | bytes 5373952 | tf_op jit(solution)/shard_map/rh,chk->rck/dot_general | solution.py:99
  113.9 45.6 %reduce-scatter.2.cloned.1.call-done = bf16[128,512]{1,0:T(8,128)(2,1)} async-done(((bf16[128,4096]{1,0:T(8,128)(2,1)}), bf16[128,512]{1,0:T(8,128)(2,1)}) %reduce-scatter.2.cloned.1.call-update) | async-done | bytes 131088 | tf_op jit(solution)/shard_map/reduce_scatter | solution.py:102
  (29 shorter events, 1.0 us)
Async XLA Ops:
  6.5 152.9 %reduce-scatter.2.cloned.1.call-start = ((), (), s32[]{:S(2)}) async-start(), calls=%async_computation.1 | async-start | bytes 1179648 | tf_op jit(solution)/shard_map/reduce_scatter | solution.py:102
  7.4 6.2 %collective-permute-start.8 = (bf16[1,128,256]{2,1,0:T(8,128)(2,1)S(1)}, bf16[1,128,256]{2,1,0:T(8,128)(2,1)S(1)}, u32[]{:S(2)}, u32[]{:S(2)}) collective-permute-start(bf16[1,128,256]{2,1,0:T(8,128)(2,1)S(1)} %get-tuple-element.6), channel_id=1, source_target_pairs={{0,32},{8,40},{16,48},{24,56},{32,0},{40,8},{48,16},{56,24},{64,96... | collective-permute-start | bytes 196616 | tf_op jit(solution)/shard_map/ppermute | solution.py:17
  10.9 7.3 %collective-permute-start.4 = (bf16[1,128,256]{2,1,0:T(8,128)(2,1)S(1)}, bf16[1,128,256]{2,1,0:T(8,128)(2,1)S(1)}, u32[]{:S(2)}, u32[]{:S(2)}) collective-permute-start(bf16[1,128,256]{2,1,0:T(8,128)(2,1)S(1)} %get-tuple-element.5), channel_id=1, source_target_pairs={{0,8},{8,0},{16,24},{24,16},{32,40},{40,32},{48,56},{56,48},{64,72... | collective-permute-start | bytes 196616 | tf_op jit(solution)/shard_map/ppermute | solution.py:17
  13.7 10.3 %collective-permute-start.9 = (bf16[2,128,256]{2,1,0:T(8,128)(2,1)S(1)}, bf16[2,128,256]{2,1,0:T(8,128)(2,1)S(1)}, u32[]{:S(2)}, u32[]{:S(2)}) collective-permute-start(bf16[2,128,256]{2,1,0:T(8,128)(2,1)S(1)} %maximum_select_fusion.12), channel_id=1, source_target_pairs={{0,64},{8,72},{16,80},{24,88},{32,96},{40,104},{48,112},{56,120},{... | collective-permute-start | bytes 393224 | tf_op jit(solution)/shard_map/ppermute | solution.py:17
  18.2 12.4 %collective-permute-start.5 = (bf16[2,128,256]{2,1,0:T(8,128)(2,1)S(1)}, bf16[2,128,256]{2,1,0:T(8,128)(2,1)S(1)}, u32[]{:S(2)}, u32[]{:S(2)}) collective-permute-start(bf16[2,128,256]{2,1,0:T(8,128)(2,1)S(1)} %maximum_select_fusion.11), channel_id=1, source_target_pairs={{0,16},{8,24},{16,0},{24,8},{32,48},{40,56},{48,32},{56,40},{64,80... | collective-permute-start | bytes 393224 | tf_op jit(solution)/shard_map/ppermute | solution.py:17
  24.0 16.3 %collective-permute-start.10 = (bf16[4,128,256]{2,1,0:T(8,128)(2,1)S(1)}, bf16[4,128,256]{2,1,0:T(8,128)(2,1)S(1)}, u32[]{:S(2)}, u32[]{:S(2)}) collective-permute-start(bf16[4,128,256]{2,1,0:T(8,128)(2,1)S(1)} %maximum_select_fusion.9), channel_id=1, source_target_pairs={{0,8},{8,0},{16,24},{24,16},{32,40},{40,32},{48,56},{56,48},{64,72... | collective-permute-start | bytes 786440 | tf_op jit(solution)/shard_map/ppermute | solution.py:17
  27.9 7.3 %collective-permute-start = (bf16[1,128,256]{2,1,0:T(8,128)(2,1)S(1)}, bf16[1,128,256]{2,1,0:T(8,128)(2,1)S(1)}, u32[]{:S(2)}, u32[]{:S(2)}) collective-permute-start(bf16[1,128,256]{2,1,0:T(8,128)(2,1)S(1)} %maximum_bitcast_fusion), channel_id=1, source_target_pairs={{0,8},{8,0},{16,24},{24,16},{32,40},{40,32},{48,56},{56,48},{64,72... | collective-permute-start | bytes 196616 | tf_op jit(solution)/shard_map/ppermute | solution.py:17
  30.7 17.1 %collective-permute-start.6 = (bf16[4,128,256]{2,1,0:T(8,128)(2,1)S(1)}, bf16[4,128,256]{2,1,0:T(8,128)(2,1)S(1)}, u32[]{:S(2)}, u32[]{:S(2)}) collective-permute-start(bf16[4,128,256]{2,1,0:T(8,128)(2,1)S(1)} %maximum_select_fusion.8), channel_id=1, source_target_pairs={{0,32},{8,40},{16,48},{24,56},{32,0},{40,8},{48,16},{56,24},{64,96... | collective-permute-start | bytes 786440 | tf_op jit(solution)/shard_map/ppermute | solution.py:17
  35.2 9.8 %collective-permute-start.1 = (bf16[2,128,256]{2,1,0:T(8,128)(2,1)S(1)}, bf16[2,128,256]{2,1,0:T(8,128)(2,1)S(1)}, u32[]{:S(2)}, u32[]{:S(2)}) collective-permute-start(bf16[2,128,256]{2,1,0:T(8,128)(2,1)S(1)} %maximum_select_fusion.10), channel_id=1, source_target_pairs={{0,16},{8,24},{16,0},{24,8},{32,48},{40,56},{48,32},{56,40},{64,80... | collective-permute-start | bytes 393224 | tf_op jit(solution)/shard_map/ppermute | solution.py:17
  40.4 18.7 %collective-permute-start.11 = (bf16[8,128,256]{2,1,0:T(8,128)(2,1)S(1)}, bf16[8,128,256]{2,1,0:T(8,128)(2,1)S(1)}, u32[]{:S(2)}, u32[]{:S(2)}) collective-permute-start(bf16[8,128,256]{2,1,0:T(8,128)(2,1)S(1)} %maximum_select_fusion.6), channel_id=1, source_target_pairs={{0,16},{8,24},{16,0},{24,8},{32,48},{40,56},{48,32},{56,40},{64,80... | collective-permute-start | bytes 1572872 | tf_op jit(solution)/shard_map/ppermute | solution.py:17
  45.0 10.5 %collective-permute-start.2 = (bf16[4,128,256]{2,1,0:T(8,128)(2,1)S(1)}, bf16[4,128,256]{2,1,0:T(8,128)(2,1)S(1)}, u32[]{:S(2)}, u32[]{:S(2)}) collective-permute-start(bf16[4,128,256]{2,1,0:T(8,128)(2,1)S(1)} %maximum_select_fusion.7), channel_id=1, source_target_pairs={{0,32},{8,40},{16,48},{24,56},{32,0},{40,8},{48,16},{56,24},{64,96... | collective-permute-start | bytes 786440 | tf_op jit(solution)/shard_map/ppermute | solution.py:17
  47.9 37.4 %collective-permute-start.7 = (bf16[8,128,256]{2,1,0:T(8,128)(2,1)S(1)}, bf16[8,128,256]{2,1,0:T(8,128)(2,1)S(1)}, u32[]{:S(2)}, u32[]{:S(2)}) collective-permute-start(bf16[8,128,256]{2,1,0:T(8,128)(2,1)S(1)} %maximum_select_fusion.5), channel_id=1, source_target_pairs={{0,64},{8,72},{16,80},{24,88},{32,96},{40,104},{48,112},{56,120},{... | collective-permute-start | bytes 1572872 | tf_op jit(solution)/shard_map/ppermute | solution.py:17
  55.6 38.7 %collective-permute-start.3 = (bf16[8,128,256]{2,1,0:T(8,128)(2,1)S(1)}, bf16[8,128,256]{2,1,0:T(8,128)(2,1)S(1)}, u32[]{:S(2)}, u32[]{:S(2)}) collective-permute-start(bf16[8,128,256]{2,1,0:T(8,128)(2,1)S(1)} %maximum_select_fusion.4), channel_id=1, source_target_pairs={{0,64},{8,72},{16,80},{24,88},{32,96},{40,104},{48,112},{56,120},{... | collective-permute-start | bytes 1572872 | tf_op jit(solution)/shard_map/ppermute | solution.py:17
  59.3 29.6 %copy-start = (bf16[128,512]{1,0:T(8,128)(2,1)S(1)}, bf16[128,512]{1,0:T(8,128)(2,1)}, u32[]{:S(2)}) copy-start(bf16[128,512]{1,0:T(8,128)(2,1)} %param.5) | copy-start | bytes 393220
  59.3 29.8 %copy-start.1 = (s32[2048]{0:T(1024)S(1)}, s32[2048]{0:T(1024)}, u32[]{:S(2)}) copy-start(s32[2048]{0:T(1024)} %param.8) | copy-start | bytes 24580
  87.0 11.3 %collective-permute-start.12 = (bf16[16,256,256]{2,1,0:T(8,128)(2,1)}, bf16[16,256,256]{2,1,0:T(8,128)(2,1)}, u32[]{:S(2)}, u32[]{:S(2)}) collective-permute-start(bf16[16,256,256]{2,1,0:T(8,128)(2,1)} %pad_maximum_fusion), channel_id=1, source_target_pairs={{0,128},{128,0},{256,384},{384,256},{1,129},{129,1},{257,385},{385... | collective-permute-start | bytes 6291464 | tf_op jit(solution)/shard_map/ppermute | solution.py:56
Sparse Core Ops, SparseCore 0:
  114.0 45.4 reduce-scatter.1

commit v3 on v1

--- a/solution.py
+++ b/solution.py
@@ -8,6 +8,70 @@
 QUERY_HEADS = 32
 KEY_VALUE_HEADS = 8
 HEAD_SIZE = 128
+X_SIZE = 4
+
+
+def chain_plan(context_size, x_size, x_first_mask):
+    y_bits = [x_size << k for k in range((context_size // x_size).bit_length() - 1)]
+    steps = [(bit, bit) for bit in y_bits]
+    if x_size == 4:
+        steps += [(1, 1), (3, 2)] if x_first_mask == 1 else [(3, 2), (1, 3)]
+    else:
+        steps += [(1 << k, 1 << k) for k in range(x_size.bit_length() - 1)]
+    return steps
+
+
+def upper_of(index, mask):
+    bits = index & mask
+    parity = jnp.zeros_like(index)
+    for k in range(mask.bit_length()):
+        parity = parity ^ ((bits >> k) & 1)
+    return parity != 0
+
+
+def upper_static(index, mask):
+    return bin(index & mask).count("1") % 2 == 1
+
+
+def stacked_sources(context_size, steps):
+    lists = [[c] for c in range(context_size)]
+    for mask, side in steps:
+        lists = [
+            (lists[c ^ mask] + lists[c]) if upper_static(c, side) else (lists[c] + lists[c ^ mask])
+            for c in range(context_size)
+        ]
+    assert all(entry == lists[0] for entry in lists)
+    return lists[0]
+
+
+def exchange_gather(block, steps, axis_name, count):
+    index = lax.axis_index(axis_name)
+    stack = block
+    for mask, side in steps:
+        received = lax.ppermute(stack, axis_name, [(i, i ^ mask) for i in range(count)])
+        stack = jnp.where(
+            upper_of(index, side),
+            jnp.concatenate([received, stack], 1),
+            jnp.concatenate([stack, received], 1),
+        )
+    return stack
+
+
+def unpermute_blocks(product, sources, x_size):
+    rows = product.shape[0]
+    count = len(sources)
+    y_count = count // x_size
+    x_order = [sources[ix * y_count] for ix in range(x_size)]
+    assert all(
+        sources[ix * y_count + iy] == iy * x_size + x_order[ix]
+        for ix in range(x_size)
+        for iy in range(y_count)
+    )
+    product = product.reshape(rows, x_size, y_count, -1)
+    inverse = [x_order.index(x) for x in range(x_size)]
+    if inverse != list(range(x_size)):
+        product = jnp.concatenate([product[:, i : i + 1] for i in inverse], axis=1)
+    return jnp.swapaxes(product, 1, 2).reshape(rows, -1)
 
 
 def per_device(queries, keys, values, order, out_weight):
@@ -15,6 +79,30 @@
     local_groups = keys.shape[1] // HEAD_SIZE
     query_head_group = QUERY_HEADS // KEY_VALUE_HEADS
     score_scale = 1.0 / math.sqrt(HEAD_SIZE)
+    context_size = lax.axis_size("context")
+    dp_size = lax.axis_size("dp")
+    x_size = X_SIZE if context_size % X_SIZE == 0 and context_size > X_SIZE else 1
+
+    core = lax.axis_index("dp") % 2
+    weight_rows = out_weight.shape[0]
+    half_rows = weight_rows // 2
+    quarter = half_rows // 2
+    mine = lax.dynamic_slice_in_dim(out_weight, core * half_rows, half_rows, 0)
+    kv_width = keys.shape[1] + values.shape[1]
+    steps_a = chain_plan(context_size, x_size, 1)
+    steps_b = chain_plan(context_size, x_size, 3)
+    block_a = jnp.concatenate([keys, values, mine[:quarter]], axis=1)[:, None, :]
+    gathered_a = exchange_gather(block_a, steps_a, "context", context_size)
+    gathered_b = exchange_gather(mine[quarter:][:, None, :], steps_b, "context", context_size)
+    sources_a = stacked_sources(context_size, steps_a)
+    sources_b = stacked_sources(context_size, steps_b)
+
+    mine_weights = jnp.concatenate([gathered_a[:, :, kv_width:], gathered_b], axis=0)
+    other_weights = lax.ppermute(mine_weights, "dp", [(i, i ^ 1) for i in range(dp_size)])
+
+    kv_all = jnp.swapaxes(gathered_a[:, :, :kv_width], 0, 1).reshape(context_size * row_count, kv_width)
+    key_pos = order.reshape(context_size, row_count)[jnp.array(sources_a)].reshape(-1)
+
     first_row = lax.axis_index("context") * row_count
     query_pos = lax.dynamic_slice_in_dim(order, first_row, row_count, 0)
     stacked = queries.reshape(row_count, local_groups, query_head_group, HEAD_SIZE)
@@ -23,11 +111,8 @@
     )
     stacked_pos = jnp.tile(query_pos, query_head_group)
     stacked_rows = query_head_group * row_count
-    kv_part = lax.all_gather(
-        jnp.concatenate([keys, values], axis=1), "context", axis=0, tiled=True
-    )
-    key_part = kv_part[:, : keys.shape[1]]
-    value_part = kv_part[:, keys.shape[1] :]
+    key_part = kv_all[:, : keys.shape[1]]
+    value_part = kv_all[:, keys.shape[1] :]
     key_count = key_part.shape[0]
     running_max = jnp.full((local_groups, stacked_rows), -1e30, jnp.float32)
     key_heads = key_part.reshape(key_count, local_groups, HEAD_SIZE)
@@ -36,7 +121,7 @@
         jnp.einsum("grd,kgd->grk", stacked, key_heads, preferred_element_type=jnp.float32)
         * score_scale
     )
-    visible = order[None, None, :] <= stacked_pos[None, :, None]
+    visible = key_pos[None, None, :] <= stacked_pos[None, :, None]
     scores = jnp.where(visible, scores, -1e30)
     new_max = jnp.maximum(running_max, jnp.max(scores, axis=2))
     weights = jnp.where(visible, jnp.exp(scores - new_max[..., None]), 0.0)
@@ -52,11 +137,25 @@
         2, 0, 1, 3
     )
     attended = attended.reshape(row_count, local_groups * query_head_group * HEAD_SIZE)
-    partial_out = jnp.dot(
-        attended,
-        lax.all_gather(out_weight, "context", axis=1, tiled=True),
-        preferred_element_type=jnp.float32,
-    )
+
+    total = None
+    for piece, sources in ((0, sources_a), (1, sources_b)):
+        mine_piece = mine_weights[piece * quarter : (piece + 1) * quarter]
+        other_piece = other_weights[piece * quarter : (piece + 1) * quarter]
+        low = jnp.where(core == 0, mine_piece, other_piece)
+        high = jnp.where(core == 0, other_piece, mine_piece)
+        piece_weight = jnp.concatenate([low, high], axis=0).reshape(2 * quarter, -1)
+        piece_rows = jnp.concatenate(
+            [
+                attended[:, piece * quarter : (piece + 1) * quarter],
+                attended[:, half_rows + piece * quarter : half_rows + (piece + 1) * quarter],
+            ],
+            axis=1,
+        )
+        product_out = jnp.dot(piece_rows, piece_weight, preferred_element_type=jnp.float32)
+        product_out = unpermute_blocks(product_out, sources, x_size)
+        total = product_out if total is None else total + product_out
+    partial_out = total
     return lax.psum_scatter(
         partial_out.astype(jnp.bfloat16), "tensor", scatter_dimension=1, tiled=True
     )

time: 243 us -> 172 us (0.71)
  the two profiles are of different devices: /device:TPU:1 before, /device:TPU:2 now
where the time goes in v3:
time: 172 us; the launch traced here: 171 us
  waiting for transfers between devices  98.8 us (57%)
  starting transfers between devices  27.7 us (16%)
  between operations  13.7 us (8%)
  local copies, waits for them, and re-layouts  13.1 us (8%)
  other arithmetic  11.8 us (7%)
  matrix products  5.84 us (3%)
    reduce_scatter x1, waiting for transfers between devices, per_device(): lax.psum_scatter(partial_out.astype(jnp.bfloat16), 'tensor', scatter_dime...  49.4 us
    ppermute x8, waiting for transfers between devices, exchange_gather(): lax.ppermute(stack, axis_name, [(i, i ^ mask) for i in range(count)])  45.8 us
    ppermute x8, starting transfers between devices, exchange_gather(): lax.ppermute(stack, axis_name, [(i, i ^ mask) for i in range(count)])  25.8 us
    concatenate x2, local copies, waits for them, and re-layouts, per_device(): piece_weight = jnp.concatenate([low, high], axis=0).reshape(2 * quarter, -1)  5.33 us
    ppermute x1, waiting for transfers between devices, per_device(): lax.ppermute(mine_weights, 'dp', [(i, i ^ 1) for i in range(dp_size)])  3.51 us
    dot_general x2, matrix products, per_device(): jnp.dot(piece_rows, piece_weight, preferred_element_type=jnp.float32)  3.48 us
  transfers between devices with their start and end apart: 10, of which 9 were waited for; matrix products, arithmetic and copies ran while one was open for 1% of the time, Pallas kernels for 0%

profile of v3, /device:TPU:2, one launch (start us, length us, event | category | flops | bytes accessed | tf_op | source)
XLA Modules:
  0.0 170.9 jit_solution(14685938575408645592)
XLA Ops:
  6.5 0.9 constant_dynamic-slice_fusion
  8.2 3.5 %collective-permute-start = (bf16[128,1,512]{2,0,1:T(8,128)(2,1)S(1)}, bf16[128,1,512]{2,0,1:T(8,128)(2,1)S(1)}, u32[]{:S(2)}, u32[]{:S(2)}) collective-permute-start(bf16[128,1,512]{2,0,1:T(8,128)(2,1)S(1)} %maximum_bitcast_fusion), channel_id=1, source_target_pairs={{0,32},{8,40},{16,48},{24,56},{32,0},{40,8},{48,16},{56,24},{64,96... | collective-permute-start | bytes 393224 | tf_op jit(solution)/shard_map/ppermute | solution.py:51
  11.7 3.6 %collective-permute-done = bf16[128,1,512]{2,0,1:T(8,128)(2,1)S(1)} collective-permute-done((bf16[128,1,512]{2,0,1:T(8,128)(2,1)S(1)}, bf16[128,1,512]{2,0,1:T(8,128)(2,1)S(1)}, u32[]{:S(2)}, u32[]{:S(2)}) %collective-permute-start) | collective-permute-done | bytes 131104 | tf_op jit(solution)/shard_map/ppermute | solution.py:51
  15.4 4.5 %collective-permute-start.1 = (bf16[128,2,512]{2,0,1:T(8,128)(2,1)S(1)}, bf16[128,2,512]{2,0,1:T(8,128)(2,1)S(1)}, u32[]{:S(2)}, u32[]{:S(2)}) collective-permute-start(bf16[128,2,512]{2,0,1:T(8,128)(2,1)S(1)} %maximum_select_fusion.5), channel_id=1, source_target_pairs={{0,64},{8,72},{16,80},{24,88},{32,96},{40,104},{48,112},{56,120},{... | collective-permute-start | bytes 786440 | tf_op jit(solution)/shard_map/ppermute | solution.py:51
  19.9 11.1 %collective-permute-done.1 = bf16[128,2,512]{2,0,1:T(8,128)(2,1)S(1)} collective-permute-done((bf16[128,2,512]{2,0,1:T(8,128)(2,1)S(1)}, bf16[128,2,512]{2,0,1:T(8,128)(2,1)S(1)}, u32[]{:S(2)}, u32[]{:S(2)}) %collective-permute-start.1) | collective-permute-done | bytes 262176 | tf_op jit(solution)/shard_map/ppermute | solution.py:51
  31.1 3.9 %collective-permute-start.2 = (bf16[128,4,512]{2,0,1:T(8,128)(2,1)S(1)}, bf16[128,4,512]{2,0,1:T(8,128)(2,1)S(1)}, u32[]{:S(2)}, u32[]{:S(2)}) collective-permute-start(bf16[128,4,512]{2,0,1:T(8,128)(2,1)S(1)} %maximum_select_fusion.3), channel_id=1, source_target_pairs={{0,8},{8,0},{16,24},{24,16},{32,40},{40,32},{48,56},{56,48},{64,72... | collective-permute-start | bytes 1572872 | tf_op jit(solution)/shard_map/ppermute | solution.py:51
  35.0 1.9 %collective-permute-start.4 = (bf16[128,1,256]{2,0,1:T(8,128)(2,1)S(1)}, bf16[128,1,256]{2,0,1:T(8,128)(2,1)S(1)}, u32[]{:S(2)}, u32[]{:S(2)}) collective-permute-start(bf16[128,1,256]{2,0,1:T(8,128)(2,1)S(1)} %get-tuple-element.15), channel_id=1, source_target_pairs={{0,32},{8,40},{16,48},{24,56},{32,0},{40,8},{48,16},{56,24},{64,96... | collective-permute-start | bytes 196616 | tf_op jit(solution)/shard_map/ppermute | solution.py:51
  36.9 4.2 %collective-permute-done.4 = bf16[128,1,256]{2,0,1:T(8,128)(2,1)S(1)} collective-permute-done((bf16[128,1,256]{2,0,1:T(8,128)(2,1)S(1)}, bf16[128,1,256]{2,0,1:T(8,128)(2,1)S(1)}, u32[]{:S(2)}, u32[]{:S(2)}) %collective-permute-start.4) | collective-permute-done | bytes 65568 | tf_op jit(solution)/shard_map/ppermute | solution.py:51
  41.2 2.5 %collective-permute-start.5 = (bf16[128,2,256]{2,0,1:T(8,128)(2,1)S(1)}, bf16[128,2,256]{2,0,1:T(8,128)(2,1)S(1)}, u32[]{:S(2)}, u32[]{:S(2)}) collective-permute-start(bf16[128,2,256]{2,0,1:T(8,128)(2,1)S(1)} %maximum_select_fusion.7), channel_id=1, source_target_pairs={{0,64},{8,72},{16,80},{24,88},{32,96},{40,104},{48,112},{56,120},{... | collective-permute-start | bytes 393224 | tf_op jit(solution)/shard_map/ppermute | solution.py:51
  43.7 6.2 %collective-permute-done.5 = bf16[128,2,256]{2,0,1:T(8,128)(2,1)S(1)} collective-permute-done((bf16[128,2,256]{2,0,1:T(8,128)(2,1)S(1)}, bf16[128,2,256]{2,0,1:T(8,128)(2,1)S(1)}, u32[]{:S(2)}, u32[]{:S(2)}) %collective-permute-start.5) | collective-permute-done | bytes 131104 | tf_op jit(solution)/shard_map/ppermute | solution.py:51
  49.8 3.5 %collective-permute-start.6 = (bf16[128,4,256]{2,0,1:T(8,128)(2,1)S(1)}, bf16[128,4,256]{2,0,1:T(8,128)(2,1)S(1)}, u32[]{:S(2)}, u32[]{:S(2)}) collective-permute-start(bf16[128,4,256]{2,0,1:T(8,128)(2,1)S(1)} %maximum_select_fusion.6), channel_id=1, source_target_pairs={{0,24},{8,16},{16,8},{24,0},{32,56},{40,48},{48,40},{56,32},{64,88... | collective-permute-start | bytes 786440 | tf_op jit(solution)/shard_map/ppermute | solution.py:51
  53.6 2.3 %collective-permute-start.3 = (bf16[128,8,512]{2,0,1:T(8,128)(2,1)S(1)}, bf16[128,8,512]{2,0,1:T(8,128)(2,1)}, u32[]{:S(2)}, u32[]{:S(2)}) collective-permute-start(bf16[128,8,512]{2,0,1:T(8,128)(2,1)S(1)} %maximum_select_fusion.1), channel_id=1, source_target_pairs={{0,24},{8,16},{16,8},{24,0},{32,56},{40,48},{48,40},{56,32},{64,88... | collective-permute-start | bytes 3145736 | tf_op jit(solution)/shard_map/ppermute | solution.py:51
  55.9 5.0 %collective-permute-done.6 = bf16[128,4,256]{2,0,1:T(8,128)(2,1)S(1)} collective-permute-done((bf16[128,4,256]{2,0,1:T(8,128)(2,1)S(1)}, bf16[128,4,256]{2,0,1:T(8,128)(2,1)S(1)}, u32[]{:S(2)}, u32[]{:S(2)}) %collective-permute-start.6) | collective-permute-done | bytes 262176 | tf_op jit(solution)/shard_map/ppermute | solution.py:51
  61.0 3.7 %collective-permute-start.7 = (bf16[128,8,256]{2,0,1:T(8,128)(2,1)S(1)}, bf16[128,8,256]{2,0,1:T(8,128)(2,1)S(1)}, u32[]{:S(2)}, u32[]{:S(2)}) collective-permute-start(bf16[128,8,256]{2,0,1:T(8,128)(2,1)S(1)} %maximum_select_fusion.4), channel_id=1, source_target_pairs={{0,8},{8,0},{16,24},{24,16},{32,40},{40,32},{48,56},{56,48},{64,72... | collective-permute-start | bytes 1572872 | tf_op jit(solution)/shard_map/ppermute | solution.py:51
  64.7 7.4 %collective-permute-done.7 = bf16[128,8,256]{2,0,1:T(8,128)(2,1)S(1)} collective-permute-done((bf16[128,8,256]{2,0,1:T(8,128)(2,1)S(1)}, bf16[128,8,256]{2,0,1:T(8,128)(2,1)S(1)}, u32[]{:S(2)}, u32[]{:S(2)}) %collective-permute-start.7) | collective-permute-done | bytes 524320 | tf_op jit(solution)/shard_map/ppermute | solution.py:51
  72.2 8.4 %collective-permute-done.3 = bf16[128,8,512]{2,0,1:T(8,128)(2,1)} collective-permute-done((bf16[128,8,512]{2,0,1:T(8,128)(2,1)S(1)}, bf16[128,8,512]{2,0,1:T(8,128)(2,1)}, u32[]{:S(2)}, u32[]{:S(2)}) %collective-permute-start.3) | collective-permute-done | bytes 1048608 | tf_op jit(solution)/shard_map/ppermute | solution.py:51
  80.6 2.6 %maximum_select_fusion = bf16[128,16,512]{2,0,1:T(8,128)(2,1)S(1)} fusion(bf16[128,8,512]{2,0,1:T(8,128)(2,1)} %copy-done.3, bf16[128,8,512]{2,0,1:T(8,128)(2,1)} %collective-permute-done.3, pred[]{:T(512)S(6)} %ne.24), kind=kLoop, calls=%fused_computation.6 | loop fusion | flops 3145728 | bytes 4194305 | tf_op jit(solution)/shard_map/jit(_where)/select_n | solution.py:52
  83.3 1.5 pad_maximum_fusion
  84.8 1.9 %collective-permute-start.8 = (bf16[256,16,256]{2,0,1:T(8,128)(2,1)}, bf16[256,16,256]{2,0,1:T(8,128)(2,1)}, u32[]{:S(2)}, u32[]{:S(2)}) collective-permute-start(bf16[256,16,256]{2,0,1:T(8,128)(2,1)} %pad_maximum_fusion), channel_id=1, source_target_pairs={{0,128},{128,0},{256,384},{384,256},{1,129},{129,1},{257,385},{385... | collective-permute-start | bytes 6291464 | tf_op jit(solution)/shard_map/ppermute | solution.py:101
  87.6 3.5 %collective-permute-done.8 = bf16[256,16,256]{2,0,1:T(8,128)(2,1)} collective-permute-done((bf16[256,16,256]{2,0,1:T(8,128)(2,1)}, bf16[256,16,256]{2,0,1:T(8,128)(2,1)}, u32[]{:S(2)}, u32[]{:S(2)}) %collective-permute-start.8) | collective-permute-done | bytes 2097184 | tf_op jit(solution)/shard_map/ppermute | solution.py:101
  91.1 2.9 %broadcast_select_fusion.3 = (bf16[128,16,256]{2,0,1:T(8,128)(2,1)S(1)}, bf16[128,16,256]{2,0,1:T(8,128)(2,1)S(1)}, bf16[128,16,256]{2,0,1:T(8,128)(2,1)}, bf16[...) fusion(pred[]{:T(512)S(6)} %eq.4, bf16[256,16,256]{2,0,1:T(8,128)(2,1)} %collective-permute-done.8, ...), kind=kLoop, calls=%fused_computation.21 | loop fusion | flops 2097152 | bytes 10485761 | tf_op jit(solution)/shard_map/jit(_where)/select_n | solution.py:145
  94.0 2.2 %pad_maximum_fusion.1 = (bf16[256,16,256]{2,0,1:T(8,128)(2,1)}, bf16[256,16,256]{2,0,1:T(8,128)(2,1)}) fusion(bf16[128,16,256]{2,0,1:T(8,128)(2,1)S(1)} %get-tuple-element.6, bf16[128,16,256]{2,0,1:T(8,128)(2,1)S(1)} %get-tuple-element.5, bf16[128,16,256]{2,0,1:T(8,128)(2,1)S(1)} %get-tuple-element.10, bf16[128,16,256]{2,0,1:T(8,128)(2,1)S(1)} %get-tuple-element.11), kind=kLoop, calls=%fused_computation.8 | loop fusion | flops 8388608 | bytes 8388608 | tf_op jit(solution)/shard_map/concatenate | solution.py:147
  96.3 2.9 %copy.18 = bf16[256,16,256]{0,2,1:T(8,128)(2,1)S(1)} copy(bf16[256,16,256]{2,0,1:T(8,128)(2,1)} %get-tuple-element.23) | data formatting | bytes 4194304 | tf_op jit(solution)/shard_map/concatenate | solution.py:147
  100.0 1.3 fusion.1
  101.3 1.6 fusion.10
  103.9 1.0 fusion.26
  105.5 1.1 copy-done.2
  106.6 2.4 %copy.17 = bf16[256,16,256]{0,2,1:T(8,128)(2,1)} copy(bf16[256,16,256]{2,0,1:T(8,128)(2,1)S(1)} %copy-done.2) | data formatting | bytes 4194304 | tf_op jit(solution)/shard_map/concatenate | solution.py:147
  109.0 2.7 %fusion.6 = bf16[128,4,4,256]{3,0,1,2:T(8,128)(2,1)S(1)} fusion(f32[128,1,4,256]{3,0,2,1:T(8,128)} %get-tuple-element.13, f32[128,2,4,256]{3,0,2,1:T(8,128)S(1)} %slice-done, f32[128,1,4,256]{3,0,2,1:T(8,128)} %get-tuple-element.12, bf16[4,4,256,256]{3,2,1,0:T(8,128)(2,1)} %bitcast.67, bf16[128,128]{1,0:T(8,128)(2,1)S(1)} %get-tuple-element.19, ...), kind=kOutput, calls=%fused_computation.13 | convolution fusion | flops 270663680 | bytes 5308416 | tf_op jit(solution)/shard_map/dot_general | solution.py:155
  111.7 1.3 copy.19
  113.0 49.4 %reduce-scatter.2.cloned.1.call-done = bf16[128,512]{0,1:T(8,128)(2,1)} async-done(((bf16[128,4096]{0,1:T(8,128)(2,1)}), bf16[128,512]{0,1:T(8,128)(2,1)}) %reduce-scatter.2.cloned.1.call-update) | async-done | bytes 131088 | tf_op jit(solution)/shard_map/reduce_scatter | solution.py:159
  162.4 1.7 copy.20
  (39 shorter events, 4.7 us)
Async XLA Ops:
  6.5 80.4 %copy-start = (s32[2048]{0:T(1024)S(1)}, s32[2048]{0:T(1024)}, u32[]{:S(2)}) copy-start(s32[2048]{0:T(1024)} %param.9) | copy-start | bytes 24580
  6.5 155.9 %reduce-scatter.2.cloned.1.call-start = ((), (), s32[]{:S(2)}) async-start(), calls=%async_computation.1 | async-start | bytes 1179648 | tf_op jit(solution)/shard_map/reduce_scatter | solution.py:159
  8.2 7.1 %collective-permute-start = (bf16[128,1,512]{2,0,1:T(8,128)(2,1)S(1)}, bf16[128,1,512]{2,0,1:T(8,128)(2,1)S(1)}, u32[]{:S(2)}, u32[]{:S(2)}) collective-permute-start(bf16[128,1,512]{2,0,1:T(8,128)(2,1)S(1)} %maximum_bitcast_fusion), channel_id=1, source_target_pairs={{0,32},{8,40},{16,48},{24,56},{32,0},{40,8},{48,16},{56,24},{64,96... | collective-permute-start | bytes 393224 | tf_op jit(solution)/shard_map/ppermute | solution.py:51
  15.4 15.6 %collective-permute-start.1 = (bf16[128,2,512]{2,0,1:T(8,128)(2,1)S(1)}, bf16[128,2,512]{2,0,1:T(8,128)(2,1)S(1)}, u32[]{:S(2)}, u32[]{:S(2)}) collective-permute-start(bf16[128,2,512]{2,0,1:T(8,128)(2,1)S(1)} %maximum_select_fusion.5), channel_id=1, source_target_pairs={{0,64},{8,72},{16,80},{24,88},{32,96},{40,104},{48,112},{56,120},{... | collective-permute-start | bytes 786440 | tf_op jit(solution)/shard_map/ppermute | solution.py:51
  31.1 22.3 %collective-permute-start.2 = (bf16[128,4,512]{2,0,1:T(8,128)(2,1)S(1)}, bf16[128,4,512]{2,0,1:T(8,128)(2,1)S(1)}, u32[]{:S(2)}, u32[]{:S(2)}) collective-permute-start(bf16[128,4,512]{2,0,1:T(8,128)(2,1)S(1)} %maximum_select_fusion.3), channel_id=1, source_target_pairs={{0,8},{8,0},{16,24},{24,16},{32,40},{40,32},{48,56},{56,48},{64,72... | collective-permute-start | bytes 1572872 | tf_op jit(solution)/shard_map/ppermute | solution.py:51
  35.0 6.2 %collective-permute-start.4 = (bf16[128,1,256]{2,0,1:T(8,128)(2,1)S(1)}, bf16[128,1,256]{2,0,1:T(8,128)(2,1)S(1)}, u32[]{:S(2)}, u32[]{:S(2)}) collective-permute-start(bf16[128,1,256]{2,0,1:T(8,128)(2,1)S(1)} %get-tuple-element.15), channel_id=1, source_target_pairs={{0,32},{8,40},{16,48},{24,56},{32,0},{40,8},{48,16},{56,24},{64,96... | collective-permute-start | bytes 196616 | tf_op jit(solution)/shard_map/ppermute | solution.py:51
  41.2 8.6 %collective-permute-start.5 = (bf16[128,2,256]{2,0,1:T(8,128)(2,1)S(1)}, bf16[128,2,256]{2,0,1:T(8,128)(2,1)S(1)}, u32[]{:S(2)}, u32[]{:S(2)}) collective-permute-start(bf16[128,2,256]{2,0,1:T(8,128)(2,1)S(1)} %maximum_select_fusion.7), channel_id=1, source_target_pairs={{0,64},{8,72},{16,80},{24,88},{32,96},{40,104},{48,112},{56,120},{... | collective-permute-start | bytes 393224 | tf_op jit(solution)/shard_map/ppermute | solution.py:51
  49.8 11.1 %collective-permute-start.6 = (bf16[128,4,256]{2,0,1:T(8,128)(2,1)S(1)}, bf16[128,4,256]{2,0,1:T(8,128)(2,1)S(1)}, u32[]{:S(2)}, u32[]{:S(2)}) collective-permute-start(bf16[128,4,256]{2,0,1:T(8,128)(2,1)S(1)} %maximum_select_fusion.6), channel_id=1, source_target_pairs={{0,24},{8,16},{16,8},{24,0},{32,56},{40,48},{48,40},{56,32},{64,88... | collective-permute-start | bytes 786440 | tf_op jit(solution)/shard_map/ppermute | solution.py:51
  53.6 18.7 %copy-start.3 = (bf16[128,8,512]{2,0,1:T(8,128)(2,1)}, bf16[128,8,512]{2,0,1:T(8,128)(2,1)S(1)}, u32[]{:S(2)}) copy-start(bf16[128,8,512]{2,0,1:T(8,128)(2,1)S(1)} %maximum_select_fusion.1) | copy-start | bytes 3145732
  53.6 27.0 %collective-permute-start.3 = (bf16[128,8,512]{2,0,1:T(8,128)(2,1)S(1)}, bf16[128,8,512]{2,0,1:T(8,128)(2,1)}, u32[]{:S(2)}, u32[]{:S(2)}) collective-permute-start(bf16[128,8,512]{2,0,1:T(8,128)(2,1)S(1)} %maximum_select_fusion.1), channel_id=1, source_target_pairs={{0,24},{8,16},{16,8},{24,0},{32,56},{40,48},{48,40},{56,32},{64,88... | collective-permute-start | bytes 3145736 | tf_op jit(solution)/shard_map/ppermute | solution.py:51
  61.0 11.1 %collective-permute-start.7 = (bf16[128,8,256]{2,0,1:T(8,128)(2,1)S(1)}, bf16[128,8,256]{2,0,1:T(8,128)(2,1)S(1)}, u32[]{:S(2)}, u32[]{:S(2)}) collective-permute-start(bf16[128,8,256]{2,0,1:T(8,128)(2,1)S(1)} %maximum_select_fusion.4), channel_id=1, source_target_pairs={{0,8},{8,0},{16,24},{24,16},{32,40},{40,32},{48,56},{56,48},{64,72... | collective-permute-start | bytes 1572872 | tf_op jit(solution)/shard_map/ppermute | solution.py:51
  83.3 3.4 %copy-start.5 = (bf16[128,512]{1,0:T(8,128)(2,1)S(1)}, bf16[128,512]{1,0:T(8,128)(2,1)}, u32[]{:S(2)}) copy-start(bf16[128,512]{1,0:T(8,128)(2,1)} %param.6) | copy-start | bytes 393220
  83.3 3.8 %copy-start.6 = (s32[16]{0:T(128)S(1)}, s32[16]{0:T(128)}, u32[]{:S(2)}) copy-start(s32[16]{0:T(128)} %constant.59) | copy-start | bytes 196
  84.8 6.4 %collective-permute-start.8 = (bf16[256,16,256]{2,0,1:T(8,128)(2,1)}, bf16[256,16,256]{2,0,1:T(8,128)(2,1)}, u32[]{:S(2)}, u32[]{:S(2)}) collective-permute-start(bf16[256,16,256]{2,0,1:T(8,128)(2,1)} %pad_maximum_fusion), channel_id=1, source_target_pairs={{0,128},{128,0},{256,384},{384,256},{1,129},{129,1},{257,385},{385... | collective-permute-start | bytes 6291464 | tf_op jit(solution)/shard_map/ppermute | solution.py:101
  96.3 2.9 %copy-start.4 = (bf16[128,16,256]{2,0,1:T(8,128)(2,1)S(1)}, bf16[128,16,256]{2,0,1:T(8,128)(2,1)}, u32[]{:S(2)}) copy-start(bf16[128,16,256]{2,0,1:T(8,128)(2,1)} %get-tuple-element.9) | copy-start | bytes 3145732
  103.9 1.7 copy-start.1
  103.9 2.7 %copy-start.2 = (bf16[256,16,256]{2,0,1:T(8,128)(2,1)S(1)}, bf16[256,16,256]{2,0,1:T(8,128)(2,1)}, u32[]{:S(2)}) copy-start(bf16[256,16,256]{2,0,1:T(8,128)(2,1)} %get-tuple-element.22) | copy-start | bytes 6291460
  106.6 2.4 %slice-start = ((f32[128,4,4,256]{3,0,2,1:T(8,128)}), f32[128,2,4,256]{3,0,2,1:T(8,128)S(1)}, s32[]{:S(2)}) async-start(f32[128,4,4,256]{3,0,2,1:T(8,128)} %copy-done.1), calls=%async_computation.2 | async-start | bytes 2097152 | tf_op jit(solution)/shard_map/slice | solution.py:73
Sparse Core Ops, SparseCore 0:
  113.1 49.2 reduce-scatter.1

commit v4 on v3

--- a/solution.py
+++ b/solution.py
@@ -156,9 +156,10 @@
         product_out = unpermute_blocks(product_out, sources, x_size)
         total = product_out if total is None else total + product_out
     partial_out = total
-    return lax.psum_scatter(
-        partial_out.astype(jnp.bfloat16), "tensor", scatter_dimension=1, tiled=True
-    )
+    tensor_size = lax.axis_size("tensor")
+    pieces = partial_out.astype(jnp.bfloat16).reshape(row_count, tensor_size, -1)
+    pieces = lax.all_to_all(pieces, "tensor", 1, 1, tiled=True)
+    return jnp.sum(pieces.astype(jnp.float32), axis=1).astype(jnp.bfloat16)
 
 
 def solution(mesh):

time: 172 us -> 150 us (0.87)
  the two profiles are of different devices: /device:TPU:2 before, /device:TPU:1 now
where the time goes in v4:
time: 150 us; the launch traced here: 147 us
  waiting for transfers between devices  41.6 us (28%)
  starting transfers between devices  38.3 us (26%)
  blocking collectives  37.8 us (25%)
  other arithmetic  11.9 us (8%)
  local copies, waits for them, and re-layouts  11.5 us (8%)
  matrix products  5.84 us (4%)
    ppermute x8, waiting for transfers between devices, exchange_gather(): lax.ppermute(stack, axis_name, [(i, i ^ mask) for i in range(count)])  38.5 us
    all_to_all x1, blocking collectives, per_device(): pieces = lax.all_to_all(pieces, 'tensor', 1, 1, tiled=True)  37.8 us
    ppermute x8, starting transfers between devices, exchange_gather(): lax.ppermute(stack, axis_name, [(i, i ^ mask) for i in range(count)])  33.6 us
    concatenate x2, local copies, waits for them, and re-layouts, per_device(): piece_weight = jnp.concatenate([low, high], axis=0).reshape(2 * quarter, -1)  5.34 us
    ppermute x1, starting transfers between devices, per_device(): lax.ppermute(mine_weights, 'dp', [(i, i ^ 1) for i in range(dp_size)])  4.71 us
    dot_general x2, matrix products, per_device(): jnp.dot(piece_rows, piece_weight, preferred_element_type=jnp.float32)  3.49 us
    ppermute x1, waiting for transfers between devices, per_device(): lax.ppermute(mine_weights, 'dp', [(i, i ^ 1) for i in range(dp_size)])  3.15 us
    select_n x8, other arithmetic, exchange_gather(): jnp.where(upper_of(index, side), jnp.concatenate([received, stack], 1), j...  3.08 us
  transfers between devices with their start and end apart: 9, of which 8 were waited for; matrix products, arithmetic and copies ran while one was open for 1% of the time, Pallas kernels for 0%

profile of v4, /device:TPU:1, one launch (start us, length us, event | category | flops | bytes accessed | tf_op | source)
XLA Modules:
  0.0 147.3 jit_solution(1967575730898646751)
XLA Ops:
  0.0 0.9 constant_dynamic-slice_fusion
  0.9 0.8 maximum_bitcast_fusion
  1.7 4.0 %collective-permute-start = (bf16[128,1,512]{2,0,1:T(8,128)(2,1)S(1)}, bf16[128,1,512]{2,0,1:T(8,128)(2,1)S(1)}, u32[]{:S(2)}, u32[]{:S(2)}) collective-permute-start(bf16[128,1,512]{2,0,1:T(8,128)(2,1)S(1)} %maximum_bitcast_fusion), channel_id=1, source_target_pairs={{0,32},{8,40},{16,48},{24,56},{32,0},{40,8},{48,16},{56,24},{64,96... | collective-permute-start | bytes 393224 | tf_op jit(solution)/shard_map/ppermute | solution.py:51
  5.7 2.3 %collective-permute-done = bf16[128,1,512]{2,0,1:T(8,128)(2,1)S(1)} collective-permute-done((bf16[128,1,512]{2,0,1:T(8,128)(2,1)S(1)}, bf16[128,1,512]{2,0,1:T(8,128)(2,1)S(1)}, u32[]{:S(2)}, u32[]{:S(2)}) %collective-permute-start) | collective-permute-done | bytes 131104 | tf_op jit(solution)/shard_map/ppermute | solution.py:51
  8.1 4.9 %collective-permute-start.1 = (bf16[128,2,512]{2,0,1:T(8,128)(2,1)S(1)}, bf16[128,2,512]{2,0,1:T(8,128)(2,1)S(1)}, u32[]{:S(2)}, u32[]{:S(2)}) collective-permute-start(bf16[128,2,512]{2,0,1:T(8,128)(2,1)S(1)} %maximum_select_fusion.5), channel_id=1, source_target_pairs={{0,64},{8,72},{16,80},{24,88},{32,96},{40,104},{48,112},{56,120},{... | collective-permute-start | bytes 786440 | tf_op jit(solution)/shard_map/ppermute | solution.py:51
  13.1 6.6 %collective-permute-done.1 = bf16[128,2,512]{2,0,1:T(8,128)(2,1)S(1)} collective-permute-done((bf16[128,2,512]{2,0,1:T(8,128)(2,1)S(1)}, bf16[128,2,512]{2,0,1:T(8,128)(2,1)S(1)}, u32[]{:S(2)}, u32[]{:S(2)}) %collective-permute-start.1) | collective-permute-done | bytes 262176 | tf_op jit(solution)/shard_map/ppermute | solution.py:51
  19.7 7.9 %collective-permute-start.2 = (bf16[128,4,512]{2,0,1:T(8,128)(2,1)S(1)}, bf16[128,4,512]{2,0,1:T(8,128)(2,1)S(1)}, u32[]{:S(2)}, u32[]{:S(2)}) collective-permute-start(bf16[128,4,512]{2,0,1:T(8,128)(2,1)S(1)} %maximum_select_fusion.3), channel_id=1, source_target_pairs={{0,8},{8,0},{16,24},{24,16},{32,40},{40,32},{48,56},{56,48},{64,72... | collective-permute-start | bytes 1572872 | tf_op jit(solution)/shard_map/ppermute | solution.py:51
  27.7 3.3 %collective-permute-start.4 = (bf16[128,1,256]{2,0,1:T(8,128)(2,1)S(1)}, bf16[128,1,256]{2,0,1:T(8,128)(2,1)S(1)}, u32[]{:S(2)}, u32[]{:S(2)}) collective-permute-start(bf16[128,1,256]{2,0,1:T(8,128)(2,1)S(1)} %get-tuple-element.15), channel_id=1, source_target_pairs={{0,32},{8,40},{16,48},{24,56},{32,0},{40,8},{48,16},{56,24},{64,96... | collective-permute-start | bytes 196616 | tf_op jit(solution)/shard_map/ppermute | solution.py:51
  31.0 2.0 %collective-permute-done.4 = bf16[128,1,256]{2,0,1:T(8,128)(2,1)S(1)} collective-permute-done((bf16[128,1,256]{2,0,1:T(8,128)(2,1)S(1)}, bf16[128,1,256]{2,0,1:T(8,128)(2,1)S(1)}, u32[]{:S(2)}, u32[]{:S(2)}) %collective-permute-start.4) | collective-permute-done | bytes 65568 | tf_op jit(solution)/shard_map/ppermute | solution.py:51
  33.0 5.0 %collective-permute-start.5 = (bf16[128,2,256]{2,0,1:T(8,128)(2,1)S(1)}, bf16[128,2,256]{2,0,1:T(8,128)(2,1)S(1)}, u32[]{:S(2)}, u32[]{:S(2)}) collective-permute-start(bf16[128,2,256]{2,0,1:T(8,128)(2,1)S(1)} %maximum_select_fusion.7), channel_id=1, source_target_pairs={{0,64},{8,72},{16,80},{24,88},{32,96},{40,104},{48,112},{56,120},{... | collective-permute-start | bytes 393224 | tf_op jit(solution)/shard_map/ppermute | solution.py:51
  37.9 4.2 %collective-permute-done.5 = bf16[128,2,256]{2,0,1:T(8,128)(2,1)S(1)} collective-permute-done((bf16[128,2,256]{2,0,1:T(8,128)(2,1)S(1)}, bf16[128,2,256]{2,0,1:T(8,128)(2,1)S(1)}, u32[]{:S(2)}, u32[]{:S(2)}) %collective-permute-start.5) | collective-permute-done | bytes 131104 | tf_op jit(solution)/shard_map/ppermute | solution.py:51
  42.1 3.7 %collective-permute-start.6 = (bf16[128,4,256]{2,0,1:T(8,128)(2,1)S(1)}, bf16[128,4,256]{2,0,1:T(8,128)(2,1)S(1)}, u32[]{:S(2)}, u32[]{:S(2)}) collective-permute-start(bf16[128,4,256]{2,0,1:T(8,128)(2,1)S(1)} %maximum_select_fusion.6), channel_id=1, source_target_pairs={{0,24},{8,16},{16,8},{24,0},{32,56},{40,48},{48,40},{56,32},{64,88... | collective-permute-start | bytes 786440 | tf_op jit(solution)/shard_map/ppermute | solution.py:51
  46.1 2.8 %collective-permute-start.3 = (bf16[128,8,512]{2,0,1:T(8,128)(2,1)S(1)}, bf16[128,8,512]{2,0,1:T(8,128)(2,1)}, u32[]{:S(2)}, u32[]{:S(2)}) collective-permute-start(bf16[128,8,512]{2,0,1:T(8,128)(2,1)S(1)} %maximum_select_fusion.1), channel_id=1, source_target_pairs={{0,24},{8,16},{16,8},{24,0},{32,56},{40,48},{48,40},{56,32},{64,88... | collective-permute-start | bytes 3145736 | tf_op jit(solution)/shard_map/ppermute | solution.py:51
  48.9 1.6 %collective-permute-done.6 = bf16[128,4,256]{2,0,1:T(8,128)(2,1)S(1)} collective-permute-done((bf16[128,4,256]{2,0,1:T(8,128)(2,1)S(1)}, bf16[128,4,256]{2,0,1:T(8,128)(2,1)S(1)}, u32[]{:S(2)}, u32[]{:S(2)}) %collective-permute-start.6) | collective-permute-done | bytes 262176 | tf_op jit(solution)/shard_map/ppermute | solution.py:51
  50.6 1.9 %collective-permute-start.7 = (bf16[128,8,256]{2,0,1:T(8,128)(2,1)S(1)}, bf16[128,8,256]{2,0,1:T(8,128)(2,1)S(1)}, u32[]{:S(2)}, u32[]{:S(2)}) collective-permute-start(bf16[128,8,256]{2,0,1:T(8,128)(2,1)S(1)} %maximum_select_fusion.4), channel_id=1, source_target_pairs={{0,8},{8,0},{16,24},{24,16},{32,40},{40,32},{48,56},{56,48},{64,72... | collective-permute-start | bytes 1572872 | tf_op jit(solution)/shard_map/ppermute | solution.py:51
  52.5 8.4 %collective-permute-done.7 = bf16[128,8,256]{2,0,1:T(8,128)(2,1)S(1)} collective-permute-done((bf16[128,8,256]{2,0,1:T(8,128)(2,1)S(1)}, bf16[128,8,256]{2,0,1:T(8,128)(2,1)S(1)}, u32[]{:S(2)}, u32[]{:S(2)}) %collective-permute-start.7) | collective-permute-done | bytes 524320 | tf_op jit(solution)/shard_map/ppermute | solution.py:51
  61.1 13.4 %collective-permute-done.3 = bf16[128,8,512]{2,0,1:T(8,128)(2,1)} collective-permute-done((bf16[128,8,512]{2,0,1:T(8,128)(2,1)S(1)}, bf16[128,8,512]{2,0,1:T(8,128)(2,1)}, u32[]{:S(2)}, u32[]{:S(2)}) %collective-permute-start.3) | collective-permute-done | bytes 1048608 | tf_op jit(solution)/shard_map/ppermute | solution.py:51
  74.5 2.5 %maximum_select_fusion = bf16[128,16,512]{2,0,1:T(8,128)(2,1)S(1)} fusion(bf16[128,8,512]{2,0,1:T(8,128)(2,1)} %copy-done.3, bf16[128,8,512]{2,0,1:T(8,128)(2,1)} %collective-permute-done.3, pred[]{:T(512)S(6)} %ne.24), kind=kLoop, calls=%fused_computation.6 | loop fusion | flops 3145728 | bytes 4194305 | tf_op jit(solution)/shard_map/jit(_where)/select_n | solution.py:52
  77.1 1.5 %pad_maximum_fusion = bf16[256,16,256]{2,0,1:T(8,128)(2,1)} fusion(bf16[128,16,256]{2,0,1:T(8,128)(2,1)S(1)} %maximum_select_fusion.2, bf16[128,16,256]{2,0,1:T(8,128)(2,1)S(1)} %slice.69), kind=kLoop, calls=%fused_computation.7 | loop fusion | flops 4194304 | bytes 4194304 | tf_op jit(solution)/shard_map/concatenate | solution.py:100
  78.6 4.7 %collective-permute-start.8 = (bf16[256,16,256]{2,0,1:T(8,128)(2,1)}, bf16[256,16,256]{2,0,1:T(8,128)(2,1)}, u32[]{:S(2)}, u32[]{:S(2)}) collective-permute-start(bf16[256,16,256]{2,0,1:T(8,128)(2,1)} %pad_maximum_fusion), channel_id=1, source_target_pairs={{0,128},{128,0},{256,384},{384,256},{1,129},{129,1},{257,385},{385... | collective-permute-start | bytes 6291464 | tf_op jit(solution)/shard_map/ppermute | solution.py:101
  84.2 3.2 %collective-permute-done.8 = bf16[256,16,256]{2,0,1:T(8,128)(2,1)} collective-permute-done((bf16[256,16,256]{2,0,1:T(8,128)(2,1)}, bf16[256,16,256]{2,0,1:T(8,128)(2,1)}, u32[]{:S(2)}, u32[]{:S(2)}) %collective-permute-start.8) | collective-permute-done | bytes 2097184 | tf_op jit(solution)/shard_map/ppermute | solution.py:101
  87.4 2.9 %broadcast_select_fusion.3 = (bf16[128,16,256]{2,0,1:T(8,128)(2,1)S(1)}, bf16[128,16,256]{2,0,1:T(8,128)(2,1)S(1)}, bf16[128,16,256]{2,0,1:T(8,128)(2,1)}, bf16[...) fusion(pred[]{:T(512)S(6)} %eq.4, bf16[256,16,256]{2,0,1:T(8,128)(2,1)} %collective-permute-done.8, ...), kind=kLoop, calls=%fused_computation.21 | loop fusion | flops 2097152 | bytes 10485761 | tf_op jit(solution)/shard_map/jit(_where)/select_n | solution.py:145
  90.3 2.2 %pad_maximum_fusion.1 = (bf16[256,16,256]{2,0,1:T(8,128)(2,1)}, bf16[256,16,256]{2,0,1:T(8,128)(2,1)}) fusion(bf16[128,16,256]{2,0,1:T(8,128)(2,1)S(1)} %get-tuple-element.6, bf16[128,16,256]{2,0,1:T(8,128)(2,1)S(1)} %get-tuple-element.5, bf16[128,16,256]{2,0,1:T(8,128)(2,1)S(1)} %get-tuple-element.10, bf16[128,16,256]{2,0,1:T(8,128)(2,1)S(1)} %get-tuple-element.11), kind=kLoop, calls=%fused_computation.8 | loop fusion | flops 8388608 | bytes 8388608 | tf_op jit(solution)/shard_map/concatenate | solution.py:147
  92.5 2.9 %copy.23 = bf16[256,16,256]{0,2,1:T(8,128)(2,1)S(1)} copy(bf16[256,16,256]{2,0,1:T(8,128)(2,1)} %get-tuple-element.23) | data formatting | bytes 4194304 | tf_op jit(solution)/shard_map/concatenate | solution.py:147
  96.2 1.3 fusion.1
  97.5 1.6 %fusion.10 = bf16[512,128]{1,0:T(8,128)(2,1)S(1)} fusion(f32[2048,512]{1,0:T(8,128)S(1)} %get-tuple-element.21, f32[512]{0:T(512)S(1)} %broadcast_maximum_fusion, s32[512]{0:T(512)S(1)} %broadcast_bitcast_fusion, s32[2048]{0:T(1024)S(1)} %bitcast.78, bf16[2048,256]{1,0:T(8,128)(2,1)S(1)} %bitcast.70, f32[512]{0:T(512)S(1)} %fusion.1), kind=kOutput, calls=%fused_computation.15 | convolution fusion | flops 274857984 | bytes 4864000 | tf_op jit(solution)/shard_map/grk,kgd->grd/dot_general | solution.py:129
  99.3 0.8 fusion.18
  100.1 1.0 fusion.26
  101.8 1.1 copy-done.2
  102.8 2.4 %copy.22 = bf16[256,16,256]{0,2,1:T(8,128)(2,1)} copy(bf16[256,16,256]{2,0,1:T(8,128)(2,1)S(1)} %copy-done.2) | data formatting | bytes 4194304 | tf_op jit(solution)/shard_map/concatenate | solution.py:147
  105.3 2.7 %fusion.6 = bf16[128,4,4,256]{3,0,1,2:T(8,128)(2,1)S(1)} fusion(f32[128,1,4,256]{3,0,2,1:T(8,128)} %get-tuple-element.13, f32[128,2,4,256]{3,0,2,1:T(8,128)S(1)} %slice-done, f32[128,1,4,256]{3,0,2,1:T(8,128)} %get-tuple-element.12, bf16[4,4,256,256]{3,2,1,0:T(8,128)(2,1)} %bitcast.67, bf16[128,128]{1,0:T(8,128)(2,1)S(1)} %get-tuple-element.19, ...), kind=kOutput, calls=%fused_computation.13 | convolution fusion | flops 270663680 | bytes 5308416 | tf_op jit(solution)/shard_map/dot_general | solution.py:155
  108.6 37.8 %all_to_all.5 = bf16[128,8,512]{0,2,1:T(8,128)(2,1)S(1)} all-to-all(bf16[128,8,512]{0,2,1:T(8,128)(2,1)S(1)} %bitcast.68), channel_id=1, replica_groups=mesh['dp'=4,'context'=16,'tensor'=8] {'tensor'}, dimensions={1} | all-to-all | bytes 2097152 | tf_op jit(solution)/shard_map/all_to_all | solution.py:161
  (38 shorter events, 4.7 us)
Async XLA Ops:
  0.0 83.6 %copy-start = (s32[2048]{0:T(1024)S(1)}, s32[2048]{0:T(1024)}, u32[]{:S(2)}) copy-start(s32[2048]{0:T(1024)} %param.9) | copy-start | bytes 24580
  1.7 6.4 %collective-permute-start = (bf16[128,1,512]{2,0,1:T(8,128)(2,1)S(1)}, bf16[128,1,512]{2,0,1:T(8,128)(2,1)S(1)}, u32[]{:S(2)}, u32[]{:S(2)}) collective-permute-start(bf16[128,1,512]{2,0,1:T(8,128)(2,1)S(1)} %maximum_bitcast_fusion), channel_id=1, source_target_pairs={{0,32},{8,40},{16,48},{24,56},{32,0},{40,8},{48,16},{56,24},{64,96... | collective-permute-start | bytes 393224 | tf_op jit(solution)/shard_map/ppermute | solution.py:51
  8.1 11.5 %collective-permute-start.1 = (bf16[128,2,512]{2,0,1:T(8,128)(2,1)S(1)}, bf16[128,2,512]{2,0,1:T(8,128)(2,1)S(1)}, u32[]{:S(2)}, u32[]{:S(2)}) collective-permute-start(bf16[128,2,512]{2,0,1:T(8,128)(2,1)S(1)} %maximum_select_fusion.5), channel_id=1, source_target_pairs={{0,64},{8,72},{16,80},{24,88},{32,96},{40,104},{48,112},{56,120},{... | collective-permute-start | bytes 786440 | tf_op jit(solution)/shard_map/ppermute | solution.py:51
  19.7 26.2 %collective-permute-start.2 = (bf16[128,4,512]{2,0,1:T(8,128)(2,1)S(1)}, bf16[128,4,512]{2,0,1:T(8,128)(2,1)S(1)}, u32[]{:S(2)}, u32[]{:S(2)}) collective-permute-start(bf16[128,4,512]{2,0,1:T(8,128)(2,1)S(1)} %maximum_select_fusion.3), channel_id=1, source_target_pairs={{0,8},{8,0},{16,24},{24,16},{32,40},{40,32},{48,56},{56,48},{64,72... | collective-permute-start | bytes 1572872 | tf_op jit(solution)/shard_map/ppermute | solution.py:51
  27.7 5.3 %collective-permute-start.4 = (bf16[128,1,256]{2,0,1:T(8,128)(2,1)S(1)}, bf16[128,1,256]{2,0,1:T(8,128)(2,1)S(1)}, u32[]{:S(2)}, u32[]{:S(2)}) collective-permute-start(bf16[128,1,256]{2,0,1:T(8,128)(2,1)S(1)} %get-tuple-element.15), channel_id=1, source_target_pairs={{0,32},{8,40},{16,48},{24,56},{32,0},{40,8},{48,16},{56,24},{64,96... | collective-permute-start | bytes 196616 | tf_op jit(solution)/shard_map/ppermute | solution.py:51
  33.0 9.1 %collective-permute-start.5 = (bf16[128,2,256]{2,0,1:T(8,128)(2,1)S(1)}, bf16[128,2,256]{2,0,1:T(8,128)(2,1)S(1)}, u32[]{:S(2)}, u32[]{:S(2)}) collective-permute-start(bf16[128,2,256]{2,0,1:T(8,128)(2,1)S(1)} %maximum_select_fusion.7), channel_id=1, source_target_pairs={{0,64},{8,72},{16,80},{24,88},{32,96},{40,104},{48,112},{56,120},{... | collective-permute-start | bytes 393224 | tf_op jit(solution)/shard_map/ppermute | solution.py:51
  42.1 8.3 %collective-permute-start.6 = (bf16[128,4,256]{2,0,1:T(8,128)(2,1)S(1)}, bf16[128,4,256]{2,0,1:T(8,128)(2,1)S(1)}, u32[]{:S(2)}, u32[]{:S(2)}) collective-permute-start(bf16[128,4,256]{2,0,1:T(8,128)(2,1)S(1)} %maximum_select_fusion.6), channel_id=1, source_target_pairs={{0,24},{8,16},{16,8},{24,0},{32,56},{40,48},{48,40},{56,32},{64,88... | collective-permute-start | bytes 786440 | tf_op jit(solution)/shard_map/ppermute | solution.py:51
  46.1 15.0 %copy-start.3 = (bf16[128,8,512]{2,0,1:T(8,128)(2,1)}, bf16[128,8,512]{2,0,1:T(8,128)(2,1)S(1)}, u32[]{:S(2)}) copy-start(bf16[128,8,512]{2,0,1:T(8,128)(2,1)S(1)} %maximum_select_fusion.1) | copy-start | bytes 3145732
  46.1 28.4 %collective-permute-start.3 = (bf16[128,8,512]{2,0,1:T(8,128)(2,1)S(1)}, bf16[128,8,512]{2,0,1:T(8,128)(2,1)}, u32[]{:S(2)}, u32[]{:S(2)}) collective-permute-start(bf16[128,8,512]{2,0,1:T(8,128)(2,1)S(1)} %maximum_select_fusion.1), channel_id=1, source_target_pairs={{0,24},{8,16},{16,8},{24,0},{32,56},{40,48},{48,40},{56,32},{64,88... | collective-permute-start | bytes 3145736 | tf_op jit(solution)/shard_map/ppermute | solution.py:51
  50.6 10.3 %collective-permute-start.7 = (bf16[128,8,256]{2,0,1:T(8,128)(2,1)S(1)}, bf16[128,8,256]{2,0,1:T(8,128)(2,1)S(1)}, u32[]{:S(2)}, u32[]{:S(2)}) collective-permute-start(bf16[128,8,256]{2,0,1:T(8,128)(2,1)S(1)} %maximum_select_fusion.4), channel_id=1, source_target_pairs={{0,8},{8,0},{16,24},{24,16},{32,40},{40,32},{48,56},{56,48},{64,72... | collective-permute-start | bytes 1572872 | tf_op jit(solution)/shard_map/ppermute | solution.py:51
  77.1 6.2 %copy-start.5 = (bf16[128,512]{1,0:T(8,128)(2,1)S(1)}, bf16[128,512]{1,0:T(8,128)(2,1)}, u32[]{:S(2)}) copy-start(bf16[128,512]{1,0:T(8,128)(2,1)} %param.6) | copy-start | bytes 393220
  77.1 6.6 %copy-start.6 = (s32[16]{0:T(128)S(1)}, s32[16]{0:T(128)}, u32[]{:S(2)}) copy-start(s32[16]{0:T(128)} %constant.61) | copy-start | bytes 196
  78.6 8.8 %collective-permute-start.8 = (bf16[256,16,256]{2,0,1:T(8,128)(2,1)}, bf16[256,16,256]{2,0,1:T(8,128)(2,1)}, u32[]{:S(2)}, u32[]{:S(2)}) collective-permute-start(bf16[256,16,256]{2,0,1:T(8,128)(2,1)} %pad_maximum_fusion), channel_id=1, source_target_pairs={{0,128},{128,0},{256,384},{384,256},{1,129},{129,1},{257,385},{385... | collective-permute-start | bytes 6291464 | tf_op jit(solution)/shard_map/ppermute | solution.py:101
  92.5 2.9 %copy-start.4 = (bf16[128,16,256]{2,0,1:T(8,128)(2,1)S(1)}, bf16[128,16,256]{2,0,1:T(8,128)(2,1)}, u32[]{:S(2)}) copy-start(bf16[128,16,256]{2,0,1:T(8,128)(2,1)} %get-tuple-element.9) | copy-start | bytes 3145732
  100.1 1.7 %copy-start.1 = (f32[128,4,4,256]{3,0,2,1:T(8,128)}, f32[128,4,4,256]{3,0,2,1:T(8,128)S(1)}, u32[]{:S(2)}) copy-start(f32[128,4,4,256]{3,0,2,1:T(8,128)S(1)} %fusion.18) | copy-start | bytes 6291460
  100.1 2.7 %copy-start.2 = (bf16[256,16,256]{2,0,1:T(8,128)(2,1)S(1)}, bf16[256,16,256]{2,0,1:T(8,128)(2,1)}, u32[]{:S(2)}) copy-start(bf16[256,16,256]{2,0,1:T(8,128)(2,1)} %get-tuple-element.22) | copy-start | bytes 6291460
  102.8 2.4 %slice-start = ((f32[128,4,4,256]{3,0,2,1:T(8,128)}), f32[128,2,4,256]{3,0,2,1:T(8,128)S(1)}, s32[]{:S(2)}) async-start(f32[128,4,4,256]{3,0,2,1:T(8,128)} %copy-done.1), calls=%async_computation.1 | async-start | bytes 2097152 | tf_op jit(solution)/shard_map/slice | solution.py:73

commit v5 on v4

--- a/solution.py
+++ b/solution.py
@@ -51,27 +51,10 @@
         received = lax.ppermute(stack, axis_name, [(i, i ^ mask) for i in range(count)])
         stack = jnp.where(
             upper_of(index, side),
-            jnp.concatenate([received, stack], 1),
-            jnp.concatenate([stack, received], 1),
+            jnp.concatenate([received, stack], 0),
+            jnp.concatenate([stack, received], 0),
         )
     return stack
-
-
-def unpermute_blocks(product, sources, x_size):
-    rows = product.shape[0]
-    count = len(sources)
-    y_count = count // x_size
-    x_order = [sources[ix * y_count] for ix in range(x_size)]
-    assert all(
-        sources[ix * y_count + iy] == iy * x_size + x_order[ix]
-        for ix in range(x_size)
-        for iy in range(y_count)
-    )
-    product = product.reshape(rows, x_size, y_count, -1)
-    inverse = [x_order.index(x) for x in range(x_size)]
-    if inverse != list(range(x_size)):
-        product = jnp.concatenate([product[:, i : i + 1] for i in inverse], axis=1)
-    return jnp.swapaxes(product, 1, 2).reshape(rows, -1)
 
 
 def per_device(queries, keys, values, order, out_weight):
@@ -84,24 +67,24 @@
     x_size = X_SIZE if context_size % X_SIZE == 0 and context_size > X_SIZE else 1
 
     core = lax.axis_index("dp") % 2
-    weight_rows = out_weight.shape[0]
+    weight_rows, weight_cols = out_weight.shape
     half_rows = weight_rows // 2
-    quarter = half_rows // 2
     mine = lax.dynamic_slice_in_dim(out_weight, core * half_rows, half_rows, 0)
     kv_width = keys.shape[1] + values.shape[1]
-    steps_a = chain_plan(context_size, x_size, 1)
-    steps_b = chain_plan(context_size, x_size, 3)
-    block_a = jnp.concatenate([keys, values, mine[:quarter]], axis=1)[:, None, :]
-    gathered_a = exchange_gather(block_a, steps_a, "context", context_size)
-    gathered_b = exchange_gather(mine[quarter:][:, None, :], steps_b, "context", context_size)
-    sources_a = stacked_sources(context_size, steps_a)
-    sources_b = stacked_sources(context_size, steps_b)
+    steps = chain_plan(context_size, x_size, 1)
+    sources = stacked_sources(context_size, steps)
+    block = jnp.concatenate([keys, values, mine.reshape(row_count, -1)], axis=1)[None]
+    stack = exchange_gather(block, steps, "context", context_size)
 
-    mine_weights = jnp.concatenate([gathered_a[:, :, kv_width:], gathered_b], axis=0)
+    weight_stack = stack[:, :, kv_width:].reshape(context_size, half_rows, weight_cols)
+    mine_weights = jnp.concatenate(
+        [weight_stack[sources.index(c)] for c in range(context_size)], axis=1
+    )
     other_weights = lax.ppermute(mine_weights, "dp", [(i, i ^ 1) for i in range(dp_size)])
+    weight_all = jnp.concatenate([mine_weights, other_weights], axis=0)
 
-    kv_all = jnp.swapaxes(gathered_a[:, :, :kv_width], 0, 1).reshape(context_size * row_count, kv_width)
-    key_pos = order.reshape(context_size, row_count)[jnp.array(sources_a)].reshape(-1)
+    kv_all = stack[:, :, :kv_width].reshape(context_size * row_count, kv_width)
+    key_pos = order.reshape(context_size, row_count)[jnp.array(sources)].reshape(-1)
 
     first_row = lax.axis_index("context") * row_count
     query_pos = lax.dynamic_slice_in_dim(order, first_row, row_count, 0)
@@ -137,25 +120,15 @@
         2, 0, 1, 3
     )
     attended = attended.reshape(row_count, local_groups * query_head_group * HEAD_SIZE)
+    attended = jnp.concatenate(
+        [
+            lax.dynamic_slice_in_dim(attended, core * half_rows, half_rows, 1),
+            lax.dynamic_slice_in_dim(attended, (1 - core) * half_rows, half_rows, 1),
+        ],
+        axis=1,
+    )
+    partial_out = jnp.dot(attended, weight_all, preferred_element_type=jnp.float32)
 
-    total = None
-    for piece, sources in ((0, sources_a), (1, sources_b)):
-        mine_piece = mine_weights[piece * quarter : (piece + 1) * quarter]
-        other_piece = other_weights[piece * quarter : (piece + 1) * quarter]
-        low = jnp.where(core == 0, mine_piece, other_piece)
-        high = jnp.where(core == 0, other_piece, mine_piece)
-        piece_weight = jnp.concatenate([low, high], axis=0).reshape(2 * quarter, -1)
-        piece_rows = jnp.concatenate(
-            [
-                attended[:, piece * quarter : (piece + 1) * quarter],
-                attended[:, half_rows + piece * quarter : half_rows + (piece + 1) * quarter],
-            ],
-            axis=1,
-        )
-        product_out = jnp.dot(piece_rows, piece_weight, preferred_element_type=jnp.float32)
-        product_out = unpermute_blocks(product_out, sources, x_size)
-        total = product_out if total is None else total + product_out
-    partial_out = total
     tensor_size = lax.axis_size("tensor")
     pieces = partial_out.astype(jnp.bfloat16).reshape(row_count, tensor_size, -1)
     pieces = lax.all_to_all(pieces, "tensor", 1, 1, tiled=True)

time: 150 us -> 194 us (1.29)
  local copies, waits for them, and re-layouts: 11.5 us -> 50.4 us
  waiting for transfers between devices: 41.6 us -> 67.5 us
  starting transfers between devices: 38.3 us -> 23.4 us
  other arithmetic: 11.9 us -> 6.97 us
    ppermute x8 -> x4, waiting for transfers between devices: 38.5 us -> 67.5 us  [exchange_gather(): lax.ppermute(stack, axis_name, [(i, i ^ mask) for i in range(count)])]
    squeeze x0 -> x16, local copies, waits for them, and re-layouts: none -> 24.7 us  [per_device(): weight_stack[sources.index(c)]]
    unnamed x16 -> x42, local copies, waits for them, and re-layouts: 1.84 us -> 20.6 us
    ppermute x8 -> x4, starting transfers between devices: 33.6 us -> 18.3 us  [exchange_gather(): lax.ppermute(stack, axis_name, [(i, i ^ mask) for i in range(count)])]
    concatenate x2 -> x1, local copies, waits for them, and re-layouts: 5.34 us -> 0.68 us  [per_device(): jnp.concatenate([weight_stack[sources.index(c)] for c in range(context_si...]
    concatenate x2 -> x0, other arithmetic: 3.71 us -> none  [the longest x1 2.23 us: per_device(): piece_weight = jnp.concatenate([low, high], axis=0).reshape(2 * quarter, -1)]
    ppermute x1, waiting for transfers between devices: 3.15 us -> 0.01 us  [per_device(): lax.ppermute(mine_weights, 'dp', [(i, i ^ 1) for i in range(dp_size)])]
    select_n x9 -> x4, other arithmetic: 5.97 us -> 3.5 us  [exchange_gather(): jnp.where(upper_of(index, side), jnp.concatenate([received, stack], 0), j...]
  transfers between devices with their start and end apart: 9 -> 5, of which waited for: 8 -> 4; matrix products, arithmetic and copies ran while one was open for 1% -> 4% of each run, Pallas kernels for 0% -> 0%
where the time goes in v5:
time: 194 us; the launch traced here: 192 us
  waiting for transfers between devices  67.5 us (35%)
  local copies, waits for them, and re-layouts  50.4 us (26%)
  blocking collectives  39.2 us (20%)
  starting transfers between devices  23.4 us (12%)
  other arithmetic  6.97 us (4%)
  matrix products  4.68 us (2%)
    ppermute x4, waiting for transfers between devices, exchange_gather(): lax.ppermute(stack, axis_name, [(i, i ^ mask) for i in range(count)])  67.5 us
    all_to_all x1, blocking collectives, per_device(): pieces = lax.all_to_all(pieces, 'tensor', 1, 1, tiled=True)  39.2 us
    squeeze x16, local copies, waits for them, and re-layouts, per_device(): weight_stack[sources.index(c)]  24.7 us
    unnamed x42, local copies, waits for them, and re-layouts  20.6 us
    ppermute x4, starting transfers between devices, exchange_gather(): lax.ppermute(stack, axis_name, [(i, i ^ mask) for i in range(count)])  18.3 us
    ppermute x1, starting transfers between devices, per_device(): lax.ppermute(mine_weights, 'dp', [(i, i ^ 1) for i in range(dp_size)])  5.06 us
  transfers between devices with their start and end apart: 5, of which 4 were waited for; matrix products, arithmetic and copies ran while one was open for 4% of the time, Pallas kernels for 0%

profile of v5, /device:TPU:1, one launch (start us, length us, event | category | flops | bytes accessed | tf_op | source)
XLA Modules:
  0.0 192.4 jit_solution(5659054980948959976)
XLA Ops:
  1.8 4.0 %collective-permute-start = (bf16[1,128,768]{2,1,0:T(8,128)(2,1)S(1)}, bf16[1,128,768]{2,1,0:T(8,128)(2,1)S(1)}, u32[]{:S(2)}, u32[]{:S(2)}) collective-permute-start(bf16[1,128,768]{2,1,0:T(8,128)(2,1)S(1)} %maximum_bitcast_fusion), channel_id=1, source_target_pairs={{0,32},{8,40},{16,48},{24,56},{32,0},{40,8},{48,16},{56,24},{64,96... | collective-permute-start | bytes 589832 | tf_op jit(solution)/shard_map/ppermute | solution.py:51
  5.9 3.0 %collective-permute-done = bf16[1,128,768]{2,1,0:T(8,128)(2,1)S(1)} collective-permute-done((bf16[1,128,768]{2,1,0:T(8,128)(2,1)S(1)}, bf16[1,128,768]{2,1,0:T(8,128)(2,1)S(1)}, u32[]{:S(2)}, u32[]{:S(2)}) %collective-permute-start) | collective-permute-done | bytes 196640 | tf_op jit(solution)/shard_map/ppermute | solution.py:51
  8.9 5.6 %collective-permute-start.1 = (bf16[2,128,768]{2,1,0:T(8,128)(2,1)S(1)}, bf16[2,128,768]{2,1,0:T(8,128)(2,1)S(1)}, u32[]{:S(2)}, u32[]{:S(2)}) collective-permute-start(bf16[2,128,768]{2,1,0:T(8,128)(2,1)S(1)} %maximum_select_fusion.3), channel_id=1, source_target_pairs={{0,64},{8,72},{16,80},{24,88},{32,96},{40,104},{48,112},{56,120},{... | collective-permute-start | bytes 1179656 | tf_op jit(solution)/shard_map/ppermute | solution.py:51
  14.6 16.3 %collective-permute-done.1 = bf16[2,128,768]{2,1,0:T(8,128)(2,1)S(1)} collective-permute-done((bf16[2,128,768]{2,1,0:T(8,128)(2,1)S(1)}, bf16[2,128,768]{2,1,0:T(8,128)(2,1)S(1)}, u32[]{:S(2)}, u32[]{:S(2)}) %collective-permute-start.1) | collective-permute-done | bytes 393248 | tf_op jit(solution)/shard_map/ppermute | solution.py:51
  31.1 3.8 %collective-permute-start.2 = (bf16[4,128,768]{2,1,0:T(8,128)(2,1)S(1)}, bf16[4,128,768]{2,1,0:T(8,128)(2,1)S(1)}, u32[]{:S(2)}, u32[]{:S(2)}) collective-permute-start(bf16[4,128,768]{2,1,0:T(8,128)(2,1)S(1)} %maximum_select_fusion.2), channel_id=1, source_target_pairs={{0,8},{8,0},{16,24},{24,16},{32,40},{40,32},{48,56},{56,48},{64,72... | collective-permute-start | bytes 2359304 | tf_op jit(solution)/shard_map/ppermute | solution.py:51
  34.9 15.9 %collective-permute-done.2 = bf16[4,128,768]{2,1,0:T(8,128)(2,1)S(1)} collective-permute-done((bf16[4,128,768]{2,1,0:T(8,128)(2,1)S(1)}, bf16[4,128,768]{2,1,0:T(8,128)(2,1)S(1)}, u32[]{:S(2)}, u32[]{:S(2)}) %collective-permute-start.2) | collective-permute-done | bytes 786464 | tf_op jit(solution)/shard_map/ppermute | solution.py:51
  51.0 4.8 %collective-permute-start.3 = (bf16[8,128,768]{2,1,0:T(8,128)(2,1)S(1)}, bf16[8,128,768]{2,1,0:T(8,128)(2,1)}, u32[]{:S(2)}, u32[]{:S(2)}) collective-permute-start(bf16[8,128,768]{2,1,0:T(8,128)(2,1)S(1)} %maximum_select_fusion.1), channel_id=1, source_target_pairs={{0,24},{8,16},{16,8},{24,0},{32,56},{40,48},{48,40},{56,32},{64,88... | collective-permute-start | bytes 4718600 | tf_op jit(solution)/shard_map/ppermute | solution.py:51
  55.9 32.3 %collective-permute-done.3 = bf16[8,128,768]{2,1,0:T(8,128)(2,1)} collective-permute-done((bf16[8,128,768]{2,1,0:T(8,128)(2,1)S(1)}, bf16[8,128,768]{2,1,0:T(8,128)(2,1)}, u32[]{:S(2)}, u32[]{:S(2)}) %collective-permute-start.3) | collective-permute-done | bytes 1572896 | tf_op jit(solution)/shard_map/ppermute | solution.py:51
  88.1 3.1 %maximum_select_fusion = bf16[16,128,768]{2,1,0:T(8,128)(2,1)S(1)} fusion(bf16[8,128,768]{2,1,0:T(8,128)(2,1)} %copy-done.1, bf16[8,128,768]{2,1,0:T(8,128)(2,1)} %collective-permute-done.3, pred[]{:T(512)S(6)} %ne.18), kind=kLoop, calls=%fused_computation.8 | loop fusion | flops 4718592 | bytes 6291457 | tf_op jit(solution)/shard_map/jit(_where)/select_n | solution.py:52
  92.5 1.6 squeeze.48
  94.1 1.6 constant_dynamic-update-slice_fusion.15
  95.7 1.6 squeeze.49
  97.3 1.6 squeeze.50
  98.9 1.6 squeeze.51
  100.5 1.6 squeeze.52
  102.1 1.6 squeeze.53
  103.7 1.6 squeeze.54
  105.3 1.6 squeeze.55
  106.9 1.6 squeeze.56
  108.5 1.6 squeeze.57
  110.1 1.6 squeeze.58
  111.7 1.6 squeeze.59
  113.4 1.6 squeeze.60
  114.9 1.6 squeeze.61
  116.5 1.6 squeeze.62
  118.9 1.7 constant_dynamic-update-slice_fusion.14
  120.6 1.6 constant_dynamic-update-slice_fusion.13
  122.2 1.6 constant_dynamic-update-slice_fusion.12
  123.8 1.6 constant_dynamic-update-slice_fusion.11
  136.5 5.1 %collective-permute-start.4 = (bf16[256,4096]{1,0:T(8,128)(2,1)}, bf16[256,4096]{1,0:T(8,128)(2,1)}, u32[]{:S(2)}, u32[]{:S(2)}) collective-permute-start(bf16[256,4096]{1,0:T(8,128)(2,1)} %constant_dynamic-update-slice_fusion), channel_id=1, source_target_pairs={{0,128},{128,0},{256,384},{384,256},{1,129},{129,1},{257,385},{385... | collective-permute-start | bytes 6291464 | tf_op jit(solution)/shard_map/ppermute | solution.py:83
  149.9 2.3 %convolution_convert_fusion = bf16[128,4096]{1,0:T(8,128)(2,1)S(1)} fusion(bf16[256,4096]{1,0:T(8,128)(2,1)} %collective-permute-done.4, bf16[256,4096]{1,0:T(8,128)(2,1)S(1)} %copy-done.11, bf16[128,256]{0,1:T(8,128)(2,1)S(1)} %get-tuple-element.22, bf16[128,256]{0,1:T(8,128)(2,1)S(1)} %get-tuple-element.21), kind=kOutput, calls=%fused_computation.3 | convolution fusion | flops 546045952 | bytes 5373952 | tf_op jit(solution)/shard_map/dot_general | solution.py:130
  152.4 39.2 %all_to_all.5 = bf16[128,8,512]{2,0,1:T(8,128)(2,1)S(1)} all-to-all(bf16[128,8,512]{2,0,1:T(8,128)(2,1)S(1)} %bitcast.35), channel_id=1, replica_groups=mesh['dp'=4,'context'=16,'tensor'=8] {'tensor'}, dimensions={1} | all-to-all | bytes 2097152 | tf_op jit(solution)/shard_map/all_to_all | solution.py:134
  (61 shorter events, 24.5 us)
Async XLA Ops:
  0.0 1.0 copy-start
  1.8 7.1 %collective-permute-start = (bf16[1,128,768]{2,1,0:T(8,128)(2,1)S(1)}, bf16[1,128,768]{2,1,0:T(8,128)(2,1)S(1)}, u32[]{:S(2)}, u32[]{:S(2)}) collective-permute-start(bf16[1,128,768]{2,1,0:T(8,128)(2,1)S(1)} %maximum_bitcast_fusion), channel_id=1, source_target_pairs={{0,32},{8,40},{16,48},{24,56},{32,0},{40,8},{48,16},{56,24},{64,96... | collective-permute-start | bytes 589832 | tf_op jit(solution)/shard_map/ppermute | solution.py:51
  8.9 22.0 %collective-permute-start.1 = (bf16[2,128,768]{2,1,0:T(8,128)(2,1)S(1)}, bf16[2,128,768]{2,1,0:T(8,128)(2,1)S(1)}, u32[]{:S(2)}, u32[]{:S(2)}) collective-permute-start(bf16[2,128,768]{2,1,0:T(8,128)(2,1)S(1)} %maximum_select_fusion.3), channel_id=1, source_target_pairs={{0,64},{8,72},{16,80},{24,88},{32,96},{40,104},{48,112},{56,120},{... | collective-permute-start | bytes 1179656 | tf_op jit(solution)/shard_map/ppermute | solution.py:51
  31.1 19.7 %collective-permute-start.2 = (bf16[4,128,768]{2,1,0:T(8,128)(2,1)S(1)}, bf16[4,128,768]{2,1,0:T(8,128)(2,1)S(1)}, u32[]{:S(2)}, u32[]{:S(2)}) collective-permute-start(bf16[4,128,768]{2,1,0:T(8,128)(2,1)S(1)} %maximum_select_fusion.2), channel_id=1, source_target_pairs={{0,8},{8,0},{16,24},{24,16},{32,40},{40,32},{48,56},{56,48},{64,72... | collective-permute-start | bytes 2359304 | tf_op jit(solution)/shard_map/ppermute | solution.py:51
  51.0 4.9 %copy-start.1 = (bf16[8,128,768]{2,1,0:T(8,128)(2,1)}, bf16[8,128,768]{2,1,0:T(8,128)(2,1)S(1)}, u32[]{:S(2)}) copy-start(bf16[8,128,768]{2,1,0:T(8,128)(2,1)S(1)} %maximum_select_fusion.1) | copy-start | bytes 4718596
  51.0 37.1 %collective-permute-start.3 = (bf16[8,128,768]{2,1,0:T(8,128)(2,1)S(1)}, bf16[8,128,768]{2,1,0:T(8,128)(2,1)}, u32[]{:S(2)}, u32[]{:S(2)}) collective-permute-start(bf16[8,128,768]{2,1,0:T(8,128)(2,1)S(1)} %maximum_select_fusion.1), channel_id=1, source_target_pairs={{0,24},{8,16},{16,8},{24,0},{32,56},{40,48},{48,40},{56,32},{64,88... | collective-permute-start | bytes 4718600 | tf_op jit(solution)/shard_map/ppermute | solution.py:51
  118.8 12.9 %copy-start.9 = (bf16[256,256]{1,0:T(8,128)(2,1)S(1)}, bf16[256,256]{1,0:T(8,128)(2,1)}, u32[]{:S(2)}) copy-start(bf16[256,256]{1,0:T(8,128)(2,1)} %squeeze.57) | copy-start | bytes 393220
  118.8 13.6 %copy-start.8 = (bf16[256,256]{1,0:T(8,128)(2,1)S(1)}, bf16[256,256]{1,0:T(8,128)(2,1)}, u32[]{:S(2)}) copy-start(bf16[256,256]{1,0:T(8,128)(2,1)} %squeeze.58) | copy-start | bytes 393220
  118.8 14.2 %copy-start.7 = (bf16[256,256]{1,0:T(8,128)(2,1)S(1)}, bf16[256,256]{1,0:T(8,128)(2,1)}, u32[]{:S(2)}) copy-start(bf16[256,256]{1,0:T(8,128)(2,1)} %squeeze.59) | copy-start | bytes 393220
  118.8 14.9 %copy-start.6 = (bf16[256,256]{1,0:T(8,128)(2,1)S(1)}, bf16[256,256]{1,0:T(8,128)(2,1)}, u32[]{:S(2)}) copy-start(bf16[256,256]{1,0:T(8,128)(2,1)} %squeeze.60) | copy-start | bytes 393220
  118.9 15.6 %copy-start.5 = (bf16[256,256]{1,0:T(8,128)(2,1)S(1)}, bf16[256,256]{1,0:T(8,128)(2,1)}, u32[]{:S(2)}) copy-start(bf16[256,256]{1,0:T(8,128)(2,1)} %squeeze.61) | copy-start | bytes 393220
  118.9 16.3 %copy-start.3 = (bf16[256,256]{1,0:T(8,128)(2,1)S(1)}, bf16[256,256]{1,0:T(8,128)(2,1)}, u32[]{:S(2)}) copy-start(bf16[256,256]{1,0:T(8,128)(2,1)} %squeeze.62) | copy-start | bytes 393220
  118.9 17.0 %copy-start.4 = (bf16[256,256]{1,0:T(8,128)(2,1)S(1)}, bf16[256,256]{1,0:T(8,128)(2,1)}, u32[]{:S(2)}) copy-start(bf16[256,256]{1,0:T(8,128)(2,1)} %squeeze.63) | copy-start | bytes 393220
  120.6 22.9 %copy-start.2 = (s32[2048]{0:T(1024)S(1)}, s32[2048]{0:T(1024)}, u32[]{:S(2)}) copy-start(s32[2048]{0:T(1024)} %param.9) | copy-start | bytes 24580
  120.6 23.5 %copy-start.12 = (s32[16]{0:T(128)S(1)}, s32[16]{0:T(128)}, u32[]{:S(2)}) copy-start(s32[16]{0:T(128)} %constant.61) | copy-start | bytes 196
  136.5 13.4 %collective-permute-start.4 = (bf16[256,4096]{1,0:T(8,128)(2,1)}, bf16[256,4096]{1,0:T(8,128)(2,1)}, u32[]{:S(2)}, u32[]{:S(2)}) collective-permute-start(bf16[256,4096]{1,0:T(8,128)(2,1)} %constant_dynamic-update-slice_fusion), channel_id=1, source_target_pairs={{0,128},{128,0},{256,384},{384,256},{1,129},{129,1},{257,385},{385... | collective-permute-start | bytes 6291464 | tf_op jit(solution)/shard_map/ppermute | solution.py:83
  143.4 2.7 %copy-start.10 = (bf16[1,4,128,128]{3,2,1,0:T(8,128)(2,1)S(1)}, bf16[1,4,128,128]{3,2,1,0:T(8,128)(2,1)}, u32[]{:S(2)}) copy-start(bf16[1,4,128,128]{3,2,1,0:T(8,128)(2,1)} %copy.12) | copy-start | bytes 393220
  148.2 1.8 copy-start.11

commit v6 on v4

--- a/solution.py
+++ b/solution.py
@@ -84,16 +84,24 @@
     x_size = X_SIZE if context_size % X_SIZE == 0 and context_size > X_SIZE else 1
 
     core = lax.axis_index("dp") % 2
-    weight_rows = out_weight.shape[0]
+    weight_rows, weight_cols = out_weight.shape
     half_rows = weight_rows // 2
     quarter = half_rows // 2
     mine = lax.dynamic_slice_in_dim(out_weight, core * half_rows, half_rows, 0)
     kv_width = keys.shape[1] + values.shape[1]
     steps_a = chain_plan(context_size, x_size, 1)
     steps_b = chain_plan(context_size, x_size, 3)
-    block_a = jnp.concatenate([keys, values, mine[:quarter]], axis=1)[:, None, :]
-    gathered_a = exchange_gather(block_a, steps_a, "context", context_size)
-    gathered_b = exchange_gather(mine[quarter:][:, None, :], steps_b, "context", context_size)
+    shared = 0
+    while shared < min(len(steps_a), len(steps_b)) and steps_a[shared] == steps_b[shared]:
+        shared += 1
+    block = jnp.concatenate([keys, values, mine[:quarter], mine[quarter:]], axis=1)[:, None, :]
+    gathered = exchange_gather(block, steps_a[:shared], "context", context_size)
+    gathered_a = exchange_gather(
+        gathered[:, :, : kv_width + weight_cols], steps_a[shared:], "context", context_size
+    )
+    gathered_b = exchange_gather(
+        gathered[:, :, kv_width + weight_cols :], steps_b[shared:], "context", context_size
+    )
     sources_a = stacked_sources(context_size, steps_a)
     sources_b = stacked_sources(context_size, steps_b)
 
@@ -142,13 +150,13 @@
     for piece, sources in ((0, sources_a), (1, sources_b)):
         mine_piece = mine_weights[piece * quarter : (piece + 1) * quarter]
         other_piece = other_weights[piece * quarter : (piece + 1) * quarter]
-        low = jnp.where(core == 0, mine_piece, other_piece)
-        high = jnp.where(core == 0, other_piece, mine_piece)
-        piece_weight = jnp.concatenate([low, high], axis=0).reshape(2 * quarter, -1)
+        piece_weight = jnp.concatenate([mine_piece, other_piece], axis=0).reshape(2 * quarter, -1)
         piece_rows = jnp.concatenate(
             [
-                attended[:, piece * quarter : (piece + 1) * quarter],
-                attended[:, half_rows + piece * quarter : half_rows + (piece + 1) * quarter],
+                lax.dynamic_slice_in_dim(attended, core * half_rows + piece * quarter, quarter, 1),
+                lax.dynamic_slice_in_dim(
+                    attended, (1 - core) * half_rows + piece * quarter, quarter, 1
+                ),
             ],
             axis=1,
         )

time: 150 us -> 146 us (0.973)
  starting transfers between devices: 38.3 us -> 29 us
  other arithmetic: 11.9 us -> 8.37 us
  local copies, waits for them, and re-layouts: 11.5 us -> 14.9 us
  waiting for transfers between devices: 41.6 us -> 44.7 us
  matrix products: 5.84 us -> 7.75 us
    ppermute x8 -> x6, starting transfers between devices: 33.6 us -> 23.9 us  [exchange_gather(): lax.ppermute(stack, axis_name, [(i, i ^ mask) for i in range(count)])]
    ppermute x8 -> x6, waiting for transfers between devices: 38.5 us -> 44.7 us  [exchange_gather(): lax.ppermute(stack, axis_name, [(i, i ^ mask) for i in range(count)])]
    ppermute x1, waiting for transfers between devices: 3.15 us -> 0.01 us  [per_device(): lax.ppermute(mine_weights, 'dp', [(i, i ^ 1) for i in range(dp_size)])]
    select_n x1 -> x0, other arithmetic: 2.89 us -> none  [per_device(): low = jnp.where(core == 0, mine_piece, other_piece)]
    dot_general x2, matrix products: 3.49 us -> 5.4 us  [per_device(): jnp.dot(piece_rows, piece_weight, preferred_element_type=jnp.float32)]
    slice x2 -> x4, local copies, waits for them, and re-layouts: 0.1 us -> 1.99 us  [the longest x1 1.69 us: per_device(): other_piece = other_weights[piece * quarter:(piece + 1) * quarter]]
    select_n x8 -> x6, other arithmetic: 3.08 us -> 2.45 us  [exchange_gather(): jnp.where(upper_of(index, side), jnp.concatenate([received, stack], 1), j...]
  transfers between devices with their start and end apart: 9 -> 7, of which waited for: 8 -> 5; matrix products, arithmetic and copies ran while one was open for 1% -> 4% of each run, Pallas kernels for 0% -> 0%
where the time goes in v6:
time: 146 us; the launch traced here: 144 us
  waiting for transfers between devices  44.7 us (31%)
  blocking collectives  39.2 us (27%)
  starting transfers between devices  29 us (20%)
  local copies, waits for them, and re-layouts  14.9 us (10%)
  other arithmetic  8.37 us (6%)
  matrix products  7.75 us (5%)
    ppermute x6, waiting for transfers between devices, exchange_gather(): lax.ppermute(stack, axis_name, [(i, i ^ mask) for i in range(count)])  44.7 us
    all_to_all x1, blocking collectives, per_device(): pieces = lax.all_to_all(pieces, 'tensor', 1, 1, tiled=True)  39.2 us
    ppermute x6, starting transfers between devices, exchange_gather(): lax.ppermute(stack, axis_name, [(i, i ^ mask) for i in range(count)])  23.9 us
    concatenate x2, local copies, waits for them, and re-layouts, per_device(): jnp.concatenate([mine_piece, other_piece], axis=0).reshape(2 * quarter, -1)  6.83 us
    dot_general x2, matrix products, per_device(): jnp.dot(piece_rows, piece_weight, preferred_element_type=jnp.float32)  5.4 us
    ppermute x1, starting transfers between devices, per_device(): lax.ppermute(mine_weights, 'dp', [(i, i ^ 1) for i in range(dp_size)])  5.06 us
  transfers between devices with their start and end apart: 7, of which 5 were waited for; matrix products, arithmetic and copies ran while one was open for 4% of the time, Pallas kernels for 0%

profile of v6, /device:TPU:1, one launch (start us, length us, event | category | flops | bytes accessed | tf_op | source)
XLA Modules:
  0.0 144.3 jit_solution(17074471126687775767)
XLA Ops:
  0.0 0.9 constant_dynamic-slice_fusion
  0.9 0.8 maximum_bitcast_fusion
  1.7 4.0 %collective-permute-start = (bf16[128,1,768]{2,0,1:T(8,128)(2,1)S(1)}, bf16[128,1,768]{2,0,1:T(8,128)(2,1)S(1)}, u32[]{:S(2)}, u32[]{:S(2)}) collective-permute-start(bf16[128,1,768]{2,0,1:T(8,128)(2,1)S(1)} %maximum_bitcast_fusion), channel_id=1, source_target_pairs={{0,32},{8,40},{16,48},{24,56},{32,0},{40,8},{48,16},{56,24},{64,96... | collective-permute-start | bytes 589832 | tf_op jit(solution)/shard_map/ppermute | solution.py:51
  5.7 3.0 %collective-permute-done = bf16[128,1,768]{2,0,1:T(8,128)(2,1)S(1)} collective-permute-done((bf16[128,1,768]{2,0,1:T(8,128)(2,1)S(1)}, bf16[128,1,768]{2,0,1:T(8,128)(2,1)S(1)}, u32[]{:S(2)}, u32[]{:S(2)}) %collective-permute-start) | collective-permute-done | bytes 196640 | tf_op jit(solution)/shard_map/ppermute | solution.py:51
  8.8 5.6 %collective-permute-start.1 = (bf16[128,2,768]{2,0,1:T(8,128)(2,1)S(1)}, bf16[128,2,768]{2,0,1:T(8,128)(2,1)S(1)}, u32[]{:S(2)}, u32[]{:S(2)}) collective-permute-start(bf16[128,2,768]{2,0,1:T(8,128)(2,1)S(1)} %maximum_select_fusion.5), channel_id=1, source_target_pairs={{0,64},{8,72},{16,80},{24,88},{32,96},{40,104},{48,112},{56,120},{... | collective-permute-start | bytes 1179656 | tf_op jit(solution)/shard_map/ppermute | solution.py:51
  14.5 16.3 %collective-permute-done.1 = bf16[128,2,768]{2,0,1:T(8,128)(2,1)S(1)} collective-permute-done((bf16[128,2,768]{2,0,1:T(8,128)(2,1)S(1)}, bf16[128,2,768]{2,0,1:T(8,128)(2,1)S(1)}, u32[]{:S(2)}, u32[]{:S(2)}) %collective-permute-start.1) | collective-permute-done | bytes 393248 | tf_op jit(solution)/shard_map/ppermute | solution.py:51
  31.0 3.8 %collective-permute-start.2 = (bf16[128,4,512]{2,0,1:T(8,128)(2,1)S(1)}, bf16[128,4,512]{2,0,1:T(8,128)(2,1)S(1)}, u32[]{:S(2)}, u32[]{:S(2)}) collective-permute-start(bf16[128,4,512]{2,0,1:T(8,128)(2,1)S(1)} %slice.56), channel_id=1, source_target_pairs={{0,8},{8,0},{16,24},{24,16},{32,40},{40,32},{48,56},{56,48},{64,72... | collective-permute-start | bytes 1572872 | tf_op jit(solution)/shard_map/ppermute | solution.py:51
  34.8 3.7 %collective-permute-start.4 = (bf16[128,4,256]{2,0,1:T(8,128)(2,1)S(1)}, bf16[128,4,256]{2,0,1:T(8,128)(2,1)S(1)}, u32[]{:S(2)}, u32[]{:S(2)}) collective-permute-start(bf16[128,4,256]{2,0,1:T(8,128)(2,1)S(1)} %slice.61), channel_id=1, source_target_pairs={{0,24},{8,16},{16,8},{24,0},{32,56},{40,48},{48,40},{56,32},{64,88... | collective-permute-start | bytes 786440 | tf_op jit(solution)/shard_map/ppermute | solution.py:51
  38.5 6.5 %collective-permute-done.2 = bf16[128,4,512]{2,0,1:T(8,128)(2,1)S(1)} collective-permute-done((bf16[128,4,512]{2,0,1:T(8,128)(2,1)S(1)}, bf16[128,4,512]{2,0,1:T(8,128)(2,1)S(1)}, u32[]{:S(2)}, u32[]{:S(2)}) %collective-permute-start.2) | collective-permute-done | bytes 524320 | tf_op jit(solution)/shard_map/ppermute | solution.py:51
  45.2 4.8 %collective-permute-start.3 = (bf16[128,8,512]{2,0,1:T(8,128)(2,1)S(1)}, bf16[128,8,512]{2,0,1:T(8,128)(2,1)}, u32[]{:S(2)}, u32[]{:S(2)}) collective-permute-start(bf16[128,8,512]{2,0,1:T(8,128)(2,1)S(1)} %maximum_select_fusion.1), channel_id=1, source_target_pairs={{0,24},{8,16},{16,8},{24,0},{32,56},{40,48},{48,40},{56,32},{64,88... | collective-permute-start | bytes 3145736 | tf_op jit(solution)/shard_map/ppermute | solution.py:51
  50.2 1.9 %collective-permute-start.5 = (bf16[128,8,256]{2,0,1:T(8,128)(2,1)S(1)}, bf16[128,8,256]{2,0,1:T(8,128)(2,1)S(1)}, u32[]{:S(2)}, u32[]{:S(2)}) collective-permute-start(bf16[128,8,256]{2,0,1:T(8,128)(2,1)S(1)} %maximum_select_fusion.4), channel_id=1, source_target_pairs={{0,8},{8,0},{16,24},{24,16},{32,40},{40,32},{48,56},{56,48},{64,72... | collective-permute-start | bytes 1572872 | tf_op jit(solution)/shard_map/ppermute | solution.py:51
  52.1 10.9 %collective-permute-done.5 = bf16[128,8,256]{2,0,1:T(8,128)(2,1)S(1)} collective-permute-done((bf16[128,8,256]{2,0,1:T(8,128)(2,1)S(1)}, bf16[128,8,256]{2,0,1:T(8,128)(2,1)S(1)}, u32[]{:S(2)}, u32[]{:S(2)}) %collective-permute-start.5) | collective-permute-done | bytes 524320 | tf_op jit(solution)/shard_map/ppermute | solution.py:51
  63.2 7.9 %collective-permute-done.3 = bf16[128,8,512]{2,0,1:T(8,128)(2,1)} collective-permute-done((bf16[128,8,512]{2,0,1:T(8,128)(2,1)S(1)}, bf16[128,8,512]{2,0,1:T(8,128)(2,1)}, u32[]{:S(2)}, u32[]{:S(2)}) %collective-permute-start.3) | collective-permute-done | bytes 1048608 | tf_op jit(solution)/shard_map/ppermute | solution.py:51
  71.1 1.9 %maximum_select_fusion = bf16[128,16,512]{2,0,1:T(8,128)(2,1)S(1)} fusion(bf16[128,8,512]{2,0,1:T(8,128)(2,1)S(1)} %maximum_select_fusion.1, bf16[128,8,512]{2,0,1:T(8,128)(2,1)} %collective-permute-done.3, pred[]{:T(512)S(6)} %ne.22), kind=kLoop, calls=%fused_computation.8 | loop fusion | flops 3145728 | bytes 4194305 | tf_op jit(solution)/shard_map/jit(_where)/select_n | solution.py:52
  73.0 0.3 fusion.28
  73.3 1.5 %pad_maximum_fusion = bf16[256,16,256]{2,0,1:T(8,128)(2,1)} fusion(bf16[128,16,256]{2,0,1:T(8,128)(2,1)S(1)} %get-tuple-element.10, bf16[128,16,256]{2,0,1:T(8,128)(2,1)S(1)} %maximum_select_fusion.2), kind=kLoop, calls=%fused_computation.6 | loop fusion | flops 4194304 | bytes 4194304 | tf_op jit(solution)/shard_map/concatenate | solution.py:108
  74.8 5.1 %collective-permute-start.6 = (bf16[256,16,256]{2,0,1:T(8,128)(2,1)}, bf16[256,16,256]{2,0,1:T(8,128)(2,1)}, u32[]{:S(2)}, u32[]{:S(2)}) collective-permute-start(bf16[256,16,256]{2,0,1:T(8,128)(2,1)} %pad_maximum_fusion), channel_id=1, source_target_pairs={{0,128},{128,0},{256,384},{384,256},{1,129},{129,1},{257,385},{385... | collective-permute-start | bytes 6291464 | tf_op jit(solution)/shard_map/ppermute | solution.py:109
  80.2 0.6 gather_fusion
  80.8 0.8 fusion
  81.6 1.3 fusion.1
  82.9 1.6 %fusion.10 = bf16[512,128]{1,0:T(8,128)(2,1)S(1)} fusion(f32[2048,512]{1,0:T(8,128)S(1)} %get-tuple-element.18, f32[512]{0:T(512)S(1)} %broadcast_maximum_fusion, s32[512]{0:T(512)S(1)} %broadcast_bitcast_fusion, s32[2048]{0:T(1024)S(1)} %bitcast.76, bf16[2048,256]{1,0:T(8,128)(2,1)S(1)} %bitcast.68, f32[512]{0:T(512)S(1)} %fusion.1), kind=kOutput, calls=%fused_computation.15 | convolution fusion | flops 274857984 | bytes 4864000 | tf_op jit(solution)/shard_map/grk,kgd->grd/dot_general | solution.py:137
  84.7 1.7 %fusion.26 = (bf16[128,16,256]{2,0,1:T(8,128)(2,1)S(1)}, bf16[128,16,256]{2,0,1:T(8,128)(2,1)S(1)}) fusion(bf16[256,16,256]{2,0,1:T(8,128)(2,1)} %collective-permute-done.6), kind=kLoop, calls=%fused_computation.47 | loop fusion | bytes 4194304 | tf_op jit(solution)/shard_map/slice | solution.py:152
  86.3 2.2 %pad_maximum_fusion.1 = (bf16[256,16,256]{2,0,1:T(8,128)(2,1)}, bf16[256,16,256]{2,0,1:T(8,128)(2,1)}) fusion(bf16[128,16,256]{2,0,1:T(8,128)(2,1)S(1)} %get-tuple-element.10, bf16[128,16,256]{2,0,1:T(8,128)(2,1)S(1)} %get-tuple-element.5, bf16[128,16,256]{2,0,1:T(8,128)(2,1)S(1)} %get-tuple-element.6, bf16[128,16,256]{2,0,1:T(8,128)(2,1)S(1)} %maximum_select_fusion.2), kind=kLoop, calls=%fused_computation.7 | loop fusion | flops 8388608 | bytes 8388608 | tf_op jit(solution)/shard_map/concatenate | solution.py:153
  88.6 3.9 %copy.23 = bf16[256,16,256]{0,2,1:T(8,128)(2,1)} copy(bf16[256,16,256]{2,0,1:T(8,128)(2,1)} %get-tuple-element.20) | data formatting | bytes 4194304 | tf_op jit(solution)/shard_map/concatenate | solution.py:153
  92.5 2.4 %fusion.18 = f32[128,4,4,256]{3,0,2,1:T(8,128)S(1)} fusion(bf16[4,4,256,256]{3,2,1,0:T(8,128)(2,1)} %bitcast.64, bf16[128,128]{1,0:T(8,128)(2,1)S(1)} %get-tuple-element.14, bf16[128,128]{1,0:T(8,128)(2,1)S(1)} %get-tuple-element.15), kind=kOutput, calls=%fused_computation.30 | convolution fusion | flops 268566528 | bytes 4259840 | tf_op jit(solution)/shard_map/dot_general | solution.py:163
  94.9 1.2 fusion.27
  96.1 0.5 copy-done.1
  96.6 2.9 %copy.22 = bf16[256,16,256]{0,2,1:T(8,128)(2,1)S(1)} copy(bf16[256,16,256]{2,0,1:T(8,128)(2,1)} %get-tuple-element.19) | data formatting | bytes 4194304 | tf_op jit(solution)/shard_map/concatenate | solution.py:153
  99.5 3.0 %fusion.6 = bf16[128,4,4,256]{3,0,1,2:T(8,128)(2,1)} fusion(f32[128,1,4,256]{3,0,2,1:T(8,128)} %get-tuple-element.8, f32[128,2,4,256]{3,0,2,1:T(8,128)S(1)} %slice-done, f32[128,1,4,256]{3,0,2,1:T(8,128)} %get-tuple-element.7, bf16[4,4,256,256]{3,2,1,0:T(8,128)(2,1)S(1)} %bitcast.65, bf16[128,128]{1,0:T(8,128)(2,1)S(1)} %get-tuple-element.16, ...), kind=kOutput, calls=%fused_computation.13 | convolution fusion | flops 270663680 | bytes 5308416 | tf_op jit(solution)/shard_map/dot_general | solution.py:163
  102.5 1.6 %copy.24 = bf16[128,4,4,256]{0,3,2,1:T(8,128)(2,1)S(1)} copy(bf16[128,4,4,256]{3,0,1,2:T(8,128)(2,1)} %fusion.6) | data formatting | bytes 2097152 | tf_op jit(solution)/shard_map/convert_element_type | solution.py:168
  104.1 39.2 %all_to_all.5 = bf16[128,8,512]{0,2,1:T(8,128)(2,1)S(1)} all-to-all(bf16[128,8,512]{0,2,1:T(8,128)(2,1)S(1)} %bitcast.66), channel_id=1, replica_groups=mesh['dp'=4,'context'=16,'tensor'=8] {'tensor'}, dimensions={1} | all-to-all | bytes 2097152 | tf_op jit(solution)/shard_map/all_to_all | solution.py:169
  143.5 0.8 copy.25
  (28 shorter events, 1.3 us)
Async XLA Ops:
  0.0 80.1 %copy-start = (s32[2048]{0:T(1024)S(1)}, s32[2048]{0:T(1024)}, u32[]{:S(2)}) copy-start(s32[2048]{0:T(1024)} %param.9) | copy-start | bytes 24580
  1.7 7.1 %collective-permute-start = (bf16[128,1,768]{2,0,1:T(8,128)(2,1)S(1)}, bf16[128,1,768]{2,0,1:T(8,128)(2,1)S(1)}, u32[]{:S(2)}, u32[]{:S(2)}) collective-permute-start(bf16[128,1,768]{2,0,1:T(8,128)(2,1)S(1)} %maximum_bitcast_fusion), channel_id=1, source_target_pairs={{0,32},{8,40},{16,48},{24,56},{32,0},{40,8},{48,16},{56,24},{64,96... | collective-permute-start | bytes 589832 | tf_op jit(solution)/shard_map/ppermute | solution.py:51
  8.8 22.0 %collective-permute-start.1 = (bf16[128,2,768]{2,0,1:T(8,128)(2,1)S(1)}, bf16[128,2,768]{2,0,1:T(8,128)(2,1)S(1)}, u32[]{:S(2)}, u32[]{:S(2)}) collective-permute-start(bf16[128,2,768]{2,0,1:T(8,128)(2,1)S(1)} %maximum_select_fusion.5), channel_id=1, source_target_pairs={{0,64},{8,72},{16,80},{24,88},{32,96},{40,104},{48,112},{56,120},{... | collective-permute-start | bytes 1179656 | tf_op jit(solution)/shard_map/ppermute | solution.py:51
  31.0 14.1 %collective-permute-start.2 = (bf16[128,4,512]{2,0,1:T(8,128)(2,1)S(1)}, bf16[128,4,512]{2,0,1:T(8,128)(2,1)S(1)}, u32[]{:S(2)}, u32[]{:S(2)}) collective-permute-start(bf16[128,4,512]{2,0,1:T(8,128)(2,1)S(1)} %slice.56), channel_id=1, source_target_pairs={{0,8},{8,0},{16,24},{24,16},{32,40},{40,32},{48,56},{56,48},{64,72... | collective-permute-start | bytes 1572872 | tf_op jit(solution)/shard_map/ppermute | solution.py:51
  34.8 15.3 %collective-permute-start.4 = (bf16[128,4,256]{2,0,1:T(8,128)(2,1)S(1)}, bf16[128,4,256]{2,0,1:T(8,128)(2,1)S(1)}, u32[]{:S(2)}, u32[]{:S(2)}) collective-permute-start(bf16[128,4,256]{2,0,1:T(8,128)(2,1)S(1)} %slice.61), channel_id=1, source_target_pairs={{0,24},{8,16},{16,8},{24,0},{32,56},{40,48},{48,40},{56,32},{64,88... | collective-permute-start | bytes 786440 | tf_op jit(solution)/shard_map/ppermute | solution.py:51
  45.2 25.9 %collective-permute-start.3 = (bf16[128,8,512]{2,0,1:T(8,128)(2,1)S(1)}, bf16[128,8,512]{2,0,1:T(8,128)(2,1)}, u32[]{:S(2)}, u32[]{:S(2)}) collective-permute-start(bf16[128,8,512]{2,0,1:T(8,128)(2,1)S(1)} %maximum_select_fusion.1), channel_id=1, source_target_pairs={{0,24},{8,16},{16,8},{24,0},{32,56},{40,48},{48,40},{56,32},{64,88... | collective-permute-start | bytes 3145736 | tf_op jit(solution)/shard_map/ppermute | solution.py:51
  50.2 12.8 %collective-permute-start.5 = (bf16[128,8,256]{2,0,1:T(8,128)(2,1)S(1)}, bf16[128,8,256]{2,0,1:T(8,128)(2,1)S(1)}, u32[]{:S(2)}, u32[]{:S(2)}) collective-permute-start(bf16[128,8,256]{2,0,1:T(8,128)(2,1)S(1)} %maximum_select_fusion.4), channel_id=1, source_target_pairs={{0,8},{8,0},{16,24},{24,16},{32,40},{40,32},{48,56},{56,48},{64,72... | collective-permute-start | bytes 1572872 | tf_op jit(solution)/shard_map/ppermute | solution.py:51
  73.3 6.6 %copy-start.2 = (bf16[128,512]{1,0:T(8,128)(2,1)S(1)}, bf16[128,512]{1,0:T(8,128)(2,1)}, u32[]{:S(2)}) copy-start(bf16[128,512]{1,0:T(8,128)(2,1)} %param.6) | copy-start | bytes 393220
  73.3 7.0 %copy-start.3 = (s32[16]{0:T(128)S(1)}, s32[16]{0:T(128)}, u32[]{:S(2)}) copy-start(s32[16]{0:T(128)} %constant.64) | copy-start | bytes 196
  74.8 9.9 %collective-permute-start.6 = (bf16[256,16,256]{2,0,1:T(8,128)(2,1)}, bf16[256,16,256]{2,0,1:T(8,128)(2,1)}, u32[]{:S(2)}, u32[]{:S(2)}) collective-permute-start(bf16[256,16,256]{2,0,1:T(8,128)(2,1)} %pad_maximum_fusion), channel_id=1, source_target_pairs={{0,128},{128,0},{256,384},{384,256},{1,129},{129,1},{257,385},{385... | collective-permute-start | bytes 6291464 | tf_op jit(solution)/shard_map/ppermute | solution.py:109
  94.9 1.7 %copy-start.1 = (f32[128,4,4,256]{3,0,2,1:T(8,128)}, f32[128,4,4,256]{3,0,2,1:T(8,128)S(1)}, u32[]{:S(2)}) copy-start(f32[128,4,4,256]{3,0,2,1:T(8,128)S(1)} %fusion.18) | copy-start | bytes 6291460
  96.6 2.9 %slice-start = ((f32[128,4,4,256]{3,0,2,1:T(8,128)}), f32[128,2,4,256]{3,0,2,1:T(8,128)S(1)}, s32[]{:S(2)}) async-start(f32[128,4,4,256]{3,0,2,1:T(8,128)} %copy-done.1), calls=%async_computation.1 | async-start | bytes 2097152 | tf_op jit(solution)/shard_map/slice | solution.py:73

commit v7 on v6

--- a/solution.py
+++ b/solution.py
@@ -74,6 +74,24 @@
     return jnp.swapaxes(product, 1, 2).reshape(rows, -1)
 
 
+def restack(stack, sources, target, x_size):
+    rows, count = stack.shape[:2]
+    y_count = count // x_size
+    x_from = [sources[ix * y_count] for ix in range(x_size)]
+    x_to = [target[ix * y_count] for ix in range(x_size)]
+    assert all(
+        sources[ix * y_count + iy] - x_from[ix] == target[ix * y_count + iy] - x_to[ix]
+        for ix in range(x_size)
+        for iy in range(y_count)
+    )
+    picks = [x_from.index(x) for x in x_to]
+    if picks == list(range(x_size)):
+        return stack
+    stack = stack.reshape(rows, x_size, y_count, -1)
+    stack = jnp.concatenate([stack[:, i : i + 1] for i in picks], axis=1)
+    return stack.reshape(rows, count, -1)
+
+
 def per_device(queries, keys, values, order, out_weight):
     row_count = queries.shape[0]
     local_groups = keys.shape[1] // HEAD_SIZE
@@ -88,27 +106,32 @@
     half_rows = weight_rows // 2
     quarter = half_rows // 2
     mine = lax.dynamic_slice_in_dim(out_weight, core * half_rows, half_rows, 0)
-    kv_width = keys.shape[1] + values.shape[1]
     steps_a = chain_plan(context_size, x_size, 1)
     steps_b = chain_plan(context_size, x_size, 3)
     shared = 0
     while shared < min(len(steps_a), len(steps_b)) and steps_a[shared] == steps_b[shared]:
         shared += 1
-    block = jnp.concatenate([keys, values, mine[:quarter], mine[quarter:]], axis=1)[:, None, :]
+    key_width = keys.shape[1]
+    block = jnp.concatenate([keys, mine[:quarter], values, mine[quarter:]], axis=1)[:, None, :]
     gathered = exchange_gather(block, steps_a[:shared], "context", context_size)
     gathered_a = exchange_gather(
-        gathered[:, :, : kv_width + weight_cols], steps_a[shared:], "context", context_size
+        gathered[:, :, : key_width + weight_cols], steps_a[shared:], "context", context_size
     )
     gathered_b = exchange_gather(
-        gathered[:, :, kv_width + weight_cols :], steps_b[shared:], "context", context_size
+        gathered[:, :, key_width + weight_cols :], steps_b[shared:], "context", context_size
     )
     sources_a = stacked_sources(context_size, steps_a)
     sources_b = stacked_sources(context_size, steps_b)
 
-    mine_weights = jnp.concatenate([gathered_a[:, :, kv_width:], gathered_b], axis=0)
+    mine_weights = jnp.concatenate(
+        [gathered_a[:, :, key_width:], gathered_b[:, :, values.shape[1] :]], axis=0
+    )
     other_weights = lax.ppermute(mine_weights, "dp", [(i, i ^ 1) for i in range(dp_size)])
 
-    kv_all = jnp.swapaxes(gathered_a[:, :, :kv_width], 0, 1).reshape(context_size * row_count, kv_width)
+    key_stack = gathered_a[:, :, :key_width]
+    value_stack = restack(gathered_b[:, :, : values.shape[1]], sources_b, sources_a, x_size)
+    key_part = jnp.swapaxes(key_stack, 0, 1).reshape(context_size * row_count, key_width)
+    value_part = jnp.swapaxes(value_stack, 0, 1).reshape(context_size * row_count, -1)
     key_pos = order.reshape(context_size, row_count)[jnp.array(sources_a)].reshape(-1)
 
     first_row = lax.axis_index("context") * row_count
@@ -119,8 +142,6 @@
     )
     stacked_pos = jnp.tile(query_pos, query_head_group)
     stacked_rows = query_head_group * row_count
-    key_part = kv_all[:, : keys.shape[1]]
-    value_part = kv_all[:, keys.shape[1] :]
     key_count = key_part.shape[0]
     running_max = jnp.full((local_groups, stacked_rows), -1e30, jnp.float32)
     key_heads = key_part.reshape(key_count, local_groups, HEAD_SIZE)

time: 146 us -> 143 us (0.979)
  waiting for transfers between devices: 44.7 us -> 40.4 us
    ppermute x6, waiting for transfers between devices: 44.7 us -> 40.4 us  [exchange_gather(): lax.ppermute(stack, axis_name, [(i, i ^ mask) for i in range(count)])]
    ppermute x6, starting transfers between devices: 23.9 us -> 22.5 us  [exchange_gather(): lax.ppermute(stack, axis_name, [(i, i ^ mask) for i in range(count)])]
  transfers between devices with their start and end apart: 7 -> 7, of which waited for: 5 -> 6; matrix products, arithmetic and copies ran while one was open for 4% -> 5% of each run, Pallas kernels for 0% -> 0%
where the time goes in v7:
time: 143 us; the launch traced here: 141 us
  waiting for transfers between devices  40.4 us (28%)
  blocking collectives  39 us (27%)
  starting transfers between devices  28.6 us (20%)
  local copies, waits for them, and re-layouts  16.1 us (11%)
  other arithmetic  8.59 us (6%)
  matrix products  7.76 us (5%)
    ppermute x6, waiting for transfers between devices, exchange_gather(): lax.ppermute(stack, axis_name, [(i, i ^ mask) for i in range(count)])  40.4 us
    all_to_all x1, blocking collectives, per_device(): pieces = lax.all_to_all(pieces, 'tensor', 1, 1, tiled=True)  39 us
    ppermute x6, starting transfers between devices, exchange_gather(): lax.ppermute(stack, axis_name, [(i, i ^ mask) for i in range(count)])  22.5 us
    concatenate x2, local copies, waits for them, and re-layouts, per_device(): jnp.concatenate([mine_piece, other_piece], axis=0).reshape(2 * quarter, -1)  6.87 us
    ppermute x1, starting transfers between devices, per_device(): lax.ppermute(mine_weights, 'dp', [(i, i ^ 1) for i in range(dp_size)])  6.13 us
    dot_general x2, matrix products, per_device(): jnp.dot(piece_rows, piece_weight, preferred_element_type=jnp.float32)  5.4 us
  transfers between devices with their start and end apart: 7, of which 6 were waited for; matrix products, arithmetic and copies ran while one was open for 5% of the time, Pallas kernels for 0%

profile of v7, /device:TPU:1, one launch (start us, length us, event | category | flops | bytes accessed | tf_op | source)
XLA Modules:
  0.0 140.9 jit_solution(9503163018761130474)
XLA Ops:
  0.0 0.9 constant_dynamic-slice_fusion
  0.9 0.8 maximum_bitcast_fusion
  1.7 4.0 %collective-permute-start = (bf16[128,1,768]{2,0,1:T(8,128)(2,1)S(1)}, bf16[128,1,768]{2,0,1:T(8,128)(2,1)S(1)}, u32[]{:S(2)}, u32[]{:S(2)}) collective-permute-start(bf16[128,1,768]{2,0,1:T(8,128)(2,1)S(1)} %maximum_bitcast_fusion), channel_id=1, source_target_pairs={{0,32},{8,40},{16,48},{24,56},{32,0},{40,8},{48,16},{56,24},{64,96... | collective-permute-start | bytes 589832 | tf_op jit(solution)/shard_map/ppermute | solution.py:51
  5.7 3.0 %collective-permute-done = bf16[128,1,768]{2,0,1:T(8,128)(2,1)S(1)} collective-permute-done((bf16[128,1,768]{2,0,1:T(8,128)(2,1)S(1)}, bf16[128,1,768]{2,0,1:T(8,128)(2,1)S(1)}, u32[]{:S(2)}, u32[]{:S(2)}) %collective-permute-start) | collective-permute-done | bytes 196640 | tf_op jit(solution)/shard_map/ppermute | solution.py:51
  8.8 5.6 %collective-permute-start.1 = (bf16[128,2,768]{2,0,1:T(8,128)(2,1)S(1)}, bf16[128,2,768]{2,0,1:T(8,128)(2,1)S(1)}, u32[]{:S(2)}, u32[]{:S(2)}) collective-permute-start(bf16[128,2,768]{2,0,1:T(8,128)(2,1)S(1)} %maximum_select_fusion.5), channel_id=1, source_target_pairs={{0,64},{8,72},{16,80},{24,88},{32,96},{40,104},{48,112},{56,120},{... | collective-permute-start | bytes 1179656 | tf_op jit(solution)/shard_map/ppermute | solution.py:51
  14.5 16.3 %collective-permute-done.1 = bf16[128,2,768]{2,0,1:T(8,128)(2,1)S(1)} collective-permute-done((bf16[128,2,768]{2,0,1:T(8,128)(2,1)S(1)}, bf16[128,2,768]{2,0,1:T(8,128)(2,1)S(1)}, u32[]{:S(2)}, u32[]{:S(2)}) %collective-permute-start.1) | collective-permute-done | bytes 393248 | tf_op jit(solution)/shard_map/ppermute | solution.py:51
  31.1 5.1 %collective-permute-start.4 = (bf16[128,4,384]{2,0,1:T(8,128)(2,1)S(1)}, bf16[128,4,384]{2,0,1:T(8,128)(2,1)S(1)}, u32[]{:S(2)}, u32[]{:S(2)}) collective-permute-start(bf16[128,4,384]{2,0,1:T(8,128)(2,1)S(1)} %get-tuple-element.9), channel_id=1, source_target_pairs={{0,24},{8,16},{16,8},{24,0},{32,56},{40,48},{48,40},{56,32},{64,88... | collective-permute-start | bytes 1179656 | tf_op jit(solution)/shard_map/ppermute | solution.py:51
  36.1 1.9 %collective-permute-start.2 = (bf16[128,4,384]{2,0,1:T(8,128)(2,1)S(1)}, bf16[128,4,384]{2,0,1:T(8,128)(2,1)S(1)}, u32[]{:S(2)}, u32[]{:S(2)}) collective-permute-start(bf16[128,4,384]{2,0,1:T(8,128)(2,1)S(1)} %get-tuple-element.10), channel_id=1, source_target_pairs={{0,8},{8,0},{16,24},{24,16},{32,40},{40,32},{48,56},{56,48},{64,72... | collective-permute-start | bytes 1179656 | tf_op jit(solution)/shard_map/ppermute | solution.py:51
  38.1 5.6 %collective-permute-done.4 = bf16[128,4,384]{2,0,1:T(8,128)(2,1)S(1)} collective-permute-done((bf16[128,4,384]{2,0,1:T(8,128)(2,1)S(1)}, bf16[128,4,384]{2,0,1:T(8,128)(2,1)S(1)}, u32[]{:S(2)}, u32[]{:S(2)}) %collective-permute-start.4) | collective-permute-done | bytes 393248 | tf_op jit(solution)/shard_map/ppermute | solution.py:51
  43.8 2.2 %collective-permute-start.5 = (bf16[128,8,384]{2,0,1:T(8,128)(2,1)S(1)}, bf16[128,8,384]{2,0,1:T(8,128)(2,1)S(1)}, u32[]{:S(2)}, u32[]{:S(2)}) collective-permute-start(bf16[128,8,384]{2,0,1:T(8,128)(2,1)S(1)} %maximum_select_fusion.4), channel_id=1, source_target_pairs={{0,8},{8,0},{16,24},{24,16},{32,40},{40,32},{48,56},{56,48},{64,72... | collective-permute-start | bytes 2359304 | tf_op jit(solution)/shard_map/ppermute | solution.py:51
  46.1 0.8 collective-permute-done.2
  47.0 3.6 %collective-permute-start.3 = (bf16[128,8,384]{2,0,1:T(8,128)(2,1)S(1)}, bf16[128,8,384]{2,0,1:T(8,128)(2,1)}, u32[]{:S(2)}, u32[]{:S(2)}) collective-permute-start(bf16[128,8,384]{2,0,1:T(8,128)(2,1)S(1)} %maximum_select_fusion.3), channel_id=1, source_target_pairs={{0,24},{8,16},{16,8},{24,0},{32,56},{40,48},{48,40},{56,32},{64,88... | collective-permute-start | bytes 2359304 | tf_op jit(solution)/shard_map/ppermute | solution.py:51
  51.0 12.9 %collective-permute-done.5 = bf16[128,8,384]{2,0,1:T(8,128)(2,1)S(1)} collective-permute-done((bf16[128,8,384]{2,0,1:T(8,128)(2,1)S(1)}, bf16[128,8,384]{2,0,1:T(8,128)(2,1)S(1)}, u32[]{:S(2)}, u32[]{:S(2)}) %collective-permute-start.5) | collective-permute-done | bytes 786464 | tf_op jit(solution)/shard_map/ppermute | solution.py:51
  64.3 1.7 %collective-permute-done.3 = bf16[128,8,384]{2,0,1:T(8,128)(2,1)} collective-permute-done((bf16[128,8,384]{2,0,1:T(8,128)(2,1)S(1)}, bf16[128,8,384]{2,0,1:T(8,128)(2,1)}, u32[]{:S(2)}, u32[]{:S(2)}) %collective-permute-start.3) | collective-permute-done | bytes 786464 | tf_op jit(solution)/shard_map/ppermute | solution.py:51
  66.0 1.6 %maximum_select_fusion = bf16[128,16,384]{2,0,1:T(8,128)(2,1)S(1)} fusion(bf16[128,8,384]{2,0,1:T(8,128)(2,1)S(1)} %maximum_select_fusion.3, bf16[128,8,384]{2,0,1:T(8,128)(2,1)} %collective-permute-done.3, pred[]{:T(512)S(6)} %ne.22), kind=kLoop, calls=%fused_computation.12 | loop fusion | flops 2359296 | bytes 3145729 | tf_op jit(solution)/shard_map/jit(_where)/select_n | solution.py:52
  67.7 1.7 %pad_maximum_fusion = bf16[256,16,256]{2,0,1:T(8,128)(2,1)} fusion(bf16[128,16,256]{2,0,1:T(8,128)(2,1)S(1)} %slice.77, bf16[128,16,256]{2,0,1:T(8,128)(2,1)S(1)} %slice.78), kind=kLoop, calls=%fused_computation.6 | loop fusion | flops 4194304 | bytes 4194304 | tf_op jit(solution)/shard_map/concatenate | solution.py:126
  69.5 6.1 %collective-permute-start.6 = (bf16[256,16,256]{2,0,1:T(8,128)(2,1)}, bf16[256,16,256]{2,0,1:T(8,128)(2,1)}, u32[]{:S(2)}, u32[]{:S(2)}) collective-permute-start(bf16[256,16,256]{2,0,1:T(8,128)(2,1)} %pad_maximum_fusion), channel_id=1, source_target_pairs={{0,128},{128,0},{256,384},{384,256},{1,129},{129,1},{257,385},{385... | collective-permute-start | bytes 6291464 | tf_op jit(solution)/shard_map/ppermute | solution.py:129
  75.6 0.6 gather_fusion
  76.2 1.1 slice.73
  77.5 0.7 fusion
  78.3 1.3 fusion.1
  79.5 1.6 %fusion.10 = bf16[512,128]{1,0:T(8,128)(2,1)S(1)} fusion(bf16[2048,128]{1,0:T(8,128)(2,1)S(1)} %bitcast.78, f32[2048,512]{1,0:T(8,128)S(1)} %get-tuple-element.20, f32[512]{0:T(512)S(1)} %broadcast_maximum_fusion, s32[512]{0:T(512)S(1)} %broadcast_bitcast_fusion, s32[2048]{0:T(1024)S(1)} %bitcast.86, f32[512]{0:T(512)S(1)} %fusion.1), kind=kOutput, calls=%fused_computation.16 | convolution fusion | flops 274857984 | bytes 4864000 | tf_op jit(solution)/shard_map/grk,kgd->grd/dot_general | solution.py:158
  81.3 1.7 %fusion.23 = (bf16[128,16,256]{2,0,1:T(8,128)(2,1)S(1)}, bf16[128,16,256]{2,0,1:T(8,128)(2,1)S(1)}) fusion(bf16[256,16,256]{2,0,1:T(8,128)(2,1)} %collective-permute-done.6), kind=kLoop, calls=%fused_computation.45 | loop fusion | bytes 4194304 | tf_op jit(solution)/shard_map/slice | solution.py:173
  83.0 2.2 %pad_maximum_fusion.1 = (bf16[256,16,256]{2,0,1:T(8,128)(2,1)}, bf16[256,16,256]{2,0,1:T(8,128)(2,1)}) fusion(bf16[128,16,256]{2,0,1:T(8,128)(2,1)S(1)} %slice.77, bf16[128,16,256]{2,0,1:T(8,128)(2,1)S(1)} %get-tuple-element.5, bf16[128,16,256]{2,0,1:T(8,128)(2,1)S(1)} %get-tuple-element.6, bf16[128,16,256]{2,0,1:T(8,128)(2,1)S(1)} %slice.78), kind=kLoop, calls=%fused_computation.7 | loop fusion | flops 8388608 | bytes 8388608 | tf_op jit(solution)/shard_map/concatenate | solution.py:174
  85.3 3.9 %copy.23 = bf16[256,16,256]{0,2,1:T(8,128)(2,1)} copy(bf16[256,16,256]{2,0,1:T(8,128)(2,1)} %get-tuple-element.22) | data formatting | bytes 4194304 | tf_op jit(solution)/shard_map/concatenate | solution.py:174
  89.2 2.4 %fusion.15 = f32[128,4,4,256]{3,0,2,1:T(8,128)S(1)} fusion(bf16[4,4,256,256]{3,2,1,0:T(8,128)(2,1)} %bitcast.72, bf16[128,128]{1,0:T(8,128)(2,1)S(1)} %get-tuple-element.16, bf16[128,128]{1,0:T(8,128)(2,1)S(1)} %get-tuple-element.17), kind=kOutput, calls=%fused_computation.28 | convolution fusion | flops 268566528 | bytes 4259840 | tf_op jit(solution)/shard_map/dot_general | solution.py:184
  91.6 1.2 fusion.24
  93.3 2.9 %copy.22 = bf16[256,16,256]{0,2,1:T(8,128)(2,1)S(1)} copy(bf16[256,16,256]{2,0,1:T(8,128)(2,1)} %get-tuple-element.21) | data formatting | bytes 4194304 | tf_op jit(solution)/shard_map/concatenate | solution.py:174
  96.3 3.0 %fusion.6 = bf16[128,4,4,256]{3,0,1,2:T(8,128)(2,1)} fusion(f32[128,1,4,256]{3,0,2,1:T(8,128)} %get-tuple-element.8, f32[128,2,4,256]{3,0,2,1:T(8,128)S(1)} %slice-done, f32[128,1,4,256]{3,0,2,1:T(8,128)} %get-tuple-element.7, bf16[4,4,256,256]{3,2,1,0:T(8,128)(2,1)S(1)} %bitcast.73, bf16[128,128]{1,0:T(8,128)(2,1)S(1)} %get-tuple-element.18, ...), kind=kOutput, calls=%fused_computation.14 | convolution fusion | flops 270663680 | bytes 5308416 | tf_op jit(solution)/shard_map/dot_general | solution.py:184
  99.3 1.6 %copy.24 = bf16[128,4,4,256]{0,3,2,1:T(8,128)(2,1)S(1)} copy(bf16[128,4,4,256]{3,0,1,2:T(8,128)(2,1)} %fusion.6) | data formatting | bytes 2097152 | tf_op jit(solution)/shard_map/convert_element_type | solution.py:189
  100.9 39.0 %all_to_all.5 = bf16[128,8,512]{0,2,1:T(8,128)(2,1)S(1)} all-to-all(bf16[128,8,512]{0,2,1:T(8,128)(2,1)S(1)} %bitcast.75), channel_id=1, replica_groups=mesh['dp'=4,'context'=16,'tensor'=8] {'tensor'}, dimensions={1} | all-to-all | bytes 2097152 | tf_op jit(solution)/shard_map/all_to_all | solution.py:190
  140.1 0.8 copy.25
  (38 shorter events, 2.3 us)
Async XLA Ops:
  0.0 50.9 %copy-start = (s32[2048]{0:T(1024)S(1)}, s32[2048]{0:T(1024)}, u32[]{:S(2)}) copy-start(s32[2048]{0:T(1024)} %param.9) | copy-start | bytes 24580
  1.7 7.1 %collective-permute-start = (bf16[128,1,768]{2,0,1:T(8,128)(2,1)S(1)}, bf16[128,1,768]{2,0,1:T(8,128)(2,1)S(1)}, u32[]{:S(2)}, u32[]{:S(2)}) collective-permute-start(bf16[128,1,768]{2,0,1:T(8,128)(2,1)S(1)} %maximum_bitcast_fusion), channel_id=1, source_target_pairs={{0,32},{8,40},{16,48},{24,56},{32,0},{40,8},{48,16},{56,24},{64,96... | collective-permute-start | bytes 589832 | tf_op jit(solution)/shard_map/ppermute | solution.py:51
  8.8 22.0 %collective-permute-start.1 = (bf16[128,2,768]{2,0,1:T(8,128)(2,1)S(1)}, bf16[128,2,768]{2,0,1:T(8,128)(2,1)S(1)}, u32[]{:S(2)}, u32[]{:S(2)}) collective-permute-start(bf16[128,2,768]{2,0,1:T(8,128)(2,1)S(1)} %maximum_select_fusion.5), channel_id=1, source_target_pairs={{0,64},{8,72},{16,80},{24,88},{32,96},{40,104},{48,112},{56,120},{... | collective-permute-start | bytes 1179656 | tf_op jit(solution)/shard_map/ppermute | solution.py:51
  30.9 19.7 %copy-start.4 = (bf16[128,512]{1,0:T(8,128)(2,1)S(1)}, bf16[128,512]{1,0:T(8,128)(2,1)}, u32[]{:S(2)}) copy-start(bf16[128,512]{1,0:T(8,128)(2,1)} %param.6) | copy-start | bytes 393220
  31.1 12.6 %collective-permute-start.4 = (bf16[128,4,384]{2,0,1:T(8,128)(2,1)S(1)}, bf16[128,4,384]{2,0,1:T(8,128)(2,1)S(1)}, u32[]{:S(2)}, u32[]{:S(2)}) collective-permute-start(bf16[128,4,384]{2,0,1:T(8,128)(2,1)S(1)} %get-tuple-element.9), channel_id=1, source_target_pairs={{0,24},{8,16},{16,8},{24,0},{32,56},{40,48},{48,40},{56,32},{64,88... | collective-permute-start | bytes 1179656 | tf_op jit(solution)/shard_map/ppermute | solution.py:51
  36.1 10.8 %collective-permute-start.2 = (bf16[128,4,384]{2,0,1:T(8,128)(2,1)S(1)}, bf16[128,4,384]{2,0,1:T(8,128)(2,1)S(1)}, u32[]{:S(2)}, u32[]{:S(2)}) collective-permute-start(bf16[128,4,384]{2,0,1:T(8,128)(2,1)S(1)} %get-tuple-element.10), channel_id=1, source_target_pairs={{0,8},{8,0},{16,24},{24,16},{32,40},{40,32},{48,56},{56,48},{64,72... | collective-permute-start | bytes 1179656 | tf_op jit(solution)/shard_map/ppermute | solution.py:51
  43.8 20.1 %collective-permute-start.5 = (bf16[128,8,384]{2,0,1:T(8,128)(2,1)S(1)}, bf16[128,8,384]{2,0,1:T(8,128)(2,1)S(1)}, u32[]{:S(2)}, u32[]{:S(2)}) collective-permute-start(bf16[128,8,384]{2,0,1:T(8,128)(2,1)S(1)} %maximum_select_fusion.4), channel_id=1, source_target_pairs={{0,8},{8,0},{16,24},{24,16},{32,40},{40,32},{48,56},{56,48},{64,72... | collective-permute-start | bytes 2359304 | tf_op jit(solution)/shard_map/ppermute | solution.py:51
  47.0 18.9 %collective-permute-start.3 = (bf16[128,8,384]{2,0,1:T(8,128)(2,1)S(1)}, bf16[128,8,384]{2,0,1:T(8,128)(2,1)}, u32[]{:S(2)}, u32[]{:S(2)}) collective-permute-start(bf16[128,8,384]{2,0,1:T(8,128)(2,1)S(1)} %maximum_select_fusion.3), channel_id=1, source_target_pairs={{0,24},{8,16},{16,8},{24,0},{32,56},{40,48},{48,40},{56,32},{64,88... | collective-permute-start | bytes 2359304 | tf_op jit(solution)/shard_map/ppermute | solution.py:51
  64.2 3.5 %copy-start.2 = (bf16[128,16,384]{2,0,1:T(8,128)(2,1)}, bf16[128,16,384]{2,0,1:T(8,128)(2,1)S(1)}, u32[]{:S(2)}) copy-start(bf16[128,16,384]{2,0,1:T(8,128)(2,1)S(1)} %maximum_select_fusion.1) | copy-start | bytes 4718596
  67.6 1.8 %copy-start.3 = (bf16[128,16,384]{2,0,1:T(8,128)(2,1)}, bf16[128,16,384]{2,0,1:T(8,128)(2,1)S(1)}, u32[]{:S(2)}) copy-start(bf16[128,16,384]{2,0,1:T(8,128)(2,1)S(1)} %maximum_select_fusion) | copy-start | bytes 4718596
  67.7 7.9 %copy-start.5 = (s32[16]{0:T(128)S(1)}, s32[16]{0:T(128)}, u32[]{:S(2)}) copy-start(s32[16]{0:T(128)} %constant.64) | copy-start | bytes 196
  69.5 11.9 %collective-permute-start.6 = (bf16[256,16,256]{2,0,1:T(8,128)(2,1)}, bf16[256,16,256]{2,0,1:T(8,128)(2,1)}, u32[]{:S(2)}, u32[]{:S(2)}) collective-permute-start(bf16[256,16,256]{2,0,1:T(8,128)(2,1)} %pad_maximum_fusion), channel_id=1, source_target_pairs={{0,128},{128,0},{256,384},{384,256},{1,129},{129,1},{257,385},{385... | collective-permute-start | bytes 6291464 | tf_op jit(solution)/shard_map/ppermute | solution.py:129
  76.2 1.3 slice-start.1
  91.6 1.7 %copy-start.1 = (f32[128,4,4,256]{3,0,2,1:T(8,128)}, f32[128,4,4,256]{3,0,2,1:T(8,128)S(1)}, u32[]{:S(2)}) copy-start(f32[128,4,4,256]{3,0,2,1:T(8,128)S(1)} %fusion.15) | copy-start | bytes 6291460
  93.3 2.9 %slice-start = ((f32[128,4,4,256]{3,0,2,1:T(8,128)}), f32[128,2,4,256]{3,0,2,1:T(8,128)S(1)}, s32[]{:S(2)}) async-start(f32[128,4,4,256]{3,0,2,1:T(8,128)} %copy-done.1), calls=%async_computation.1 | async-start | bytes 2097152 | tf_op jit(solution)/shard_map/slice | solution.py:73

commit v8 on v7

--- a/solution.py
+++ b/solution.py
@@ -112,7 +112,10 @@
     while shared < min(len(steps_a), len(steps_b)) and steps_a[shared] == steps_b[shared]:
         shared += 1
     key_width = keys.shape[1]
-    block = jnp.concatenate([keys, mine[:quarter], values, mine[quarter:]], axis=1)[:, None, :]
+    quarters = [
+        mine[k * quarter : (k + 1) * quarter].T.reshape(row_count, -1) for k in range(2)
+    ]
+    block = jnp.concatenate([keys, quarters[0], values, quarters[1]], axis=1)[:, None, :]
     gathered = exchange_gather(block, steps_a[:shared], "context", context_size)
     gathered_a = exchange_gather(
         gathered[:, :, : key_width + weight_cols], steps_a[shared:], "context", context_size
@@ -169,21 +172,18 @@
 
     total = None
     for piece, sources in ((0, sources_a), (1, sources_b)):
-        mine_piece = mine_weights[piece * quarter : (piece + 1) * quarter]
-        other_piece = other_weights[piece * quarter : (piece + 1) * quarter]
-        piece_weight = jnp.concatenate([mine_piece, other_piece], axis=0).reshape(2 * quarter, -1)
-        piece_rows = jnp.concatenate(
-            [
-                lax.dynamic_slice_in_dim(attended, core * half_rows + piece * quarter, quarter, 1),
-                lax.dynamic_slice_in_dim(
-                    attended, (1 - core) * half_rows + piece * quarter, quarter, 1
-                ),
-            ],
-            axis=1,
-        )
-        product_out = jnp.dot(piece_rows, piece_weight, preferred_element_type=jnp.float32)
-        product_out = unpermute_blocks(product_out, sources, x_size)
-        total = product_out if total is None else total + product_out
+        for which, held in ((0, mine_weights), (1, other_weights)):
+            piece_t = held[piece * row_count : (piece + 1) * row_count]
+            piece_t = jnp.swapaxes(piece_t, 0, 1).reshape(context_size, weight_cols, quarter)
+            owner = core if which == 0 else 1 - core
+            piece_rows = lax.dynamic_slice_in_dim(
+                attended, owner * half_rows + piece * quarter, quarter, 1
+            )
+            product_out = jnp.einsum(
+                "rh,nkh->rnk", piece_rows, piece_t, preferred_element_type=jnp.float32
+            ).reshape(row_count, -1)
+            product_out = unpermute_blocks(product_out, sources, x_size)
+            total = product_out if total is None else total + product_out
     partial_out = total
     tensor_size = lax.axis_size("tensor")
     pieces = partial_out.astype(jnp.bfloat16).reshape(row_count, tensor_size, -1)

time: 143 us -> 140 us (0.979)
  other arithmetic: 8.59 us -> 4.8 us
  waiting for transfers between devices: 40.4 us -> 38.1 us
  matrix products: 7.76 us -> 10 us
    concatenate x2 -> x0, local copies, waits for them, and re-layouts: 6.87 us -> none  [per_device(): jnp.concatenate([mine_piece, other_piece], axis=0).reshape(2 * quarter, -1)]
    transpose x0 -> x6, local copies, waits for them, and re-layouts: none -> 4.11 us  [the longest x3 3 us: per_device(): jnp.swapaxes(piece_t, 0, 1).reshape(context_size, weight_cols, quarter)]
    dot_general x0 -> x4, local copies, waits for them, and re-layouts: none -> 3.45 us  [per_device(): jnp.einsum('rh,nkh->rnk', piece_rows, piece_t, preferred_element_type=jnp...]
    slice x5 -> x1, local copies, waits for them, and re-layouts: 2.83 us -> 0.09 us  [per_device(): gathered[:, :, :key_width + weight_cols]]
    unnamed x14, local copies, waits for them, and re-layouts: 0.68 us -> 3.04 us
    ppermute x6, waiting for transfers between devices: 40.4 us -> 38.1 us  [exchange_gather(): lax.ppermute(stack, axis_name, [(i, i ^ mask) for i in range(count)])]
    concatenate x1 -> x0, other arithmetic: 2.25 us -> none  [per_device(): jnp.concatenate([mine_piece, other_piece], axis=0).reshape(2 * quarter, -1)]
    dot_general x2 -> x4, matrix products: 5.4 us -> 7.64 us  [per_device(): jnp.einsum('rh,nkh->rnk', piece_rows, piece_t, preferred_element_type=jnp...]
  transfers between devices with their start and end apart: 7 -> 7, of which waited for: 6 -> 6; matrix products, arithmetic and copies ran while one was open for 5% -> 10% of each run, Pallas kernels for 0% -> 0%
where the time goes in v8:
time: 140 us; the launch traced here: 138 us
  blocking collectives  39 us (28%)
  waiting for transfers between devices  38.1 us (27%)
  starting transfers between devices  28.6 us (20%)
  local copies, waits for them, and re-layouts  17.4 us (12%)
  matrix products  10 us (7%)
  other arithmetic  4.8 us (3%)
    all_to_all x1, blocking collectives, per_device(): pieces = lax.all_to_all(pieces, 'tensor', 1, 1, tiled=True)  39 us
    ppermute x6, waiting for transfers between devices, exchange_gather(): lax.ppermute(stack, axis_name, [(i, i ^ mask) for i in range(count)])  38.1 us
    ppermute x6, starting transfers between devices, exchange_gather(): lax.ppermute(stack, axis_name, [(i, i ^ mask) for i in range(count)])  22.4 us
    dot_general x4, matrix products, per_device(): jnp.einsum('rh,nkh->rnk', piece_rows, piece_t, preferred_element_type=jnp...  7.64 us
    ppermute x1, starting transfers between devices, per_device(): lax.ppermute(mine_weights, 'dp', [(i, i ^ 1) for i in range(dp_size)])  6.14 us
    dot_general x4, local copies, waits for them, and re-layouts, per_device(): jnp.einsum('rh,nkh->rnk', piece_rows, piece_t, preferred_element_type=jnp...  3.45 us
    unnamed x14, local copies, waits for them, and re-layouts  3.04 us
    transpose x3, local copies, waits for them, and re-layouts, per_device(): jnp.swapaxes(piece_t, 0, 1).reshape(context_size, weight_cols, quarter)  3 us
  transfers between devices with their start and end apart: 7, of which 6 were waited for; matrix products, arithmetic and copies ran while one was open for 10% of the time, Pallas kernels for 0%

profile of v8, /device:TPU:1, one launch (start us, length us, event | category | flops | bytes accessed | tf_op | source)
XLA Modules:
  0.0 138.4 jit_solution(5962558584303970988)
XLA Ops:
  0.0 0.9 dynamic-slice_bitcast_fusion.1
  1.2 0.8 maximum_bitcast_fusion
  2.0 4.0 %collective-permute-start = (bf16[128,1,768]{2,0,1:T(8,128)(2,1)S(1)}, bf16[128,1,768]{2,0,1:T(8,128)(2,1)S(1)}, u32[]{:S(2)}, u32[]{:S(2)}) collective-permute-start(bf16[128,1,768]{2,0,1:T(8,128)(2,1)S(1)} %maximum_bitcast_fusion), channel_id=1, source_target_pairs={{0,32},{8,40},{16,48},{24,56},{32,0},{40,8},{48,16},{56,24},{64,96... | collective-permute-start | bytes 589832 | tf_op jit(solution)/shard_map/ppermute | solution.py:51
  6.1 3.0 %collective-permute-done = bf16[128,1,768]{2,0,1:T(8,128)(2,1)S(1)} collective-permute-done((bf16[128,1,768]{2,0,1:T(8,128)(2,1)S(1)}, bf16[128,1,768]{2,0,1:T(8,128)(2,1)S(1)}, u32[]{:S(2)}, u32[]{:S(2)}) %collective-permute-start) | collective-permute-done | bytes 196640 | tf_op jit(solution)/shard_map/ppermute | solution.py:51
  9.1 5.6 %collective-permute-start.1 = (bf16[128,2,768]{2,0,1:T(8,128)(2,1)S(1)}, bf16[128,2,768]{2,0,1:T(8,128)(2,1)S(1)}, u32[]{:S(2)}, u32[]{:S(2)}) collective-permute-start(bf16[128,2,768]{2,0,1:T(8,128)(2,1)S(1)} %maximum_select_fusion.5), channel_id=1, source_target_pairs={{0,64},{8,72},{16,80},{24,88},{32,96},{40,104},{48,112},{56,120},{... | collective-permute-start | bytes 1179656 | tf_op jit(solution)/shard_map/ppermute | solution.py:51
  14.8 16.3 %collective-permute-done.1 = bf16[128,2,768]{2,0,1:T(8,128)(2,1)S(1)} collective-permute-done((bf16[128,2,768]{2,0,1:T(8,128)(2,1)S(1)}, bf16[128,2,768]{2,0,1:T(8,128)(2,1)S(1)}, u32[]{:S(2)}, u32[]{:S(2)}) %collective-permute-start.1) | collective-permute-done | bytes 393248 | tf_op jit(solution)/shard_map/ppermute | solution.py:51
  31.4 5.1 %collective-permute-start.4 = (bf16[128,4,384]{2,0,1:T(8,128)(2,1)S(1)}, bf16[128,4,384]{2,0,1:T(8,128)(2,1)S(1)}, u32[]{:S(2)}, u32[]{:S(2)}) collective-permute-start(bf16[128,4,384]{2,0,1:T(8,128)(2,1)S(1)} %get-tuple-element.16), channel_id=1, source_target_pairs={{0,24},{8,16},{16,8},{24,0},{32,56},{40,48},{48,40},{56,32},{64,88... | collective-permute-start | bytes 1179656 | tf_op jit(solution)/shard_map/ppermute | solution.py:51
  36.4 1.9 %collective-permute-start.2 = (bf16[128,4,384]{2,0,1:T(8,128)(2,1)S(1)}, bf16[128,4,384]{2,0,1:T(8,128)(2,1)S(1)}, u32[]{:S(2)}, u32[]{:S(2)}) collective-permute-start(bf16[128,4,384]{2,0,1:T(8,128)(2,1)S(1)} %get-tuple-element.15), channel_id=1, source_target_pairs={{0,8},{8,0},{16,24},{24,16},{32,40},{40,32},{48,56},{56,48},{64,72... | collective-permute-start | bytes 1179656 | tf_op jit(solution)/shard_map/ppermute | solution.py:51
  38.4 5.6 %collective-permute-done.4 = bf16[128,4,384]{2,0,1:T(8,128)(2,1)S(1)} collective-permute-done((bf16[128,4,384]{2,0,1:T(8,128)(2,1)S(1)}, bf16[128,4,384]{2,0,1:T(8,128)(2,1)S(1)}, u32[]{:S(2)}, u32[]{:S(2)}) %collective-permute-start.4) | collective-permute-done | bytes 393248 | tf_op jit(solution)/shard_map/ppermute | solution.py:51
  44.1 2.2 %collective-permute-start.5 = (bf16[128,8,384]{2,0,1:T(8,128)(2,1)S(1)}, bf16[128,8,384]{2,0,1:T(8,128)(2,1)S(1)}, u32[]{:S(2)}, u32[]{:S(2)}) collective-permute-start(bf16[128,8,384]{2,0,1:T(8,128)(2,1)S(1)} %maximum_select_fusion.4), channel_id=1, source_target_pairs={{0,8},{8,0},{16,24},{24,16},{32,40},{40,32},{48,56},{56,48},{64,72... | collective-permute-start | bytes 2359304 | tf_op jit(solution)/shard_map/ppermute | solution.py:51
  46.4 0.8 collective-permute-done.2
  47.4 3.6 %collective-permute-start.3 = (bf16[128,8,384]{2,0,1:T(8,128)(2,1)S(1)}, bf16[128,8,384]{2,0,1:T(8,128)(2,1)S(1)}, u32[]{:S(2)}, u32[]{:S(2)}) collective-permute-start(bf16[128,8,384]{2,0,1:T(8,128)(2,1)S(1)} %maximum_select_fusion.3), channel_id=1, source_target_pairs={{0,24},{8,16},{16,8},{24,0},{32,56},{40,48},{48,40},{56,32},{64,88... | collective-permute-start | bytes 2359304 | tf_op jit(solution)/shard_map/ppermute | solution.py:51
  50.9 1.0 copy.20
  52.0 0.8 copy.21
  53.4 10.7 %collective-permute-done.5 = bf16[128,8,384]{2,0,1:T(8,128)(2,1)S(1)} collective-permute-done((bf16[128,8,384]{2,0,1:T(8,128)(2,1)S(1)}, bf16[128,8,384]{2,0,1:T(8,128)(2,1)S(1)}, u32[]{:S(2)}, u32[]{:S(2)}) %collective-permute-start.5) | collective-permute-done | bytes 786464 | tf_op jit(solution)/shard_map/ppermute | solution.py:51
  64.5 1.7 %collective-permute-done.3 = bf16[128,8,384]{2,0,1:T(8,128)(2,1)S(1)} collective-permute-done((bf16[128,8,384]{2,0,1:T(8,128)(2,1)S(1)}, bf16[128,8,384]{2,0,1:T(8,128)(2,1)S(1)}, u32[]{:S(2)}, u32[]{:S(2)}) %collective-permute-start.3) | collective-permute-done | bytes 786464 | tf_op jit(solution)/shard_map/ppermute | solution.py:51
  66.6 1.0 copy-done.3
  67.8 1.5 %pad_maximum_fusion = bf16[256,16,256]{2,0,1:T(8,128)(2,1)} fusion(bf16[128,16,256]{2,0,1:T(8,128)(2,1)S(1)} %get-tuple-element.14, bf16[128,16,256]{2,0,1:T(8,128)(2,1)S(1)} %get-tuple-element.12), kind=kLoop, calls=%fused_computation.6 | loop fusion | flops 4194304 | bytes 4194304 | tf_op jit(solution)/shard_map/concatenate | solution.py:129
  69.3 6.1 %collective-permute-start.6 = (bf16[256,16,256]{2,0,1:T(8,128)(2,1)}, bf16[256,16,256]{2,0,1:T(8,128)(2,1)}, u32[]{:S(2)}, u32[]{:S(2)}) collective-permute-start(bf16[256,16,256]{2,0,1:T(8,128)(2,1)} %pad_maximum_fusion), channel_id=1, source_target_pairs={{0,128},{128,0},{256,384},{384,256},{1,129},{129,1},{257,385},{385... | collective-permute-start | bytes 6291464 | tf_op jit(solution)/shard_map/ppermute | solution.py:132
  76.3 1.3 fusion.1
  77.6 1.6 %fusion.11 = bf16[512,128]{1,0:T(8,128)(2,1)S(1)} fusion(bf16[2048,128]{1,0:T(8,128)(2,1)S(1)} %bitcast.94, f32[2048,512]{1,0:T(8,128)S(1)} %get-tuple-element.22, f32[512]{0:T(512)S(1)} %broadcast_maximum_fusion, s32[512]{0:T(512)S(1)} %broadcast_bitcast_fusion, s32[2048]{0:T(1024)S(1)} %bitcast.101, f32[512]{0:T(512)S(1)} %fusion.1), kind=kOutput, calls=%fused_computation.15 | convolution fusion | flops 274857984 | bytes 4864000 | tf_op jit(solution)/shard_map/grk,kgd->grd/dot_general | solution.py:161
  79.8 1.2 dot_general.32
  80.9 1.7 %fusion.16 = f32[128,4,4,256]{3,0,2,1:T(8,128)S(1)} fusion(bf16[4,4,256,128]{3,2,1,0:T(8,128)(2,1)} %dot_general.32, bf16[128,512]{1,0:T(8,128)(2,1)S(1)} %bitcast.90, s32[]{:T(128)S(6)} %select_n.98), kind=kOutput, calls=%fused_computation.29 | convolution fusion | flops 134217728 | bytes 3178500 | tf_op jit(solution)/shard_map/rh,nkh->rnk/dot_general | solution.py:182
  82.6 1.3 fusion.32
  84.4 1.8 %fusion.19 = f32[128,4,4,256]{3,0,2,1:T(8,128)} fusion(bf16[4,4,256,128]{3,2,1,0:T(8,128)(2,1)S(1)} %dot_general.28, bf16[128,512]{1,0:T(8,128)(2,1)S(1)} %bitcast.91, s32[]{:T(128)S(6)} %select_n.86), kind=kOutput, calls=%fused_computation.32 | convolution fusion | flops 134217728 | bytes 3178500 | tf_op jit(solution)/shard_map/rh,nkh->rnk/dot_general | solution.py:182
  86.2 2.7 %slice_bitcast_fusion.1 = (bf16[16,128,256]{2,1,0:T(8,128)(2,1)}, bf16[16,128,256]{2,1,0:T(8,128)(2,1)S(1)}) fusion(bf16[256,16,256]{2,0,1:T(8,128)(2,1)} %collective-permute-done.6), kind=kLoop, calls=%fused_computation.17 | loop fusion | bytes 4194304 | tf_op jit(solution)/shard_map/transpose | solution.py:177
  89.7 1.2 fusion.33
  91.4 1.5 %dot_general.30 = bf16[4,4,256,128]{3,2,1,0:T(8,128)(2,1)S(1)} reshape(bf16[16,128,256]{2,1,0:T(8,128)(2,1)} %get-tuple-element.5) | data formatting | bytes 2097152 | tf_op jit(solution)/shard_map/rh,nkh->rnk/dot_general | solution.py:182
  93.0 3.8 %fusion.7 = bf16[128,4,4,256]{3,0,1,2:T(8,128)(2,1)} fusion(f32[128,1,4,256]{3,0,2,1:T(8,128)} %get-tuple-element.10, f32[128,2,4,256]{3,0,2,1:T(8,128)S(1)} %slice-done.1, f32[128,1,4,256]{3,0,2,1:T(8,128)} %get-tuple-element.9, f32[128,1,4,256]{3,0,2,1:T(8,128)} %get-tuple-element.8, f32[128,2,4,256]{3,0,2,1:T(8,128)S(1)} %slice-done, ...), kind=kOutput, calls=%fused_computation.13 | convolution fusion | flops 138412032 | bytes 8421380 | tf_op jit(solution)/shard_map/rh,nkh->rnk/dot_general | solution.py:182
  96.8 1.6 %copy.23 = bf16[128,4,4,256]{0,3,2,1:T(8,128)(2,1)S(1)} copy(bf16[128,4,4,256]{3,0,1,2:T(8,128)(2,1)} %fusion.7) | data formatting | bytes 2097152 | tf_op jit(solution)/shard_map/add | solution.py:186
  98.4 39.0 %all_to_all.5 = bf16[128,8,512]{0,2,1:T(8,128)(2,1)S(1)} all-to-all(bf16[128,8,512]{0,2,1:T(8,128)(2,1)S(1)} %bitcast.87), channel_id=1, replica_groups=mesh['dp'=4,'context'=16,'tensor'=8] {'tensor'}, dimensions={1} | all-to-all | bytes 2097152 | tf_op jit(solution)/shard_map/all_to_all | solution.py:190
  137.6 0.8 copy.24
  (47 shorter events, 5.8 us)
Async XLA Ops:
  0.0 52.8 %copy-start = (s32[2048]{0:T(1024)S(1)}, s32[2048]{0:T(1024)}, u32[]{:S(2)}) copy-start(s32[2048]{0:T(1024)} %param.9) | copy-start | bytes 24580
  2.0 7.1 %collective-permute-start = (bf16[128,1,768]{2,0,1:T(8,128)(2,1)S(1)}, bf16[128,1,768]{2,0,1:T(8,128)(2,1)S(1)}, u32[]{:S(2)}, u32[]{:S(2)}) collective-permute-start(bf16[128,1,768]{2,0,1:T(8,128)(2,1)S(1)} %maximum_bitcast_fusion), channel_id=1, source_target_pairs={{0,32},{8,40},{16,48},{24,56},{32,0},{40,8},{48,16},{56,24},{64,96... | collective-permute-start | bytes 589832 | tf_op jit(solution)/shard_map/ppermute | solution.py:51
  9.1 22.0 %collective-permute-start.1 = (bf16[128,2,768]{2,0,1:T(8,128)(2,1)S(1)}, bf16[128,2,768]{2,0,1:T(8,128)(2,1)S(1)}, u32[]{:S(2)}, u32[]{:S(2)}) collective-permute-start(bf16[128,2,768]{2,0,1:T(8,128)(2,1)S(1)} %maximum_select_fusion.5), channel_id=1, source_target_pairs={{0,64},{8,72},{16,80},{24,88},{32,96},{40,104},{48,112},{56,120},{... | collective-permute-start | bytes 1179656 | tf_op jit(solution)/shard_map/ppermute | solution.py:51
  31.4 21.5 %copy-start.5 = (s32[16]{0:T(128)S(1)}, s32[16]{0:T(128)}, u32[]{:S(2)}) copy-start(s32[16]{0:T(128)} %constant.64) | copy-start | bytes 196
  31.4 12.6 %collective-permute-start.4 = (bf16[128,4,384]{2,0,1:T(8,128)(2,1)S(1)}, bf16[128,4,384]{2,0,1:T(8,128)(2,1)S(1)}, u32[]{:S(2)}, u32[]{:S(2)}) collective-permute-start(bf16[128,4,384]{2,0,1:T(8,128)(2,1)S(1)} %get-tuple-element.16), channel_id=1, source_target_pairs={{0,24},{8,16},{16,8},{24,0},{32,56},{40,48},{48,40},{56,32},{64,88... | collective-permute-start | bytes 1179656 | tf_op jit(solution)/shard_map/ppermute | solution.py:51
  36.4 10.8 %collective-permute-start.2 = (bf16[128,4,384]{2,0,1:T(8,128)(2,1)S(1)}, bf16[128,4,384]{2,0,1:T(8,128)(2,1)S(1)}, u32[]{:S(2)}, u32[]{:S(2)}) collective-permute-start(bf16[128,4,384]{2,0,1:T(8,128)(2,1)S(1)} %get-tuple-element.15), channel_id=1, source_target_pairs={{0,8},{8,0},{16,24},{24,16},{32,40},{40,32},{48,56},{56,48},{64,72... | collective-permute-start | bytes 1179656 | tf_op jit(solution)/shard_map/ppermute | solution.py:51
  44.1 20.0 %collective-permute-start.5 = (bf16[128,8,384]{2,0,1:T(8,128)(2,1)S(1)}, bf16[128,8,384]{2,0,1:T(8,128)(2,1)S(1)}, u32[]{:S(2)}, u32[]{:S(2)}) collective-permute-start(bf16[128,8,384]{2,0,1:T(8,128)(2,1)S(1)} %maximum_select_fusion.4), channel_id=1, source_target_pairs={{0,8},{8,0},{16,24},{24,16},{32,40},{40,32},{48,56},{56,48},{64,72... | collective-permute-start | bytes 2359304 | tf_op jit(solution)/shard_map/ppermute | solution.py:51
  47.4 18.8 %collective-permute-start.3 = (bf16[128,8,384]{2,0,1:T(8,128)(2,1)S(1)}, bf16[128,8,384]{2,0,1:T(8,128)(2,1)S(1)}, u32[]{:S(2)}, u32[]{:S(2)}) collective-permute-start(bf16[128,8,384]{2,0,1:T(8,128)(2,1)S(1)} %maximum_select_fusion.3), channel_id=1, source_target_pairs={{0,24},{8,16},{16,8},{24,0},{32,56},{40,48},{48,40},{56,32},{64,88... | collective-permute-start | bytes 2359304 | tf_op jit(solution)/shard_map/ppermute | solution.py:51
  66.5 1.2 copy-start.3
  67.8 7.7 %slice-start.2 = ((bf16[128,16,384]{2,0,1:T(8,128)(2,1)}), bf16[128,16,128]{2,0,1:T(8,128)(2,1)S(1)}, s32[]{:S(2)}) async-start(bf16[128,16,384]{2,0,1:T(8,128)(2,1)} %copy-done.3), calls=%async_computation.3 | async-start | bytes 1048576 | tf_op jit(solution)/shard_map/slice | solution.py:134
  67.8 7.7 %copy-start.4 = (bf16[1,4,128,128]{3,2,1,0:T(8,128)(2,1)S(1)}, bf16[1,4,128,128]{3,2,1,0:T(8,128)(2,1)}, u32[]{:S(2)}) copy-start(bf16[1,4,128,128]{3,2,1,0:T(8,128)(2,1)} %copy.21) | copy-start | bytes 393220
  69.3 16.8 %collective-permute-start.6 = (bf16[256,16,256]{2,0,1:T(8,128)(2,1)}, bf16[256,16,256]{2,0,1:T(8,128)(2,1)}, u32[]{:S(2)}, u32[]{:S(2)}) collective-permute-start(bf16[256,16,256]{2,0,1:T(8,128)(2,1)} %pad_maximum_fusion), channel_id=1, source_target_pairs={{0,128},{128,0},{256,384},{384,256},{1,129},{129,1},{257,385},{385... | collective-permute-start | bytes 6291464 | tf_op jit(solution)/shard_map/ppermute | solution.py:132
  82.6 1.8 %copy-start.1 = (f32[128,4,4,256]{3,0,2,1:T(8,128)}, f32[128,4,4,256]{3,0,2,1:T(8,128)S(1)}, u32[]{:S(2)}) copy-start(f32[128,4,4,256]{3,0,2,1:T(8,128)S(1)} %fusion.16) | copy-start | bytes 6291460
  89.7 1.7 %copy-start.2 = (f32[128,4,4,256]{3,0,2,1:T(8,128)}, f32[128,4,4,256]{3,0,2,1:T(8,128)S(1)}, u32[]{:S(2)}) copy-start(f32[128,4,4,256]{3,0,2,1:T(8,128)S(1)} %fusion.14) | copy-start | bytes 6291460
  90.9 2.0 %slice-start = ((f32[128,4,4,256]{3,0,2,1:T(8,128)}), f32[128,2,4,256]{3,0,2,1:T(8,128)S(1)}, s32[]{:S(2)}) async-start(f32[128,4,4,256]{3,0,2,1:T(8,128)} %copy-done.1), calls=%async_computation.1 | async-start | bytes 2097152 | tf_op jit(solution)/shard_map/slice | solution.py:73
  91.4 1.6 %slice-start.1 = ((f32[128,4,4,256]{3,0,2,1:T(8,128)}), f32[128,2,4,256]{3,0,2,1:T(8,128)S(1)}, s32[]{:S(2)}) async-start(f32[128,4,4,256]{3,0,2,1:T(8,128)} %copy-done.2), calls=%async_computation.2 | async-start | bytes 2097152 | tf_op jit(solution)/shard_map/slice | solution.py:73

commit v9 on v8

--- a/solution.py
+++ b/solution.py
@@ -12,7 +12,7 @@
 
 
 def chain_plan(context_size, x_size, x_first_mask):
-    y_bits = [x_size << k for k in range((context_size // x_size).bit_length() - 1)]
+    y_bits = [x_size << k for k in range((context_size // x_size).bit_length() - 1)][::-1]
     steps = [(bit, bit) for bit in y_bits]
     if x_size == 4:
         steps += [(1, 1), (3, 2)] if x_first_mask == 1 else [(3, 2), (1, 3)]
@@ -58,20 +58,23 @@
 
 
 def unpermute_blocks(product, sources, x_size):
-    rows = product.shape[0]
-    count = len(sources)
+    rows, count = product.shape[:2]
     y_count = count // x_size
-    x_order = [sources[ix * y_count] for ix in range(x_size)]
+    x_order = [sources[ix * y_count] % x_size for ix in range(x_size)]
+    y_order = [sources[iy] // x_size for iy in range(y_count)]
     assert all(
-        sources[ix * y_count + iy] == iy * x_size + x_order[ix]
+        sources[ix * y_count + iy] == y_order[iy] * x_size + x_order[ix]
         for ix in range(x_size)
         for iy in range(y_count)
     )
     product = product.reshape(rows, x_size, y_count, -1)
-    inverse = [x_order.index(x) for x in range(x_size)]
-    if inverse != list(range(x_size)):
-        product = jnp.concatenate([product[:, i : i + 1] for i in inverse], axis=1)
-    return jnp.swapaxes(product, 1, 2).reshape(rows, -1)
+    x_inverse = [x_order.index(x) for x in range(x_size)]
+    y_inverse = [y_order.index(y) for y in range(y_count)]
+    if x_inverse != list(range(x_size)):
+        product = jnp.concatenate([product[:, i : i + 1] for i in x_inverse], axis=1)
+    if y_inverse != list(range(y_count)):
+        product = jnp.concatenate([product[:, :, i : i + 1] for i in y_inverse], axis=2)
+    return jnp.swapaxes(product, 1, 2).reshape(rows, count, -1)
 
 
 def restack(stack, sources, target, x_size):
@@ -127,7 +130,7 @@
     sources_b = stacked_sources(context_size, steps_b)
 
     mine_weights = jnp.concatenate(
-        [gathered_a[:, :, key_width:], gathered_b[:, :, values.shape[1] :]], axis=0
+        [gathered_a[:, :, key_width:], gathered_b[:, :, values.shape[1] :]], axis=1
     )
     other_weights = lax.ppermute(mine_weights, "dp", [(i, i ^ 1) for i in range(dp_size)])
 
@@ -173,7 +176,7 @@
     total = None
     for piece, sources in ((0, sources_a), (1, sources_b)):
         for which, held in ((0, mine_weights), (1, other_weights)):
-            piece_t = held[piece * row_count : (piece + 1) * row_count]
+            piece_t = held[:, piece * context_size : (piece + 1) * context_size]
             piece_t = jnp.swapaxes(piece_t, 0, 1).reshape(context_size, weight_cols, quarter)
             owner = core if which == 0 else 1 - core
             piece_rows = lax.dynamic_slice_in_dim(
@@ -181,14 +184,14 @@
             )
             product_out = jnp.einsum(
                 "rh,nkh->rnk", piece_rows, piece_t, preferred_element_type=jnp.float32
-            ).reshape(row_count, -1)
+            )
             product_out = unpermute_blocks(product_out, sources, x_size)
             total = product_out if total is None else total + product_out
-    partial_out = total
     tensor_size = lax.axis_size("tensor")
-    pieces = partial_out.astype(jnp.bfloat16).reshape(row_count, tensor_size, -1)
-    pieces = lax.all_to_all(pieces, "tensor", 1, 1, tiled=True)
-    return jnp.sum(pieces.astype(jnp.float32), axis=1).astype(jnp.bfloat16)
+    pieces = total.astype(jnp.bfloat16).reshape(row_count, tensor_size, -1)
+    pieces = jnp.swapaxes(pieces, 0, 1)
+    pieces = lax.all_to_all(pieces, "tensor", 0, 0, tiled=True)
+    return jnp.sum(pieces.astype(jnp.float32), axis=0).astype(jnp.bfloat16)
 
 
 def solution(mesh):

time: 140 us -> 160 us (1.14)
  the two profiles are of different devices: /device:TPU:1 before, /device:TPU:23 now
where the time goes in v9:
time: 160 us; the launch traced here: 159 us
  waiting for transfers between devices  61.9 us (39%)
  blocking collectives  39.1 us (24%)
  starting transfers between devices  24.2 us (15%)
  local copies, waits for them, and re-layouts  21.1 us (13%)
  other arithmetic  7.13 us (4%)
  matrix products  5.4 us (3%)
    ppermute x6, waiting for transfers between devices, exchange_gather(): lax.ppermute(stack, axis_name, [(i, i ^ mask) for i in range(count)])  61.9 us
    all_to_all x1, blocking collectives, per_device(): pieces = lax.all_to_all(pieces, 'tensor', 0, 0, tiled=True)  39.1 us
    ppermute x6, starting transfers between devices, exchange_gather(): lax.ppermute(stack, axis_name, [(i, i ^ mask) for i in range(count)])  18.6 us
    ppermute x1, starting transfers between devices, per_device(): lax.ppermute(mine_weights, 'dp', [(i, i ^ 1) for i in range(dp_size)])  5.55 us
    unnamed x36, local copies, waits for them, and re-layouts  4.36 us
    transpose x3, local copies, waits for them, and re-layouts, per_device(): jnp.swapaxes(piece_t, 0, 1).reshape(context_size, weight_cols, quarter)  4.01 us
    dot_general x4, local copies, waits for them, and re-layouts, per_device(): jnp.einsum('rh,nkh->rnk', piece_rows, piece_t, preferred_element_type=jnp...  3.48 us
  transfers between devices with their start and end apart: 7, of which 5 were waited for; matrix products, arithmetic and copies ran while one was open for 8% of the time, Pallas kernels for 0%

profile of v9, /device:TPU:23, one launch (start us, length us, event | category | flops | bytes accessed | tf_op | source)
XLA Modules:
  0.0 159.2 jit_solution(12210554962086769900)
XLA Ops:
  0.0 0.9 dynamic-slice_bitcast_fusion.1
  1.2 0.8 maximum_bitcast_fusion
  2.0 2.0 %collective-permute-start = (bf16[128,1,768]{2,0,1:T(8,128)(2,1)S(1)}, bf16[128,1,768]{2,0,1:T(8,128)(2,1)S(1)}, u32[]{:S(2)}, u32[]{:S(2)}) collective-permute-start(bf16[128,1,768]{2,0,1:T(8,128)(2,1)S(1)} %maximum_bitcast_fusion), channel_id=1, source_target_pairs={{0,64},{8,72},{16,80},{24,88},{32,96},{40,104},{48,112},{56,120},{... | collective-permute-start | bytes 589832 | tf_op jit(solution)/shard_map/ppermute | solution.py:51
  4.0 7.8 %collective-permute-done = bf16[128,1,768]{2,0,1:T(8,128)(2,1)S(1)} collective-permute-done((bf16[128,1,768]{2,0,1:T(8,128)(2,1)S(1)}, bf16[128,1,768]{2,0,1:T(8,128)(2,1)S(1)}, u32[]{:S(2)}, u32[]{:S(2)}) %collective-permute-start) | collective-permute-done | bytes 196640 | tf_op jit(solution)/shard_map/ppermute | solution.py:51
  11.8 7.1 %collective-permute-start.1 = (bf16[128,2,768]{2,0,1:T(8,128)(2,1)S(1)}, bf16[128,2,768]{2,0,1:T(8,128)(2,1)S(1)}, u32[]{:S(2)}, u32[]{:S(2)}) collective-permute-start(bf16[128,2,768]{2,0,1:T(8,128)(2,1)S(1)} %maximum_select_fusion.5), channel_id=1, source_target_pairs={{0,32},{8,40},{16,48},{24,56},{32,0},{40,8},{48,16},{56,24},{64,96... | collective-permute-start | bytes 1179656 | tf_op jit(solution)/shard_map/ppermute | solution.py:51
  19.0 9.0 %collective-permute-done.1 = bf16[128,2,768]{2,0,1:T(8,128)(2,1)S(1)} collective-permute-done((bf16[128,2,768]{2,0,1:T(8,128)(2,1)S(1)}, bf16[128,2,768]{2,0,1:T(8,128)(2,1)S(1)}, u32[]{:S(2)}, u32[]{:S(2)}) %collective-permute-start.1) | collective-permute-done | bytes 393248 | tf_op jit(solution)/shard_map/ppermute | solution.py:51
  28.2 2.1 %collective-permute-start.4 = (bf16[128,4,384]{2,0,1:T(8,128)(2,1)S(1)}, bf16[128,4,384]{2,0,1:T(8,128)(2,1)S(1)}, u32[]{:S(2)}, u32[]{:S(2)}) collective-permute-start(bf16[128,4,384]{2,0,1:T(8,128)(2,1)S(1)} %get-tuple-element.32), channel_id=1, source_target_pairs={{0,24},{8,16},{16,8},{24,0},{32,56},{40,48},{48,40},{56,32},{64,88... | collective-permute-start | bytes 1179656 | tf_op jit(solution)/shard_map/ppermute | solution.py:51
  30.3 10.6 %collective-permute-done.4 = bf16[128,4,384]{2,0,1:T(8,128)(2,1)S(1)} collective-permute-done((bf16[128,4,384]{2,0,1:T(8,128)(2,1)S(1)}, bf16[128,4,384]{2,0,1:T(8,128)(2,1)S(1)}, u32[]{:S(2)}, u32[]{:S(2)}) %collective-permute-start.4) | collective-permute-done | bytes 393248 | tf_op jit(solution)/shard_map/ppermute | solution.py:51
  41.1 1.9 %collective-permute-start.5 = (bf16[128,8,384]{2,0,1:T(8,128)(2,1)S(1)}, bf16[128,8,384]{2,0,1:T(8,128)(2,1)S(1)}, u32[]{:S(2)}, u32[]{:S(2)}) collective-permute-start(bf16[128,8,384]{2,0,1:T(8,128)(2,1)S(1)} %maximum_select_fusion.4), channel_id=1, source_target_pairs={{0,8},{8,0},{16,24},{24,16},{32,40},{40,32},{48,56},{56,48},{64,72... | collective-permute-start | bytes 2359304 | tf_op jit(solution)/shard_map/ppermute | solution.py:51
  43.0 3.4 %collective-permute-start.2 = (bf16[128,4,384]{2,0,1:T(8,128)(2,1)S(1)}, bf16[128,4,384]{2,0,1:T(8,128)(2,1)S(1)}, u32[]{:S(2)}, u32[]{:S(2)}) collective-permute-start(bf16[128,4,384]{2,0,1:T(8,128)(2,1)S(1)} %get-tuple-element.31), channel_id=1, source_target_pairs={{0,8},{8,0},{16,24},{24,16},{32,40},{40,32},{48,56},{56,48},{64,72... | collective-permute-start | bytes 1179656 | tf_op jit(solution)/shard_map/ppermute | solution.py:51
  46.5 0.8 copy.21
  47.9 20.6 %collective-permute-done.2 = bf16[128,4,384]{2,0,1:T(8,128)(2,1)S(1)} collective-permute-done((bf16[128,4,384]{2,0,1:T(8,128)(2,1)S(1)}, bf16[128,4,384]{2,0,1:T(8,128)(2,1)S(1)}, u32[]{:S(2)}, u32[]{:S(2)}) %collective-permute-start.2) | collective-permute-done | bytes 393248 | tf_op jit(solution)/shard_map/ppermute | solution.py:51
  68.7 2.1 %collective-permute-start.3 = (bf16[128,8,384]{2,0,1:T(8,128)(2,1)S(1)}, bf16[128,8,384]{2,0,1:T(8,128)(2,1)}, u32[]{:S(2)}, u32[]{:S(2)}) collective-permute-start(bf16[128,8,384]{2,0,1:T(8,128)(2,1)S(1)} %maximum_select_fusion.3), channel_id=1, source_target_pairs={{0,24},{8,16},{16,8},{24,0},{32,56},{40,48},{48,40},{56,32},{64,88... | collective-permute-start | bytes 2359304 | tf_op jit(solution)/shard_map/ppermute | solution.py:51
  73.2 1.1 slice_bitcast_fusion.2
  74.3 13.9 %collective-permute-done.3 = bf16[128,8,384]{2,0,1:T(8,128)(2,1)} collective-permute-done((bf16[128,8,384]{2,0,1:T(8,128)(2,1)S(1)}, bf16[128,8,384]{2,0,1:T(8,128)(2,1)}, u32[]{:S(2)}, u32[]{:S(2)}) %collective-permute-start.3) | collective-permute-done | bytes 786464 | tf_op jit(solution)/shard_map/ppermute | solution.py:51
  88.2 1.7 %maximum_select_fusion = bf16[128,16,384]{2,0,1:T(8,128)(2,1)S(1)} fusion(bf16[128,8,384]{2,0,1:T(8,128)(2,1)S(1)} %maximum_select_fusion.3, bf16[128,8,384]{2,0,1:T(8,128)(2,1)} %collective-permute-done.3, pred[]{:T(512)S(6)} %ne.22), kind=kLoop, calls=%fused_computation.14 | loop fusion | flops 2359296 | bytes 3145729 | tf_op jit(solution)/shard_map/jit(_where)/select_n | solution.py:52
  89.9 1.8 %slice_bitcast_fusion.3 = (bf16[16,128,256]{2,1,0:T(8,128)(2,1)}, bf16[128,16,256]{2,0,1:T(8,128)(2,1)}) fusion(bf16[128,16,384]{2,0,1:T(8,128)(2,1)S(1)} %maximum_select_fusion), kind=kLoop, calls=%fused_computation.53 | loop fusion | bytes 3145728 | tf_op jit(solution)/shard_map/transpose | solution.py:180
  91.7 1.2 dot_general.32
  92.9 1.6 dot_general.28
  94.9 5.5 %collective-permute-start.6 = (bf16[128,32,256]{2,0,1:T(8,128)(2,1)S(1)}, bf16[128,32,256]{2,0,1:T(8,128)(2,1)S(1)}, u32[]{:S(2)}, u32[]{:S(2)}) collective-permute-start(bf16[128,32,256]{2,0,1:T(8,128)(2,1)S(1)} %pad_maximum_fusion), channel_id=1, source_target_pairs={{0,128},{128,0},{256,384},{384,256},{1,129},{129,1},{257,385},{385... | collective-permute-start | bytes 6291464 | tf_op jit(solution)/shard_map/ppermute | solution.py:135
  100.5 0.7 fusion
  101.6 1.3 fusion.1
  102.8 1.6 %fusion.11 = bf16[512,128]{1,0:T(8,128)(2,1)S(1)} fusion(bf16[2048,128]{1,0:T(8,128)(2,1)S(1)} %bitcast.96, f32[2048,512]{1,0:T(8,128)S(1)} %get-tuple-element.38, f32[512]{0:T(512)S(1)} %broadcast_maximum_fusion, s32[512]{0:T(512)S(1)} %copy-done.15, s32[2048]{0:T(1024)S(1)} %bitcast.103, f32[512]{0:T(512)S(1)} %fusion.1), kind=kOutput, calls=%fused_computation.17 | convolution fusion | flops 274857984 | bytes 4864000 | tf_op jit(solution)/shard_map/grk,kgd->grd/dot_general | solution.py:164
  105.2 1.5 pad_maximum_fusion.1
  106.7 1.7 %fusion.21 = f32[128,4,4,256]{3,0,2,1:T(8,128)} fusion(bf16[4,4,256,128]{3,2,1,0:T(8,128)(2,1)S(1)} %dot_general.28, bf16[128,512]{1,0:T(8,128)(2,1)S(1)} %bitcast.93, s32[]{:T(128)S(6)} %select_n.86), kind=kOutput, calls=%fused_computation.36 | convolution fusion | flops 134217728 | bytes 3178500 | tf_op jit(solution)/shard_map/rh,nkh->rnk/dot_general | solution.py:185
  108.5 1.1 slice_bitcast_fusion.1
  110.4 1.1 fusion.39
  113.2 1.1 copy-done.3
  114.8 0.8 slice-done
  116.1 1.4 copy-done.2
  119.2 39.1 %all_to_all.5 = bf16[8,128,512]{1,2,0:T(8,128)(2,1)S(1)} all-to-all(bf16[8,128,512]{1,2,0:T(8,128)(2,1)S(1)} %bitcast.89), channel_id=1, replica_groups=mesh['dp'=4,'context'=16,'tensor'=8] {'tensor'}, dimensions={0} | all-to-all | bytes 2097152 | tf_op jit(solution)/shard_map/all_to_all | solution.py:193
  158.4 0.8 copy.24
  (73 shorter events, 10.6 us)
Async XLA Ops:
  0.0 47.3 %copy-start = (s32[2048]{0:T(1024)S(1)}, s32[2048]{0:T(1024)}, u32[]{:S(2)}) copy-start(s32[2048]{0:T(1024)} %param.9) | copy-start | bytes 24580
  2.0 9.8 %collective-permute-start = (bf16[128,1,768]{2,0,1:T(8,128)(2,1)S(1)}, bf16[128,1,768]{2,0,1:T(8,128)(2,1)S(1)}, u32[]{:S(2)}, u32[]{:S(2)}) collective-permute-start(bf16[128,1,768]{2,0,1:T(8,128)(2,1)S(1)} %maximum_bitcast_fusion), channel_id=1, source_target_pairs={{0,64},{8,72},{16,80},{24,88},{32,96},{40,104},{48,112},{56,120},{... | collective-permute-start | bytes 589832 | tf_op jit(solution)/shard_map/ppermute | solution.py:51
  11.8 16.1 %collective-permute-start.1 = (bf16[128,2,768]{2,0,1:T(8,128)(2,1)S(1)}, bf16[128,2,768]{2,0,1:T(8,128)(2,1)S(1)}, u32[]{:S(2)}, u32[]{:S(2)}) collective-permute-start(bf16[128,2,768]{2,0,1:T(8,128)(2,1)S(1)} %maximum_select_fusion.5), channel_id=1, source_target_pairs={{0,32},{8,40},{16,48},{24,56},{32,0},{40,8},{48,16},{56,24},{64,96... | collective-permute-start | bytes 1179656 | tf_op jit(solution)/shard_map/ppermute | solution.py:51
  19.0 27.4 %copy-start.13 = (bf16[128,512]{1,0:T(8,128)(2,1)S(1)}, bf16[128,512]{1,0:T(8,128)(2,1)}, u32[]{:S(2)}) copy-start(bf16[128,512]{1,0:T(8,128)(2,1)} %param.6) | copy-start | bytes 393220
  28.2 42.6 %copy-start.16 = (s32[16]{0:T(128)S(1)}, s32[16]{0:T(128)}, u32[]{:S(2)}) copy-start(s32[16]{0:T(128)} %constant.64) | copy-start | bytes 196
  28.2 12.7 %collective-permute-start.4 = (bf16[128,4,384]{2,0,1:T(8,128)(2,1)S(1)}, bf16[128,4,384]{2,0,1:T(8,128)(2,1)S(1)}, u32[]{:S(2)}, u32[]{:S(2)}) collective-permute-start(bf16[128,4,384]{2,0,1:T(8,128)(2,1)S(1)} %get-tuple-element.32), channel_id=1, source_target_pairs={{0,24},{8,16},{16,8},{24,0},{32,56},{40,48},{48,40},{56,32},{64,88... | collective-permute-start | bytes 1179656 | tf_op jit(solution)/shard_map/ppermute | solution.py:51
  41.1 30.3 %collective-permute-start.5 = (bf16[128,8,384]{2,0,1:T(8,128)(2,1)S(1)}, bf16[128,8,384]{2,0,1:T(8,128)(2,1)S(1)}, u32[]{:S(2)}, u32[]{:S(2)}) collective-permute-start(bf16[128,8,384]{2,0,1:T(8,128)(2,1)S(1)} %maximum_select_fusion.4), channel_id=1, source_target_pairs={{0,8},{8,0},{16,24},{24,16},{32,40},{40,32},{48,56},{56,48},{64,72... | collective-permute-start | bytes 2359304 | tf_op jit(solution)/shard_map/ppermute | solution.py:51
  43.0 25.6 %collective-permute-start.2 = (bf16[128,4,384]{2,0,1:T(8,128)(2,1)S(1)}, bf16[128,4,384]{2,0,1:T(8,128)(2,1)S(1)}, u32[]{:S(2)}, u32[]{:S(2)}) collective-permute-start(bf16[128,4,384]{2,0,1:T(8,128)(2,1)S(1)} %get-tuple-element.31), channel_id=1, source_target_pairs={{0,8},{8,0},{16,24},{24,16},{32,40},{40,32},{48,56},{56,48},{64,72... | collective-permute-start | bytes 1179656 | tf_op jit(solution)/shard_map/ppermute | solution.py:51
  68.7 19.5 %collective-permute-start.3 = (bf16[128,8,384]{2,0,1:T(8,128)(2,1)S(1)}, bf16[128,8,384]{2,0,1:T(8,128)(2,1)}, u32[]{:S(2)}, u32[]{:S(2)}) collective-permute-start(bf16[128,8,384]{2,0,1:T(8,128)(2,1)S(1)} %maximum_select_fusion.3), channel_id=1, source_target_pairs={{0,24},{8,16},{16,8},{24,0},{32,56},{40,48},{48,40},{56,32},{64,88... | collective-permute-start | bytes 2359304 | tf_op jit(solution)/shard_map/ppermute | solution.py:51
  89.9 1.8 %copy-start.4 = (bf16[128,16,384]{2,0,1:T(8,128)(2,1)}, bf16[128,16,384]{2,0,1:T(8,128)(2,1)S(1)}, u32[]{:S(2)}) copy-start(bf16[128,16,384]{2,0,1:T(8,128)(2,1)S(1)} %maximum_select_fusion) | copy-start | bytes 4718596
  92.9 1.6 copy-start.6
  92.9 1.9 %copy-start.7 = (bf16[128,16,256]{2,0,1:T(8,128)(2,1)S(1)}, bf16[128,16,256]{2,0,1:T(8,128)(2,1)}, u32[]{:S(2)}) copy-start(bf16[128,16,256]{2,0,1:T(8,128)(2,1)} %get-tuple-element.28) | copy-start | bytes 3145732
  94.8 5.7 %slice-start.1 = ((bf16[128,16,384]{2,0,1:T(8,128)(2,1)}), bf16[128,16,128]{2,0,1:T(8,128)(2,1)S(1)}, s32[]{:S(2)}) async-start(bf16[128,16,384]{2,0,1:T(8,128)(2,1)} %copy-done.4), calls=%async_computation.2 | async-start | bytes 1048576 | tf_op jit(solution)/shard_map/slice | solution.py:137
  94.8 5.8 %copy-start.14 = (bf16[1,4,128,128]{3,2,1,0:T(8,128)(2,1)S(1)}, bf16[1,4,128,128]{3,2,1,0:T(8,128)(2,1)}, u32[]{:S(2)}) copy-start(bf16[1,4,128,128]{3,2,1,0:T(8,128)(2,1)} %copy.21) | copy-start | bytes 393220
  94.8 5.8 %copy-start.15 = (s32[512]{0:T(512)S(1)}, s32[512]{0:T(512)}, u32[]{:S(2)}) copy-start(s32[512]{0:T(512)} %broadcast_bitcast_fusion) | copy-start | bytes 6148
  94.9 13.5 %collective-permute-start.6 = (bf16[128,32,256]{2,0,1:T(8,128)(2,1)S(1)}, bf16[128,32,256]{2,0,1:T(8,128)(2,1)S(1)}, u32[]{:S(2)}, u32[]{:S(2)}) collective-permute-start(bf16[128,32,256]{2,0,1:T(8,128)(2,1)S(1)} %pad_maximum_fusion), channel_id=1, source_target_pairs={{0,128},{128,0},{256,384},{384,256},{1,129},{129,1},{257,385},{385... | collective-permute-start | bytes 6291464 | tf_op jit(solution)/shard_map/ppermute | solution.py:135
  100.5 1.0 copy-start.11
  100.5 1.0 copy-start.12
  102.8 1.8 %copy-start.5 = (bf16[4,4,256,128]{3,2,1,0:T(8,128)(2,1)S(1)}, bf16[4,4,256,128]{3,2,1,0:T(8,128)(2,1)}, u32[]{:S(2)}) copy-start(bf16[4,4,256,128]{3,2,1,0:T(8,128)(2,1)} %dot_general.32) | copy-start | bytes 3145732
  110.4 1.7 %copy-start.1 = (f32[128,4,4,256]{3,0,2,1:T(8,128)}, f32[128,4,4,256]{3,0,2,1:T(8,128)S(1)}, u32[]{:S(2)}) copy-start(f32[128,4,4,256]{3,0,2,1:T(8,128)S(1)} %fusion.15) | copy-start | bytes 6291460
  110.4 2.0 %copy-start.8 = (bf16[16,128,256]{2,1,0:T(8,128)(2,1)S(1)}, bf16[16,128,256]{2,1,0:T(8,128)(2,1)}, u32[]{:S(2)}) copy-start(bf16[16,128,256]{2,1,0:T(8,128)(2,1)} %get-tuple-element.13) | copy-start | bytes 3145732
  112.8 1.6 %copy-start.3 = (f32[128,4,4,256]{3,0,2,1:T(8,128)S(1)}, f32[128,4,4,256]{3,0,2,1:T(8,128)}, u32[]{:S(2)}) copy-start(f32[128,4,4,256]{3,0,2,1:T(8,128)} %fusion.21) | copy-start | bytes 6291460
  114.4 1.2 slice-start
  114.4 1.4 copy-start.9
  114.4 1.5 copy-start.10
  115.9 1.6 copy-start.2

commit v10 on v8

--- a/solution.py
+++ b/solution.py
@@ -12,7 +12,7 @@
 
 
 def chain_plan(context_size, x_size, x_first_mask):
-    y_bits = [x_size << k for k in range((context_size // x_size).bit_length() - 1)]
+    y_bits = [x_size << k for k in range((context_size // x_size).bit_length() - 1)][::-1]
     steps = [(bit, bit) for bit in y_bits]
     if x_size == 4:
         steps += [(1, 1), (3, 2)] if x_first_mask == 1 else [(3, 2), (1, 3)]
@@ -61,17 +61,40 @@
     rows = product.shape[0]
     count = len(sources)
     y_count = count // x_size
-    x_order = [sources[ix * y_count] for ix in range(x_size)]
+    x_order = [sources[ix * y_count] % x_size for ix in range(x_size)]
+    y_order = [sources[iy] // x_size for iy in range(y_count)]
     assert all(
-        sources[ix * y_count + iy] == iy * x_size + x_order[ix]
+        sources[ix * y_count + iy] == y_order[iy] * x_size + x_order[ix]
         for ix in range(x_size)
         for iy in range(y_count)
     )
     product = product.reshape(rows, x_size, y_count, -1)
-    inverse = [x_order.index(x) for x in range(x_size)]
-    if inverse != list(range(x_size)):
-        product = jnp.concatenate([product[:, i : i + 1] for i in inverse], axis=1)
+    x_inverse = [x_order.index(x) for x in range(x_size)]
+    y_inverse = [y_order.index(y) for y in range(y_count)]
+    if x_inverse != list(range(x_size)):
+        product = jnp.concatenate([product[:, i : i + 1] for i in x_inverse], axis=1)
+    if y_inverse != list(range(y_count)):
+        product = jnp.concatenate([product[:, :, i : i + 1] for i in y_inverse], axis=2)
     return jnp.swapaxes(product, 1, 2).reshape(rows, -1)
+
+
+def exchange_gather_pair(stack_a, steps_a, stack_b, steps_b, axis_name, count):
+    index = lax.axis_index(axis_name)
+    for (mask_a, side_a), (mask_b, side_b) in zip(steps_a, steps_b):
+        received_a = lax.ppermute(stack_a, axis_name, [(i, i ^ mask_a) for i in range(count)])
+        received_b = lax.ppermute(stack_b, axis_name, [(i, i ^ mask_b) for i in range(count)])
+        stack_a = jnp.where(
+            upper_of(index, side_a),
+            jnp.concatenate([received_a, stack_a], 1),
+            jnp.concatenate([stack_a, received_a], 1),
+        )
+        stack_b = jnp.where(
+            upper_of(index, side_b),
+            jnp.concatenate([received_b, stack_b], 1),
+            jnp.concatenate([stack_b, received_b], 1),
+        )
+        stack_a, stack_b = lax.optimization_barrier((stack_a, stack_b))
+    return stack_a, stack_b
 
 
 def restack(stack, sources, target, x_size):
@@ -117,11 +140,13 @@
     ]
     block = jnp.concatenate([keys, quarters[0], values, quarters[1]], axis=1)[:, None, :]
     gathered = exchange_gather(block, steps_a[:shared], "context", context_size)
-    gathered_a = exchange_gather(
-        gathered[:, :, : key_width + weight_cols], steps_a[shared:], "context", context_size
-    )
-    gathered_b = exchange_gather(
-        gathered[:, :, key_width + weight_cols :], steps_b[shared:], "context", context_size
+    gathered_a, gathered_b = exchange_gather_pair(
+        gathered[:, :, : key_width + weight_cols],
+        steps_a[shared:],
+        gathered[:, :, key_width + weight_cols :],
+        steps_b[shared:],
+        "context",
+        context_size,
     )
     sources_a = stacked_sources(context_size, steps_a)
     sources_b = stacked_sources(context_size, steps_b)

time: 140 us -> 138 us (0.986)
  matrix products: 10 us -> 4.1 us
  other arithmetic: 4.8 us -> 9.37 us
  starting transfers between devices: 28.6 us -> 26.1 us
  local copies, waits for them, and re-layouts: 17.4 us -> 19.8 us
  waiting for transfers between devices: 38.1 us -> 36 us
    ppermute x6 -> x2, waiting for transfers between devices: 38.1 us -> 15.2 us  [exchange_gather(): lax.ppermute(stack, axis_name, [(i, i ^ mask) for i in range(count)])]
    ppermute x0 -> x4, waiting for transfers between devices: none -> 20.8 us  [the longest x2 15.5 us: exchange_gather_pair(): lax.ppermute(stack_a, axis_name, [(i, i ^ mask_a) for i in range(count)])]
    ppermute x6 -> x2, starting transfers between devices: 22.4 us -> 9.68 us  [exchange_gather(): lax.ppermute(stack, axis_name, [(i, i ^ mask) for i in range(count)])]
    ppermute x0 -> x4, starting transfers between devices: none -> 10.4 us  [the longest x2 6.31 us: exchange_gather_pair(): lax.ppermute(stack_b, axis_name, [(i, i ^ mask_b) for i in range(count)])]
    dot_general x4, matrix products: 7.64 us -> 1.75 us  [per_device(): jnp.einsum('rh,nkh->rnk', piece_rows, piece_t, preferred_element_type=jnp...]
    select_n x0 -> x4, other arithmetic: none -> 4.24 us  [the longest x2 2.35 us: exchange_gather_pair(): jnp.where(upper_of(index, side_b), jnp.concatenate([received_b, stack_b],...]
    slice x7 -> x10, local copies, waits for them, and re-layouts: 2.7 us -> 5.48 us  [the longest x4 3.1 us: unpermute_blocks(): product[:, :, i:i + 1]]
    unnamed x14 -> x40, local copies, waits for them, and re-layouts: 3.04 us -> 3.21 us
  transfers between devices with their start and end apart: 7 -> 7, of which waited for: 6 -> 5; matrix products, arithmetic and copies ran while one was open for 10% -> 9% of each run, Pallas kernels for 0% -> 0%
where the time goes in v10:
time: 138 us; the launch traced here: 135 us
  blocking collectives  39.1 us (28%)
  waiting for transfers between devices  36 us (26%)
  starting transfers between devices  26.1 us (19%)
  local copies, waits for them, and re-layouts  19.8 us (14%)
  other arithmetic  9.37 us (7%)
  matrix products  4.1 us (3%)
    all_to_all x1, blocking collectives, per_device(): pieces = lax.all_to_all(pieces, 'tensor', 1, 1, tiled=True)  39.1 us
    ppermute x2, waiting for transfers between devices, exchange_gather_pair(): lax.ppermute(stack_a, axis_name, [(i, i ^ mask_a) for i in range(count)])  15.5 us
    ppermute x2, waiting for transfers between devices, exchange_gather(): lax.ppermute(stack, axis_name, [(i, i ^ mask) for i in range(count)])  15.2 us
    ppermute x2, starting transfers between devices, exchange_gather(): lax.ppermute(stack, axis_name, [(i, i ^ mask) for i in range(count)])  9.68 us
    ppermute x2, starting transfers between devices, exchange_gather_pair(): lax.ppermute(stack_b, axis_name, [(i, i ^ mask_b) for i in range(count)])  6.31 us
    ppermute x1, starting transfers between devices, per_device(): lax.ppermute(mine_weights, 'dp', [(i, i ^ 1) for i in range(dp_size)])  6.04 us
    ppermute x2, waiting for transfers between devices, exchange_gather_pair(): lax.ppermute(stack_b, axis_name, [(i, i ^ mask_b) for i in range(count)])  5.35 us
    ppermute x2, starting transfers between devices, exchange_gather_pair(): lax.ppermute(stack_a, axis_name, [(i, i ^ mask_a) for i in range(count)])  4.07 us
  transfers between devices with their start and end apart: 7, of which 5 were waited for; matrix products, arithmetic and copies ran while one was open for 9% of the time, Pallas kernels for 0%

profile of v10, /device:TPU:1, one launch (start us, length us, event | category | flops | bytes accessed | tf_op | source)
XLA Modules:
  0.0 135.1 jit_solution(11729369959339368998)
XLA Ops:
  0.0 0.9 dynamic-slice_bitcast_fusion.1
  1.2 0.8 maximum_bitcast_fusion
  2.0 5.0 %collective-permute-start = (bf16[128,1,768]{2,0,1:T(8,128)(2,1)S(1)}, bf16[128,1,768]{2,0,1:T(8,128)(2,1)S(1)}, u32[]{:S(2)}, u32[]{:S(2)}) collective-permute-start(bf16[128,1,768]{2,0,1:T(8,128)(2,1)S(1)} %maximum_bitcast_fusion), channel_id=1, source_target_pairs={{0,64},{8,72},{16,80},{24,88},{32,96},{40,104},{48,112},{56,120},{... | collective-permute-start | bytes 589832 | tf_op jit(solution)/shard_map/ppermute | solution.py:51
  7.1 7.2 %collective-permute-done = bf16[128,1,768]{2,0,1:T(8,128)(2,1)S(1)} collective-permute-done((bf16[128,1,768]{2,0,1:T(8,128)(2,1)S(1)}, bf16[128,1,768]{2,0,1:T(8,128)(2,1)S(1)}, u32[]{:S(2)}, u32[]{:S(2)}) %collective-permute-start) | collective-permute-done | bytes 196640 | tf_op jit(solution)/shard_map/ppermute | solution.py:51
  14.4 4.6 %collective-permute-start.1 = (bf16[128,2,768]{2,0,1:T(8,128)(2,1)S(1)}, bf16[128,2,768]{2,0,1:T(8,128)(2,1)S(1)}, u32[]{:S(2)}, u32[]{:S(2)}) collective-permute-start(bf16[128,2,768]{2,0,1:T(8,128)(2,1)S(1)} %maximum_select_fusion.5), channel_id=1, source_target_pairs={{0,32},{8,40},{16,48},{24,56},{32,0},{40,8},{48,16},{56,24},{64,96... | collective-permute-start | bytes 1179656 | tf_op jit(solution)/shard_map/ppermute | solution.py:51
  19.0 7.9 %collective-permute-done.1 = bf16[128,2,768]{2,0,1:T(8,128)(2,1)S(1)} collective-permute-done((bf16[128,2,768]{2,0,1:T(8,128)(2,1)S(1)}, bf16[128,2,768]{2,0,1:T(8,128)(2,1)S(1)}, u32[]{:S(2)}, u32[]{:S(2)}) %collective-permute-start.1) | collective-permute-done | bytes 393248 | tf_op jit(solution)/shard_map/ppermute | solution.py:51
  27.2 4.4 %collective-permute-start.3 = (bf16[128,4,384]{2,0,1:T(8,128)(2,1)S(1)}, bf16[128,4,384]{2,0,1:T(8,128)(2,1)S(1)}, u32[]{:S(2)}, u32[]{:S(2)}) collective-permute-start(bf16[128,4,384]{2,0,1:T(8,128)(2,1)S(1)} %get-tuple-element.39), channel_id=1, source_target_pairs={{0,24},{8,16},{16,8},{24,0},{32,56},{40,48},{48,40},{56,32},{64,88... | collective-permute-start | bytes 1179656 | tf_op jit(solution)/shard_map/ppermute | solution.py:85
  31.6 1.9 %collective-permute-start.2 = (bf16[128,4,384]{2,0,1:T(8,128)(2,1)S(1)}, bf16[128,4,384]{2,0,1:T(8,128)(2,1)S(1)}, u32[]{:S(2)}, u32[]{:S(2)}) collective-permute-start(bf16[128,4,384]{2,0,1:T(8,128)(2,1)S(1)} %get-tuple-element.40), channel_id=1, source_target_pairs={{0,8},{8,0},{16,24},{24,16},{32,40},{40,32},{48,56},{56,48},{64,72... | collective-permute-start | bytes 1179656 | tf_op jit(solution)/shard_map/ppermute | solution.py:84
  33.6 5.4 %collective-permute-done.3 = bf16[128,4,384]{2,0,1:T(8,128)(2,1)S(1)} collective-permute-done((bf16[128,4,384]{2,0,1:T(8,128)(2,1)S(1)}, bf16[128,4,384]{2,0,1:T(8,128)(2,1)S(1)}, u32[]{:S(2)}, u32[]{:S(2)}) %collective-permute-start.3) | collective-permute-done | bytes 393248 | tf_op jit(solution)/shard_map/ppermute | solution.py:85
  39.0 2.7 %collective-permute-done.2 = bf16[128,4,384]{2,0,1:T(8,128)(2,1)S(1)} collective-permute-done((bf16[128,4,384]{2,0,1:T(8,128)(2,1)S(1)}, bf16[128,4,384]{2,0,1:T(8,128)(2,1)S(1)}, u32[]{:S(2)}, u32[]{:S(2)}) %collective-permute-start.2) | collective-permute-done | bytes 393248 | tf_op jit(solution)/shard_map/ppermute | solution.py:84
  41.9 2.2 %collective-permute-start.4 = (bf16[128,8,384]{2,0,1:T(8,128)(2,1)S(1)}, bf16[128,8,384]{2,0,1:T(8,128)(2,1)}, u32[]{:S(2)}, u32[]{:S(2)}) collective-permute-start(bf16[128,8,384]{2,0,1:T(8,128)(2,1)S(1)} %maximum_select_fusion.3), channel_id=1, source_target_pairs={{0,24},{8,16},{16,8},{24,0},{32,56},{40,48},{48,40},{56,32},{64,88... | collective-permute-start | bytes 2359304 | tf_op jit(solution)/shard_map/ppermute | solution.py:84
  44.1 1.9 %collective-permute-start.5 = (bf16[128,8,384]{2,0,1:T(8,128)(2,1)S(1)}, bf16[128,8,384]{2,0,1:T(8,128)(2,1)}, u32[]{:S(2)}, u32[]{:S(2)}) collective-permute-start(bf16[128,8,384]{2,0,1:T(8,128)(2,1)S(1)} %maximum_select_fusion.4), channel_id=1, source_target_pairs={{0,8},{8,0},{16,24},{24,16},{32,40},{40,32},{48,56},{56,48},{64,72... | collective-permute-start | bytes 2359304 | tf_op jit(solution)/shard_map/ppermute | solution.py:85
  46.1 0.8 copy.21
  48.2 12.8 %collective-permute-done.4 = bf16[128,8,384]{2,0,1:T(8,128)(2,1)} collective-permute-done((bf16[128,8,384]{2,0,1:T(8,128)(2,1)S(1)}, bf16[128,8,384]{2,0,1:T(8,128)(2,1)}, u32[]{:S(2)}, u32[]{:S(2)}) %collective-permute-start.4) | collective-permute-done | bytes 786464 | tf_op jit(solution)/shard_map/ppermute | solution.py:84
  60.9 1.7 %maximum_select_fusion = bf16[128,16,384]{2,0,1:T(8,128)(2,1)S(1)} fusion(bf16[128,8,384]{2,0,1:T(8,128)(2,1)S(1)} %maximum_select_fusion.3, bf16[128,8,384]{2,0,1:T(8,128)(2,1)} %collective-permute-done.4, pred[]{:T(512)S(6)} %ne.22), kind=kLoop, calls=%fused_computation.14 | loop fusion | flops 2359296 | bytes 3145729 | tf_op jit(solution)/shard_map/jit(_where)/select_n | solution.py:86
  62.7 2.2 %maximum_select_fusion.1 = bf16[128,16,384]{2,0,1:T(8,128)(2,1)S(1)} fusion(bf16[128,8,384]{2,0,1:T(8,128)(2,1)S(1)} %maximum_select_fusion.4, bf16[128,8,384]{2,0,1:T(8,128)(2,1)} %collective-permute-done.5, pred[]{:T(512)S(6)} %ne.27), kind=kLoop, calls=%fused_computation.15 | loop fusion | flops 2359296 | bytes 3145729 | tf_op jit(solution)/shard_map/jit(_where)/select_n | solution.py:91
  65.0 0.7 fusion.41
  65.7 1.9 %slice_bitcast_fusion.2 = (bf16[16,128,256]{2,1,0:T(8,128)(2,1)}, bf16[128,16,256]{2,0,1:T(8,128)(2,1)}, bf16[128,16,256]{2,0,1:T(8,128)(2,1)}, bf16[16,128,256]{2,1,0:T(8,128)(2,1)S(1)}) fusion(bf16[128,16,384]{2,0,1:T(8,128)(2,1)S(1)} %maximum_select_fusion.1, bf16[128,16,384]{2,0,1:T(8,128)(2,1)S(1)} %maximum_select_fusion), kind=kLoop, calls=%fused_computation.52 | loop fusion | bytes 6291456 | tf_op jit(solution)/shard_map/transpose | solution.py:202
  67.6 1.4 %dot_general.32 = bf16[4,4,256,128]{3,2,1,0:T(8,128)(2,1)S(1)} reshape(bf16[16,128,256]{2,1,0:T(8,128)(2,1)} %get-tuple-element.37) | data formatting | bytes 2097152 | tf_op jit(solution)/shard_map/rh,nkh->rnk/dot_general | solution.py:207
  69.5 1.8 %pad_maximum_fusion = bf16[256,16,256]{2,0,1:T(8,128)(2,1)S(1)} fusion(bf16[128,16,256]{2,0,1:T(8,128)(2,1)} %get-tuple-element.38, bf16[128,16,256]{2,0,1:T(8,128)(2,1)} %get-tuple-element.47), kind=kLoop, calls=%fused_computation.10 | loop fusion | flops 4194304 | bytes 4194304 | tf_op jit(solution)/shard_map/concatenate | solution.py:154
  71.3 6.0 %collective-permute-start.6 = (bf16[256,16,256]{2,0,1:T(8,128)(2,1)S(1)}, bf16[256,16,256]{2,0,1:T(8,128)(2,1)S(1)}, u32[]{:S(2)}, u32[]{:S(2)}) collective-permute-start(bf16[256,16,256]{2,0,1:T(8,128)(2,1)S(1)} %pad_maximum_fusion), channel_id=1, source_target_pairs={{0,128},{128,0},{256,384},{384,256},{1,129},{129,1},{257,385},{385... | collective-permute-start | bytes 6291464 | tf_op jit(solution)/shard_map/ppermute | solution.py:157
  77.4 0.7 fusion
  78.1 1.3 fusion.1
  79.5 1.6 %fusion.11 = bf16[512,128]{1,0:T(8,128)(2,1)S(1)} fusion(bf16[2048,128]{1,0:T(8,128)(2,1)S(1)} %bitcast.94, f32[2048,512]{1,0:T(8,128)S(1)} %get-tuple-element.46, f32[512]{0:T(512)S(1)} %broadcast_maximum_fusion, s32[512]{0:T(512)S(1)} %copy-done.17, s32[2048]{0:T(1024)S(1)} %bitcast.101, f32[512]{0:T(512)S(1)} %fusion.1), kind=kOutput, calls=%fused_computation.17 | convolution fusion | flops 274857984 | bytes 4864000 | tf_op jit(solution)/shard_map/grk,kgd->grd/dot_general | solution.py:186
  82.5 1.4 %fusion.34 = (f32[128,4,1,256]{3,0,2,1:T(8,128)}, f32[128,4,1,256]{3,0,2,1:T(8,128)}, f32[128,4,1,256]{3,0,2,1:T(8,128)}, f32[128,4,1,256]{3,0,2,1:T(8,128)}) fusion(f32[128,4,4,256]{3,0,2,1:T(8,128)S(1)} %fusion.21), kind=kLoop, calls=%fused_computation.54 | loop fusion | bytes 4194304 | tf_op jit(solution)/shard_map/slice | solution.py:77
  83.8 1.4 %fusion.36 = (f32[128,4,1,256]{3,0,2,1:T(8,128)}, f32[128,4,1,256]{3,0,2,1:T(8,128)}, f32[128,4,1,256]{3,0,2,1:T(8,128)}, f32[128,4,1,256]{3,0,2,1:T(8,128)}) fusion(f32[128,4,4,256]{3,0,2,1:T(8,128)S(1)} %pad_maximum_fusion.1), kind=kLoop, calls=%fused_computation.56 | loop fusion | bytes 4194304 | tf_op jit(solution)/shard_map/slice | solution.py:77
  85.2 1.1 slice_bitcast_fusion.1
  87.2 1.1 fusion.39
  90.2 1.0 slice-done
  92.0 0.8 copy-done.4
  95.1 39.1 %all_to_all.5 = bf16[128,8,512]{0,2,1:T(8,128)(2,1)S(1)} all-to-all(bf16[128,8,512]{0,2,1:T(8,128)(2,1)S(1)} %bitcast.87), channel_id=1, replica_groups=mesh['dp'=4,'context'=16,'tensor'=8] {'tensor'}, dimensions={1} | all-to-all | bytes 2097152 | tf_op jit(solution)/shard_map/all_to_all | solution.py:215
  134.3 0.8 copy.24
  (78 shorter events, 9.9 us)
Async XLA Ops:
  0.0 46.9 %copy-start = (s32[2048]{0:T(1024)S(1)}, s32[2048]{0:T(1024)}, u32[]{:S(2)}) copy-start(s32[2048]{0:T(1024)} %param.9) | copy-start | bytes 24580
  2.0 12.3 %collective-permute-start = (bf16[128,1,768]{2,0,1:T(8,128)(2,1)S(1)}, bf16[128,1,768]{2,0,1:T(8,128)(2,1)S(1)}, u32[]{:S(2)}, u32[]{:S(2)}) collective-permute-start(bf16[128,1,768]{2,0,1:T(8,128)(2,1)S(1)} %maximum_bitcast_fusion), channel_id=1, source_target_pairs={{0,64},{8,72},{16,80},{24,88},{32,96},{40,104},{48,112},{56,120},{... | collective-permute-start | bytes 589832 | tf_op jit(solution)/shard_map/ppermute | solution.py:51
  14.4 12.6 %collective-permute-start.1 = (bf16[128,2,768]{2,0,1:T(8,128)(2,1)S(1)}, bf16[128,2,768]{2,0,1:T(8,128)(2,1)S(1)}, u32[]{:S(2)}, u32[]{:S(2)}) collective-permute-start(bf16[128,2,768]{2,0,1:T(8,128)(2,1)S(1)} %maximum_select_fusion.5), channel_id=1, source_target_pairs={{0,32},{8,40},{16,48},{24,56},{32,0},{40,8},{48,16},{56,24},{64,96... | collective-permute-start | bytes 1179656 | tf_op jit(solution)/shard_map/ppermute | solution.py:51
  27.1 18.9 %copy-start.15 = (bf16[128,512]{1,0:T(8,128)(2,1)S(1)}, bf16[128,512]{1,0:T(8,128)(2,1)}, u32[]{:S(2)}) copy-start(bf16[128,512]{1,0:T(8,128)(2,1)} %param.6) | copy-start | bytes 393220
  27.2 19.8 %copy-start.18 = (s32[16]{0:T(128)S(1)}, s32[16]{0:T(128)}, u32[]{:S(2)}) copy-start(s32[16]{0:T(128)} %constant.64) | copy-start | bytes 196
  27.2 11.7 %collective-permute-start.3 = (bf16[128,4,384]{2,0,1:T(8,128)(2,1)S(1)}, bf16[128,4,384]{2,0,1:T(8,128)(2,1)S(1)}, u32[]{:S(2)}, u32[]{:S(2)}) collective-permute-start(bf16[128,4,384]{2,0,1:T(8,128)(2,1)S(1)} %get-tuple-element.39), channel_id=1, source_target_pairs={{0,24},{8,16},{16,8},{24,0},{32,56},{40,48},{48,40},{56,32},{64,88... | collective-permute-start | bytes 1179656 | tf_op jit(solution)/shard_map/ppermute | solution.py:85
  31.6 10.1 %collective-permute-start.2 = (bf16[128,4,384]{2,0,1:T(8,128)(2,1)S(1)}, bf16[128,4,384]{2,0,1:T(8,128)(2,1)S(1)}, u32[]{:S(2)}, u32[]{:S(2)}) collective-permute-start(bf16[128,4,384]{2,0,1:T(8,128)(2,1)S(1)} %get-tuple-element.40), channel_id=1, source_target_pairs={{0,8},{8,0},{16,24},{24,16},{32,40},{40,32},{48,56},{56,48},{64,72... | collective-permute-start | bytes 1179656 | tf_op jit(solution)/shard_map/ppermute | solution.py:84
  41.9 19.0 %collective-permute-start.4 = (bf16[128,8,384]{2,0,1:T(8,128)(2,1)S(1)}, bf16[128,8,384]{2,0,1:T(8,128)(2,1)}, u32[]{:S(2)}, u32[]{:S(2)}) collective-permute-start(bf16[128,8,384]{2,0,1:T(8,128)(2,1)S(1)} %maximum_select_fusion.3), channel_id=1, source_target_pairs={{0,24},{8,16},{16,8},{24,0},{32,56},{40,48},{48,40},{56,32},{64,88... | collective-permute-start | bytes 2359304 | tf_op jit(solution)/shard_map/ppermute | solution.py:84
  44.1 18.6 %collective-permute-start.5 = (bf16[128,8,384]{2,0,1:T(8,128)(2,1)S(1)}, bf16[128,8,384]{2,0,1:T(8,128)(2,1)}, u32[]{:S(2)}, u32[]{:S(2)}) collective-permute-start(bf16[128,8,384]{2,0,1:T(8,128)(2,1)S(1)} %maximum_select_fusion.4), channel_id=1, source_target_pairs={{0,8},{8,0},{16,24},{24,16},{32,40},{40,32},{48,56},{56,48},{64,72... | collective-permute-start | bytes 2359304 | tf_op jit(solution)/shard_map/ppermute | solution.py:85
  62.7 3.0 %copy-start.2 = (bf16[128,16,384]{2,0,1:T(8,128)(2,1)}, bf16[128,16,384]{2,0,1:T(8,128)(2,1)S(1)}, u32[]{:S(2)}) copy-start(bf16[128,16,384]{2,0,1:T(8,128)(2,1)S(1)} %maximum_select_fusion) | copy-start | bytes 4718596
  69.5 7.9 %slice-start.1 = ((bf16[128,16,384]{2,0,1:T(8,128)(2,1)}), bf16[128,16,128]{2,0,1:T(8,128)(2,1)S(1)}, s32[]{:S(2)}) async-start(bf16[128,16,384]{2,0,1:T(8,128)(2,1)} %copy-done.2), calls=%async_computation.2 | async-start | bytes 1048576 | tf_op jit(solution)/shard_map/slice | solution.py:159
  69.5 7.9 %copy-start.16 = (bf16[1,4,128,128]{3,2,1,0:T(8,128)(2,1)S(1)}, bf16[1,4,128,128]{3,2,1,0:T(8,128)(2,1)}, u32[]{:S(2)}) copy-start(bf16[1,4,128,128]{3,2,1,0:T(8,128)(2,1)} %copy.21) | copy-start | bytes 393220
  69.5 7.9 %copy-start.17 = (s32[512]{0:T(512)S(1)}, s32[512]{0:T(512)}, u32[]{:S(2)}) copy-start(s32[512]{0:T(512)} %broadcast_bitcast_fusion) | copy-start | bytes 6148
  71.3 13.9 %collective-permute-start.6 = (bf16[256,16,256]{2,0,1:T(8,128)(2,1)S(1)}, bf16[256,16,256]{2,0,1:T(8,128)(2,1)S(1)}, u32[]{:S(2)}, u32[]{:S(2)}) collective-permute-start(bf16[256,16,256]{2,0,1:T(8,128)(2,1)S(1)} %pad_maximum_fusion), channel_id=1, source_target_pairs={{0,128},{128,0},{256,384},{384,256},{1,129},{129,1},{257,385},{385... | collective-permute-start | bytes 6291464 | tf_op jit(solution)/shard_map/ppermute | solution.py:157
  78.1 1.3 copy-start.14
  87.2 1.7 %copy-start.1 = (f32[128,4,4,256]{3,0,2,1:T(8,128)}, f32[128,4,4,256]{3,0,2,1:T(8,128)S(1)}, u32[]{:S(2)}) copy-start(f32[128,4,4,256]{3,0,2,1:T(8,128)S(1)} %fusion.15) | copy-start | bytes 6291460
  87.2 2.0 %copy-start.3 = (bf16[16,128,256]{2,1,0:T(8,128)(2,1)S(1)}, bf16[16,128,256]{2,1,0:T(8,128)(2,1)}, u32[]{:S(2)}) copy-start(bf16[16,128,256]{2,1,0:T(8,128)(2,1)} %get-tuple-element.21) | copy-start | bytes 3145732
  90.0 1.2 slice-start
  90.0 1.3 copy-start.12
  90.0 1.5 %copy-start.13 = (f32[128,1,4,256]{3,0,2,1:T(8,128)S(1)}, f32[128,1,4,256]{3,0,2,1:T(8,128)}, u32[]{:S(2)}) copy-start(f32[128,1,4,256]{3,0,2,1:T(8,128)} %get-tuple-element.34) | copy-start | bytes 1572868
  91.7 1.0 copy-start.4
  91.7 1.2 copy-start.5
  91.7 1.3 copy-start.6
  91.7 1.5 %copy-start.7 = (f32[128,4,1,256]{3,0,2,1:T(8,128)S(1)}, f32[128,4,1,256]{3,0,2,1:T(8,128)}, u32[]{:S(2)}) copy-start(f32[128,4,1,256]{3,0,2,1:T(8,128)} %get-tuple-element.16) | copy-start | bytes 1572868
  91.7 1.6 %copy-start.8 = (f32[128,4,1,256]{3,0,2,1:T(8,128)S(1)}, f32[128,4,1,256]{3,0,2,1:T(8,128)}, u32[]{:S(2)}) copy-start(f32[128,4,1,256]{3,0,2,1:T(8,128)} %get-tuple-element.23) | copy-start | bytes 1572868
  91.7 1.8 %copy-start.9 = (f32[128,4,1,256]{3,0,2,1:T(8,128)S(1)}, f32[128,4,1,256]{3,0,2,1:T(8,128)}, u32[]{:S(2)}) copy-start(f32[128,4,1,256]{3,0,2,1:T(8,128)} %get-tuple-element.24) | copy-start | bytes 1572868
  91.8 1.9 %copy-start.10 = (f32[128,4,1,256]{3,0,2,1:T(8,128)S(1)}, f32[128,4,1,256]{3,0,2,1:T(8,128)}, u32[]{:S(2)}) copy-start(f32[128,4,1,256]{3,0,2,1:T(8,128)} %get-tuple-element.25) | copy-start | bytes 1572868
  91.8 2.1 %copy-start.11 = (f32[128,4,1,256]{3,0,2,1:T(8,128)S(1)}, f32[128,4,1,256]{3,0,2,1:T(8,128)}, u32[]{:S(2)}) copy-start(f32[128,4,1,256]{3,0,2,1:T(8,128)} %get-tuple-element.26) | copy-start | bytes 1572868

commit v11 on v10

--- a/solution.py
+++ b/solution.py
@@ -197,6 +197,7 @@
 
     total = None
     for piece, sources in ((0, sources_a), (1, sources_b)):
+        piece_sum = None
         for which, held in ((0, mine_weights), (1, other_weights)):
             piece_t = held[piece * row_count : (piece + 1) * row_count]
             piece_t = jnp.swapaxes(piece_t, 0, 1).reshape(context_size, weight_cols, quarter)
@@ -207,8 +208,9 @@
             product_out = jnp.einsum(
                 "rh,nkh->rnk", piece_rows, piece_t, preferred_element_type=jnp.float32
             ).reshape(row_count, -1)
-            product_out = unpermute_blocks(product_out, sources, x_size)
-            total = product_out if total is None else total + product_out
+            piece_sum = product_out if piece_sum is None else piece_sum + product_out
+        piece_sum = unpermute_blocks(piece_sum, sources, x_size)
+        total = piece_sum if total is None else total + piece_sum
     partial_out = total
     tensor_size = lax.axis_size("tensor")
     pieces = partial_out.astype(jnp.bfloat16).reshape(row_count, tensor_size, -1)

time: 138 us -> 161 us (1.17)
  local copies, waits for them, and re-layouts: 19.8 us -> 34 us
  matrix products: 4.1 us -> 12.6 us
    unnamed x40 -> x28, local copies, waits for them, and re-layouts: 3.21 us -> 12.4 us
    dot_general x4, matrix products: 1.75 us -> 10.3 us  [per_device(): jnp.einsum('rh,nkh->rnk', piece_rows, piece_t, preferred_element_type=jnp...]
    reshape x0 -> x3, local copies, waits for them, and re-layouts: none -> 6.43 us  [the longest x2 6.3 us: unpermute_blocks(): product = product.reshape(rows, x_size, y_count, -1)]
    select_n x2, other arithmetic: 2.35 us -> 0.41 us  [exchange_gather_pair(): jnp.where(upper_of(index, side_b), jnp.concatenate([received_b, stack_b],...]
    slice x4 -> x2, local copies, waits for them, and re-layouts: 3.1 us -> 4.16 us  [unpermute_blocks(): product[:, :, i:i + 1]]
  transfers between devices with their start and end apart: 7 -> 7, of which waited for: 5 -> 6; matrix products, arithmetic and copies ran while one was open for 9% -> 6% of each run, Pallas kernels for 0% -> 0%
where the time goes in v11:
time: 161 us; the launch traced here: 158 us
  blocking collectives  39 us (24%)
  waiting for transfers between devices  37.5 us (23%)
  local copies, waits for them, and re-layouts  34 us (21%)
  starting transfers between devices  26.3 us (16%)
  matrix products  12.6 us (8%)
  other arithmetic  7.76 us (5%)
    all_to_all x1, blocking collectives, per_device(): pieces = lax.all_to_all(pieces, 'tensor', 1, 1, tiled=True)  39 us
    ppermute x2, waiting for transfers between devices, exchange_gather_pair(): lax.ppermute(stack_a, axis_name, [(i, i ^ mask_a) for i in range(count)])  16.6 us
    ppermute x2, waiting for transfers between devices, exchange_gather(): lax.ppermute(stack, axis_name, [(i, i ^ mask) for i in range(count)])  15.2 us
    unnamed x28, local copies, waits for them, and re-layouts  12.4 us
    dot_general x4, matrix products, per_device(): jnp.einsum('rh,nkh->rnk', piece_rows, piece_t, preferred_element_type=jnp...  10.3 us
    ppermute x2, starting transfers between devices, exchange_gather(): lax.ppermute(stack, axis_name, [(i, i ^ mask) for i in range(count)])  9.68 us
    ppermute x2, starting transfers between devices, exchange_gather_pair(): lax.ppermute(stack_b, axis_name, [(i, i ^ mask_b) for i in range(count)])  6.31 us
    reshape x2, local copies, waits for them, and re-layouts, unpermute_blocks(): product = product.reshape(rows, x_size, y_count, -1)  6.3 us
  transfers between devices with their start and end apart: 7, of which 6 were waited for; matrix products, arithmetic and copies ran while one was open for 6% of the time, Pallas kernels for 0%

profile of v11, /device:TPU:1, one launch (start us, length us, event | category | flops | bytes accessed | tf_op | source)
XLA Modules:
  0.0 157.6 jit_solution(8391241282479891635)
XLA Ops:
  2.0 5.0 %collective-permute-start = (bf16[128,1,768]{2,0,1:T(8,128)(2,1)S(1)}, bf16[128,1,768]{2,0,1:T(8,128)(2,1)S(1)}, u32[]{:S(2)}, u32[]{:S(2)}) collective-permute-start(bf16[128,1,768]{2,0,1:T(8,128)(2,1)S(1)} %maximum_bitcast_fusion), channel_id=1, source_target_pairs={{0,64},{8,72},{16,80},{24,88},{32,96},{40,104},{48,112},{56,120},{... | collective-permute-start | bytes 589832 | tf_op jit(solution)/shard_map/ppermute | solution.py:51
  7.1 7.2 %collective-permute-done = bf16[128,1,768]{2,0,1:T(8,128)(2,1)S(1)} collective-permute-done((bf16[128,1,768]{2,0,1:T(8,128)(2,1)S(1)}, bf16[128,1,768]{2,0,1:T(8,128)(2,1)S(1)}, u32[]{:S(2)}, u32[]{:S(2)}) %collective-permute-start) | collective-permute-done | bytes 196640 | tf_op jit(solution)/shard_map/ppermute | solution.py:51
  14.4 4.6 %collective-permute-start.1 = (bf16[128,2,768]{2,0,1:T(8,128)(2,1)S(1)}, bf16[128,2,768]{2,0,1:T(8,128)(2,1)S(1)}, u32[]{:S(2)}, u32[]{:S(2)}) collective-permute-start(bf16[128,2,768]{2,0,1:T(8,128)(2,1)S(1)} %maximum_select_fusion.5), channel_id=1, source_target_pairs={{0,32},{8,40},{16,48},{24,56},{32,0},{40,8},{48,16},{56,24},{64,96... | collective-permute-start | bytes 1179656 | tf_op jit(solution)/shard_map/ppermute | solution.py:51
  19.0 7.9 %collective-permute-done.1 = bf16[128,2,768]{2,0,1:T(8,128)(2,1)S(1)} collective-permute-done((bf16[128,2,768]{2,0,1:T(8,128)(2,1)S(1)}, bf16[128,2,768]{2,0,1:T(8,128)(2,1)S(1)}, u32[]{:S(2)}, u32[]{:S(2)}) %collective-permute-start.1) | collective-permute-done | bytes 393248 | tf_op jit(solution)/shard_map/ppermute | solution.py:51
  27.2 4.4 %collective-permute-start.3 = (bf16[128,4,384]{2,0,1:T(8,128)(2,1)S(1)}, bf16[128,4,384]{2,0,1:T(8,128)(2,1)S(1)}, u32[]{:S(2)}, u32[]{:S(2)}) collective-permute-start(bf16[128,4,384]{2,0,1:T(8,128)(2,1)S(1)} %get-tuple-element.29), channel_id=1, source_target_pairs={{0,24},{8,16},{16,8},{24,0},{32,56},{40,48},{48,40},{56,32},{64,88... | collective-permute-start | bytes 1179656 | tf_op jit(solution)/shard_map/ppermute | solution.py:85
  31.6 1.9 %collective-permute-start.2 = (bf16[128,4,384]{2,0,1:T(8,128)(2,1)S(1)}, bf16[128,4,384]{2,0,1:T(8,128)(2,1)S(1)}, u32[]{:S(2)}, u32[]{:S(2)}) collective-permute-start(bf16[128,4,384]{2,0,1:T(8,128)(2,1)S(1)} %get-tuple-element.30), channel_id=1, source_target_pairs={{0,8},{8,0},{16,24},{24,16},{32,40},{40,32},{48,56},{56,48},{64,72... | collective-permute-start | bytes 1179656 | tf_op jit(solution)/shard_map/ppermute | solution.py:84
  33.6 5.4 %collective-permute-done.3 = bf16[128,4,384]{2,0,1:T(8,128)(2,1)S(1)} collective-permute-done((bf16[128,4,384]{2,0,1:T(8,128)(2,1)S(1)}, bf16[128,4,384]{2,0,1:T(8,128)(2,1)S(1)}, u32[]{:S(2)}, u32[]{:S(2)}) %collective-permute-start.3) | collective-permute-done | bytes 393248 | tf_op jit(solution)/shard_map/ppermute | solution.py:85
  39.0 2.7 %collective-permute-done.2 = bf16[128,4,384]{2,0,1:T(8,128)(2,1)S(1)} collective-permute-done((bf16[128,4,384]{2,0,1:T(8,128)(2,1)S(1)}, bf16[128,4,384]{2,0,1:T(8,128)(2,1)S(1)}, u32[]{:S(2)}, u32[]{:S(2)}) %collective-permute-start.2) | collective-permute-done | bytes 393248 | tf_op jit(solution)/shard_map/ppermute | solution.py:84
  41.9 2.2 %collective-permute-start.4 = (bf16[128,8,384]{2,0,1:T(8,128)(2,1)S(1)}, bf16[128,8,384]{2,0,1:T(8,128)(2,1)S(1)}, u32[]{:S(2)}, u32[]{:S(2)}) collective-permute-start(bf16[128,8,384]{2,0,1:T(8,128)(2,1)S(1)} %maximum_select_fusion.3), channel_id=1, source_target_pairs={{0,24},{8,16},{16,8},{24,0},{32,56},{40,48},{48,40},{56,32},{64,88... | collective-permute-start | bytes 2359304 | tf_op jit(solution)/shard_map/ppermute | solution.py:84
  44.1 1.9 %collective-permute-start.5 = (bf16[128,8,384]{2,0,1:T(8,128)(2,1)S(1)}, bf16[128,8,384]{2,0,1:T(8,128)(2,1)S(1)}, u32[]{:S(2)}, u32[]{:S(2)}) collective-permute-start(bf16[128,8,384]{2,0,1:T(8,128)(2,1)S(1)} %maximum_select_fusion.4), channel_id=1, source_target_pairs={{0,8},{8,0},{16,24},{24,16},{32,40},{40,32},{48,56},{56,48},{64,72... | collective-permute-start | bytes 2359304 | tf_op jit(solution)/shard_map/ppermute | solution.py:85
  47.0 13.8 %collective-permute-done.4 = bf16[128,8,384]{2,0,1:T(8,128)(2,1)S(1)} collective-permute-done((bf16[128,8,384]{2,0,1:T(8,128)(2,1)S(1)}, bf16[128,8,384]{2,0,1:T(8,128)(2,1)S(1)}, u32[]{:S(2)}, u32[]{:S(2)}) %collective-permute-start.4) | collective-permute-done | bytes 786464 | tf_op jit(solution)/shard_map/ppermute | solution.py:84
  62.7 1.5 pad_maximum_fusion
  64.1 6.2 %collective-permute-start.6 = (bf16[256,16,256]{2,0,1:T(8,128)(2,1)}, bf16[256,16,256]{2,0,1:T(8,128)(2,1)}, u32[]{:S(2)}, u32[]{:S(2)}) collective-permute-start(bf16[256,16,256]{2,0,1:T(8,128)(2,1)} %pad_maximum_fusion), channel_id=1, source_target_pairs={{0,128},{128,0},{256,384},{384,256},{1,129},{129,1},{257,385},{385... | collective-permute-start | bytes 6291464 | tf_op jit(solution)/shard_map/ppermute | solution.py:157
  71.2 1.3 fusion.1
  72.4 1.6 %fusion.9 = bf16[512,128]{1,0:T(8,128)(2,1)S(1)} fusion(bf16[2048,128]{1,0:T(8,128)(2,1)S(1)} %bitcast.69, f32[2048,512]{1,0:T(8,128)S(1)} %get-tuple-element.36, f32[512]{0:T(512)S(1)} %broadcast_maximum_fusion, s32[512]{0:T(512)S(1)} %broadcast_bitcast_fusion, s32[2048]{0:T(1024)S(1)} %bitcast.75, f32[512]{0:T(512)S(1)} %fusion.1), kind=kOutput, calls=%fused_computation.16 | convolution fusion | flops 274857984 | bytes 4864000 | tf_op jit(solution)/shard_map/grk,kgd->grd/dot_general | solution.py:186
  75.7 1.7 %fusion.16 = f32[128,4096]{1,0:T(8,128)S(1)} fusion(bf16[4096,128]{1,0:T(8,128)(2,1)} %dot_general.28, bf16[128,512]{0,1:T(8,128)(2,1)S(1)} %bitcast.65, s32[]{:T(128)S(6)} %select_n.86), kind=kOutput, calls=%fused_computation.31 | convolution fusion | flops 134217728 | bytes 3178500 | tf_op jit(solution)/shard_map/rh,nkh->rnk/dot_general | solution.py:208
  77.4 1.8 %fusion.13 = f32[128,4096]{1,0:T(8,128)} fusion(bf16[4096,128]{1,0:T(8,128)(2,1)S(1)} %dot_general.32, bf16[128,512]{0,1:T(8,128)(2,1)S(1)} %bitcast.66, s32[]{:T(128)S(6)} %select_n.98), kind=kOutput, calls=%fused_computation.28 | convolution fusion | flops 134217728 | bytes 3178500 | tf_op jit(solution)/shard_map/rh,nkh->rnk/dot_general | solution.py:208
  79.3 2.7 %slice_bitcast_fusion = (bf16[16,128,256]{2,1,0:T(8,128)(2,1)S(1)}, bf16[16,128,256]{2,1,0:T(8,128)(2,1)}) fusion(bf16[256,16,256]{2,0,1:T(8,128)(2,1)} %collective-permute-done.6), kind=kLoop, calls=%fused_computation.17 | loop fusion | bytes 4194304 | tf_op jit(solution)/shard_map/transpose | solution.py:203
  83.1 3.7 %convolution_add_fusion = f32[128,4096]{1,0:T(8,128)} fusion(f32[128,4096]{1,0:T(8,128)} %fusion.13, bf16[4096,128]{1,0:T(8,128)(2,1)} %dot_general.34, bf16[128,512]{0,1:T(8,128)(2,1)S(1)} %bitcast.67, s32[]{:T(128)S(6)} %select_n.99), kind=kOutput, calls=%fused_computation.3 | convolution fusion | flops 134742016 | bytes 5275652 | tf_op jit(solution)/shard_map/rh,nkh->rnk/dot_general | solution.py:208
  86.8 3.6 %reshape.113 = f32[128,4,4,256]{3,2,1,0:T(4,128)} reshape(f32[128,4096]{1,0:T(8,128)} %convolution_add_fusion) | data formatting | bytes 4194304 | tf_op jit(solution)/shard_map/reshape | solution.py:71
  90.5 1.6 %copy-done.1 = f32[128,4,4,256]{3,2,1,0:T(4,128)S(1)} copy-done((f32[128,4,4,256]{3,2,1,0:T(4,128)S(1)}, f32[128,4,4,256]{3,2,1,0:T(4,128)}, u32[]{:S(2)}) %copy-start.1) | copy-done | bytes 2097176
  93.2 1.4 copy.47
  94.6 2.1 %copy.46 = f32[128,1,4,256]{0,3,1,2:T(8,128)} copy(f32[128,1,4,256]{3,2,1,0:T(4,128)} %get-tuple-element.17) | data formatting | bytes 1048576
  96.8 2.1 %copy.48 = f32[128,1,4,256]{0,3,1,2:T(8,128)} copy(f32[128,1,4,256]{3,2,1,0:T(4,128)} %get-tuple-element.18) | data formatting | bytes 1048576
  98.8 1.5 pad_maximum_fusion.1
  100.3 1.4 fusion.25
  103.3 3.0 %convolution_add_fusion.1 = f32[128,4096]{1,0:T(8,128)} fusion(f32[128,4096]{1,0:T(8,128)S(1)} %fusion.16, bf16[4096,128]{1,0:T(8,128)(2,1)} %dot_general.30, bf16[128,512]{0,1:T(8,128)(2,1)S(1)} %bitcast.68, s32[]{:T(128)S(6)} %select_n.97), kind=kOutput, calls=%fused_computation.4 | convolution fusion | flops 134742016 | bytes 5275652 | tf_op jit(solution)/shard_map/rh,nkh->rnk/dot_general | solution.py:208
  106.4 2.7 %reshape.112 = f32[128,4,4,256]{3,2,1,0:T(4,128)S(1)} reshape(f32[128,4096]{1,0:T(8,128)} %convolution_add_fusion.1) | data formatting | bytes 4194304 | tf_op jit(solution)/shard_map/reshape | solution.py:71
  109.0 2.8 %fusion.27 = (f32[128,4,1,256]{3,2,1,0:T(1,128)}, f32[128,4,1,256]{3,2,1,0:T(1,128)}, f32[128,4,1,256]{3,2,1,0:T(1,128)}, f32[128,4,1,256]{3,2,1,0:T(1,128)}) fusion(f32[128,4,4,256]{3,2,1,0:T(4,128)S(1)} %reshape.112), kind=kLoop, calls=%fused_computation.47 | loop fusion | bytes 4194304 | tf_op jit(solution)/shard_map/slice | solution.py:77
  111.8 1.4 copy.42
  116.1 1.6 fusion.3
  117.7 39.0 %all_to_all.5 = bf16[128,8,512]{0,2,1:T(8,128)(2,1)S(1)} all-to-all(bf16[128,8,512]{0,2,1:T(8,128)(2,1)S(1)} %bitcast.62), channel_id=1, replica_groups=mesh['dp'=4,'context'=16,'tensor'=8] {'tensor'}, dimensions={1} | all-to-all | bytes 2097152 | tf_op jit(solution)/shard_map/all_to_all | solution.py:217
  (62 shorter events, 15.5 us)
Async XLA Ops:
  0.0 46.3 %copy-start = (s32[2048]{0:T(1024)S(1)}, s32[2048]{0:T(1024)}, u32[]{:S(2)}) copy-start(s32[2048]{0:T(1024)} %param.9) | copy-start | bytes 24580
  2.0 12.3 %collective-permute-start = (bf16[128,1,768]{2,0,1:T(8,128)(2,1)S(1)}, bf16[128,1,768]{2,0,1:T(8,128)(2,1)S(1)}, u32[]{:S(2)}, u32[]{:S(2)}) collective-permute-start(bf16[128,1,768]{2,0,1:T(8,128)(2,1)S(1)} %maximum_bitcast_fusion), channel_id=1, source_target_pairs={{0,64},{8,72},{16,80},{24,88},{32,96},{40,104},{48,112},{56,120},{... | collective-permute-start | bytes 589832 | tf_op jit(solution)/shard_map/ppermute | solution.py:51
  14.4 12.6 %collective-permute-start.1 = (bf16[128,2,768]{2,0,1:T(8,128)(2,1)S(1)}, bf16[128,2,768]{2,0,1:T(8,128)(2,1)S(1)}, u32[]{:S(2)}, u32[]{:S(2)}) collective-permute-start(bf16[128,2,768]{2,0,1:T(8,128)(2,1)S(1)} %maximum_select_fusion.5), channel_id=1, source_target_pairs={{0,32},{8,40},{16,48},{24,56},{32,0},{40,8},{48,16},{56,24},{64,96... | collective-permute-start | bytes 1179656 | tf_op jit(solution)/shard_map/ppermute | solution.py:51
  27.1 18.9 %copy-start.8 = (bf16[128,512]{1,0:T(8,128)(2,1)S(1)}, bf16[128,512]{1,0:T(8,128)(2,1)}, u32[]{:S(2)}) copy-start(bf16[128,512]{1,0:T(8,128)(2,1)} %param.6) | copy-start | bytes 393220
  27.2 19.2 %copy-start.9 = (s32[16]{0:T(128)S(1)}, s32[16]{0:T(128)}, u32[]{:S(2)}) copy-start(s32[16]{0:T(128)} %constant.64) | copy-start | bytes 196
  27.2 11.7 %collective-permute-start.3 = (bf16[128,4,384]{2,0,1:T(8,128)(2,1)S(1)}, bf16[128,4,384]{2,0,1:T(8,128)(2,1)S(1)}, u32[]{:S(2)}, u32[]{:S(2)}) collective-permute-start(bf16[128,4,384]{2,0,1:T(8,128)(2,1)S(1)} %get-tuple-element.29), channel_id=1, source_target_pairs={{0,24},{8,16},{16,8},{24,0},{32,56},{40,48},{48,40},{56,32},{64,88... | collective-permute-start | bytes 1179656 | tf_op jit(solution)/shard_map/ppermute | solution.py:85
  31.6 10.1 %collective-permute-start.2 = (bf16[128,4,384]{2,0,1:T(8,128)(2,1)S(1)}, bf16[128,4,384]{2,0,1:T(8,128)(2,1)S(1)}, u32[]{:S(2)}, u32[]{:S(2)}) collective-permute-start(bf16[128,4,384]{2,0,1:T(8,128)(2,1)S(1)} %get-tuple-element.30), channel_id=1, source_target_pairs={{0,8},{8,0},{16,24},{24,16},{32,40},{40,32},{48,56},{56,48},{64,72... | collective-permute-start | bytes 1179656 | tf_op jit(solution)/shard_map/ppermute | solution.py:84
  41.9 18.9 %collective-permute-start.4 = (bf16[128,8,384]{2,0,1:T(8,128)(2,1)S(1)}, bf16[128,8,384]{2,0,1:T(8,128)(2,1)S(1)}, u32[]{:S(2)}, u32[]{:S(2)}) collective-permute-start(bf16[128,8,384]{2,0,1:T(8,128)(2,1)S(1)} %maximum_select_fusion.3), channel_id=1, source_target_pairs={{0,24},{8,16},{16,8},{24,0},{32,56},{40,48},{48,40},{56,32},{64,88... | collective-permute-start | bytes 2359304 | tf_op jit(solution)/shard_map/ppermute | solution.py:84
  44.1 17.5 %collective-permute-start.5 = (bf16[128,8,384]{2,0,1:T(8,128)(2,1)S(1)}, bf16[128,8,384]{2,0,1:T(8,128)(2,1)S(1)}, u32[]{:S(2)}, u32[]{:S(2)}) collective-permute-start(bf16[128,8,384]{2,0,1:T(8,128)(2,1)S(1)} %maximum_select_fusion.4), channel_id=1, source_target_pairs={{0,8},{8,0},{16,24},{24,16},{32,40},{40,32},{48,56},{56,48},{64,72... | collective-permute-start | bytes 2359304 | tf_op jit(solution)/shard_map/ppermute | solution.py:85
  61.1 1.2 copy-start.2
  62.6 7.8 %slice-start.1 = ((bf16[128,16,384]{2,0,1:T(8,128)(2,1)}), bf16[128,16,128]{2,0,1:T(8,128)(2,1)S(1)}, s32[]{:S(2)}) async-start(bf16[128,16,384]{2,0,1:T(8,128)(2,1)} %copy-done.2), calls=%async_computation.2 | async-start | bytes 1048576 | tf_op jit(solution)/shard_map/slice | solution.py:159
  64.1 15.1 %collective-permute-start.6 = (bf16[256,16,256]{2,0,1:T(8,128)(2,1)}, bf16[256,16,256]{2,0,1:T(8,128)(2,1)}, u32[]{:S(2)}, u32[]{:S(2)}) collective-permute-start(bf16[256,16,256]{2,0,1:T(8,128)(2,1)} %pad_maximum_fusion), channel_id=1, source_target_pairs={{0,128},{128,0},{256,384},{384,256},{1,129},{129,1},{257,385},{385... | collective-permute-start | bytes 6291464 | tf_op jit(solution)/shard_map/ppermute | solution.py:157
  90.5 1.6 %copy-start.1 = (f32[128,4,4,256]{3,2,1,0:T(4,128)S(1)}, f32[128,4,4,256]{3,2,1,0:T(4,128)}, u32[]{:S(2)}) copy-start(f32[128,4,4,256]{3,2,1,0:T(4,128)} %reshape.113) | copy-start | bytes 6291460
  90.5 2.8 %slice-start = ((f32[128,4,4,256]{3,2,1,0:T(4,128)}), f32[128,2,4,256]{3,2,1,0:T(4,128)S(1)}, s32[]{:S(2)}) async-start(f32[128,4,4,256]{3,2,1,0:T(4,128)} %reshape.113), calls=%async_computation.1 | async-start | bytes 2097152 | tf_op jit(solution)/shard_map/slice | solution.py:75
  94.6 4.2 %copy-start.4 = (f32[128,2,4,256]{0,3,1,2:T(8,128)S(1)}, f32[128,2,4,256]{0,3,1,2:T(8,128)}, u32[]{:S(2)}) copy-start(f32[128,2,4,256]{0,3,1,2:T(8,128)} %copy.47) | copy-start | bytes 3145732
  100.3 1.9 %copy-start.3 = (bf16[16,128,256]{2,1,0:T(8,128)(2,1)S(1)}, bf16[16,128,256]{2,1,0:T(8,128)(2,1)}, u32[]{:S(2)}) copy-start(bf16[16,128,256]{2,1,0:T(8,128)(2,1)} %get-tuple-element.20) | copy-start | bytes 3145732
  111.8 2.6 %copy-start.7 = (f32[128,4,1,256]{3,2,1,0:T(1,128)S(1)}, f32[128,4,1,256]{3,2,1,0:T(1,128)}, u32[]{:S(2)}) copy-start(f32[128,4,1,256]{3,2,1,0:T(1,128)} %get-tuple-element.22) | copy-start | bytes 1572868
  111.8 4.3 %copy-start.5 = (f32[128,4,1,256]{0,3,1,2:T(8,128)S(1)}, f32[128,4,1,256]{0,3,1,2:T(8,128)}, u32[]{:S(2)}) copy-start(f32[128,4,1,256]{0,3,1,2:T(8,128)} %get-tuple-element.13) | copy-start | bytes 1572868
  111.8 4.3 %copy-start.6 = (f32[128,4,1,256]{0,3,1,2:T(8,128)S(1)}, f32[128,4,1,256]{0,3,1,2:T(8,128)}, u32[]{:S(2)}) copy-start(f32[128,4,1,256]{0,3,1,2:T(8,128)} %get-tuple-element.14) | copy-start | bytes 1572868

commit v12 on v10

--- a/solution.py
+++ b/solution.py
@@ -151,10 +151,11 @@
     sources_a = stacked_sources(context_size, steps_a)
     sources_b = stacked_sources(context_size, steps_b)
 
-    mine_weights = jnp.concatenate(
-        [gathered_a[:, :, key_width:], gathered_b[:, :, values.shape[1] :]], axis=0
-    )
-    other_weights = lax.ppermute(mine_weights, "dp", [(i, i ^ 1) for i in range(dp_size)])
+    other_a, other_b = lax.ppermute(
+        (gathered_a, gathered_b), "dp", [(i, i ^ 1) for i in range(dp_size)]
+    )
+    mine_weights = (gathered_a[:, :, key_width:], gathered_b[:, :, values.shape[1] :])
+    other_weights = (other_a[:, :, key_width:], other_b[:, :, values.shape[1] :])
 
     key_stack = gathered_a[:, :, :key_width]
     value_stack = restack(gathered_b[:, :, : values.shape[1]], sources_b, sources_a, x_size)
@@ -198,7 +199,7 @@
     total = None
     for piece, sources in ((0, sources_a), (1, sources_b)):
         for which, held in ((0, mine_weights), (1, other_weights)):
-            piece_t = held[piece * row_count : (piece + 1) * row_count]
+            piece_t = held[piece]
             piece_t = jnp.swapaxes(piece_t, 0, 1).reshape(context_size, weight_cols, quarter)
             owner = core if which == 0 else 1 - core
             piece_rows = lax.dynamic_slice_in_dim(

time: 138 us -> 139 us (level)
  the two profiles are of different devices: /device:TPU:1 before, /device:TPU:16 now
where the time goes in v12:
time: 139 us; the launch traced here: 138 us
  blocking collectives  39 us (28%)
  waiting for transfers between devices  37.1 us (27%)
  starting transfers between devices  30.9 us (22%)
  local copies, waits for them, and re-layouts  21.2 us (15%)
  other arithmetic  5.3 us (4%)
  matrix products  4.1 us (3%)
    all_to_all x1, blocking collectives, per_device(): pieces = lax.all_to_all(pieces, 'tensor', 1, 1, tiled=True)  39 us
    ppermute x2, waiting for transfers between devices, exchange_gather_pair(): lax.ppermute(stack_a, axis_name, [(i, i ^ mask_a) for i in range(count)])  18.8 us
    ppermute x2, starting transfers between devices, exchange_gather(): lax.ppermute(stack, axis_name, [(i, i ^ mask) for i in range(count)])  13.3 us
    ppermute x2, waiting for transfers between devices, exchange_gather(): lax.ppermute(stack, axis_name, [(i, i ^ mask) for i in range(count)])  13 us
    ppermute x2, starting transfers between devices, exchange_gather_pair(): lax.ppermute(stack_a, axis_name, [(i, i ^ mask_a) for i in range(count)])  7.4 us
    ppermute x2, starting transfers between devices, exchange_gather_pair(): lax.ppermute(stack_b, axis_name, [(i, i ^ mask_b) for i in range(count)])  5.92 us
    transpose x3, local copies, waits for them, and re-layouts, per_device(): jnp.swapaxes(piece_t, 0, 1).reshape(context_size, weight_cols, quarter)  5.45 us
    ppermute x2, waiting for transfers between devices, exchange_gather_pair(): lax.ppermute(stack_b, axis_name, [(i, i ^ mask_b) for i in range(count)])  5.3 us
  transfers between devices with their start and end apart: 8, of which 6 were waited for; matrix products, arithmetic and copies ran while one was open for 14% of the time, Pallas kernels for 0%

profile of v12, /device:TPU:16, one launch (start us, length us, event | category | flops | bytes accessed | tf_op | source)
XLA Modules:
  0.0 138.2 jit_solution(14877890197682674873)
XLA Ops:
  0.0 0.9 dynamic-slice_bitcast_fusion.1
  1.2 0.8 maximum_bitcast_fusion
  2.0 7.6 %collective-permute-start = (bf16[128,1,768]{2,0,1:T(8,128)(2,1)S(1)}, bf16[128,1,768]{2,0,1:T(8,128)(2,1)S(1)}, u32[]{:S(2)}, u32[]{:S(2)}) collective-permute-start(bf16[128,1,768]{2,0,1:T(8,128)(2,1)S(1)} %maximum_bitcast_fusion), channel_id=1, source_target_pairs={{0,64},{8,72},{16,80},{24,88},{32,96},{40,104},{48,112},{56,120},{... | collective-permute-start | bytes 589832 | tf_op jit(solution)/shard_map/ppermute | solution.py:51
  9.6 3.7 %collective-permute-done = bf16[128,1,768]{2,0,1:T(8,128)(2,1)S(1)} collective-permute-done((bf16[128,1,768]{2,0,1:T(8,128)(2,1)S(1)}, bf16[128,1,768]{2,0,1:T(8,128)(2,1)S(1)}, u32[]{:S(2)}, u32[]{:S(2)}) %collective-permute-start) | collective-permute-done | bytes 196640 | tf_op jit(solution)/shard_map/ppermute | solution.py:51
  13.4 5.7 %collective-permute-start.1 = (bf16[128,2,768]{2,0,1:T(8,128)(2,1)S(1)}, bf16[128,2,768]{2,0,1:T(8,128)(2,1)S(1)}, u32[]{:S(2)}, u32[]{:S(2)}) collective-permute-start(bf16[128,2,768]{2,0,1:T(8,128)(2,1)S(1)} %maximum_select_fusion.5), channel_id=1, source_target_pairs={{0,32},{8,40},{16,48},{24,56},{32,0},{40,8},{48,16},{56,24},{64,96... | collective-permute-start | bytes 1179656 | tf_op jit(solution)/shard_map/ppermute | solution.py:51
  19.1 9.3 %collective-permute-done.1 = bf16[128,2,768]{2,0,1:T(8,128)(2,1)S(1)} collective-permute-done((bf16[128,2,768]{2,0,1:T(8,128)(2,1)S(1)}, bf16[128,2,768]{2,0,1:T(8,128)(2,1)S(1)}, u32[]{:S(2)}, u32[]{:S(2)}) %collective-permute-start.1) | collective-permute-done | bytes 393248 | tf_op jit(solution)/shard_map/ppermute | solution.py:51
  28.6 3.4 %collective-permute-start.2 = (bf16[128,4,384]{2,0,1:T(8,128)(2,1)S(1)}, bf16[128,4,384]{2,0,1:T(8,128)(2,1)S(1)}, u32[]{:S(2)}, u32[]{:S(2)}) collective-permute-start(bf16[128,4,384]{2,0,1:T(8,128)(2,1)S(1)} %get-tuple-element.34), channel_id=1, source_target_pairs={{0,8},{8,0},{16,24},{24,16},{32,40},{40,32},{48,56},{56,48},{64,72... | collective-permute-start | bytes 1179656 | tf_op jit(solution)/shard_map/ppermute | solution.py:84
  32.0 4.0 %collective-permute-start.3 = (bf16[128,4,384]{2,0,1:T(8,128)(2,1)S(1)}, bf16[128,4,384]{2,0,1:T(8,128)(2,1)S(1)}, u32[]{:S(2)}, u32[]{:S(2)}) collective-permute-start(bf16[128,4,384]{2,0,1:T(8,128)(2,1)S(1)} %get-tuple-element.33), channel_id=1, source_target_pairs={{0,24},{8,16},{16,8},{24,0},{32,56},{40,48},{48,40},{56,32},{64,88... | collective-permute-start | bytes 1179656 | tf_op jit(solution)/shard_map/ppermute | solution.py:85
  36.0 4.9 %collective-permute-done.2 = bf16[128,4,384]{2,0,1:T(8,128)(2,1)S(1)} collective-permute-done((bf16[128,4,384]{2,0,1:T(8,128)(2,1)S(1)}, bf16[128,4,384]{2,0,1:T(8,128)(2,1)S(1)}, u32[]{:S(2)}, u32[]{:S(2)}) %collective-permute-start.2) | collective-permute-done | bytes 393248 | tf_op jit(solution)/shard_map/ppermute | solution.py:84
  41.1 4.2 %collective-permute-done.3 = bf16[128,4,384]{2,0,1:T(8,128)(2,1)S(1)} collective-permute-done((bf16[128,4,384]{2,0,1:T(8,128)(2,1)S(1)}, bf16[128,4,384]{2,0,1:T(8,128)(2,1)S(1)}, u32[]{:S(2)}, u32[]{:S(2)}) %collective-permute-start.3) | collective-permute-done | bytes 393248 | tf_op jit(solution)/shard_map/ppermute | solution.py:85
  45.5 4.0 %collective-permute-start.4 = (bf16[128,8,384]{2,0,1:T(8,128)(2,1)S(1)}, bf16[128,8,384]{2,0,1:T(8,128)(2,1)S(1)}, u32[]{:S(2)}, u32[]{:S(2)}) collective-permute-start(bf16[128,8,384]{2,0,1:T(8,128)(2,1)S(1)} %maximum_select_fusion.3), channel_id=1, source_target_pairs={{0,24},{8,16},{16,8},{24,0},{32,56},{40,48},{48,40},{56,32},{64,88... | collective-permute-start | bytes 2359304 | tf_op jit(solution)/shard_map/ppermute | solution.py:84
  49.5 1.9 %collective-permute-start.5 = (bf16[128,8,384]{2,0,1:T(8,128)(2,1)S(1)}, bf16[128,8,384]{2,0,1:T(8,128)(2,1)S(1)}, u32[]{:S(2)}, u32[]{:S(2)}) collective-permute-start(bf16[128,8,384]{2,0,1:T(8,128)(2,1)S(1)} %maximum_select_fusion.4), channel_id=1, source_target_pairs={{0,8},{8,0},{16,24},{24,16},{32,40},{40,32},{48,56},{56,48},{64,72... | collective-permute-start | bytes 2359304 | tf_op jit(solution)/shard_map/ppermute | solution.py:85
  52.4 13.9 %collective-permute-done.4 = bf16[128,8,384]{2,0,1:T(8,128)(2,1)S(1)} collective-permute-done((bf16[128,8,384]{2,0,1:T(8,128)(2,1)S(1)}, bf16[128,8,384]{2,0,1:T(8,128)(2,1)S(1)}, u32[]{:S(2)}, u32[]{:S(2)}) %collective-permute-start.4) | collective-permute-done | bytes 786464 | tf_op jit(solution)/shard_map/ppermute | solution.py:84
  66.3 1.4 %maximum_select_fusion = bf16[128,16,384]{2,0,1:T(8,128)(2,1)} fusion(bf16[128,8,384]{2,0,1:T(8,128)(2,1)S(1)} %maximum_select_fusion.3, bf16[128,8,384]{2,0,1:T(8,128)(2,1)S(1)} %collective-permute-done.4, pred[]{:T(512)S(6)} %ne.22), kind=kLoop, calls=%fused_computation.13 | loop fusion | flops 2359296 | bytes 3145729 | tf_op jit(solution)/shard_map/jit(_where)/select_n | solution.py:86
  67.7 1.1 collective-permute-done.5
  69.3 1.9 %collective-permute-start.6 = (bf16[128,16,384]{2,0,1:T(8,128)(2,1)}, bf16[128,16,384]{2,0,1:T(8,128)(2,1)}, u32[]{:S(2)}, u32[]{:S(2)}) collective-permute-start(bf16[128,16,384]{2,0,1:T(8,128)(2,1)} %maximum_select_fusion), channel_id=1, source_target_pairs={{0,128},{128,0},{256,384},{384,256},{1,129},{129,1},{257,385},{385... | collective-permute-start | bytes 4718600 | tf_op jit(solution)/shard_map/ppermute | solution.py:154
  71.2 1.1 slice.115
  72.3 2.4 %collective-permute-start.7 = (bf16[128,16,384]{2,0,1:T(8,128)(2,1)S(1)}, bf16[128,16,384]{2,0,1:T(8,128)(2,1)}, u32[]{:S(2)}, u32[]{:S(2)}) collective-permute-start(bf16[128,16,384]{2,0,1:T(8,128)(2,1)S(1)} %maximum_select_fusion.1), channel_id=1, source_target_pairs={{0,128},{128,0},{256,384},{384,256},{1,129},{129,1},{257,385},{385... | collective-permute-start | bytes 4718600 | tf_op jit(solution)/shard_map/ppermute | solution.py:154
  74.7 2.9 %slice_bitcast_fusion.2 = (bf16[16,128,256]{2,1,0:T(8,128)(2,1)}, bf16[16,128,256]{2,1,0:T(8,128)(2,1)}) fusion(bf16[128,16,384]{2,0,1:T(8,128)(2,1)S(1)} %maximum_select_fusion.1, bf16[128,16,384]{2,0,1:T(8,128)(2,1)} %maximum_select_fusion), kind=kLoop, calls=%fused_computation.19 | loop fusion | bytes 4194304 | tf_op jit(solution)/shard_map/transpose | solution.py:203
  77.6 0.7 fusion
  78.3 1.3 fusion.1
  79.6 1.6 %fusion.11 = bf16[512,128]{1,0:T(8,128)(2,1)S(1)} fusion(bf16[2048,128]{1,0:T(8,128)(2,1)S(1)} %bitcast.94, f32[2048,512]{1,0:T(8,128)S(1)} %get-tuple-element.40, f32[512]{0:T(512)S(1)} %broadcast_maximum_fusion, s32[512]{0:T(512)S(1)} %broadcast_bitcast_fusion, s32[2048]{0:T(1024)S(1)} %bitcast.101, f32[512]{0:T(512)S(1)} %fusion.1), kind=kOutput, calls=%fused_computation.16 | convolution fusion | flops 274857984 | bytes 4864000 | tf_op jit(solution)/shard_map/grk,kgd->grd/dot_general | solution.py:187
  81.4 1.4 %dot_general.32 = bf16[4,4,256,128]{3,2,1,0:T(8,128)(2,1)S(1)} reshape(bf16[16,128,256]{2,1,0:T(8,128)(2,1)} %get-tuple-element.41) | data formatting | bytes 2097152 | tf_op jit(solution)/shard_map/rh,nkh->rnk/dot_general | solution.py:208
  83.6 1.4 %fusion.36 = (f32[128,4,1,256]{3,0,2,1:T(8,128)}, f32[128,4,1,256]{3,0,2,1:T(8,128)}, f32[128,4,1,256]{3,0,2,1:T(8,128)}, f32[128,4,1,256]{3,0,2,1:T(8,128)}) fusion(f32[128,4,4,256]{3,0,2,1:T(8,128)S(1)} %pad_maximum_fusion), kind=kLoop, calls=%fused_computation.55 | loop fusion | bytes 4194304 | tf_op jit(solution)/shard_map/slice | solution.py:77
  85.0 1.4 %dot_general.28 = bf16[4,4,256,128]{3,2,1,0:T(8,128)(2,1)S(1)} reshape(bf16[16,128,256]{2,1,0:T(8,128)(2,1)} %get-tuple-element.42) | data formatting | bytes 2097152 | tf_op jit(solution)/shard_map/rh,nkh->rnk/dot_general | solution.py:208
  86.9 1.4 %fusion.34 = (f32[128,4,1,256]{3,0,2,1:T(8,128)}, f32[128,4,1,256]{3,0,2,1:T(8,128)}, f32[128,4,1,256]{3,0,2,1:T(8,128)}, f32[128,4,1,256]{3,0,2,1:T(8,128)}) fusion(f32[128,4,4,256]{3,0,2,1:T(8,128)S(1)} %fusion.21), kind=kLoop, calls=%fused_computation.53 | loop fusion | bytes 4194304 | tf_op jit(solution)/shard_map/slice | solution.py:77
  88.3 1.3 slice_bitcast_fusion
  90.6 1.2 copy-done.1
  91.8 1.3 slice_bitcast_fusion.1
  94.0 0.8 slice-done
  98.3 39.0 %all_to_all.5 = bf16[128,8,512]{0,2,1:T(8,128)(2,1)S(1)} all-to-all(bf16[128,8,512]{0,2,1:T(8,128)(2,1)S(1)} %bitcast.86), channel_id=1, replica_groups=mesh['dp'=4,'context'=16,'tensor'=8] {'tensor'}, dimensions={1} | all-to-all | bytes 2097152 | tf_op jit(solution)/shard_map/all_to_all | solution.py:216
  137.4 0.8 copy.24
  (64 shorter events, 8.9 us)
Async XLA Ops:
  0.0 51.7 %copy-start = (s32[2048]{0:T(1024)S(1)}, s32[2048]{0:T(1024)}, u32[]{:S(2)}) copy-start(s32[2048]{0:T(1024)} %param.9) | copy-start | bytes 24580
  2.0 11.3 %collective-permute-start = (bf16[128,1,768]{2,0,1:T(8,128)(2,1)S(1)}, bf16[128,1,768]{2,0,1:T(8,128)(2,1)S(1)}, u32[]{:S(2)}, u32[]{:S(2)}) collective-permute-start(bf16[128,1,768]{2,0,1:T(8,128)(2,1)S(1)} %maximum_bitcast_fusion), channel_id=1, source_target_pairs={{0,64},{8,72},{16,80},{24,88},{32,96},{40,104},{48,112},{56,120},{... | collective-permute-start | bytes 589832 | tf_op jit(solution)/shard_map/ppermute | solution.py:51
  13.4 15.0 %collective-permute-start.1 = (bf16[128,2,768]{2,0,1:T(8,128)(2,1)S(1)}, bf16[128,2,768]{2,0,1:T(8,128)(2,1)S(1)}, u32[]{:S(2)}, u32[]{:S(2)}) collective-permute-start(bf16[128,2,768]{2,0,1:T(8,128)(2,1)S(1)} %maximum_select_fusion.5), channel_id=1, source_target_pairs={{0,32},{8,40},{16,48},{24,56},{32,0},{40,8},{48,16},{56,24},{64,96... | collective-permute-start | bytes 1179656 | tf_op jit(solution)/shard_map/ppermute | solution.py:51
  28.5 22.9 %copy-start.10 = (bf16[128,512]{1,0:T(8,128)(2,1)S(1)}, bf16[128,512]{1,0:T(8,128)(2,1)}, u32[]{:S(2)}) copy-start(bf16[128,512]{1,0:T(8,128)(2,1)} %param.6) | copy-start | bytes 393220
  28.6 23.2 %copy-start.11 = (s32[16]{0:T(128)S(1)}, s32[16]{0:T(128)}, u32[]{:S(2)}) copy-start(s32[16]{0:T(128)} %constant.64) | copy-start | bytes 196
  28.6 12.4 %collective-permute-start.2 = (bf16[128,4,384]{2,0,1:T(8,128)(2,1)S(1)}, bf16[128,4,384]{2,0,1:T(8,128)(2,1)S(1)}, u32[]{:S(2)}, u32[]{:S(2)}) collective-permute-start(bf16[128,4,384]{2,0,1:T(8,128)(2,1)S(1)} %get-tuple-element.34), channel_id=1, source_target_pairs={{0,8},{8,0},{16,24},{24,16},{32,40},{40,32},{48,56},{56,48},{64,72... | collective-permute-start | bytes 1179656 | tf_op jit(solution)/shard_map/ppermute | solution.py:84
  32.0 13.3 %collective-permute-start.3 = (bf16[128,4,384]{2,0,1:T(8,128)(2,1)S(1)}, bf16[128,4,384]{2,0,1:T(8,128)(2,1)S(1)}, u32[]{:S(2)}, u32[]{:S(2)}) collective-permute-start(bf16[128,4,384]{2,0,1:T(8,128)(2,1)S(1)} %get-tuple-element.33), channel_id=1, source_target_pairs={{0,24},{8,16},{16,8},{24,0},{32,56},{40,48},{48,40},{56,32},{64,88... | collective-permute-start | bytes 1179656 | tf_op jit(solution)/shard_map/ppermute | solution.py:85
  45.5 20.9 %collective-permute-start.4 = (bf16[128,8,384]{2,0,1:T(8,128)(2,1)S(1)}, bf16[128,8,384]{2,0,1:T(8,128)(2,1)S(1)}, u32[]{:S(2)}, u32[]{:S(2)}) collective-permute-start(bf16[128,8,384]{2,0,1:T(8,128)(2,1)S(1)} %maximum_select_fusion.3), channel_id=1, source_target_pairs={{0,24},{8,16},{16,8},{24,0},{32,56},{40,48},{48,40},{56,32},{64,88... | collective-permute-start | bytes 2359304 | tf_op jit(solution)/shard_map/ppermute | solution.py:84
  49.5 19.4 %collective-permute-start.5 = (bf16[128,8,384]{2,0,1:T(8,128)(2,1)S(1)}, bf16[128,8,384]{2,0,1:T(8,128)(2,1)S(1)}, u32[]{:S(2)}, u32[]{:S(2)}) collective-permute-start(bf16[128,8,384]{2,0,1:T(8,128)(2,1)S(1)} %maximum_select_fusion.4), channel_id=1, source_target_pairs={{0,8},{8,0},{16,24},{24,16},{32,40},{40,32},{48,56},{56,48},{64,72... | collective-permute-start | bytes 2359304 | tf_op jit(solution)/shard_map/ppermute | solution.py:85
  69.3 22.5 %collective-permute-start.6 = (bf16[128,16,384]{2,0,1:T(8,128)(2,1)}, bf16[128,16,384]{2,0,1:T(8,128)(2,1)}, u32[]{:S(2)}, u32[]{:S(2)}) collective-permute-start(bf16[128,16,384]{2,0,1:T(8,128)(2,1)} %maximum_select_fusion), channel_id=1, source_target_pairs={{0,128},{128,0},{256,384},{384,256},{1,129},{129,1},{257,385},{385... | collective-permute-start | bytes 4718600 | tf_op jit(solution)/shard_map/ppermute | solution.py:154
  72.3 16.1 %collective-permute-start.7 = (bf16[128,16,384]{2,0,1:T(8,128)(2,1)S(1)}, bf16[128,16,384]{2,0,1:T(8,128)(2,1)}, u32[]{:S(2)}, u32[]{:S(2)}) collective-permute-start(bf16[128,16,384]{2,0,1:T(8,128)(2,1)S(1)} %maximum_select_fusion.1), channel_id=1, source_target_pairs={{0,128},{128,0},{256,384},{384,256},{1,129},{129,1},{257,385},{385... | collective-permute-start | bytes 4718600 | tf_op jit(solution)/shard_map/ppermute | solution.py:154
  90.5 1.3 copy-start.1
  93.5 1.2 slice-start
  94.9 1.0 copy-start.2
  94.9 1.2 copy-start.3
  94.9 1.3 copy-start.4
  94.9 1.5 %copy-start.5 = (f32[128,4,1,256]{3,0,2,1:T(8,128)S(1)}, f32[128,4,1,256]{3,0,2,1:T(8,128)}, u32[]{:S(2)}) copy-start(f32[128,4,1,256]{3,0,2,1:T(8,128)} %get-tuple-element.24) | copy-start | bytes 1572868
  94.9 1.6 %copy-start.6 = (f32[128,4,1,256]{3,0,2,1:T(8,128)S(1)}, f32[128,4,1,256]{3,0,2,1:T(8,128)}, u32[]{:S(2)}) copy-start(f32[128,4,1,256]{3,0,2,1:T(8,128)} %get-tuple-element.13) | copy-start | bytes 1572868
  94.9 1.8 %copy-start.7 = (f32[128,4,1,256]{3,0,2,1:T(8,128)S(1)}, f32[128,4,1,256]{3,0,2,1:T(8,128)}, u32[]{:S(2)}) copy-start(f32[128,4,1,256]{3,0,2,1:T(8,128)} %get-tuple-element.14) | copy-start | bytes 1572868
  95.0 1.9 %copy-start.8 = (f32[128,4,1,256]{3,0,2,1:T(8,128)S(1)}, f32[128,4,1,256]{3,0,2,1:T(8,128)}, u32[]{:S(2)}) copy-start(f32[128,4,1,256]{3,0,2,1:T(8,128)} %get-tuple-element.15) | copy-start | bytes 1572868
  95.0 2.1 %copy-start.9 = (f32[128,4,1,256]{3,0,2,1:T(8,128)S(1)}, f32[128,4,1,256]{3,0,2,1:T(8,128)}, u32[]{:S(2)}) copy-start(f32[128,4,1,256]{3,0,2,1:T(8,128)} %get-tuple-element.16) | copy-start | bytes 1572868

commit v13 on v12

--- a/solution.py
+++ b/solution.py
@@ -135,15 +135,15 @@
     while shared < min(len(steps_a), len(steps_b)) and steps_a[shared] == steps_b[shared]:
         shared += 1
     key_width = keys.shape[1]
-    quarters = [
-        mine[k * quarter : (k + 1) * quarter].T.reshape(row_count, -1) for k in range(2)
-    ]
-    block = jnp.concatenate([keys, quarters[0], values, quarters[1]], axis=1)[:, None, :]
+    assert keys.shape[1] == quarter and values.shape[1] == quarter
+    block_a = jnp.concatenate([keys, mine[:quarter].T], axis=0)[:, None, :]
+    block_b = jnp.concatenate([values, mine[quarter:].T], axis=0)[:, None, :]
+    block = jnp.concatenate([block_a, block_b], axis=2)
     gathered = exchange_gather(block, steps_a[:shared], "context", context_size)
     gathered_a, gathered_b = exchange_gather_pair(
-        gathered[:, :, : key_width + weight_cols],
+        gathered[:, :, :quarter],
         steps_a[shared:],
-        gathered[:, :, key_width + weight_cols :],
+        gathered[:, :, quarter:],
         steps_b[shared:],
         "context",
         context_size,
@@ -154,11 +154,11 @@
     other_a, other_b = lax.ppermute(
         (gathered_a, gathered_b), "dp", [(i, i ^ 1) for i in range(dp_size)]
     )
-    mine_weights = (gathered_a[:, :, key_width:], gathered_b[:, :, values.shape[1] :])
-    other_weights = (other_a[:, :, key_width:], other_b[:, :, values.shape[1] :])
-
-    key_stack = gathered_a[:, :, :key_width]
-    value_stack = restack(gathered_b[:, :, : values.shape[1]], sources_b, sources_a, x_size)
+    mine_weights = (gathered_a, gathered_b)
+    other_weights = (other_a, other_b)
+
+    key_stack = gathered_a[:row_count]
+    value_stack = restack(gathered_b[:row_count], sources_b, sources_a, x_size)
     key_part = jnp.swapaxes(key_stack, 0, 1).reshape(context_size * row_count, key_width)
     value_part = jnp.swapaxes(value_stack, 0, 1).reshape(context_size * row_count, -1)
     key_pos = order.reshape(context_size, row_count)[jnp.array(sources_a)].reshape(-1)
@@ -199,15 +199,14 @@
     total = None
     for piece, sources in ((0, sources_a), (1, sources_b)):
         for which, held in ((0, mine_weights), (1, other_weights)):
-            piece_t = held[piece]
-            piece_t = jnp.swapaxes(piece_t, 0, 1).reshape(context_size, weight_cols, quarter)
+            piece_t = jnp.swapaxes(held[piece], 0, 1)
             owner = core if which == 0 else 1 - core
             piece_rows = lax.dynamic_slice_in_dim(
                 attended, owner * half_rows + piece * quarter, quarter, 1
             )
             product_out = jnp.einsum(
                 "rh,nkh->rnk", piece_rows, piece_t, preferred_element_type=jnp.float32
-            ).reshape(row_count, -1)
+            )[:, :, row_count:].reshape(row_count, -1)
             product_out = unpermute_blocks(product_out, sources, x_size)
             total = product_out if total is None else total + product_out
     partial_out = total

time: 139 us -> 157 us (1.13)
  local copies, waits for them, and re-layouts: 21.2 us -> 33 us
  matrix products: 4.1 us -> 7.75 us
  other arithmetic: 5.3 us -> 8.88 us
  starting transfers between devices: 30.9 us -> 29 us
    unnamed x26 -> x38, local copies, waits for them, and re-layouts: 3.04 us -> 21.5 us
    transpose x6 -> x0, local copies, waits for them, and re-layouts: 6.57 us -> none  [the longest x3 5.45 us: per_device(): jnp.swapaxes(piece_t, 0, 1).reshape(context_size, weight_cols, quarter)]
    dot_general x4, matrix products: 1.75 us -> 5.43 us  [per_device(): jnp.einsum('rh,nkh->rnk', piece_rows, piece_t, preferred_element_type=jnp...]
    dot_general x4 -> x0, local copies, waits for them, and re-layouts: 3.62 us -> none  [per_device(): jnp.einsum('rh,nkh->rnk', piece_rows, piece_t, preferred_element_type=jnp...]
    ppermute x2, starting transfers between devices: 7.4 us -> 4.52 us  [exchange_gather_pair(): lax.ppermute(stack_a, axis_name, [(i, i ^ mask_a) for i in range(count)])]
    another operation x0 -> x1, other arithmetic: none -> 2.85 us
    slice x3 -> x4, local copies, waits for them, and re-layouts: 3.29 us -> 5.46 us  [unpermute_blocks(): product[:, :, i:i + 1]]
  transfers between devices with their start and end apart: 8 -> 8, of which waited for: 6 -> 5; matrix products, arithmetic and copies ran while one was open for 14% -> 22% of each run, Pallas kernels for 0% -> 0%
where the time goes in v13:
time: 157 us; the launch traced here: 156 us
  blocking collectives  39 us (25%)
  waiting for transfers between devices  38.1 us (24%)
  local copies, waits for them, and re-layouts  33 us (21%)
  starting transfers between devices  29 us (18%)
  other arithmetic  8.88 us (6%)
  matrix products  7.75 us (5%)
    all_to_all x1, blocking collectives, per_device(): pieces = lax.all_to_all(pieces, 'tensor', 1, 1, tiled=True)  39 us
    unnamed x38, local copies, waits for them, and re-layouts  21.5 us
    ppermute x2, waiting for transfers between devices, exchange_gather_pair(): lax.ppermute(stack_a, axis_name, [(i, i ^ mask_a) for i in range(count)])  18.3 us
    ppermute x2, starting transfers between devices, exchange_gather(): lax.ppermute(stack, axis_name, [(i, i ^ mask) for i in range(count)])  13.3 us
    ppermute x2, waiting for transfers between devices, exchange_gather(): lax.ppermute(stack, axis_name, [(i, i ^ mask) for i in range(count)])  13 us
    ppermute x2, starting transfers between devices, exchange_gather_pair(): lax.ppermute(stack_b, axis_name, [(i, i ^ mask_b) for i in range(count)])  6.86 us
    ppermute x2, waiting for transfers between devices, exchange_gather_pair(): lax.ppermute(stack_b, axis_name, [(i, i ^ mask_b) for i in range(count)])  6.74 us
    slice x4, local copies, waits for them, and re-layouts, unpermute_blocks(): product[:, :, i:i + 1]  5.46 us
  transfers between devices with their start and end apart: 8, of which 5 were waited for; matrix products, arithmetic and copies ran while one was open for 22% of the time, Pallas kernels for 0%

profile of v13, /device:TPU:16, one launch (start us, length us, event | category | flops | bytes accessed | tf_op | source)
XLA Modules:
  0.0 156.1 jit_solution(16676538045598865563)
XLA Ops:
  2.0 7.6 %collective-permute-start = (bf16[384,1,256]{2,0,1:T(8,128)(2,1)S(1)}, bf16[384,1,256]{2,0,1:T(8,128)(2,1)S(1)}, u32[]{:S(2)}, u32[]{:S(2)}) collective-permute-start(bf16[384,1,256]{2,0,1:T(8,128)(2,1)S(1)} %pad_maximum_fusion.3), channel_id=1, source_target_pairs={{0,64},{8,72},{16,80},{24,88},{32,96},{40,104},{48,112},{56,120},{... | collective-permute-start | bytes 589832 | tf_op jit(solution)/shard_map/ppermute | solution.py:51
  9.6 3.7 %collective-permute-done = bf16[384,1,256]{2,0,1:T(8,128)(2,1)S(1)} collective-permute-done((bf16[384,1,256]{2,0,1:T(8,128)(2,1)S(1)}, bf16[384,1,256]{2,0,1:T(8,128)(2,1)S(1)}, u32[]{:S(2)}, u32[]{:S(2)}) %collective-permute-start) | collective-permute-done | bytes 196640 | tf_op jit(solution)/shard_map/ppermute | solution.py:51
  13.4 5.7 %collective-permute-start.1 = (bf16[384,2,256]{2,0,1:T(8,128)(2,1)S(1)}, bf16[384,2,256]{2,0,1:T(8,128)(2,1)S(1)}, u32[]{:S(2)}, u32[]{:S(2)}) collective-permute-start(bf16[384,2,256]{2,0,1:T(8,128)(2,1)S(1)} %maximum_select_fusion.5), channel_id=1, source_target_pairs={{0,32},{8,40},{16,48},{24,56},{32,0},{40,8},{48,16},{56,24},{64,96... | collective-permute-start | bytes 1179656 | tf_op jit(solution)/shard_map/ppermute | solution.py:51
  19.1 9.3 %collective-permute-done.1 = bf16[384,2,256]{2,0,1:T(8,128)(2,1)S(1)} collective-permute-done((bf16[384,2,256]{2,0,1:T(8,128)(2,1)S(1)}, bf16[384,2,256]{2,0,1:T(8,128)(2,1)S(1)}, u32[]{:S(2)}, u32[]{:S(2)}) %collective-permute-start.1) | collective-permute-done | bytes 393248 | tf_op jit(solution)/shard_map/ppermute | solution.py:51
  28.7 4.7 %collective-permute-start.3 = (bf16[384,4,128]{2,0,1:T(8,128)(2,1)S(1)}, bf16[384,4,128]{2,0,1:T(8,128)(2,1)S(1)}, u32[]{:S(2)}, u32[]{:S(2)}) collective-permute-start(bf16[384,4,128]{2,0,1:T(8,128)(2,1)S(1)} %get-tuple-element.33), channel_id=1, source_target_pairs={{0,24},{8,16},{16,8},{24,0},{32,56},{40,48},{48,40},{56,32},{64,88... | collective-permute-start | bytes 1179656 | tf_op jit(solution)/shard_map/ppermute | solution.py:85
  33.3 2.1 %collective-permute-start.2 = (bf16[384,4,128]{2,0,1:T(8,128)(2,1)S(1)}, bf16[384,4,128]{2,0,1:T(8,128)(2,1)S(1)}, u32[]{:S(2)}, u32[]{:S(2)}) collective-permute-start(bf16[384,4,128]{2,0,1:T(8,128)(2,1)S(1)} %get-tuple-element.34), channel_id=1, source_target_pairs={{0,8},{8,0},{16,24},{24,16},{32,40},{40,32},{48,56},{56,48},{64,72... | collective-permute-start | bytes 1179656 | tf_op jit(solution)/shard_map/ppermute | solution.py:84
  35.5 6.7 %collective-permute-done.3 = bf16[384,4,128]{2,0,1:T(8,128)(2,1)S(1)} collective-permute-done((bf16[384,4,128]{2,0,1:T(8,128)(2,1)S(1)}, bf16[384,4,128]{2,0,1:T(8,128)(2,1)S(1)}, u32[]{:S(2)}, u32[]{:S(2)}) %collective-permute-start.3) | collective-permute-done | bytes 393248 | tf_op jit(solution)/shard_map/ppermute | solution.py:85
  42.4 3.1 %collective-permute-done.2 = bf16[384,4,128]{2,0,1:T(8,128)(2,1)S(1)} collective-permute-done((bf16[384,4,128]{2,0,1:T(8,128)(2,1)S(1)}, bf16[384,4,128]{2,0,1:T(8,128)(2,1)S(1)}, u32[]{:S(2)}, u32[]{:S(2)}) %collective-permute-start.2) | collective-permute-done | bytes 393248 | tf_op jit(solution)/shard_map/ppermute | solution.py:84
  45.5 2.4 %collective-permute-start.4 = (bf16[384,8,128]{2,0,1:T(8,128)(2,1)S(1)}, bf16[384,8,128]{2,0,1:T(8,128)(2,1)S(1)}, u32[]{:S(2)}, u32[]{:S(2)}) collective-permute-start(bf16[384,8,128]{2,0,1:T(8,128)(2,1)S(1)} %maximum_select_fusion.3), channel_id=1, source_target_pairs={{0,24},{8,16},{16,8},{24,0},{32,56},{40,48},{48,40},{56,32},{64,88... | collective-permute-start | bytes 2359304 | tf_op jit(solution)/shard_map/ppermute | solution.py:84
  47.9 2.2 %collective-permute-start.5 = (bf16[384,8,128]{2,0,1:T(8,128)(2,1)S(1)}, bf16[384,8,128]{2,0,1:T(8,128)(2,1)S(1)}, u32[]{:S(2)}, u32[]{:S(2)}) collective-permute-start(bf16[384,8,128]{2,0,1:T(8,128)(2,1)S(1)} %maximum_select_fusion.4), channel_id=1, source_target_pairs={{0,8},{8,0},{16,24},{24,16},{32,40},{40,32},{48,56},{56,48},{64,72... | collective-permute-start | bytes 2359304 | tf_op jit(solution)/shard_map/ppermute | solution.py:85
  51.1 15.3 %collective-permute-done.4 = bf16[384,8,128]{2,0,1:T(8,128)(2,1)S(1)} collective-permute-done((bf16[384,8,128]{2,0,1:T(8,128)(2,1)S(1)}, bf16[384,8,128]{2,0,1:T(8,128)(2,1)S(1)}, u32[]{:S(2)}, u32[]{:S(2)}) %collective-permute-start.4) | collective-permute-done | bytes 786464 | tf_op jit(solution)/shard_map/ppermute | solution.py:84
  66.4 1.4 maximum_select_fusion
  68.2 1.9 %collective-permute-start.7 = (bf16[384,16,128]{2,0,1:T(8,128)(2,1)S(1)}, bf16[384,16,128]{2,0,1:T(8,128)(2,1)}, u32[]{:S(2)}, u32[]{:S(2)}) collective-permute-start(bf16[384,16,128]{2,0,1:T(8,128)(2,1)S(1)} %maximum_select_fusion.1), channel_id=1, source_target_pairs={{0,128},{128,0},{256,384},{384,256},{1,129},{129,1},{257,385},{385... | collective-permute-start | bytes 4718600 | tf_op jit(solution)/shard_map/ppermute | solution.py:154
  71.2 2.4 %collective-permute-start.6 = (bf16[384,16,128]{2,0,1:T(8,128)(2,1)}, bf16[384,16,128]{2,0,1:T(8,128)(2,1)}, u32[]{:S(2)}, u32[]{:S(2)}) collective-permute-start(bf16[384,16,128]{2,0,1:T(8,128)(2,1)} %maximum_select_fusion), channel_id=1, source_target_pairs={{0,128},{128,0},{256,384},{384,256},{1,129},{129,1},{257,385},{385... | collective-permute-start | bytes 4718600 | tf_op jit(solution)/shard_map/ppermute | solution.py:154
  75.7 1.6 %fusion.11 = bf16[512,128]{1,0:T(8,128)(2,1)S(1)} fusion(bf16[2048,128]{1,0:T(8,128)(2,1)S(1)} %bitcast.88, f32[2048,512]{1,0:T(8,128)S(1)} %get-tuple-element.40, f32[512]{0:T(512)S(1)} %broadcast_maximum_fusion, s32[512]{0:T(512)S(1)} %broadcast_bitcast_fusion, s32[2048]{0:T(1024)S(1)} %bitcast.98, f32[512]{0:T(512)S(1)} %fusion.1), kind=kOutput, calls=%fused_computation.16 | convolution fusion | flops 274857984 | bytes 4864000 | tf_op jit(solution)/shard_map/grk,kgd->grd/dot_general | solution.py:187
  77.4 1.7 %fusion.20 = f32[128,16,256]{2,0,1:T(8,128)S(1)} fusion(bf16[16,384,128]{2,1,0:T(8,128)(2,1)} %bitcast.20, bf16[128,512]{1,0:T(8,128)(2,1)S(1)} %bitcast.84, s32[]{:T(128)S(6)} %select_n.86), kind=kOutput, calls=%fused_computation.23 | convolution fusion | flops 134217728 | bytes 3178500 | tf_op jit(solution)/shard_map/rh,nkh->rnk/dot_general | solution.py:207
  79.1 1.4 fusion.42
  81.9 1.3 copy.74
  83.2 2.1 %copy.73 = f32[128,1,4,256]{0,3,1,2:T(8,128)} copy(f32[128,1,4,256]{3,0,2,1:T(8,128)} %get-tuple-element.23) | data formatting | bytes 1048576
  86.4 2.1 %copy.65 = f32[128,4,1,256]{0,3,1,2:T(8,128)} copy(f32[128,4,1,256]{3,0,2,1:T(8,128)} %get-tuple-element.29) | data formatting | bytes 1048576
  88.5 2.0 %copy.66 = f32[128,4,1,256]{0,3,1,2:T(8,128)} copy(f32[128,4,1,256]{3,0,2,1:T(8,128)} %get-tuple-element.31) | data formatting | bytes 1048576
  90.5 2.0 %copy.67 = f32[128,4,1,256]{0,3,1,2:T(8,128)} copy(f32[128,4,1,256]{3,0,2,1:T(8,128)} %get-tuple-element.30) | data formatting | bytes 1048576
  93.6 1.5 pad_maximum_fusion
  95.1 1.4 fusion.39
  96.5 1.7 %fusion.14 = f32[128,16,256]{2,0,1:T(8,128)S(1)} fusion(bf16[16,384,128]{2,1,0:T(8,128)(2,1)} %bitcast.29, bf16[128,512]{1,0:T(8,128)(2,1)S(1)} %bitcast.86, s32[]{:T(128)S(6)} %select_n.99), kind=kOutput, calls=%fused_computation.17 | convolution fusion | flops 134217728 | bytes 3178500 | tf_op jit(solution)/shard_map/rh,nkh->rnk/dot_general | solution.py:207
  103.4 1.4 fusion.37
  104.8 1.7 %fusion.18 = f32[128,16,256]{2,0,1:T(8,128)S(1)} fusion(bf16[16,384,128]{2,1,0:T(8,128)(2,1)} %bitcast.23, bf16[128,512]{1,0:T(8,128)(2,1)S(1)} %bitcast.87, s32[]{:T(128)S(6)} %select_n.97), kind=kOutput, calls=%fused_computation.21 | convolution fusion | flops 134217728 | bytes 3178500 | tf_op jit(solution)/shard_map/rh,nkh->rnk/dot_general | solution.py:207
  107.9 1.3 copy.70
  109.2 2.0 %copy.71 = f32[128,4,1,256]{0,3,1,2:T(8,128)} copy(f32[128,4,1,256]{3,0,2,1:T(8,128)} %get-tuple-element.26) | data formatting | bytes 1048576
  111.3 2.0 %copy.72 = f32[128,4,1,256]{0,3,1,2:T(8,128)} copy(f32[128,4,1,256]{3,0,2,1:T(8,128)} %get-tuple-element.28) | data formatting | bytes 1048576
  113.3 2.9 %fusion.5 = bf16[128,4,4,256]{0,3,1,2:T(8,128)(2,1)S(1)} fusion(f32[128,4,1,256]{0,3,1,2:T(8,128)S(1)} %copy-done.6, f32[128,4,1,256]{0,3,1,2:T(8,128)S(1)} %copy-done.5, f32[128,4,1,256]{0,3,1,2:T(8,128)S(1)} %copy-done.4, f32[128,4,1,256]{0,3,1,2:T(8,128)S(1)} %copy-done.3, f32[128,4,1,256]{0,3,1,2:T(8,128)} %copy.72, f32[128,4,1,256]{0,3,1,2:T(8,128)} %copy.71, ...), kind=kLoop, calls=%fused_computation.9 | loop fusion | flops 8388608 | bytes 9437184 | tf_op jit(solution)/shard_map/convert.1
  116.2 39.0 %all_to_all.5 = bf16[128,8,512]{0,2,1:T(8,128)(2,1)S(1)} all-to-all(bf16[128,8,512]{0,2,1:T(8,128)(2,1)S(1)} %bitcast.81), channel_id=1, replica_groups=mesh['dp'=4,'context'=16,'tensor'=8] {'tensor'}, dimensions={1} | all-to-all | bytes 2097152 | tf_op jit(solution)/shard_map/all_to_all | solution.py:215
  (65 shorter events, 18.0 us)
Async XLA Ops:
  0.0 50.4 %copy-start = (s32[2048]{0:T(1024)S(1)}, s32[2048]{0:T(1024)}, u32[]{:S(2)}) copy-start(s32[2048]{0:T(1024)} %param.9) | copy-start | bytes 24580
  2.0 11.3 %collective-permute-start = (bf16[384,1,256]{2,0,1:T(8,128)(2,1)S(1)}, bf16[384,1,256]{2,0,1:T(8,128)(2,1)S(1)}, u32[]{:S(2)}, u32[]{:S(2)}) collective-permute-start(bf16[384,1,256]{2,0,1:T(8,128)(2,1)S(1)} %pad_maximum_fusion.3), channel_id=1, source_target_pairs={{0,64},{8,72},{16,80},{24,88},{32,96},{40,104},{48,112},{56,120},{... | collective-permute-start | bytes 589832 | tf_op jit(solution)/shard_map/ppermute | solution.py:51
  13.4 15.0 %collective-permute-start.1 = (bf16[384,2,256]{2,0,1:T(8,128)(2,1)S(1)}, bf16[384,2,256]{2,0,1:T(8,128)(2,1)S(1)}, u32[]{:S(2)}, u32[]{:S(2)}) collective-permute-start(bf16[384,2,256]{2,0,1:T(8,128)(2,1)S(1)} %maximum_select_fusion.5), channel_id=1, source_target_pairs={{0,32},{8,40},{16,48},{24,56},{32,0},{40,8},{48,16},{56,24},{64,96... | collective-permute-start | bytes 1179656 | tf_op jit(solution)/shard_map/ppermute | solution.py:51
  28.5 21.7 %copy-start.8 = (bf16[128,512]{1,0:T(8,128)(2,1)S(1)}, bf16[128,512]{1,0:T(8,128)(2,1)}, u32[]{:S(2)}) copy-start(bf16[128,512]{1,0:T(8,128)(2,1)} %param.6) | copy-start | bytes 393220
  28.6 21.9 %copy-start.9 = (s32[16]{0:T(128)S(1)}, s32[16]{0:T(128)}, u32[]{:S(2)}) copy-start(s32[16]{0:T(128)} %constant.64) | copy-start | bytes 196
  28.7 13.6 %collective-permute-start.3 = (bf16[384,4,128]{2,0,1:T(8,128)(2,1)S(1)}, bf16[384,4,128]{2,0,1:T(8,128)(2,1)S(1)}, u32[]{:S(2)}, u32[]{:S(2)}) collective-permute-start(bf16[384,4,128]{2,0,1:T(8,128)(2,1)S(1)} %get-tuple-element.33), channel_id=1, source_target_pairs={{0,24},{8,16},{16,8},{24,0},{32,56},{40,48},{48,40},{56,32},{64,88... | collective-permute-start | bytes 1179656 | tf_op jit(solution)/shard_map/ppermute | solution.py:85
  33.3 12.1 %collective-permute-start.2 = (bf16[384,4,128]{2,0,1:T(8,128)(2,1)S(1)}, bf16[384,4,128]{2,0,1:T(8,128)(2,1)S(1)}, u32[]{:S(2)}, u32[]{:S(2)}) collective-permute-start(bf16[384,4,128]{2,0,1:T(8,128)(2,1)S(1)} %get-tuple-element.34), channel_id=1, source_target_pairs={{0,8},{8,0},{16,24},{24,16},{32,40},{40,32},{48,56},{56,48},{64,72... | collective-permute-start | bytes 1179656 | tf_op jit(solution)/shard_map/ppermute | solution.py:84
  45.5 20.9 %collective-permute-start.4 = (bf16[384,8,128]{2,0,1:T(8,128)(2,1)S(1)}, bf16[384,8,128]{2,0,1:T(8,128)(2,1)S(1)}, u32[]{:S(2)}, u32[]{:S(2)}) collective-permute-start(bf16[384,8,128]{2,0,1:T(8,128)(2,1)S(1)} %maximum_select_fusion.3), channel_id=1, source_target_pairs={{0,24},{8,16},{16,8},{24,0},{32,56},{40,48},{48,40},{56,32},{64,88... | collective-permute-start | bytes 2359304 | tf_op jit(solution)/shard_map/ppermute | solution.py:84
  47.9 19.9 %collective-permute-start.5 = (bf16[384,8,128]{2,0,1:T(8,128)(2,1)S(1)}, bf16[384,8,128]{2,0,1:T(8,128)(2,1)S(1)}, u32[]{:S(2)}, u32[]{:S(2)}) collective-permute-start(bf16[384,8,128]{2,0,1:T(8,128)(2,1)S(1)} %maximum_select_fusion.4), channel_id=1, source_target_pairs={{0,8},{8,0},{16,24},{24,16},{32,40},{40,32},{48,56},{56,48},{64,72... | collective-permute-start | bytes 2359304 | tf_op jit(solution)/shard_map/ppermute | solution.py:85
  68.2 28.3 %collective-permute-start.7 = (bf16[384,16,128]{2,0,1:T(8,128)(2,1)S(1)}, bf16[384,16,128]{2,0,1:T(8,128)(2,1)}, u32[]{:S(2)}, u32[]{:S(2)}) collective-permute-start(bf16[384,16,128]{2,0,1:T(8,128)(2,1)S(1)} %maximum_select_fusion.1), channel_id=1, source_target_pairs={{0,128},{128,0},{256,384},{384,256},{1,129},{129,1},{257,385},{385... | collective-permute-start | bytes 4718600 | tf_op jit(solution)/shard_map/ppermute | solution.py:154
  71.2 33.6 %collective-permute-start.6 = (bf16[384,16,128]{2,0,1:T(8,128)(2,1)}, bf16[384,16,128]{2,0,1:T(8,128)(2,1)}, u32[]{:S(2)}, u32[]{:S(2)}) collective-permute-start(bf16[384,16,128]{2,0,1:T(8,128)(2,1)} %maximum_select_fusion), channel_id=1, source_target_pairs={{0,128},{128,0},{256,384},{384,256},{1,129},{129,1},{257,385},{385... | collective-permute-start | bytes 4718600 | tf_op jit(solution)/shard_map/ppermute | solution.py:154
  85.3 7.2 %copy-start.7 = (f32[128,4,1,256]{3,0,2,1:T(8,128)S(1)}, f32[128,4,1,256]{3,0,2,1:T(8,128)}, u32[]{:S(2)}) copy-start(f32[128,4,1,256]{3,0,2,1:T(8,128)} %get-tuple-element.32) | copy-start | bytes 1572868
  86.4 7.2 %copy-start.1 = (f32[128,2,4,256]{0,3,1,2:T(8,128)S(1)}, f32[128,2,4,256]{0,3,1,2:T(8,128)}, u32[]{:S(2)}) copy-start(f32[128,2,4,256]{0,3,1,2:T(8,128)} %copy.74) | copy-start | bytes 3145732
  99.6 3.6 %copy-start.2 = (f32[128,2,4,256]{0,3,1,2:T(8,128)S(1)}, f32[128,2,4,256]{0,3,1,2:T(8,128)}, u32[]{:S(2)}) copy-start(f32[128,2,4,256]{0,3,1,2:T(8,128)} %copy.77) | copy-start | bytes 3145732
  107.7 5.6 %copy-start.3 = (f32[128,4,1,256]{0,3,1,2:T(8,128)S(1)}, f32[128,4,1,256]{0,3,1,2:T(8,128)}, u32[]{:S(2)}) copy-start(f32[128,4,1,256]{0,3,1,2:T(8,128)} %copy.65) | copy-start | bytes 1572868
  107.7 5.6 %copy-start.4 = (f32[128,4,1,256]{0,3,1,2:T(8,128)S(1)}, f32[128,4,1,256]{0,3,1,2:T(8,128)}, u32[]{:S(2)}) copy-start(f32[128,4,1,256]{0,3,1,2:T(8,128)} %copy.66) | copy-start | bytes 1572868
  107.7 5.6 %copy-start.5 = (f32[128,4,1,256]{0,3,1,2:T(8,128)S(1)}, f32[128,4,1,256]{0,3,1,2:T(8,128)}, u32[]{:S(2)}) copy-start(f32[128,4,1,256]{0,3,1,2:T(8,128)} %copy.67) | copy-start | bytes 1572868
  107.7 5.6 %copy-start.6 = (f32[128,4,1,256]{0,3,1,2:T(8,128)S(1)}, f32[128,4,1,256]{0,3,1,2:T(8,128)}, u32[]{:S(2)}) copy-start(f32[128,4,1,256]{0,3,1,2:T(8,128)} %copy.68) | copy-start | bytes 1572868

commit v14 on v10

--- a/solution.py
+++ b/solution.py
@@ -115,6 +115,41 @@
     return stack.reshape(rows, count, -1)
 
 
+def context_order(stack, sources, x_size):
+    rows, count = stack.shape[:2]
+    y_count = count // x_size
+    tail = stack.shape[2:]
+    x_major = all(
+        sources[ix * y_count + iy]
+        == (sources[iy] // x_size) * x_size + sources[ix * y_count] % x_size
+        for ix in range(x_size)
+        for iy in range(y_count)
+    )
+    if x_major:
+        outer = [sources[ix * y_count] % x_size for ix in range(x_size)]
+        inner = [sources[iy] // x_size for iy in range(y_count)]
+        shape = (rows, x_size, y_count) + tail
+    else:
+        outer = [sources[iy * x_size] // x_size for iy in range(y_count)]
+        inner = [sources[ix] % x_size for ix in range(x_size)]
+        assert all(
+            sources[iy * x_size + ix] == outer[iy] * x_size + inner[ix]
+            for iy in range(y_count)
+            for ix in range(x_size)
+        )
+        shape = (rows, y_count, x_size) + tail
+    stack = stack.reshape(shape)
+    outer_pick = [outer.index(v) for v in range(len(outer))]
+    inner_pick = [inner.index(v) for v in range(len(inner))]
+    if outer_pick != list(range(len(outer))):
+        stack = jnp.concatenate([stack[:, i : i + 1] for i in outer_pick], axis=1)
+    if inner_pick != list(range(len(inner))):
+        stack = jnp.concatenate([stack[:, :, i : i + 1] for i in inner_pick], axis=2)
+    if x_major:
+        stack = jnp.swapaxes(stack, 1, 2)
+    return stack.reshape((rows, count) + tail)
+
+
 def per_device(queries, keys, values, order, out_weight):
     row_count = queries.shape[0]
     local_groups = keys.shape[1] // HEAD_SIZE
@@ -131,20 +166,18 @@
     mine = lax.dynamic_slice_in_dim(out_weight, core * half_rows, half_rows, 0)
     steps_a = chain_plan(context_size, x_size, 1)
     steps_b = chain_plan(context_size, x_size, 3)
-    shared = 0
-    while shared < min(len(steps_a), len(steps_b)) and steps_a[shared] == steps_b[shared]:
-        shared += 1
-    key_width = keys.shape[1]
+    if x_size > 1:
+        y_steps = len(steps_b) - 2
+        steps_b = steps_b[y_steps:] + steps_b[:y_steps]
     quarters = [
         mine[k * quarter : (k + 1) * quarter].T.reshape(row_count, -1) for k in range(2)
     ]
-    block = jnp.concatenate([keys, quarters[0], values, quarters[1]], axis=1)[:, None, :]
-    gathered = exchange_gather(block, steps_a[:shared], "context", context_size)
+    key_width = keys.shape[1]
     gathered_a, gathered_b = exchange_gather_pair(
-        gathered[:, :, : key_width + weight_cols],
-        steps_a[shared:],
-        gathered[:, :, key_width + weight_cols :],
-        steps_b[shared:],
+        jnp.concatenate([keys, quarters[0]], axis=1)[:, None, :],
+        steps_a,
+        jnp.concatenate([values, quarters[1]], axis=1)[:, None, :],
+        steps_b,
         "context",
         context_size,
     )
@@ -156,11 +189,11 @@
     )
     other_weights = lax.ppermute(mine_weights, "dp", [(i, i ^ 1) for i in range(dp_size)])
 
-    key_stack = gathered_a[:, :, :key_width]
-    value_stack = restack(gathered_b[:, :, : values.shape[1]], sources_b, sources_a, x_size)
+    key_stack = context_order(gathered_a[:, :, :key_width], sources_a, x_size)
+    value_stack = context_order(gathered_b[:, :, : values.shape[1]], sources_b, x_size)
     key_part = jnp.swapaxes(key_stack, 0, 1).reshape(context_size * row_count, key_width)
     value_part = jnp.swapaxes(value_stack, 0, 1).reshape(context_size * row_count, -1)
-    key_pos = order.reshape(context_size, row_count)[jnp.array(sources_a)].reshape(-1)
+    key_pos = order
 
     first_row = lax.axis_index("context") * row_count
     query_pos = lax.dynamic_slice_in_dim(order, first_row, row_count, 0)
@@ -207,7 +240,9 @@
             product_out = jnp.einsum(
                 "rh,nkh->rnk", piece_rows, piece_t, preferred_element_type=jnp.float32
             ).reshape(row_count, -1)
-            product_out = unpermute_blocks(product_out, sources, x_size)
+            product_out = context_order(
+                product_out.reshape(row_count, context_size, -1), sources, x_size
+            ).reshape(row_count, -1)
             total = product_out if total is None else total + product_out
     partial_out = total
     tensor_size = lax.axis_size("tensor")

time: 138 us -> 141 us (1.022); the launches traced: 135 us -> 140 us
  starting transfers between devices: 26.1 us -> 30.4 us
  waiting for transfers between devices: 36 us -> 40.1 us
  local copies, waits for them, and re-layouts: 19.8 us -> 17.1 us
  other arithmetic: 9.37 us -> 6.74 us
  matrix products: 4.1 us -> 6 us
    ppermute x2 -> x4, waiting for transfers between devices: 5.35 us -> 24.4 us  [exchange_gather_pair(): lax.ppermute(stack_b, axis_name, [(i, i ^ mask_b) for i in range(count)])]
    ppermute x2 -> x0, waiting for transfers between devices: 15.2 us -> none  [exchange_gather(): lax.ppermute(stack, axis_name, [(i, i ^ mask) for i in range(count)])]
    ppermute x2 -> x4, starting transfers between devices: 4.07 us -> 16.5 us  [exchange_gather_pair(): lax.ppermute(stack_a, axis_name, [(i, i ^ mask_a) for i in range(count)])]
    ppermute x2 -> x0, starting transfers between devices: 9.68 us -> none  [exchange_gather(): lax.ppermute(stack, axis_name, [(i, i ^ mask) for i in range(count)])]
    ppermute x2 -> x4, starting transfers between devices: 6.31 us -> 10.2 us  [exchange_gather_pair(): lax.ppermute(stack_b, axis_name, [(i, i ^ mask_b) for i in range(count)])]
    slice x14 -> x10, local copies, waits for them, and re-layouts: 6.17 us -> 2.45 us  [the longest x6 2.04 us: context_order(): stack = jnp.concatenate([stack[:, :, i:i + 1] for i in inner_pick], axis=2)]
    ppermute x1, starting transfers between devices: 6.04 us -> 3.71 us  [per_device(): lax.ppermute(mine_weights, 'dp', [(i, i ^ 1) for i in range(dp_size)])]
    unnamed x40 -> x29, local copies, waits for them, and re-layouts: 3.21 us -> 5.14 us
  transfers between devices with their start and end apart: 7 -> 9, of which waited for: 5 -> 6; matrix products, arithmetic and copies ran while one was open for 9% -> 8% of each run, Pallas kernels for 0% -> 0%
where the time goes in v14:
time: 141 us; the launch traced here: 140 us
  waiting for transfers between devices  40.1 us (28%)
  blocking collectives  39 us (28%)
  starting transfers between devices  30.4 us (22%)
  local copies, waits for them, and re-layouts  17.1 us (12%)
  other arithmetic  6.74 us (5%)
  matrix products  6 us (4%)
    all_to_all x1, blocking collectives, per_device(): pieces = lax.all_to_all(pieces, 'tensor', 1, 1, tiled=True)  39 us
    ppermute x4, waiting for transfers between devices, exchange_gather_pair(): lax.ppermute(stack_b, axis_name, [(i, i ^ mask_b) for i in range(count)])  24.4 us
    ppermute x4, starting transfers between devices, exchange_gather_pair(): lax.ppermute(stack_a, axis_name, [(i, i ^ mask_a) for i in range(count)])  16.5 us
    ppermute x4, waiting for transfers between devices, exchange_gather_pair(): lax.ppermute(stack_a, axis_name, [(i, i ^ mask_a) for i in range(count)])  15.7 us
    ppermute x4, starting transfers between devices, exchange_gather_pair(): lax.ppermute(stack_b, axis_name, [(i, i ^ mask_b) for i in range(count)])  10.2 us
    unnamed x29, local copies, waits for them, and re-layouts  5.14 us
    ppermute x1, starting transfers between devices, per_device(): lax.ppermute(mine_weights, 'dp', [(i, i ^ 1) for i in range(dp_size)])  3.71 us
    dot_general x1, matrix products, per_device(): jnp.einsum('grk,kgd->grd', weights.astype(jnp.bfloat16), value_heads, pre...  3.51 us
  transfers between devices with their start and end apart: 9, of which 6 were waited for; matrix products, arithmetic and copies ran while one was open for 8% of the time, Pallas kernels for 0%

profile of v14, /device:TPU:1, one launch (start us, length us, event | category | flops | bytes accessed | tf_op | source)
XLA Modules:
  0.0 140.0 jit_solution(8046721830036445923)
XLA Ops:
  0.0 0.9 dynamic-slice_bitcast_fusion
  1.0 0.8 maximum_bitcast_fusion
  1.8 5.0 %collective-permute-start = (bf16[128,1,384]{2,0,1:T(8,128)(2,1)S(1)}, bf16[128,1,384]{2,0,1:T(8,128)(2,1)S(1)}, u32[]{:S(2)}, u32[]{:S(2)}) collective-permute-start(bf16[128,1,384]{2,0,1:T(8,128)(2,1)S(1)} %maximum_bitcast_fusion), channel_id=1, source_target_pairs={{0,64},{8,72},{16,80},{24,88},{32,96},{40,104},{48,112},{56,120},{... | collective-permute-start | bytes 294920 | tf_op jit(solution)/shard_map/ppermute | solution.py:84
  7.0 0.8 maximum_bitcast_fusion.1
  7.8 4.4 %collective-permute-start.1 = (bf16[128,1,384]{2,0,1:T(8,128)(2,1)S(1)}, bf16[128,1,384]{2,0,1:T(8,128)(2,1)S(1)}, u32[]{:S(2)}, u32[]{:S(2)}) collective-permute-start(bf16[128,1,384]{2,0,1:T(8,128)(2,1)S(1)} %maximum_bitcast_fusion.1), channel_id=1, source_target_pairs={{0,24},{8,16},{16,8},{24,0},{32,56},{40,48},{48,40},{56,32},{64,88... | collective-permute-start | bytes 294920 | tf_op jit(solution)/shard_map/ppermute | solution.py:85
  12.3 2.1 %collective-permute-done.1 = bf16[128,1,384]{2,0,1:T(8,128)(2,1)S(1)} collective-permute-done((bf16[128,1,384]{2,0,1:T(8,128)(2,1)S(1)}, bf16[128,1,384]{2,0,1:T(8,128)(2,1)S(1)}, u32[]{:S(2)}, u32[]{:S(2)}) %collective-permute-start.1) | collective-permute-done | bytes 98336 | tf_op jit(solution)/shard_map/ppermute | solution.py:85
  14.4 3.2 %collective-permute-start.2 = (bf16[128,2,384]{2,0,1:T(8,128)(2,1)S(1)}, bf16[128,2,384]{2,0,1:T(8,128)(2,1)S(1)}, u32[]{:S(2)}, u32[]{:S(2)}) collective-permute-start(bf16[128,2,384]{2,0,1:T(8,128)(2,1)S(1)} %maximum_select_fusion.6), channel_id=1, source_target_pairs={{0,32},{8,40},{16,48},{24,56},{32,0},{40,8},{48,16},{56,24},{64,96... | collective-permute-start | bytes 589832 | tf_op jit(solution)/shard_map/ppermute | solution.py:84
  17.6 1.9 %collective-permute-start.3 = (bf16[128,2,384]{2,0,1:T(8,128)(2,1)S(1)}, bf16[128,2,384]{2,0,1:T(8,128)(2,1)S(1)}, u32[]{:S(2)}, u32[]{:S(2)}) collective-permute-start(bf16[128,2,384]{2,0,1:T(8,128)(2,1)S(1)} %maximum_select_fusion.7), channel_id=1, source_target_pairs={{0,8},{8,0},{16,24},{24,16},{32,40},{40,32},{48,56},{56,48},{64,72... | collective-permute-start | bytes 589832 | tf_op jit(solution)/shard_map/ppermute | solution.py:85
  19.6 1.3 collective-permute-done.2
  20.9 3.1 %collective-permute-done.3 = bf16[128,2,384]{2,0,1:T(8,128)(2,1)S(1)} collective-permute-done((bf16[128,2,384]{2,0,1:T(8,128)(2,1)S(1)}, bf16[128,2,384]{2,0,1:T(8,128)(2,1)S(1)}, u32[]{:S(2)}, u32[]{:S(2)}) %collective-permute-start.3) | collective-permute-done | bytes 196640 | tf_op jit(solution)/shard_map/ppermute | solution.py:85
  24.1 2.0 %collective-permute-start.5 = (bf16[128,4,384]{2,0,1:T(8,128)(2,1)S(1)}, bf16[128,4,384]{2,0,1:T(8,128)(2,1)S(1)}, u32[]{:S(2)}, u32[]{:S(2)}) collective-permute-start(bf16[128,4,384]{2,0,1:T(8,128)(2,1)S(1)} %maximum_select_fusion.5), channel_id=1, source_target_pairs={{0,64},{8,72},{16,80},{24,88},{32,96},{40,104},{48,112},{56,120},{... | collective-permute-start | bytes 1179656 | tf_op jit(solution)/shard_map/ppermute | solution.py:85
  26.1 3.2 %collective-permute-start.4 = (bf16[128,4,384]{2,0,1:T(8,128)(2,1)S(1)}, bf16[128,4,384]{2,0,1:T(8,128)(2,1)S(1)}, u32[]{:S(2)}, u32[]{:S(2)}) collective-permute-start(bf16[128,4,384]{2,0,1:T(8,128)(2,1)S(1)} %maximum_select_fusion.4), channel_id=1, source_target_pairs={{0,8},{8,0},{16,24},{24,16},{32,40},{40,32},{48,56},{56,48},{64,72... | collective-permute-start | bytes 1179656 | tf_op jit(solution)/shard_map/ppermute | solution.py:84
  29.3 16.2 %collective-permute-done.5 = bf16[128,4,384]{2,0,1:T(8,128)(2,1)S(1)} collective-permute-done((bf16[128,4,384]{2,0,1:T(8,128)(2,1)S(1)}, bf16[128,4,384]{2,0,1:T(8,128)(2,1)S(1)}, u32[]{:S(2)}, u32[]{:S(2)}) %collective-permute-start.5) | collective-permute-done | bytes 393248 | tf_op jit(solution)/shard_map/ppermute | solution.py:85
  45.8 5.1 %collective-permute-start.6 = (bf16[128,8,384]{2,0,1:T(8,128)(2,1)S(1)}, bf16[128,8,384]{2,0,1:T(8,128)(2,1)S(1)}, u32[]{:S(2)}, u32[]{:S(2)}) collective-permute-start(bf16[128,8,384]{2,0,1:T(8,128)(2,1)S(1)} %maximum_select_fusion.2), channel_id=1, source_target_pairs={{0,24},{8,16},{16,8},{24,0},{32,56},{40,48},{48,40},{56,32},{64,88... | collective-permute-start | bytes 2359304 | tf_op jit(solution)/shard_map/ppermute | solution.py:84
  50.9 1.9 %collective-permute-start.7 = (bf16[128,8,384]{2,0,1:T(8,128)(2,1)S(1)}, bf16[128,8,384]{2,0,1:T(8,128)(2,1)S(1)}, u32[]{:S(2)}, u32[]{:S(2)}) collective-permute-start(bf16[128,8,384]{2,0,1:T(8,128)(2,1)S(1)} %maximum_select_fusion.3), channel_id=1, source_target_pairs={{0,32},{8,40},{16,48},{24,56},{32,0},{40,8},{48,16},{56,24},{64,96... | collective-permute-start | bytes 2359304 | tf_op jit(solution)/shard_map/ppermute | solution.py:85
  53.2 14.4 %collective-permute-done.6 = bf16[128,8,384]{2,0,1:T(8,128)(2,1)S(1)} collective-permute-done((bf16[128,8,384]{2,0,1:T(8,128)(2,1)S(1)}, bf16[128,8,384]{2,0,1:T(8,128)(2,1)S(1)}, u32[]{:S(2)}, u32[]{:S(2)}) %collective-permute-start.6) | collective-permute-done | bytes 786464 | tf_op jit(solution)/shard_map/ppermute | solution.py:84
  67.9 3.0 %collective-permute-done.7 = bf16[128,8,384]{2,0,1:T(8,128)(2,1)S(1)} collective-permute-done((bf16[128,8,384]{2,0,1:T(8,128)(2,1)S(1)}, bf16[128,8,384]{2,0,1:T(8,128)(2,1)S(1)}, u32[]{:S(2)}, u32[]{:S(2)}) %collective-permute-start.7) | collective-permute-done | bytes 786464 | tf_op jit(solution)/shard_map/ppermute | solution.py:85
  71.8 1.5 %pad_maximum_fusion.6 = bf16[256,16,256]{2,0,1:T(8,128)(2,1)} fusion(bf16[128,16,256]{2,0,1:T(8,128)(2,1)S(1)} %get-tuple-element.56, bf16[128,16,256]{2,0,1:T(8,128)(2,1)S(1)} %get-tuple-element.40), kind=kLoop, calls=%fused_computation.42 | loop fusion | flops 4194304 | bytes 4194304 | tf_op jit(solution)/shard_map/concatenate | solution.py:187
  73.4 3.7 %collective-permute-start.8 = (bf16[256,16,256]{2,0,1:T(8,128)(2,1)}, bf16[256,16,256]{2,0,1:T(8,128)(2,1)}, u32[]{:S(2)}, u32[]{:S(2)}) collective-permute-start(bf16[256,16,256]{2,0,1:T(8,128)(2,1)} %pad_maximum_fusion.6), channel_id=1, source_target_pairs={{0,128},{128,0},{256,384},{384,256},{1,129},{129,1},{257,385},{385... | collective-permute-start | bytes 6291464 | tf_op jit(solution)/shard_map/ppermute | solution.py:190
  77.2 0.7 fusion
  77.9 1.3 fusion.1
  80.0 1.3 dot_general.28
  81.7 3.5 %fusion.22 = bf16[512,128]{1,0:T(8,128)(2,1)S(1)} fusion(bf16[2048,128]{1,0:T(8,128)(2,1)S(1)} %bitcast.101, f32[2048,512]{1,0:T(8,128)} %copy-done.5, f32[512]{0:T(512)S(1)} %broadcast_maximum_fusion, s32[512]{0:T(512)S(1)} %broadcast_bitcast_fusion, s32[2048]{0:T(1024)S(1)} %copy-done.12, f32[512]{0:T(512)S(1)} %fusion.1), kind=kOutput, calls=%fused_computation.47 | convolution fusion | flops 274857984 | bytes 4864000 | tf_op jit(solution)/shard_map/grk,kgd->grd/dot_general | solution.py:219
  86.9 2.0 %copy-done.6 = bf16[4,4,256,128]{3,2,1,0:T(8,128)(2,1)S(1)} copy-done((bf16[4,4,256,128]{3,2,1,0:T(8,128)(2,1)S(1)}, bf16[4,4,256,128]{3,2,1,0:T(8,128)(2,1)}, u32[]{:S(2)}) %copy-start.6) | copy-done | bytes 1048600
  89.3 1.4 %fusion.63 = (f32[128,4,1,256]{3,0,2,1:T(8,128)}, f32[128,4,1,256]{3,0,2,1:T(8,128)}, f32[128,4,1,256]{3,0,2,1:T(8,128)}, f32[128,4,1,256]{3,0,2,1:T(8,128)}) fusion(f32[128,4,4,256]{3,0,2,1:T(8,128)S(1)} %fusion.47), kind=kLoop, calls=%fused_computation.113 | loop fusion | bytes 4194304 | tf_op jit(solution)/shard_map/slice | solution.py:147
  90.7 2.7 %slice_bitcast_fusion.1 = (bf16[16,128,256]{2,1,0:T(8,128)(2,1)S(1)}, bf16[16,128,256]{2,1,0:T(8,128)(2,1)}) fusion(bf16[256,16,256]{2,0,1:T(8,128)(2,1)} %collective-permute-done.8), kind=kLoop, calls=%fused_computation.49 | loop fusion | bytes 4194304 | tf_op jit(solution)/shard_map/transpose | solution.py:235
  93.8 1.4 %dot_general.34 = bf16[4,4,256,128]{3,2,1,0:T(8,128)(2,1)S(1)} reshape(bf16[16,128,256]{2,1,0:T(8,128)(2,1)} %get-tuple-element.26) | data formatting | bytes 2097152 | tf_op jit(solution)/shard_map/rh,nkh->rnk/dot_general | solution.py:240
  96.7 0.7 copy-done.7
  98.6 0.7 fusion.10
  99.4 0.7 copy.66
  100.0 39.0 %all_to_all.5 = bf16[128,8,512]{0,2,1:T(8,128)(2,1)S(1)} all-to-all(bf16[128,8,512]{0,2,1:T(8,128)(2,1)S(1)} %bitcast.94), channel_id=1, replica_groups=mesh['dp'=4,'context'=16,'tensor'=8] {'tensor'}, dimensions={1} | all-to-all | bytes 2097152 | tf_op jit(solution)/shard_map/all_to_all | solution.py:250
  139.2 0.8 copy.67
  (70 shorter events, 8.6 us)
Async XLA Ops:
  1.8 10.4 %collective-permute-start = (bf16[128,1,384]{2,0,1:T(8,128)(2,1)S(1)}, bf16[128,1,384]{2,0,1:T(8,128)(2,1)S(1)}, u32[]{:S(2)}, u32[]{:S(2)}) collective-permute-start(bf16[128,1,384]{2,0,1:T(8,128)(2,1)S(1)} %maximum_bitcast_fusion), channel_id=1, source_target_pairs={{0,64},{8,72},{16,80},{24,88},{32,96},{40,104},{48,112},{56,120},{... | collective-permute-start | bytes 294920 | tf_op jit(solution)/shard_map/ppermute | solution.py:84
  7.8 6.6 %collective-permute-start.1 = (bf16[128,1,384]{2,0,1:T(8,128)(2,1)S(1)}, bf16[128,1,384]{2,0,1:T(8,128)(2,1)S(1)}, u32[]{:S(2)}, u32[]{:S(2)}) collective-permute-start(bf16[128,1,384]{2,0,1:T(8,128)(2,1)S(1)} %maximum_bitcast_fusion.1), channel_id=1, source_target_pairs={{0,24},{8,16},{16,8},{24,0},{32,56},{40,48},{48,40},{56,32},{64,88... | collective-permute-start | bytes 294920 | tf_op jit(solution)/shard_map/ppermute | solution.py:85
  14.4 6.4 %collective-permute-start.2 = (bf16[128,2,384]{2,0,1:T(8,128)(2,1)S(1)}, bf16[128,2,384]{2,0,1:T(8,128)(2,1)S(1)}, u32[]{:S(2)}, u32[]{:S(2)}) collective-permute-start(bf16[128,2,384]{2,0,1:T(8,128)(2,1)S(1)} %maximum_select_fusion.6), channel_id=1, source_target_pairs={{0,32},{8,40},{16,48},{24,56},{32,0},{40,8},{48,16},{56,24},{64,96... | collective-permute-start | bytes 589832 | tf_op jit(solution)/shard_map/ppermute | solution.py:84
  17.6 6.4 %collective-permute-start.3 = (bf16[128,2,384]{2,0,1:T(8,128)(2,1)S(1)}, bf16[128,2,384]{2,0,1:T(8,128)(2,1)S(1)}, u32[]{:S(2)}, u32[]{:S(2)}) collective-permute-start(bf16[128,2,384]{2,0,1:T(8,128)(2,1)S(1)} %maximum_select_fusion.7), channel_id=1, source_target_pairs={{0,8},{8,0},{16,24},{24,16},{32,40},{40,32},{48,56},{56,48},{64,72... | collective-permute-start | bytes 589832 | tf_op jit(solution)/shard_map/ppermute | solution.py:85
  20.9 31.9 %copy-start.11 = (bf16[128,512]{1,0:T(8,128)(2,1)S(1)}, bf16[128,512]{1,0:T(8,128)(2,1)}, u32[]{:S(2)}) copy-start(bf16[128,512]{1,0:T(8,128)(2,1)} %param.5) | copy-start | bytes 393220
  20.9 32.2 %copy-start.12 = (s32[2048]{0:T(1024)S(1)}, s32[2048]{0:T(1024)}, u32[]{:S(2)}) copy-start(s32[2048]{0:T(1024)} %param.8) | copy-start | bytes 24580
  24.1 21.4 %collective-permute-start.5 = (bf16[128,4,384]{2,0,1:T(8,128)(2,1)S(1)}, bf16[128,4,384]{2,0,1:T(8,128)(2,1)S(1)}, u32[]{:S(2)}, u32[]{:S(2)}) collective-permute-start(bf16[128,4,384]{2,0,1:T(8,128)(2,1)S(1)} %maximum_select_fusion.5), channel_id=1, source_target_pairs={{0,64},{8,72},{16,80},{24,88},{32,96},{40,104},{48,112},{56,120},{... | collective-permute-start | bytes 1179656 | tf_op jit(solution)/shard_map/ppermute | solution.py:85
  26.1 19.5 %collective-permute-start.4 = (bf16[128,4,384]{2,0,1:T(8,128)(2,1)S(1)}, bf16[128,4,384]{2,0,1:T(8,128)(2,1)S(1)}, u32[]{:S(2)}, u32[]{:S(2)}) collective-permute-start(bf16[128,4,384]{2,0,1:T(8,128)(2,1)S(1)} %maximum_select_fusion.4), channel_id=1, source_target_pairs={{0,8},{8,0},{16,24},{24,16},{32,40},{40,32},{48,56},{56,48},{64,72... | collective-permute-start | bytes 1179656 | tf_op jit(solution)/shard_map/ppermute | solution.py:84
  45.8 21.9 %collective-permute-start.6 = (bf16[128,8,384]{2,0,1:T(8,128)(2,1)S(1)}, bf16[128,8,384]{2,0,1:T(8,128)(2,1)S(1)}, u32[]{:S(2)}, u32[]{:S(2)}) collective-permute-start(bf16[128,8,384]{2,0,1:T(8,128)(2,1)S(1)} %maximum_select_fusion.2), channel_id=1, source_target_pairs={{0,24},{8,16},{16,8},{24,0},{32,56},{40,48},{48,40},{56,32},{64,88... | collective-permute-start | bytes 2359304 | tf_op jit(solution)/shard_map/ppermute | solution.py:84
  50.9 20.0 %collective-permute-start.7 = (bf16[128,8,384]{2,0,1:T(8,128)(2,1)S(1)}, bf16[128,8,384]{2,0,1:T(8,128)(2,1)S(1)}, u32[]{:S(2)}, u32[]{:S(2)}) collective-permute-start(bf16[128,8,384]{2,0,1:T(8,128)(2,1)S(1)} %maximum_select_fusion.3), channel_id=1, source_target_pairs={{0,32},{8,40},{16,48},{24,56},{32,0},{40,8},{48,16},{56,24},{64,96... | collective-permute-start | bytes 2359304 | tf_op jit(solution)/shard_map/ppermute | solution.py:85
  73.4 17.4 %collective-permute-start.8 = (bf16[256,16,256]{2,0,1:T(8,128)(2,1)}, bf16[256,16,256]{2,0,1:T(8,128)(2,1)}, u32[]{:S(2)}, u32[]{:S(2)}) collective-permute-start(bf16[256,16,256]{2,0,1:T(8,128)(2,1)} %pad_maximum_fusion.6), channel_id=1, source_target_pairs={{0,128},{128,0},{256,384},{384,256},{1,129},{129,1},{257,385},{385... | collective-permute-start | bytes 6291464 | tf_op jit(solution)/shard_map/ppermute | solution.py:190
  77.9 1.9 %copy-start.5 = (f32[2048,512]{1,0:T(8,128)}, f32[2048,512]{1,0:T(8,128)S(1)}, u32[]{:S(2)}) copy-start(f32[2048,512]{1,0:T(8,128)S(1)} %get-tuple-element.54) | copy-start | bytes 12582916
  85.9 0.8 copy-start.1
  85.9 0.9 copy-start.3
  86.9 2.4 %copy-start = (f32[128,4,4,256]{3,0,1,2:T(8,128)}, f32[128,4,4,256]{3,0,1,2:T(8,128)S(1)}, u32[]{:S(2)}) copy-start(f32[128,4,4,256]{3,0,1,2:T(8,128)S(1)} %pad_maximum_fusion.3) | copy-start | bytes 6291460
  86.9 2.0 %copy-start.6 = (bf16[4,4,256,128]{3,2,1,0:T(8,128)(2,1)S(1)}, bf16[4,4,256,128]{3,2,1,0:T(8,128)(2,1)}, u32[]{:S(2)}) copy-start(bf16[4,4,256,128]{3,2,1,0:T(8,128)(2,1)} %dot_general.28) | copy-start | bytes 3145732
  96.4 1.0 copy-start.7
  96.5 1.2 copy-start.8
  96.5 1.3 copy-start.9
  96.5 1.5 %copy-start.10 = (f32[128,4,1,256]{3,0,2,1:T(8,128)S(1)}, f32[128,4,1,256]{3,0,2,1:T(8,128)}, u32[]{:S(2)}) copy-start(f32[128,4,1,256]{3,0,2,1:T(8,128)} %get-tuple-element.30) | copy-start | bytes 1572868
  96.6 1.7 %slice-start = ((f32[128,4,4,256]{3,0,1,2:T(8,128)}), f32[128,4,2,256]{3,0,1,2:T(8,128)S(1)}, s32[]{:S(2)}) async-start(f32[128,4,4,256]{3,0,1,2:T(8,128)} %copy-done), calls=%async_computation.1 | async-start | bytes 2097152 | tf_op jit(solution)/shard_map/slice | solution.py:147
  96.6 1.8 %copy-start.2 = (f32[128,1,4,256]{3,0,1,2:T(8,128)S(1)}, f32[128,1,4,256]{3,0,1,2:T(8,128)}, u32[]{:S(2)}) copy-start(f32[128,1,4,256]{3,0,1,2:T(8,128)} %copy-done.1) | copy-start | bytes 1572868
  96.6 2.0 %copy-start.4 = (f32[128,1,4,256]{3,0,1,2:T(8,128)S(1)}, f32[128,1,4,256]{3,0,1,2:T(8,128)}, u32[]{:S(2)}) copy-start(f32[128,1,4,256]{3,0,1,2:T(8,128)} %copy-done.3) | copy-start | bytes 1572868

commit v15 on v10

--- a/solution.py
+++ b/solution.py
@@ -44,15 +44,15 @@
     return lists[0]
 
 
-def exchange_gather(block, steps, axis_name, count):
+def exchange_gather(block, steps, axis_name, count, axis=1):
     index = lax.axis_index(axis_name)
     stack = block
     for mask, side in steps:
         received = lax.ppermute(stack, axis_name, [(i, i ^ mask) for i in range(count)])
         stack = jnp.where(
             upper_of(index, side),
-            jnp.concatenate([received, stack], 1),
-            jnp.concatenate([stack, received], 1),
+            jnp.concatenate([received, stack], axis),
+            jnp.concatenate([stack, received], axis),
         )
     return stack
 
@@ -138,12 +138,17 @@
     quarters = [
         mine[k * quarter : (k + 1) * quarter].T.reshape(row_count, -1) for k in range(2)
     ]
-    block = jnp.concatenate([keys, quarters[0], values, quarters[1]], axis=1)[:, None, :]
-    gathered = exchange_gather(block, steps_a[:shared], "context", context_size)
+    block = jnp.stack(
+        [
+            jnp.concatenate([keys, quarters[0]], axis=1)[:, None, :],
+            jnp.concatenate([values, quarters[1]], axis=1)[:, None, :],
+        ]
+    )
+    gathered = exchange_gather(block, steps_a[:shared], "context", context_size, axis=2)
     gathered_a, gathered_b = exchange_gather_pair(
-        gathered[:, :, : key_width + weight_cols],
+        gathered[0],
         steps_a[shared:],
-        gathered[:, :, key_width + weight_cols :],
+        gathered[1],
         steps_b[shared:],
         "context",
         context_size,

time: 138 us -> 139 us (level)
  local copies, waits for them, and re-layouts: 19.8 us -> 21.3 us
    unnamed x40 -> x46, local copies, waits for them, and re-layouts: 3.21 us -> 4.18 us
    transpose x2 -> x3, local copies, waits for them, and re-layouts: 3.06 us -> 3.85 us  [per_device(): jnp.swapaxes(piece_t, 0, 1).reshape(context_size, weight_cols, quarter)]
where the time goes in v15:
time: 139 us; the launch traced here: 136 us
  blocking collectives  39 us (28%)
  waiting for transfers between devices  36 us (26%)
  starting transfers between devices  26.1 us (19%)
  local copies, waits for them, and re-layouts  21.3 us (15%)
  other arithmetic  9.05 us (7%)
  matrix products  4.12 us (3%)
    all_to_all x1, blocking collectives, per_device(): pieces = lax.all_to_all(pieces, 'tensor', 1, 1, tiled=True)  39 us
    ppermute x2, waiting for transfers between devices, exchange_gather_pair(): lax.ppermute(stack_a, axis_name, [(i, i ^ mask_a) for i in range(count)])  15.5 us
    ppermute x2, waiting for transfers between devices, exchange_gather(): lax.ppermute(stack, axis_name, [(i, i ^ mask) for i in range(count)])  15.2 us
    ppermute x2, starting transfers between devices, exchange_gather(): lax.ppermute(stack, axis_name, [(i, i ^ mask) for i in range(count)])  9.68 us
    ppermute x2, starting transfers between devices, exchange_gather_pair(): lax.ppermute(stack_b, axis_name, [(i, i ^ mask_b) for i in range(count)])  6.31 us
    ppermute x1, starting transfers between devices, per_device(): lax.ppermute(mine_weights, 'dp', [(i, i ^ 1) for i in range(dp_size)])  6.04 us
    ppermute x2, waiting for transfers between devices, exchange_gather_pair(): lax.ppermute(stack_b, axis_name, [(i, i ^ mask_b) for i in range(count)])  5.35 us
    unnamed x46, local copies, waits for them, and re-layouts  4.18 us
  transfers between devices with their start and end apart: 7, of which 5 were waited for; matrix products, arithmetic and copies ran while one was open for 9% of the time, Pallas kernels for 0%

profile of v15, /device:TPU:1, one launch (start us, length us, event | category | flops | bytes accessed | tf_op | source)
XLA Modules:
  0.0 136.2 jit_solution(16859746726025869775)
XLA Ops:
  0.0 0.9 dynamic-slice_bitcast_fusion.1
  1.2 0.8 maximum_bitcast_fusion
  2.1 5.0 %collective-permute-start = (bf16[2,128,1,384]{3,1,2,0:T(8,128)(2,1)S(1)}, bf16[2,128,1,384]{3,1,2,0:T(8,128)(2,1)S(1)}, u32[]{:S(2)}, u32[]{:S(2)}) collective-permute-start(bf16[2,128,1,384]{3,1,2,0:T(8,128)(2,1)S(1)} %pad_maximum_fusion.4), channel_id=1, source_target_pairs={{0,64},{8,72},{16,80},{24,88},{32,96},{40,104},{48,112},{56,120},{... | collective-permute-start | bytes 589832 | tf_op jit(solution)/shard_map/ppermute | solution.py:51
  7.1 7.2 %collective-permute-done = bf16[2,128,1,384]{3,1,2,0:T(8,128)(2,1)S(1)} collective-permute-done((bf16[2,128,1,384]{3,1,2,0:T(8,128)(2,1)S(1)}, bf16[2,128,1,384]{3,1,2,0:T(8,128)(2,1)S(1)}, u32[]{:S(2)}, u32[]{:S(2)}) %collective-permute-start) | collective-permute-done | bytes 196640 | tf_op jit(solution)/shard_map/ppermute | solution.py:51
  14.4 4.6 %collective-permute-start.1 = (bf16[2,128,2,384]{3,1,2,0:T(8,128)(2,1)S(1)}, bf16[2,128,2,384]{3,1,2,0:T(8,128)(2,1)S(1)}, u32[]{:S(2)}, u32[]{:S(2)}) collective-permute-start(bf16[2,128,2,384]{3,1,2,0:T(8,128)(2,1)S(1)} %maximum_select_fusion.5), channel_id=1, source_target_pairs={{0,32},{8,40},{16,48},{24,56},{32,0},{40,8},{48,16},{56,24},{64,96... | collective-permute-start | bytes 1179656 | tf_op jit(solution)/shard_map/ppermute | solution.py:51
  19.1 7.9 %collective-permute-done.1 = bf16[2,128,2,384]{3,1,2,0:T(8,128)(2,1)S(1)} collective-permute-done((bf16[2,128,2,384]{3,1,2,0:T(8,128)(2,1)S(1)}, bf16[2,128,2,384]{3,1,2,0:T(8,128)(2,1)S(1)}, u32[]{:S(2)}, u32[]{:S(2)}) %collective-permute-start.1) | collective-permute-done | bytes 393248 | tf_op jit(solution)/shard_map/ppermute | solution.py:51
  27.3 4.4 %collective-permute-start.3 = (bf16[128,4,384]{2,0,1:T(8,128)(2,1)S(1)}, bf16[128,4,384]{2,0,1:T(8,128)(2,1)S(1)}, u32[]{:S(2)}, u32[]{:S(2)}) collective-permute-start(bf16[128,4,384]{2,0,1:T(8,128)(2,1)S(1)} %get-tuple-element.39), channel_id=1, source_target_pairs={{0,24},{8,16},{16,8},{24,0},{32,56},{40,48},{48,40},{56,32},{64,88... | collective-permute-start | bytes 1179656 | tf_op jit(solution)/shard_map/ppermute | solution.py:85
  31.7 1.9 %collective-permute-start.2 = (bf16[128,4,384]{2,0,1:T(8,128)(2,1)S(1)}, bf16[128,4,384]{2,0,1:T(8,128)(2,1)S(1)}, u32[]{:S(2)}, u32[]{:S(2)}) collective-permute-start(bf16[128,4,384]{2,0,1:T(8,128)(2,1)S(1)} %get-tuple-element.40), channel_id=1, source_target_pairs={{0,8},{8,0},{16,24},{24,16},{32,40},{40,32},{48,56},{56,48},{64,72... | collective-permute-start | bytes 1179656 | tf_op jit(solution)/shard_map/ppermute | solution.py:84
  33.6 5.4 %collective-permute-done.3 = bf16[128,4,384]{2,0,1:T(8,128)(2,1)S(1)} collective-permute-done((bf16[128,4,384]{2,0,1:T(8,128)(2,1)S(1)}, bf16[128,4,384]{2,0,1:T(8,128)(2,1)S(1)}, u32[]{:S(2)}, u32[]{:S(2)}) %collective-permute-start.3) | collective-permute-done | bytes 393248 | tf_op jit(solution)/shard_map/ppermute | solution.py:85
  39.1 2.7 %collective-permute-done.2 = bf16[128,4,384]{2,0,1:T(8,128)(2,1)S(1)} collective-permute-done((bf16[128,4,384]{2,0,1:T(8,128)(2,1)S(1)}, bf16[128,4,384]{2,0,1:T(8,128)(2,1)S(1)}, u32[]{:S(2)}, u32[]{:S(2)}) %collective-permute-start.2) | collective-permute-done | bytes 393248 | tf_op jit(solution)/shard_map/ppermute | solution.py:84
  42.0 2.2 %collective-permute-start.4 = (bf16[128,8,384]{2,0,1:T(8,128)(2,1)S(1)}, bf16[128,8,384]{2,0,1:T(8,128)(2,1)}, u32[]{:S(2)}, u32[]{:S(2)}) collective-permute-start(bf16[128,8,384]{2,0,1:T(8,128)(2,1)S(1)} %maximum_select_fusion.3), channel_id=1, source_target_pairs={{0,24},{8,16},{16,8},{24,0},{32,56},{40,48},{48,40},{56,32},{64,88... | collective-permute-start | bytes 2359304 | tf_op jit(solution)/shard_map/ppermute | solution.py:84
  44.1 1.9 %collective-permute-start.5 = (bf16[128,8,384]{2,0,1:T(8,128)(2,1)S(1)}, bf16[128,8,384]{2,0,1:T(8,128)(2,1)}, u32[]{:S(2)}, u32[]{:S(2)}) collective-permute-start(bf16[128,8,384]{2,0,1:T(8,128)(2,1)S(1)} %maximum_select_fusion.4), channel_id=1, source_target_pairs={{0,8},{8,0},{16,24},{24,16},{32,40},{40,32},{48,56},{56,48},{64,72... | collective-permute-start | bytes 2359304 | tf_op jit(solution)/shard_map/ppermute | solution.py:85
  46.2 0.8 copy.21
  48.2 12.8 %collective-permute-done.4 = bf16[128,8,384]{2,0,1:T(8,128)(2,1)} collective-permute-done((bf16[128,8,384]{2,0,1:T(8,128)(2,1)S(1)}, bf16[128,8,384]{2,0,1:T(8,128)(2,1)}, u32[]{:S(2)}, u32[]{:S(2)}) %collective-permute-start.4) | collective-permute-done | bytes 786464 | tf_op jit(solution)/shard_map/ppermute | solution.py:84
  61.0 1.7 %maximum_select_fusion = bf16[128,16,384]{2,0,1:T(8,128)(2,1)S(1)} fusion(bf16[128,8,384]{2,0,1:T(8,128)(2,1)S(1)} %maximum_select_fusion.3, bf16[128,8,384]{2,0,1:T(8,128)(2,1)} %collective-permute-done.4, pred[]{:T(512)S(6)} %ne.22), kind=kLoop, calls=%fused_computation.14 | loop fusion | flops 2359296 | bytes 3145729 | tf_op jit(solution)/shard_map/jit(_where)/select_n | solution.py:86
  62.7 2.2 %maximum_select_fusion.1 = bf16[128,16,384]{2,0,1:T(8,128)(2,1)S(1)} fusion(bf16[128,8,384]{2,0,1:T(8,128)(2,1)S(1)} %maximum_select_fusion.4, bf16[128,8,384]{2,0,1:T(8,128)(2,1)} %collective-permute-done.5, pred[]{:T(512)S(6)} %ne.27), kind=kLoop, calls=%fused_computation.15 | loop fusion | flops 2359296 | bytes 3145729 | tf_op jit(solution)/shard_map/jit(_where)/select_n | solution.py:91
  65.8 1.1 slice_bitcast_fusion.4
  66.9 1.6 %slice_bitcast_fusion.5 = (bf16[16,128,256]{2,1,0:T(8,128)(2,1)}, bf16[128,16,256]{2,0,1:T(8,128)(2,1)}) fusion(bf16[128,16,384]{2,0,1:T(8,128)(2,1)S(1)} %maximum_select_fusion), kind=kLoop, calls=%fused_computation.57 | loop fusion | bytes 3145728 | tf_op jit(solution)/shard_map/transpose | solution.py:207
  68.5 1.2 dot_general.32
  71.0 1.4 %pad_maximum_fusion = bf16[256,16,256]{2,0,1:T(8,128)(2,1)S(1)} fusion(bf16[128,16,256]{2,0,1:T(8,128)(2,1)S(1)} %copy-done.5, bf16[128,16,256]{2,0,1:T(8,128)(2,1)} %get-tuple-element.36), kind=kLoop, calls=%fused_computation.10 | loop fusion | flops 4194304 | bytes 4194304 | tf_op jit(solution)/shard_map/concatenate | solution.py:159
  72.4 6.0 %collective-permute-start.6 = (bf16[256,16,256]{2,0,1:T(8,128)(2,1)S(1)}, bf16[256,16,256]{2,0,1:T(8,128)(2,1)S(1)}, u32[]{:S(2)}, u32[]{:S(2)}) collective-permute-start(bf16[256,16,256]{2,0,1:T(8,128)(2,1)S(1)} %pad_maximum_fusion), channel_id=1, source_target_pairs={{0,128},{128,0},{256,384},{384,256},{1,129},{129,1},{257,385},{385... | collective-permute-start | bytes 6291464 | tf_op jit(solution)/shard_map/ppermute | solution.py:162
  78.5 0.7 fusion
  79.3 1.3 fusion.1
  80.6 1.6 %fusion.11 = bf16[512,128]{1,0:T(8,128)(2,1)S(1)} fusion(bf16[2048,128]{1,0:T(8,128)(2,1)S(1)} %bitcast.100, f32[2048,512]{1,0:T(8,128)S(1)} %get-tuple-element.46, f32[512]{0:T(512)S(1)} %broadcast_maximum_fusion, s32[512]{0:T(512)S(1)} %copy-done.20, s32[2048]{0:T(1024)S(1)} %bitcast.107, f32[512]{0:T(512)S(1)} %fusion.1), kind=kOutput, calls=%fused_computation.17 | convolution fusion | flops 274857984 | bytes 4864000 | tf_op jit(solution)/shard_map/grk,kgd->grd/dot_general | solution.py:191
  83.6 1.3 fusion.34
  85.0 1.4 %fusion.36 = (f32[128,4,1,256]{3,0,2,1:T(8,128)}, f32[128,4,1,256]{3,0,2,1:T(8,128)}, f32[128,4,1,256]{3,0,2,1:T(8,128)}, f32[128,4,1,256]{3,0,2,1:T(8,128)}) fusion(f32[128,4,4,256]{3,0,2,1:T(8,128)S(1)} %pad_maximum_fusion.1), kind=kLoop, calls=%fused_computation.60 | loop fusion | bytes 4194304 | tf_op jit(solution)/shard_map/slice | solution.py:77
  86.4 1.1 slice_bitcast_fusion.1
  88.3 1.1 fusion.39
  91.4 1.0 slice-done
  93.1 0.8 copy-done.7
  96.3 39.0 %all_to_all.5 = bf16[128,8,512]{0,2,1:T(8,128)(2,1)S(1)} all-to-all(bf16[128,8,512]{0,2,1:T(8,128)(2,1)S(1)} %bitcast.93), channel_id=1, replica_groups=mesh['dp'=4,'context'=16,'tensor'=8] {'tensor'}, dimensions={1} | all-to-all | bytes 2097152 | tf_op jit(solution)/shard_map/all_to_all | solution.py:220
  135.5 0.8 copy.24
  (86 shorter events, 11.5 us)
Async XLA Ops:
  0.0 47.0 %copy-start = (s32[2048]{0:T(1024)S(1)}, s32[2048]{0:T(1024)}, u32[]{:S(2)}) copy-start(s32[2048]{0:T(1024)} %param.9) | copy-start | bytes 24580
  2.1 12.3 %collective-permute-start = (bf16[2,128,1,384]{3,1,2,0:T(8,128)(2,1)S(1)}, bf16[2,128,1,384]{3,1,2,0:T(8,128)(2,1)S(1)}, u32[]{:S(2)}, u32[]{:S(2)}) collective-permute-start(bf16[2,128,1,384]{3,1,2,0:T(8,128)(2,1)S(1)} %pad_maximum_fusion.4), channel_id=1, source_target_pairs={{0,64},{8,72},{16,80},{24,88},{32,96},{40,104},{48,112},{56,120},{... | collective-permute-start | bytes 589832 | tf_op jit(solution)/shard_map/ppermute | solution.py:51
  14.4 12.6 %collective-permute-start.1 = (bf16[2,128,2,384]{3,1,2,0:T(8,128)(2,1)S(1)}, bf16[2,128,2,384]{3,1,2,0:T(8,128)(2,1)S(1)}, u32[]{:S(2)}, u32[]{:S(2)}) collective-permute-start(bf16[2,128,2,384]{3,1,2,0:T(8,128)(2,1)S(1)} %maximum_select_fusion.5), channel_id=1, source_target_pairs={{0,32},{8,40},{16,48},{24,56},{32,0},{40,8},{48,16},{56,24},{64,96... | collective-permute-start | bytes 1179656 | tf_op jit(solution)/shard_map/ppermute | solution.py:51
  27.2 18.9 %copy-start.18 = (bf16[128,512]{1,0:T(8,128)(2,1)S(1)}, bf16[128,512]{1,0:T(8,128)(2,1)}, u32[]{:S(2)}) copy-start(bf16[128,512]{1,0:T(8,128)(2,1)} %param.6) | copy-start | bytes 393220
  27.3 19.8 %copy-start.21 = (s32[16]{0:T(128)S(1)}, s32[16]{0:T(128)}, u32[]{:S(2)}) copy-start(s32[16]{0:T(128)} %constant.64) | copy-start | bytes 196
  27.3 11.7 %collective-permute-start.3 = (bf16[128,4,384]{2,0,1:T(8,128)(2,1)S(1)}, bf16[128,4,384]{2,0,1:T(8,128)(2,1)S(1)}, u32[]{:S(2)}, u32[]{:S(2)}) collective-permute-start(bf16[128,4,384]{2,0,1:T(8,128)(2,1)S(1)} %get-tuple-element.39), channel_id=1, source_target_pairs={{0,24},{8,16},{16,8},{24,0},{32,56},{40,48},{48,40},{56,32},{64,88... | collective-permute-start | bytes 1179656 | tf_op jit(solution)/shard_map/ppermute | solution.py:85
  31.7 10.1 %collective-permute-start.2 = (bf16[128,4,384]{2,0,1:T(8,128)(2,1)S(1)}, bf16[128,4,384]{2,0,1:T(8,128)(2,1)S(1)}, u32[]{:S(2)}, u32[]{:S(2)}) collective-permute-start(bf16[128,4,384]{2,0,1:T(8,128)(2,1)S(1)} %get-tuple-element.40), channel_id=1, source_target_pairs={{0,8},{8,0},{16,24},{24,16},{32,40},{40,32},{48,56},{56,48},{64,72... | collective-permute-start | bytes 1179656 | tf_op jit(solution)/shard_map/ppermute | solution.py:84
  42.0 19.0 %collective-permute-start.4 = (bf16[128,8,384]{2,0,1:T(8,128)(2,1)S(1)}, bf16[128,8,384]{2,0,1:T(8,128)(2,1)}, u32[]{:S(2)}, u32[]{:S(2)}) collective-permute-start(bf16[128,8,384]{2,0,1:T(8,128)(2,1)S(1)} %maximum_select_fusion.3), channel_id=1, source_target_pairs={{0,24},{8,16},{16,8},{24,0},{32,56},{40,48},{48,40},{56,32},{64,88... | collective-permute-start | bytes 2359304 | tf_op jit(solution)/shard_map/ppermute | solution.py:84
  44.1 18.6 %collective-permute-start.5 = (bf16[128,8,384]{2,0,1:T(8,128)(2,1)S(1)}, bf16[128,8,384]{2,0,1:T(8,128)(2,1)}, u32[]{:S(2)}, u32[]{:S(2)}) collective-permute-start(bf16[128,8,384]{2,0,1:T(8,128)(2,1)S(1)} %maximum_select_fusion.4), channel_id=1, source_target_pairs={{0,8},{8,0},{16,24},{24,16},{32,40},{40,32},{48,56},{56,48},{64,72... | collective-permute-start | bytes 2359304 | tf_op jit(solution)/shard_map/ppermute | solution.py:85
  62.7 4.2 %copy-start.2 = (bf16[128,16,384]{2,0,1:T(8,128)(2,1)}, bf16[128,16,384]{2,0,1:T(8,128)(2,1)S(1)}, u32[]{:S(2)}) copy-start(bf16[128,16,384]{2,0,1:T(8,128)(2,1)S(1)} %maximum_select_fusion) | copy-start | bytes 4718596
  68.5 1.5 %copy-start.3 = (bf16[16,128,256]{2,1,0:T(8,128)(2,1)S(1)}, bf16[16,128,256]{2,1,0:T(8,128)(2,1)}, u32[]{:S(2)}) copy-start(bf16[16,128,256]{2,1,0:T(8,128)(2,1)} %get-tuple-element.35) | copy-start | bytes 3145732
  69.7 1.3 copy-start.5
  71.0 7.5 %slice-start.1 = ((bf16[128,16,384]{2,0,1:T(8,128)(2,1)}), bf16[128,16,128]{2,0,1:T(8,128)(2,1)S(1)}, s32[]{:S(2)}) async-start(bf16[128,16,384]{2,0,1:T(8,128)(2,1)} %copy-done.2), calls=%async_computation.2 | async-start | bytes 1048576 | tf_op jit(solution)/shard_map/slice | solution.py:164
  71.0 7.5 %copy-start.19 = (bf16[1,4,128,128]{3,2,1,0:T(8,128)(2,1)S(1)}, bf16[1,4,128,128]{3,2,1,0:T(8,128)(2,1)}, u32[]{:S(2)}) copy-start(bf16[1,4,128,128]{3,2,1,0:T(8,128)(2,1)} %copy.21) | copy-start | bytes 393220
  71.0 7.5 %copy-start.20 = (s32[512]{0:T(512)S(1)}, s32[512]{0:T(512)}, u32[]{:S(2)}) copy-start(s32[512]{0:T(512)} %broadcast_bitcast_fusion) | copy-start | bytes 6148
  72.4 13.9 %collective-permute-start.6 = (bf16[256,16,256]{2,0,1:T(8,128)(2,1)S(1)}, bf16[256,16,256]{2,0,1:T(8,128)(2,1)S(1)}, u32[]{:S(2)}, u32[]{:S(2)}) collective-permute-start(bf16[256,16,256]{2,0,1:T(8,128)(2,1)S(1)} %pad_maximum_fusion), channel_id=1, source_target_pairs={{0,128},{128,0},{256,384},{384,256},{1,129},{129,1},{257,385},{385... | collective-permute-start | bytes 6291464 | tf_op jit(solution)/shard_map/ppermute | solution.py:162
  79.3 1.3 copy-start.17
  80.6 1.8 %copy-start.4 = (bf16[4,4,256,128]{3,2,1,0:T(8,128)(2,1)S(1)}, bf16[4,4,256,128]{3,2,1,0:T(8,128)(2,1)}, u32[]{:S(2)}) copy-start(bf16[4,4,256,128]{3,2,1,0:T(8,128)(2,1)} %dot_general.32) | copy-start | bytes 3145732
  88.3 1.7 %copy-start.1 = (f32[128,4,4,256]{3,0,2,1:T(8,128)}, f32[128,4,4,256]{3,0,2,1:T(8,128)S(1)}, u32[]{:S(2)}) copy-start(f32[128,4,4,256]{3,0,2,1:T(8,128)S(1)} %fusion.15) | copy-start | bytes 6291460
  88.3 2.0 %copy-start.6 = (bf16[16,128,256]{2,1,0:T(8,128)(2,1)S(1)}, bf16[16,128,256]{2,1,0:T(8,128)(2,1)}, u32[]{:S(2)}) copy-start(bf16[16,128,256]{2,1,0:T(8,128)(2,1)} %get-tuple-element.21) | copy-start | bytes 3145732
  91.2 1.2 slice-start
  91.2 1.3 copy-start.15
  91.2 1.5 %copy-start.16 = (f32[128,1,4,256]{3,0,2,1:T(8,128)S(1)}, f32[128,1,4,256]{3,0,2,1:T(8,128)}, u32[]{:S(2)}) copy-start(f32[128,1,4,256]{3,0,2,1:T(8,128)} %get-tuple-element.34) | copy-start | bytes 1572868
  92.9 1.0 copy-start.7
  92.9 1.2 copy-start.8
  92.9 1.3 copy-start.9
  92.9 1.5 %copy-start.10 = (f32[128,4,1,256]{3,0,2,1:T(8,128)S(1)}, f32[128,4,1,256]{3,0,2,1:T(8,128)}, u32[]{:S(2)}) copy-start(f32[128,4,1,256]{3,0,2,1:T(8,128)} %get-tuple-element.16) | copy-start | bytes 1572868
  92.9 1.6 %copy-start.11 = (f32[128,4,1,256]{3,0,2,1:T(8,128)S(1)}, f32[128,4,1,256]{3,0,2,1:T(8,128)}, u32[]{:S(2)}) copy-start(f32[128,4,1,256]{3,0,2,1:T(8,128)} %get-tuple-element.23) | copy-start | bytes 1572868
  92.9 1.8 %copy-start.12 = (f32[128,4,1,256]{3,0,2,1:T(8,128)S(1)}, f32[128,4,1,256]{3,0,2,1:T(8,128)}, u32[]{:S(2)}) copy-start(f32[128,4,1,256]{3,0,2,1:T(8,128)} %get-tuple-element.24) | copy-start | bytes 1572868
  92.9 1.9 %copy-start.13 = (f32[128,4,1,256]{3,0,2,1:T(8,128)S(1)}, f32[128,4,1,256]{3,0,2,1:T(8,128)}, u32[]{:S(2)}) copy-start(f32[128,4,1,256]{3,0,2,1:T(8,128)} %get-tuple-element.25) | copy-start | bytes 1572868
  92.9 2.1 %copy-start.14 = (f32[128,4,1,256]{3,0,2,1:T(8,128)S(1)}, f32[128,4,1,256]{3,0,2,1:T(8,128)}, u32[]{:S(2)}) copy-start(f32[128,4,1,256]{3,0,2,1:T(8,128)} %get-tuple-element.26) | copy-start | bytes 1572868

commit v16 on v10

--- a/solution.py
+++ b/solution.py
@@ -95,6 +95,24 @@
         )
         stack_a, stack_b = lax.optimization_barrier((stack_a, stack_b))
     return stack_a, stack_b
+
+
+def exchange_last_pair(stack_a, step_a, stack_b, step_b, axis_name, count):
+    index = lax.axis_index(axis_name)
+    (mask_a, side_a), (mask_b, side_b) = step_a, step_b
+    received_a = lax.ppermute(stack_a, axis_name, [(i, i ^ mask_a) for i in range(count)])
+    received_b = lax.ppermute(stack_b, axis_name, [(i, i ^ mask_b) for i in range(count)])
+    return (
+        jnp.concatenate([stack_a, received_a], 1),
+        jnp.concatenate([stack_b, received_b], 1),
+        upper_of(index, side_a),
+        upper_of(index, side_b),
+    )
+
+
+def swap_halves(stack, upper):
+    half = stack.shape[1] // 2
+    return jnp.where(upper, jnp.concatenate([stack[:, half:], stack[:, :half]], 1), stack)
 
 
 def restack(stack, sources, target, x_size):
@@ -142,12 +160,15 @@
     gathered = exchange_gather(block, steps_a[:shared], "context", context_size)
     gathered_a, gathered_b = exchange_gather_pair(
         gathered[:, :, : key_width + weight_cols],
-        steps_a[shared:],
+        steps_a[shared:-1],
         gathered[:, :, key_width + weight_cols :],
-        steps_b[shared:],
+        steps_b[shared:-1],
         "context",
         context_size,
     )
+    gathered_a, gathered_b, upper_a, upper_b = exchange_last_pair(
+        gathered_a, steps_a[-1], gathered_b, steps_b[-1], "context", context_size
+    )
     sources_a = stacked_sources(context_size, steps_a)
     sources_b = stacked_sources(context_size, steps_b)
 
@@ -156,8 +177,9 @@
     )
     other_weights = lax.ppermute(mine_weights, "dp", [(i, i ^ 1) for i in range(dp_size)])
 
-    key_stack = gathered_a[:, :, :key_width]
-    value_stack = restack(gathered_b[:, :, : values.shape[1]], sources_b, sources_a, x_size)
+    key_stack = swap_halves(gathered_a[:, :, :key_width], upper_a)
+    value_stack = swap_halves(gathered_b[:, :, : values.shape[1]], upper_b)
+    value_stack = restack(value_stack, sources_b, sources_a, x_size)
     key_part = jnp.swapaxes(key_stack, 0, 1).reshape(context_size * row_count, key_width)
     value_part = jnp.swapaxes(value_stack, 0, 1).reshape(context_size * row_count, -1)
     key_pos = order.reshape(context_size, row_count)[jnp.array(sources_a)].reshape(-1)
@@ -196,7 +218,9 @@
     attended = attended.reshape(row_count, local_groups * query_head_group * HEAD_SIZE)
 
     total = None
-    for piece, sources in ((0, sources_a), (1, sources_b)):
+    for piece, sources, upper in ((0, sources_a, upper_a), (1, sources_b, upper_b)):
+        half = context_size // 2
+        swapped = sources[half:] + sources[:half]
         for which, held in ((0, mine_weights), (1, other_weights)):
             piece_t = held[piece * row_count : (piece + 1) * row_count]
             piece_t = jnp.swapaxes(piece_t, 0, 1).reshape(context_size, weight_cols, quarter)
@@ -207,7 +231,11 @@
             product_out = jnp.einsum(
                 "rh,nkh->rnk", piece_rows, piece_t, preferred_element_type=jnp.float32
             ).reshape(row_count, -1)
-            product_out = unpermute_blocks(product_out, sources, x_size)
+            product_out = jnp.where(
+                upper,
+                unpermute_blocks(product_out, swapped, x_size),
+                unpermute_blocks(product_out, sources, x_size),
+            )
             total = product_out if total is None else total + product_out
     partial_out = total
     tensor_size = lax.axis_size("tensor")

time: 138 us -> 147 us (1.065)
  local copies, waits for them, and re-layouts: 19.8 us -> 26.5 us
  starting transfers between devices: 26.1 us -> 28.4 us
    ppermute x0 -> x2, waiting for transfers between devices: none -> 14.5 us  [the longest x1 10.8 us: exchange_last_pair(): lax.ppermute(stack_b, axis_name, [(i, i ^ mask_b) for i in range(count)])]
    ppermute x2 -> x1, waiting for transfers between devices: 15.5 us -> 3.6 us  [exchange_gather_pair(): lax.ppermute(stack_a, axis_name, [(i, i ^ mask_a) for i in range(count)])]
    ppermute x0 -> x2, starting transfers between devices: none -> 5.64 us  [the longest x1 3.72 us: exchange_last_pair(): lax.ppermute(stack_a, axis_name, [(i, i ^ mask_a) for i in range(count)])]
    unnamed x40 -> x55, local copies, waits for them, and re-layouts: 3.21 us -> 6.48 us
    ppermute x2 -> x1, starting transfers between devices: 6.31 us -> 3.72 us  [exchange_gather_pair(): lax.ppermute(stack_b, axis_name, [(i, i ^ mask_b) for i in range(count)])]
    select_n x2 -> x1, other arithmetic: 2.35 us -> 0.14 us  [exchange_gather_pair(): jnp.where(upper_of(index, side_b), jnp.concatenate([received_b, stack_b],...]
    dot_general x4, local copies, waits for them, and re-layouts: 2.55 us -> 4.42 us  [per_device(): jnp.einsum('rh,nkh->rnk', piece_rows, piece_t, preferred_element_type=jnp...]
    select_n x2 -> x1, other arithmetic: 1.88 us -> 0.14 us  [exchange_gather_pair(): jnp.where(upper_of(index, side_a), jnp.concatenate([received_a, stack_a],...]
  transfers between devices with their start and end apart: 7 -> 7, of which waited for: 5 -> 6; matrix products, arithmetic and copies ran while one was open for 9% -> 10% of each run, Pallas kernels for 0% -> 0%
where the time goes in v16:
time: 147 us; the launch traced here: 144 us
  blocking collectives  39.1 us (27%)
  waiting for transfers between devices  37.1 us (25%)
  starting transfers between devices  28.4 us (19%)
  local copies, waits for them, and re-layouts  26.5 us (18%)
  other arithmetic  8.01 us (5%)
  matrix products  4.06 us (3%)
    all_to_all x1, blocking collectives, per_device(): pieces = lax.all_to_all(pieces, 'tensor', 1, 1, tiled=True)  39.1 us
    ppermute x2, waiting for transfers between devices, exchange_gather(): lax.ppermute(stack, axis_name, [(i, i ^ mask) for i in range(count)])  15.2 us
    ppermute x1, waiting for transfers between devices, exchange_last_pair(): lax.ppermute(stack_b, axis_name, [(i, i ^ mask_b) for i in range(count)])  10.8 us
    ppermute x2, starting transfers between devices, exchange_gather(): lax.ppermute(stack, axis_name, [(i, i ^ mask) for i in range(count)])  9.68 us
    unnamed x55, local copies, waits for them, and re-layouts  6.48 us
    ppermute x1, starting transfers between devices, per_device(): lax.ppermute(mine_weights, 'dp', [(i, i ^ 1) for i in range(dp_size)])  6.21 us
    slice x6, local copies, waits for them, and re-layouts, unpermute_blocks(): product[:, :, i:i + 1]  4.63 us
    dot_general x4, local copies, waits for them, and re-layouts, per_device(): jnp.einsum('rh,nkh->rnk', piece_rows, piece_t, preferred_element_type=jnp...  4.42 us
  transfers between devices with their start and end apart: 7, of which 6 were waited for; matrix products, arithmetic and copies ran while one was open for 10% of the time, Pallas kernels for 0%

profile of v16, /device:TPU:1, one launch (start us, length us, event | category | flops | bytes accessed | tf_op | source)
XLA Modules:
  0.0 143.9 jit_solution(16968674790343506459)
XLA Ops:
  0.0 0.9 dynamic-slice_bitcast_fusion.1
  1.2 0.8 maximum_bitcast_fusion
  2.0 5.0 %collective-permute-start = (bf16[128,1,768]{2,0,1:T(8,128)(2,1)S(1)}, bf16[128,1,768]{2,0,1:T(8,128)(2,1)S(1)}, u32[]{:S(2)}, u32[]{:S(2)}) collective-permute-start(bf16[128,1,768]{2,0,1:T(8,128)(2,1)S(1)} %maximum_bitcast_fusion), channel_id=1, source_target_pairs={{0,64},{8,72},{16,80},{24,88},{32,96},{40,104},{48,112},{56,120},{... | collective-permute-start | bytes 589832 | tf_op jit(solution)/shard_map/ppermute | solution.py:51
  7.1 7.2 %collective-permute-done = bf16[128,1,768]{2,0,1:T(8,128)(2,1)S(1)} collective-permute-done((bf16[128,1,768]{2,0,1:T(8,128)(2,1)S(1)}, bf16[128,1,768]{2,0,1:T(8,128)(2,1)S(1)}, u32[]{:S(2)}, u32[]{:S(2)}) %collective-permute-start) | collective-permute-done | bytes 196640 | tf_op jit(solution)/shard_map/ppermute | solution.py:51
  14.4 4.6 %collective-permute-start.1 = (bf16[128,2,768]{2,0,1:T(8,128)(2,1)S(1)}, bf16[128,2,768]{2,0,1:T(8,128)(2,1)S(1)}, u32[]{:S(2)}, u32[]{:S(2)}) collective-permute-start(bf16[128,2,768]{2,0,1:T(8,128)(2,1)S(1)} %maximum_select_fusion.5), channel_id=1, source_target_pairs={{0,32},{8,40},{16,48},{24,56},{32,0},{40,8},{48,16},{56,24},{64,96... | collective-permute-start | bytes 1179656 | tf_op jit(solution)/shard_map/ppermute | solution.py:51
  19.0 7.9 %collective-permute-done.1 = bf16[128,2,768]{2,0,1:T(8,128)(2,1)S(1)} collective-permute-done((bf16[128,2,768]{2,0,1:T(8,128)(2,1)S(1)}, bf16[128,2,768]{2,0,1:T(8,128)(2,1)S(1)}, u32[]{:S(2)}, u32[]{:S(2)}) %collective-permute-start.1) | collective-permute-done | bytes 393248 | tf_op jit(solution)/shard_map/ppermute | solution.py:51
  27.2 3.1 %collective-permute-start.2 = (bf16[128,4,384]{2,0,1:T(8,128)(2,1)S(1)}, bf16[128,4,384]{2,0,1:T(8,128)(2,1)S(1)}, u32[]{:S(2)}, u32[]{:S(2)}) collective-permute-start(bf16[128,4,384]{2,0,1:T(8,128)(2,1)S(1)} %get-tuple-element.62), channel_id=1, source_target_pairs={{0,8},{8,0},{16,24},{24,16},{32,40},{40,32},{48,56},{56,48},{64,72... | collective-permute-start | bytes 1179656 | tf_op jit(solution)/shard_map/ppermute | solution.py:84
  30.3 3.7 %collective-permute-start.3 = (bf16[128,4,384]{2,0,1:T(8,128)(2,1)S(1)}, bf16[128,4,384]{2,0,1:T(8,128)(2,1)S(1)}, u32[]{:S(2)}, u32[]{:S(2)}) collective-permute-start(bf16[128,4,384]{2,0,1:T(8,128)(2,1)S(1)} %get-tuple-element.61), channel_id=1, source_target_pairs={{0,24},{8,16},{16,8},{24,0},{32,56},{40,48},{48,40},{56,32},{64,88... | collective-permute-start | bytes 1179656 | tf_op jit(solution)/shard_map/ppermute | solution.py:85
  34.1 3.6 %collective-permute-done.2 = bf16[128,4,384]{2,0,1:T(8,128)(2,1)S(1)} collective-permute-done((bf16[128,4,384]{2,0,1:T(8,128)(2,1)S(1)}, bf16[128,4,384]{2,0,1:T(8,128)(2,1)S(1)}, u32[]{:S(2)}, u32[]{:S(2)}) %collective-permute-start.2) | collective-permute-done | bytes 393248 | tf_op jit(solution)/shard_map/ppermute | solution.py:84
  37.8 3.9 %collective-permute-done.3 = bf16[128,4,384]{2,0,1:T(8,128)(2,1)S(1)} collective-permute-done((bf16[128,4,384]{2,0,1:T(8,128)(2,1)S(1)}, bf16[128,4,384]{2,0,1:T(8,128)(2,1)S(1)}, u32[]{:S(2)}, u32[]{:S(2)}) %collective-permute-start.3) | collective-permute-done | bytes 393248 | tf_op jit(solution)/shard_map/ppermute | solution.py:85
  41.8 1.9 %collective-permute-start.5 = (bf16[128,8,384]{2,0,1:T(8,128)(2,1)S(1)}, bf16[128,8,384]{2,0,1:T(8,128)(2,1)S(1)}, u32[]{:S(2)}, u32[]{:S(2)}) collective-permute-start(bf16[128,8,384]{2,0,1:T(8,128)(2,1)S(1)} %maximum_select_fusion.4), channel_id=1, source_target_pairs={{0,8},{8,0},{16,24},{24,16},{32,40},{40,32},{48,56},{56,48},{64,72... | collective-permute-start | bytes 2359304 | tf_op jit(solution)/shard_map/ppermute | solution.py:104
  44.8 3.7 %collective-permute-start.4 = (bf16[128,8,384]{2,0,1:T(8,128)(2,1)S(1)}, bf16[128,8,384]{2,0,1:T(8,128)(2,1)S(1)}, u32[]{:S(2)}, u32[]{:S(2)}) collective-permute-start(bf16[128,8,384]{2,0,1:T(8,128)(2,1)S(1)} %maximum_select_fusion.3), channel_id=1, source_target_pairs={{0,24},{8,16},{16,8},{24,0},{32,56},{40,48},{48,40},{56,32},{64,88... | collective-permute-start | bytes 2359304 | tf_op jit(solution)/shard_map/ppermute | solution.py:103
  48.8 10.8 %collective-permute-done.5 = bf16[128,8,384]{2,0,1:T(8,128)(2,1)S(1)} collective-permute-done((bf16[128,8,384]{2,0,1:T(8,128)(2,1)S(1)}, bf16[128,8,384]{2,0,1:T(8,128)(2,1)S(1)}, u32[]{:S(2)}, u32[]{:S(2)}) %collective-permute-start.5) | collective-permute-done | bytes 786464 | tf_op jit(solution)/shard_map/ppermute | solution.py:104
  60.1 3.7 %collective-permute-done.4 = bf16[128,8,384]{2,0,1:T(8,128)(2,1)S(1)} collective-permute-done((bf16[128,8,384]{2,0,1:T(8,128)(2,1)S(1)}, bf16[128,8,384]{2,0,1:T(8,128)(2,1)S(1)}, u32[]{:S(2)}, u32[]{:S(2)}) %collective-permute-start.4) | collective-permute-done | bytes 786464 | tf_op jit(solution)/shard_map/ppermute | solution.py:103
  64.1 1.5 %pad_maximum_fusion = bf16[256,16,256]{2,0,1:T(8,128)(2,1)} fusion(bf16[128,16,256]{2,0,1:T(8,128)(2,1)S(1)} %get-tuple-element.60, bf16[128,16,256]{2,0,1:T(8,128)(2,1)S(1)} %get-tuple-element.58), kind=kLoop, calls=%fused_computation.33 | loop fusion | flops 4194304 | bytes 4194304 | tf_op jit(solution)/shard_map/concatenate | solution.py:175
  65.6 6.2 %collective-permute-start.6 = (bf16[256,16,256]{2,0,1:T(8,128)(2,1)}, bf16[256,16,256]{2,0,1:T(8,128)(2,1)}, u32[]{:S(2)}, u32[]{:S(2)}) collective-permute-start(bf16[256,16,256]{2,0,1:T(8,128)(2,1)} %pad_maximum_fusion), channel_id=1, source_target_pairs={{0,128},{128,0},{256,384},{384,256},{1,129},{129,1},{257,385},{385... | collective-permute-start | bytes 6291464 | tf_op jit(solution)/shard_map/ppermute | solution.py:178
  72.7 1.3 fusion.1
  74.0 1.6 %fusion.18 = bf16[512,128]{1,0:T(8,128)(2,1)S(1)} fusion(bf16[2048,128]{1,0:T(8,128)(2,1)S(1)} %bitcast.93, f32[2048,512]{1,0:T(8,128)S(1)} %get-tuple-element.68, f32[512]{0:T(512)S(1)} %broadcast_maximum_fusion, s32[512]{0:T(512)S(1)} %broadcast_bitcast_fusion, s32[2048]{0:T(1024)S(1)} %bitcast.101, f32[512]{0:T(512)S(1)} %fusion.1), kind=kOutput, calls=%fused_computation.42 | convolution fusion | flops 274857984 | bytes 4864000 | tf_op jit(solution)/shard_map/grk,kgd->grd/dot_general | solution.py:208
  75.8 1.2 dot_general.32
  77.9 1.2 fusion.26
  80.9 1.4 %fusion.48 = (f32[128,4,1,256]{3,0,2,1:T(8,128)}, f32[128,4,1,256]{3,0,2,1:T(8,128)}, f32[128,4,1,256]{3,0,2,1:T(8,128)}, f32[128,4,1,256]{3,0,2,1:T(8,128)}) fusion(f32[128,4,4,256]{3,0,2,1:T(8,128)S(1)} %fusion.34), kind=kLoop, calls=%fused_computation.92 | loop fusion | bytes 4194304 | tf_op jit(solution)/shard_map/slice | solution.py:77
  82.4 1.4 fusion.54
  83.8 1.4 fusion.51
  85.1 3.1 %slice_bitcast_fusion.1 = (bf16[16,128,256]{2,1,0:T(8,128)(2,1)}, bf16[16,128,256]{2,1,0:T(8,128)(2,1)}) fusion(bf16[256,16,256]{2,0,1:T(8,128)(2,1)} %collective-permute-done.6), kind=kLoop, calls=%fused_computation.44 | loop fusion | bytes 4194304 | tf_op jit(solution)/shard_map/transpose | solution.py:226
  88.2 1.4 dot_general.34
  90.1 1.4 fusion.56
  91.5 1.5 %fusion.57 = (f32[128,2,4,256]{3,0,2,1:T(8,128)}, f32[128,2,4,256]{3,0,2,1:T(8,128)}) fusion(f32[128,4,4,256]{3,0,2,1:T(8,128)S(1)} %fusion.28), kind=kLoop, calls=%fused_computation.101 | loop fusion | bytes 4194304 | tf_op jit(solution)/shard_map/slice | solution.py:75
  92.9 1.4 dot_general.30
  95.1 1.1 copy-done.4
  96.8 1.1 copy-done.3
  101.6 1.6 %fusion.21 = bf16[128,4,4,256]{3,0,1,2:T(8,128)(2,1)S(1)} fusion(f32[128,4,1,256]{3,0,2,1:T(8,128)S(1)} %get-tuple-element.54, f32[128,4,1,256]{3,0,2,1:T(8,128)S(1)} %get-tuple-element.55, f32[128,4,1,256]{3,0,2,1:T(8,128)S(1)} %get-tuple-element.56, f32[128,4,1,256]{3,0,2,1:T(8,128)S(1)} %get-tuple-element.53, ...), kind=kLoop, calls=%fused_computation.45 | loop fusion | flops 20447232 | bytes 20971522 | tf_op jit(solution)/shard_map/convert.1
  103.9 39.1 %all_to_all.5 = bf16[128,8,512]{0,2,1:T(8,128)(2,1)S(1)} all-to-all(bf16[128,8,512]{0,2,1:T(8,128)(2,1)S(1)} %bitcast.86), channel_id=1, replica_groups=mesh['dp'=4,'context'=16,'tensor'=8] {'tensor'}, dimensions={1} | all-to-all | bytes 2097152 | tf_op jit(solution)/shard_map/all_to_all | solution.py:243
  (104 shorter events, 13.4 us)
Async XLA Ops:
  0.0 44.1 %copy-start = (s32[2048]{0:T(1024)S(1)}, s32[2048]{0:T(1024)}, u32[]{:S(2)}) copy-start(s32[2048]{0:T(1024)} %param.9) | copy-start | bytes 24580
  2.0 12.3 %collective-permute-start = (bf16[128,1,768]{2,0,1:T(8,128)(2,1)S(1)}, bf16[128,1,768]{2,0,1:T(8,128)(2,1)S(1)}, u32[]{:S(2)}, u32[]{:S(2)}) collective-permute-start(bf16[128,1,768]{2,0,1:T(8,128)(2,1)S(1)} %maximum_bitcast_fusion), channel_id=1, source_target_pairs={{0,64},{8,72},{16,80},{24,88},{32,96},{40,104},{48,112},{56,120},{... | collective-permute-start | bytes 589832 | tf_op jit(solution)/shard_map/ppermute | solution.py:51
  14.4 12.6 %collective-permute-start.1 = (bf16[128,2,768]{2,0,1:T(8,128)(2,1)S(1)}, bf16[128,2,768]{2,0,1:T(8,128)(2,1)S(1)}, u32[]{:S(2)}, u32[]{:S(2)}) collective-permute-start(bf16[128,2,768]{2,0,1:T(8,128)(2,1)S(1)} %maximum_select_fusion.5), channel_id=1, source_target_pairs={{0,32},{8,40},{16,48},{24,56},{32,0},{40,8},{48,16},{56,24},{64,96... | collective-permute-start | bytes 1179656 | tf_op jit(solution)/shard_map/ppermute | solution.py:51
  27.1 16.7 %copy-start.24 = (bf16[128,512]{1,0:T(8,128)(2,1)S(1)}, bf16[128,512]{1,0:T(8,128)(2,1)}, u32[]{:S(2)}) copy-start(bf16[128,512]{1,0:T(8,128)(2,1)} %param.6) | copy-start | bytes 393220
  27.2 17.0 %copy-start.25 = (s32[16]{0:T(128)S(1)}, s32[16]{0:T(128)}, u32[]{:S(2)}) copy-start(s32[16]{0:T(128)} %constant.64) | copy-start | bytes 196
  27.2 10.5 %collective-permute-start.2 = (bf16[128,4,384]{2,0,1:T(8,128)(2,1)S(1)}, bf16[128,4,384]{2,0,1:T(8,128)(2,1)S(1)}, u32[]{:S(2)}, u32[]{:S(2)}) collective-permute-start(bf16[128,4,384]{2,0,1:T(8,128)(2,1)S(1)} %get-tuple-element.62), channel_id=1, source_target_pairs={{0,8},{8,0},{16,24},{24,16},{32,40},{40,32},{48,56},{56,48},{64,72... | collective-permute-start | bytes 1179656 | tf_op jit(solution)/shard_map/ppermute | solution.py:84
  30.3 11.4 %collective-permute-start.3 = (bf16[128,4,384]{2,0,1:T(8,128)(2,1)S(1)}, bf16[128,4,384]{2,0,1:T(8,128)(2,1)S(1)}, u32[]{:S(2)}, u32[]{:S(2)}) collective-permute-start(bf16[128,4,384]{2,0,1:T(8,128)(2,1)S(1)} %get-tuple-element.61), channel_id=1, source_target_pairs={{0,24},{8,16},{16,8},{24,0},{32,56},{40,48},{48,40},{56,32},{64,88... | collective-permute-start | bytes 1179656 | tf_op jit(solution)/shard_map/ppermute | solution.py:85
  41.8 17.7 %collective-permute-start.5 = (bf16[128,8,384]{2,0,1:T(8,128)(2,1)S(1)}, bf16[128,8,384]{2,0,1:T(8,128)(2,1)S(1)}, u32[]{:S(2)}, u32[]{:S(2)}) collective-permute-start(bf16[128,8,384]{2,0,1:T(8,128)(2,1)S(1)} %maximum_select_fusion.4), channel_id=1, source_target_pairs={{0,8},{8,0},{16,24},{24,16},{32,40},{40,32},{48,56},{56,48},{64,72... | collective-permute-start | bytes 2359304 | tf_op jit(solution)/shard_map/ppermute | solution.py:104
  44.8 18.9 %collective-permute-start.4 = (bf16[128,8,384]{2,0,1:T(8,128)(2,1)S(1)}, bf16[128,8,384]{2,0,1:T(8,128)(2,1)S(1)}, u32[]{:S(2)}, u32[]{:S(2)}) collective-permute-start(bf16[128,8,384]{2,0,1:T(8,128)(2,1)S(1)} %maximum_select_fusion.3), channel_id=1, source_target_pairs={{0,24},{8,16},{16,8},{24,0},{32,56},{40,48},{48,40},{56,32},{64,88... | collective-permute-start | bytes 2359304 | tf_op jit(solution)/shard_map/ppermute | solution.py:103
  65.6 19.6 %collective-permute-start.6 = (bf16[256,16,256]{2,0,1:T(8,128)(2,1)}, bf16[256,16,256]{2,0,1:T(8,128)(2,1)}, u32[]{:S(2)}, u32[]{:S(2)}) collective-permute-start(bf16[256,16,256]{2,0,1:T(8,128)(2,1)} %pad_maximum_fusion), channel_id=1, source_target_pairs={{0,128},{128,0},{256,384},{384,256},{1,129},{129,1},{257,385},{385... | collective-permute-start | bytes 6291464 | tf_op jit(solution)/shard_map/ppermute | solution.py:178
  77.9 1.8 %copy-start.2 = (bf16[4,4,256,128]{3,2,1,0:T(8,128)(2,1)S(1)}, bf16[4,4,256,128]{3,2,1,0:T(8,128)(2,1)}, u32[]{:S(2)}) copy-start(bf16[4,4,256,128]{3,2,1,0:T(8,128)(2,1)} %dot_general.32) | copy-start | bytes 3145732
  95.0 1.2 copy-start.4
  95.0 1.3 copy-start.7
  95.0 1.5 %copy-start.8 = (f32[128,1,4,256]{3,0,2,1:T(8,128)S(1)}, f32[128,1,4,256]{3,0,2,1:T(8,128)}, u32[]{:S(2)}) copy-start(f32[128,1,4,256]{3,0,2,1:T(8,128)} %get-tuple-element.49) | copy-start | bytes 1572868
  96.6 1.2 copy-start.3
  96.6 1.3 copy-start.5
  96.6 1.5 %copy-start.6 = (f32[128,1,4,256]{3,0,2,1:T(8,128)S(1)}, f32[128,1,4,256]{3,0,2,1:T(8,128)}, u32[]{:S(2)}) copy-start(f32[128,1,4,256]{3,0,2,1:T(8,128)} %get-tuple-element.50) | copy-start | bytes 1572868
  98.3 1.2 copy-start.17
  98.3 1.3 copy-start.18
  98.3 1.5 %copy-start.19 = (f32[128,4,1,256]{3,0,2,1:T(8,128)S(1)}, f32[128,4,1,256]{3,0,2,1:T(8,128)}, u32[]{:S(2)}) copy-start(f32[128,4,1,256]{3,0,2,1:T(8,128)} %get-tuple-element.42) | copy-start | bytes 1572868
  98.3 1.6 %copy-start.20 = (f32[128,4,1,256]{3,0,2,1:T(8,128)S(1)}, f32[128,4,1,256]{3,0,2,1:T(8,128)}, u32[]{:S(2)}) copy-start(f32[128,4,1,256]{3,0,2,1:T(8,128)} %get-tuple-element.29) | copy-start | bytes 1572868
  98.3 1.8 %copy-start.21 = (f32[128,4,1,256]{3,0,2,1:T(8,128)S(1)}, f32[128,4,1,256]{3,0,2,1:T(8,128)}, u32[]{:S(2)}) copy-start(f32[128,4,1,256]{3,0,2,1:T(8,128)} %get-tuple-element.30) | copy-start | bytes 1572868
  98.4 1.9 %copy-start.22 = (f32[128,4,1,256]{3,0,2,1:T(8,128)S(1)}, f32[128,4,1,256]{3,0,2,1:T(8,128)}, u32[]{:S(2)}) copy-start(f32[128,4,1,256]{3,0,2,1:T(8,128)} %get-tuple-element.31) | copy-start | bytes 1572868
  98.4 2.1 %copy-start.23 = (f32[128,4,1,256]{3,0,2,1:T(8,128)S(1)}, f32[128,4,1,256]{3,0,2,1:T(8,128)}, u32[]{:S(2)}) copy-start(f32[128,4,1,256]{3,0,2,1:T(8,128)} %get-tuple-element.32) | copy-start | bytes 1572868
  98.5 2.1 %copy-start.9 = (f32[128,4,1,256]{3,0,2,1:T(8,128)S(1)}, f32[128,4,1,256]{3,0,2,1:T(8,128)}, u32[]{:S(2)}) copy-start(f32[128,4,1,256]{3,0,2,1:T(8,128)} %get-tuple-element.9) | copy-start | bytes 1572868
  98.5 2.3 %copy-start.10 = (f32[128,4,1,256]{3,0,2,1:T(8,128)S(1)}, f32[128,4,1,256]{3,0,2,1:T(8,128)}, u32[]{:S(2)}) copy-start(f32[128,4,1,256]{3,0,2,1:T(8,128)} %get-tuple-element.10) | copy-start | bytes 1572868
  98.5 2.4 %copy-start.11 = (f32[128,4,1,256]{3,0,2,1:T(8,128)S(1)}, f32[128,4,1,256]{3,0,2,1:T(8,128)}, u32[]{:S(2)}) copy-start(f32[128,4,1,256]{3,0,2,1:T(8,128)} %get-tuple-element.11) | copy-start | bytes 1572868
  98.5 2.6 %copy-start.12 = (f32[128,4,1,256]{3,0,2,1:T(8,128)S(1)}, f32[128,4,1,256]{3,0,2,1:T(8,128)}, u32[]{:S(2)}) copy-start(f32[128,4,1,256]{3,0,2,1:T(8,128)} %get-tuple-element.14) | copy-start | bytes 1572868
  98.6 2.7 %copy-start.13 = (f32[128,4,1,256]{3,0,2,1:T(8,128)S(1)}, f32[128,4,1,256]{3,0,2,1:T(8,128)}, u32[]{:S(2)}) copy-start(f32[128,4,1,256]{3,0,2,1:T(8,128)} %get-tuple-element.15) | copy-start | bytes 1572868
  98.6 2.9 %copy-start.14 = (f32[128,4,1,256]{3,0,2,1:T(8,128)S(1)}, f32[128,4,1,256]{3,0,2,1:T(8,128)}, u32[]{:S(2)}) copy-start(f32[128,4,1,256]{3,0,2,1:T(8,128)} %get-tuple-element.16) | copy-start | bytes 1572868
  98.6 3.0 %copy-start.15 = (f32[128,4,1,256]{3,0,2,1:T(8,128)S(1)}, f32[128,4,1,256]{3,0,2,1:T(8,128)}, u32[]{:S(2)}) copy-start(f32[128,4,1,256]{3,0,2,1:T(8,128)} %get-tuple-element.17) | copy-start | bytes 1572868
  103.2 40.7 %copy-start.1 = (s32[2048]{0:T(1024)S(1)}, s32[2048]{0:T(1024)}, u32[]{:S(2)}) copy-start(s32[2048]{0:T(1024)} %param.9) | copy-start | bytes 24580
  (1 other events, 1.0 us)

commit v17 on v10

--- a/solution.py
+++ b/solution.py
@@ -80,7 +80,7 @@
 
 def exchange_gather_pair(stack_a, steps_a, stack_b, steps_b, axis_name, count):
     index = lax.axis_index(axis_name)
-    for (mask_a, side_a), (mask_b, side_b) in zip(steps_a, steps_b):
+    for step, ((mask_a, side_a), (mask_b, side_b)) in enumerate(zip(steps_a, steps_b)):
         received_a = lax.ppermute(stack_a, axis_name, [(i, i ^ mask_a) for i in range(count)])
         received_b = lax.ppermute(stack_b, axis_name, [(i, i ^ mask_b) for i in range(count)])
         stack_a = jnp.where(
@@ -93,7 +93,8 @@
             jnp.concatenate([received_b, stack_b], 1),
             jnp.concatenate([stack_b, received_b], 1),
         )
-        stack_a, stack_b = lax.optimization_barrier((stack_a, stack_b))
+        if step + 1 < len(steps_a):
+            stack_a, stack_b = lax.optimization_barrier((stack_a, stack_b))
     return stack_a, stack_b
 
 

time: 138 us -> 139 us (level)
  the two profiles are of different devices: /device:TPU:1 before, /device:TPU:17 now
where the time goes in v17:
time: 139 us; the launch traced here: 138 us
  blocking collectives  39.1 us (28%)
  waiting for transfers between devices  38.8 us (28%)
  starting transfers between devices  25.4 us (18%)
  local copies, waits for them, and re-layouts  19.5 us (14%)
  other arithmetic  9.72 us (7%)
  matrix products  5.4 us (4%)
    all_to_all x1, blocking collectives, per_device(): pieces = lax.all_to_all(pieces, 'tensor', 1, 1, tiled=True)  39.1 us
    ppermute x2, waiting for transfers between devices, exchange_gather_pair(): lax.ppermute(stack_a, axis_name, [(i, i ^ mask_a) for i in range(count)])  16.6 us
    ppermute x2, waiting for transfers between devices, exchange_gather(): lax.ppermute(stack, axis_name, [(i, i ^ mask) for i in range(count)])  15.8 us
    ppermute x2, starting transfers between devices, exchange_gather(): lax.ppermute(stack, axis_name, [(i, i ^ mask) for i in range(count)])  10.1 us
    ppermute x2, waiting for transfers between devices, exchange_gather_pair(): lax.ppermute(stack_b, axis_name, [(i, i ^ mask_b) for i in range(count)])  6.38 us
    ppermute x2, starting transfers between devices, exchange_gather_pair(): lax.ppermute(stack_b, axis_name, [(i, i ^ mask_b) for i in range(count)])  6.3 us
    unnamed x32, local copies, waits for them, and re-layouts  5.15 us
    ppermute x1, starting transfers between devices, per_device(): lax.ppermute(mine_weights, 'dp', [(i, i ^ 1) for i in range(dp_size)])  4.97 us
  transfers between devices with their start and end apart: 7, of which 5 were waited for; matrix products, arithmetic and copies ran while one was open for 9% of the time, Pallas kernels for 0%

profile of v17, /device:TPU:17, one launch (start us, length us, event | category | flops | bytes accessed | tf_op | source)
XLA Modules:
  0.0 138.4 jit_solution(2264789847242793360)
XLA Ops:
  0.0 0.9 dynamic-slice_bitcast_fusion.1
  1.2 0.8 maximum_bitcast_fusion
  2.0 1.9 %collective-permute-start = (bf16[128,1,768]{2,0,1:T(8,128)(2,1)S(1)}, bf16[128,1,768]{2,0,1:T(8,128)(2,1)S(1)}, u32[]{:S(2)}, u32[]{:S(2)}) collective-permute-start(bf16[128,1,768]{2,0,1:T(8,128)(2,1)S(1)} %maximum_bitcast_fusion), channel_id=1, source_target_pairs={{0,64},{8,72},{16,80},{24,88},{32,96},{40,104},{48,112},{56,120},{... | collective-permute-start | bytes 589832 | tf_op jit(solution)/shard_map/ppermute | solution.py:51
  4.0 6.8 %collective-permute-done = bf16[128,1,768]{2,0,1:T(8,128)(2,1)S(1)} collective-permute-done((bf16[128,1,768]{2,0,1:T(8,128)(2,1)S(1)}, bf16[128,1,768]{2,0,1:T(8,128)(2,1)S(1)}, u32[]{:S(2)}, u32[]{:S(2)}) %collective-permute-start) | collective-permute-done | bytes 196640 | tf_op jit(solution)/shard_map/ppermute | solution.py:51
  10.8 8.2 %collective-permute-start.1 = (bf16[128,2,768]{2,0,1:T(8,128)(2,1)S(1)}, bf16[128,2,768]{2,0,1:T(8,128)(2,1)S(1)}, u32[]{:S(2)}, u32[]{:S(2)}) collective-permute-start(bf16[128,2,768]{2,0,1:T(8,128)(2,1)S(1)} %maximum_select_fusion.5), channel_id=1, source_target_pairs={{0,32},{8,40},{16,48},{24,56},{32,0},{40,8},{48,16},{56,24},{64,96... | collective-permute-start | bytes 1179656 | tf_op jit(solution)/shard_map/ppermute | solution.py:51
  19.0 9.0 %collective-permute-done.1 = bf16[128,2,768]{2,0,1:T(8,128)(2,1)S(1)} collective-permute-done((bf16[128,2,768]{2,0,1:T(8,128)(2,1)S(1)}, bf16[128,2,768]{2,0,1:T(8,128)(2,1)S(1)}, u32[]{:S(2)}, u32[]{:S(2)}) %collective-permute-start.1) | collective-permute-done | bytes 393248 | tf_op jit(solution)/shard_map/ppermute | solution.py:51
  28.2 4.4 %collective-permute-start.3 = (bf16[128,4,384]{2,0,1:T(8,128)(2,1)S(1)}, bf16[128,4,384]{2,0,1:T(8,128)(2,1)S(1)}, u32[]{:S(2)}, u32[]{:S(2)}) collective-permute-start(bf16[128,4,384]{2,0,1:T(8,128)(2,1)S(1)} %get-tuple-element.35), channel_id=1, source_target_pairs={{0,24},{8,16},{16,8},{24,0},{32,56},{40,48},{48,40},{56,32},{64,88... | collective-permute-start | bytes 1179656 | tf_op jit(solution)/shard_map/ppermute | solution.py:85
  32.6 1.9 %collective-permute-start.2 = (bf16[128,4,384]{2,0,1:T(8,128)(2,1)S(1)}, bf16[128,4,384]{2,0,1:T(8,128)(2,1)S(1)}, u32[]{:S(2)}, u32[]{:S(2)}) collective-permute-start(bf16[128,4,384]{2,0,1:T(8,128)(2,1)S(1)} %get-tuple-element.36), channel_id=1, source_target_pairs={{0,8},{8,0},{16,24},{24,16},{32,40},{40,32},{48,56},{56,48},{64,72... | collective-permute-start | bytes 1179656 | tf_op jit(solution)/shard_map/ppermute | solution.py:84
  34.6 6.4 %collective-permute-done.3 = bf16[128,4,384]{2,0,1:T(8,128)(2,1)S(1)} collective-permute-done((bf16[128,4,384]{2,0,1:T(8,128)(2,1)S(1)}, bf16[128,4,384]{2,0,1:T(8,128)(2,1)S(1)}, u32[]{:S(2)}, u32[]{:S(2)}) %collective-permute-start.3) | collective-permute-done | bytes 393248 | tf_op jit(solution)/shard_map/ppermute | solution.py:85
  41.1 2.8 %collective-permute-done.2 = bf16[128,4,384]{2,0,1:T(8,128)(2,1)S(1)} collective-permute-done((bf16[128,4,384]{2,0,1:T(8,128)(2,1)S(1)}, bf16[128,4,384]{2,0,1:T(8,128)(2,1)S(1)}, u32[]{:S(2)}, u32[]{:S(2)}) %collective-permute-start.2) | collective-permute-done | bytes 393248 | tf_op jit(solution)/shard_map/ppermute | solution.py:84
  44.0 2.1 %collective-permute-start.4 = (bf16[128,8,384]{2,0,1:T(8,128)(2,1)S(1)}, bf16[128,8,384]{2,0,1:T(8,128)(2,1)}, u32[]{:S(2)}, u32[]{:S(2)}) collective-permute-start(bf16[128,8,384]{2,0,1:T(8,128)(2,1)S(1)} %maximum_select_fusion.3), channel_id=1, source_target_pairs={{0,24},{8,16},{16,8},{24,0},{32,56},{40,48},{48,40},{56,32},{64,88... | collective-permute-start | bytes 2359304 | tf_op jit(solution)/shard_map/ppermute | solution.py:84
  46.3 0.8 copy.21
  47.1 1.9 %collective-permute-start.5 = (bf16[128,8,384]{2,0,1:T(8,128)(2,1)S(1)}, bf16[128,8,384]{2,0,1:T(8,128)(2,1)}, u32[]{:S(2)}, u32[]{:S(2)}) collective-permute-start(bf16[128,8,384]{2,0,1:T(8,128)(2,1)S(1)} %maximum_select_fusion.4), channel_id=1, source_target_pairs={{0,8},{8,0},{16,24},{24,16},{32,40},{40,32},{48,56},{56,48},{64,72... | collective-permute-start | bytes 2359304 | tf_op jit(solution)/shard_map/ppermute | solution.py:85
  50.2 13.9 %collective-permute-done.4 = bf16[128,8,384]{2,0,1:T(8,128)(2,1)} collective-permute-done((bf16[128,8,384]{2,0,1:T(8,128)(2,1)S(1)}, bf16[128,8,384]{2,0,1:T(8,128)(2,1)}, u32[]{:S(2)}, u32[]{:S(2)}) %collective-permute-start.4) | collective-permute-done | bytes 786464 | tf_op jit(solution)/shard_map/ppermute | solution.py:84
  64.1 1.7 %maximum_select_fusion = bf16[128,16,384]{2,0,1:T(8,128)(2,1)S(1)} fusion(bf16[128,8,384]{2,0,1:T(8,128)(2,1)S(1)} %maximum_select_fusion.3, bf16[128,8,384]{2,0,1:T(8,128)(2,1)} %collective-permute-done.4, pred[]{:T(512)S(6)} %ne.22), kind=kLoop, calls=%fused_computation.14 | loop fusion | flops 2359296 | bytes 3145729 | tf_op jit(solution)/shard_map/jit(_where)/select_n | solution.py:86
  65.8 1.3 slice_bitcast_fusion.3
  67.3 1.6 %maximum_select_fusion.1 = bf16[128,16,384]{2,0,1:T(8,128)(2,1)S(1)} fusion(bf16[128,8,384]{2,0,1:T(8,128)(2,1)S(1)} %maximum_select_fusion.4, bf16[128,8,384]{2,0,1:T(8,128)(2,1)} %collective-permute-done.5, pred[]{:T(512)S(6)} %ne.27), kind=kLoop, calls=%fused_computation.15 | loop fusion | flops 2359296 | bytes 3145729 | tf_op jit(solution)/shard_map/jit(_where)/select_n | solution.py:91
  69.7 1.2 slice_bitcast_fusion.2
  70.9 1.2 dot_general.28
  72.4 0.8 copy-done.6
  73.3 1.4 %pad_maximum_fusion = bf16[256,16,256]{2,0,1:T(8,128)(2,1)S(1)} fusion(bf16[128,16,256]{2,0,1:T(8,128)(2,1)} %get-tuple-element.34, bf16[128,16,256]{2,0,1:T(8,128)(2,1)S(1)} %copy-done.6), kind=kLoop, calls=%fused_computation.10 | loop fusion | flops 4194304 | bytes 4194304 | tf_op jit(solution)/shard_map/concatenate | solution.py:155
  74.8 5.0 %collective-permute-start.6 = (bf16[256,16,256]{2,0,1:T(8,128)(2,1)S(1)}, bf16[256,16,256]{2,0,1:T(8,128)(2,1)S(1)}, u32[]{:S(2)}, u32[]{:S(2)}) collective-permute-start(bf16[256,16,256]{2,0,1:T(8,128)(2,1)S(1)} %pad_maximum_fusion), channel_id=1, source_target_pairs={{0,128},{128,0},{256,384},{384,256},{1,129},{129,1},{257,385},{385... | collective-permute-start | bytes 6291464 | tf_op jit(solution)/shard_map/ppermute | solution.py:158
  80.7 1.3 fusion.1
  82.0 1.6 %fusion.11 = bf16[512,128]{1,0:T(8,128)(2,1)S(1)} fusion(bf16[2048,128]{1,0:T(8,128)(2,1)S(1)} %bitcast.94, f32[2048,512]{1,0:T(8,128)S(1)} %get-tuple-element.42, f32[512]{0:T(512)S(1)} %broadcast_maximum_fusion, s32[512]{0:T(512)S(1)} %copy-done.13, s32[2048]{0:T(1024)S(1)} %bitcast.101, f32[512]{0:T(512)S(1)} %fusion.1), kind=kOutput, calls=%fused_computation.17 | convolution fusion | flops 274857984 | bytes 4864000 | tf_op jit(solution)/shard_map/grk,kgd->grd/dot_general | solution.py:187
  84.4 1.5 %pad_maximum_fusion.1 = f32[128,4,4,256]{3,0,2,1:T(8,128)} fusion(f32[128,1,4,256]{3,0,2,1:T(8,128)S(1)} %get-tuple-element.24, f32[128,2,4,256]{3,0,2,1:T(8,128)S(1)} %slice.167, f32[128,1,4,256]{3,0,2,1:T(8,128)S(1)} %get-tuple-element.23), kind=kLoop, calls=%fused_computation.11 | loop fusion | flops 1048576 | bytes 4194304 | tf_op jit(solution)/shard_map/concatenate | solution.py:75
  85.9 1.7 %fusion.21 = f32[128,4,4,256]{3,0,2,1:T(8,128)} fusion(bf16[4,4,256,128]{3,2,1,0:T(8,128)(2,1)S(1)} %copy-done.5, bf16[128,512]{1,0:T(8,128)(2,1)S(1)} %bitcast.91, s32[]{:T(128)S(6)} %select_n.86), kind=kOutput, calls=%fused_computation.36 | convolution fusion | flops 134217728 | bytes 3178500 | tf_op jit(solution)/shard_map/rh,nkh->rnk/dot_general | solution.py:208
  87.7 1.1 slice_bitcast_fusion.1
  89.6 1.1 fusion.39
  92.4 1.1 copy-done.3
  95.3 1.4 %copy-done.2 = f32[128,4,4,256]{3,0,2,1:T(8,128)S(1)} copy-done((f32[128,4,4,256]{3,0,2,1:T(8,128)S(1)}, f32[128,4,4,256]{3,0,2,1:T(8,128)}, u32[]{:S(2)}) %copy-start.2) | copy-done | bytes 2097176
  98.4 39.1 %all_to_all.5 = bf16[128,8,512]{0,2,1:T(8,128)(2,1)S(1)} all-to-all(bf16[128,8,512]{0,2,1:T(8,128)(2,1)S(1)} %bitcast.87), channel_id=1, replica_groups=mesh['dp'=4,'context'=16,'tensor'=8] {'tensor'}, dimensions={1} | all-to-all | bytes 2097152 | tf_op jit(solution)/shard_map/all_to_all | solution.py:216
  137.6 0.8 copy.24
  (69 shorter events, 11.3 us)
Async XLA Ops:
  0.0 47.0 %copy-start = (s32[2048]{0:T(1024)S(1)}, s32[2048]{0:T(1024)}, u32[]{:S(2)}) copy-start(s32[2048]{0:T(1024)} %param.9) | copy-start | bytes 24580
  2.0 8.7 %collective-permute-start = (bf16[128,1,768]{2,0,1:T(8,128)(2,1)S(1)}, bf16[128,1,768]{2,0,1:T(8,128)(2,1)S(1)}, u32[]{:S(2)}, u32[]{:S(2)}) collective-permute-start(bf16[128,1,768]{2,0,1:T(8,128)(2,1)S(1)} %maximum_bitcast_fusion), channel_id=1, source_target_pairs={{0,64},{8,72},{16,80},{24,88},{32,96},{40,104},{48,112},{56,120},{... | collective-permute-start | bytes 589832 | tf_op jit(solution)/shard_map/ppermute | solution.py:51
  10.8 17.2 %collective-permute-start.1 = (bf16[128,2,768]{2,0,1:T(8,128)(2,1)S(1)}, bf16[128,2,768]{2,0,1:T(8,128)(2,1)S(1)}, u32[]{:S(2)}, u32[]{:S(2)}) collective-permute-start(bf16[128,2,768]{2,0,1:T(8,128)(2,1)S(1)} %maximum_select_fusion.5), channel_id=1, source_target_pairs={{0,32},{8,40},{16,48},{24,56},{32,0},{40,8},{48,16},{56,24},{64,96... | collective-permute-start | bytes 1179656 | tf_op jit(solution)/shard_map/ppermute | solution.py:51
  28.1 18.0 %copy-start.11 = (bf16[128,512]{1,0:T(8,128)(2,1)S(1)}, bf16[128,512]{1,0:T(8,128)(2,1)}, u32[]{:S(2)}) copy-start(bf16[128,512]{1,0:T(8,128)(2,1)} %param.6) | copy-start | bytes 393220
  28.2 20.8 %copy-start.14 = (s32[16]{0:T(128)S(1)}, s32[16]{0:T(128)}, u32[]{:S(2)}) copy-start(s32[16]{0:T(128)} %constant.64) | copy-start | bytes 196
  28.2 12.7 %collective-permute-start.3 = (bf16[128,4,384]{2,0,1:T(8,128)(2,1)S(1)}, bf16[128,4,384]{2,0,1:T(8,128)(2,1)S(1)}, u32[]{:S(2)}, u32[]{:S(2)}) collective-permute-start(bf16[128,4,384]{2,0,1:T(8,128)(2,1)S(1)} %get-tuple-element.35), channel_id=1, source_target_pairs={{0,24},{8,16},{16,8},{24,0},{32,56},{40,48},{48,40},{56,32},{64,88... | collective-permute-start | bytes 1179656 | tf_op jit(solution)/shard_map/ppermute | solution.py:85
  32.6 11.2 %collective-permute-start.2 = (bf16[128,4,384]{2,0,1:T(8,128)(2,1)S(1)}, bf16[128,4,384]{2,0,1:T(8,128)(2,1)S(1)}, u32[]{:S(2)}, u32[]{:S(2)}) collective-permute-start(bf16[128,4,384]{2,0,1:T(8,128)(2,1)S(1)} %get-tuple-element.36), channel_id=1, source_target_pairs={{0,8},{8,0},{16,24},{24,16},{32,40},{40,32},{48,56},{56,48},{64,72... | collective-permute-start | bytes 1179656 | tf_op jit(solution)/shard_map/ppermute | solution.py:84
  44.0 20.1 %collective-permute-start.4 = (bf16[128,8,384]{2,0,1:T(8,128)(2,1)S(1)}, bf16[128,8,384]{2,0,1:T(8,128)(2,1)}, u32[]{:S(2)}, u32[]{:S(2)}) collective-permute-start(bf16[128,8,384]{2,0,1:T(8,128)(2,1)S(1)} %maximum_select_fusion.3), channel_id=1, source_target_pairs={{0,24},{8,16},{16,8},{24,0},{32,56},{40,48},{48,40},{56,32},{64,88... | collective-permute-start | bytes 2359304 | tf_op jit(solution)/shard_map/ppermute | solution.py:84
  47.1 20.2 %collective-permute-start.5 = (bf16[128,8,384]{2,0,1:T(8,128)(2,1)S(1)}, bf16[128,8,384]{2,0,1:T(8,128)(2,1)}, u32[]{:S(2)}, u32[]{:S(2)}) collective-permute-start(bf16[128,8,384]{2,0,1:T(8,128)(2,1)S(1)} %maximum_select_fusion.4), channel_id=1, source_target_pairs={{0,8},{8,0},{16,24},{24,16},{32,40},{40,32},{48,56},{56,48},{64,72... | collective-permute-start | bytes 2359304 | tf_op jit(solution)/shard_map/ppermute | solution.py:85
  65.8 1.5 %copy-start.4 = (bf16[128,16,384]{2,0,1:T(8,128)(2,1)}, bf16[128,16,384]{2,0,1:T(8,128)(2,1)S(1)}, u32[]{:S(2)}) copy-start(bf16[128,16,384]{2,0,1:T(8,128)(2,1)S(1)} %maximum_select_fusion) | copy-start | bytes 4718596
  72.1 1.2 copy-start.6
  73.3 6.4 %slice-start.1 = ((bf16[128,16,384]{2,0,1:T(8,128)(2,1)}), bf16[128,16,128]{2,0,1:T(8,128)(2,1)S(1)}, s32[]{:S(2)}) async-start(bf16[128,16,384]{2,0,1:T(8,128)(2,1)} %copy-done.4), calls=%async_computation.2 | async-start | bytes 1048576 | tf_op jit(solution)/shard_map/slice | solution.py:160
  73.3 6.4 %copy-start.12 = (bf16[1,4,128,128]{3,2,1,0:T(8,128)(2,1)S(1)}, bf16[1,4,128,128]{3,2,1,0:T(8,128)(2,1)}, u32[]{:S(2)}) copy-start(bf16[1,4,128,128]{3,2,1,0:T(8,128)(2,1)} %copy.21) | copy-start | bytes 393220
  73.3 6.5 %copy-start.13 = (s32[512]{0:T(512)S(1)}, s32[512]{0:T(512)}, u32[]{:S(2)}) copy-start(s32[512]{0:T(512)} %broadcast_bitcast_fusion) | copy-start | bytes 6148
  74.8 12.9 %collective-permute-start.6 = (bf16[256,16,256]{2,0,1:T(8,128)(2,1)S(1)}, bf16[256,16,256]{2,0,1:T(8,128)(2,1)S(1)}, u32[]{:S(2)}, u32[]{:S(2)}) collective-permute-start(bf16[256,16,256]{2,0,1:T(8,128)(2,1)S(1)} %pad_maximum_fusion), channel_id=1, source_target_pairs={{0,128},{128,0},{256,384},{384,256},{1,129},{129,1},{257,385},{385... | collective-permute-start | bytes 6291464 | tf_op jit(solution)/shard_map/ppermute | solution.py:158
  79.8 0.9 copy-start.10
  84.4 1.6 %copy-start.5 = (bf16[4,4,256,128]{3,2,1,0:T(8,128)(2,1)S(1)}, bf16[4,4,256,128]{3,2,1,0:T(8,128)(2,1)}, u32[]{:S(2)}) copy-start(bf16[4,4,256,128]{3,2,1,0:T(8,128)(2,1)} %dot_general.28) | copy-start | bytes 3145732
  89.6 1.7 %copy-start.1 = (f32[128,4,4,256]{3,0,2,1:T(8,128)}, f32[128,4,4,256]{3,0,2,1:T(8,128)S(1)}, u32[]{:S(2)}) copy-start(f32[128,4,4,256]{3,0,2,1:T(8,128)S(1)} %fusion.15) | copy-start | bytes 6291460
  89.6 2.0 %copy-start.7 = (bf16[16,128,256]{2,1,0:T(8,128)(2,1)S(1)}, bf16[16,128,256]{2,1,0:T(8,128)(2,1)}, u32[]{:S(2)}) copy-start(bf16[16,128,256]{2,1,0:T(8,128)(2,1)} %get-tuple-element.17) | copy-start | bytes 3145732
  92.0 1.6 %copy-start.3 = (f32[128,4,4,256]{3,0,2,1:T(8,128)S(1)}, f32[128,4,4,256]{3,0,2,1:T(8,128)}, u32[]{:S(2)}) copy-start(f32[128,4,4,256]{3,0,2,1:T(8,128)} %fusion.21) | copy-start | bytes 6291460
  93.6 1.2 slice-start
  93.6 1.4 copy-start.8
  93.6 1.5 %copy-start.9 = (f32[128,1,4,256]{3,0,2,1:T(8,128)S(1)}, f32[128,1,4,256]{3,0,2,1:T(8,128)}, u32[]{:S(2)}) copy-start(f32[128,1,4,256]{3,0,2,1:T(8,128)} %get-tuple-element.30) | copy-start | bytes 1572868
  95.1 1.6 %copy-start.2 = (f32[128,4,4,256]{3,0,2,1:T(8,128)S(1)}, f32[128,4,4,256]{3,0,2,1:T(8,128)}, u32[]{:S(2)}) copy-start(f32[128,4,4,256]{3,0,2,1:T(8,128)} %pad_maximum_fusion.1) | copy-start | bytes 6291460

commit v18 on v10

--- a/solution.py
+++ b/solution.py
@@ -156,9 +156,10 @@
     )
     other_weights = lax.ppermute(mine_weights, "dp", [(i, i ^ 1) for i in range(dp_size)])
 
-    key_stack = gathered_a[:, :, :key_width]
+    whole_rows = local_groups == 1
+    key_stack = gathered_a if whole_rows else gathered_a[:, :, :key_width]
     value_stack = restack(gathered_b[:, :, : values.shape[1]], sources_b, sources_a, x_size)
-    key_part = jnp.swapaxes(key_stack, 0, 1).reshape(context_size * row_count, key_width)
+    key_part = jnp.swapaxes(key_stack, 0, 1).reshape(context_size * row_count, -1)
     value_part = jnp.swapaxes(value_stack, 0, 1).reshape(context_size * row_count, -1)
     key_pos = order.reshape(context_size, row_count)[jnp.array(sources_a)].reshape(-1)
 
@@ -172,7 +173,9 @@
     stacked_rows = query_head_group * row_count
     key_count = key_part.shape[0]
     running_max = jnp.full((local_groups, stacked_rows), -1e30, jnp.float32)
-    key_heads = key_part.reshape(key_count, local_groups, HEAD_SIZE)
+    key_heads = key_part.reshape(key_count, local_groups, -1)
+    if whole_rows:
+        stacked = jnp.pad(stacked, ((0, 0), (0, 0), (0, key_heads.shape[2] - HEAD_SIZE)))
     value_heads = value_part.reshape(key_count, local_groups, HEAD_SIZE)
     scores = (
         jnp.einsum("grd,kgd->grk", stacked, key_heads, preferred_element_type=jnp.float32)

time: 138 us -> 133 us (0.964)
  other arithmetic: 9.37 us -> 5.63 us
  local copies, waits for them, and re-layouts: 19.8 us -> 17.1 us
  waiting for transfers between devices: 36 us -> 37.5 us
    select_n x2, other arithmetic: 2.35 us -> 0.41 us  [exchange_gather_pair(): jnp.where(upper_of(index, side_b), jnp.concatenate([received_b, stack_b],...]
    select_n x2, other arithmetic: 1.88 us -> 0.41 us  [exchange_gather_pair(): jnp.where(upper_of(index, side_a), jnp.concatenate([received_a, stack_a],...]
    unnamed x40 -> x32, local copies, waits for them, and re-layouts: 3.21 us -> 3.28 us
  transfers between devices with their start and end apart: 7 -> 7, of which waited for: 5 -> 6; matrix products, arithmetic and copies ran while one was open for 9% -> 7% of each run, Pallas kernels for 0% -> 0%
where the time goes in v18:
time: 133 us; the launch traced here: 131 us
  blocking collectives  39 us (29%)
  waiting for transfers between devices  37.5 us (28%)
  starting transfers between devices  26.3 us (20%)
  local copies, waits for them, and re-layouts  17.1 us (13%)
  other arithmetic  5.63 us (4%)
  matrix products  4.39 us (3%)
    all_to_all x1, blocking collectives, per_device(): pieces = lax.all_to_all(pieces, 'tensor', 1, 1, tiled=True)  39 us
    ppermute x2, waiting for transfers between devices, exchange_gather_pair(): lax.ppermute(stack_a, axis_name, [(i, i ^ mask_a) for i in range(count)])  16.6 us
    ppermute x2, waiting for transfers between devices, exchange_gather(): lax.ppermute(stack, axis_name, [(i, i ^ mask) for i in range(count)])  15.2 us
    ppermute x2, starting transfers between devices, exchange_gather(): lax.ppermute(stack, axis_name, [(i, i ^ mask) for i in range(count)])  9.68 us
    ppermute x2, starting transfers between devices, exchange_gather_pair(): lax.ppermute(stack_b, axis_name, [(i, i ^ mask_b) for i in range(count)])  6.31 us
    ppermute x1, starting transfers between devices, per_device(): lax.ppermute(mine_weights, 'dp', [(i, i ^ 1) for i in range(dp_size)])  6.28 us
    ppermute x2, waiting for transfers between devices, exchange_gather_pair(): lax.ppermute(stack_b, axis_name, [(i, i ^ mask_b) for i in range(count)])  5.79 us
    ppermute x2, starting transfers between devices, exchange_gather_pair(): lax.ppermute(stack_a, axis_name, [(i, i ^ mask_a) for i in range(count)])  4.07 us
  transfers between devices with their start and end apart: 7, of which 6 were waited for; matrix products, arithmetic and copies ran while one was open for 7% of the time, Pallas kernels for 0%

profile of v18, /device:TPU:1, one launch (start us, length us, event | category | flops | bytes accessed | tf_op | source)
XLA Modules:
  0.0 130.5 jit_solution(13746158728529391113)
XLA Ops:
  0.0 0.9 dynamic-slice_bitcast_fusion.1
  1.2 0.8 maximum_bitcast_fusion
  2.0 5.0 %collective-permute-start = (bf16[128,1,768]{2,0,1:T(8,128)(2,1)S(1)}, bf16[128,1,768]{2,0,1:T(8,128)(2,1)S(1)}, u32[]{:S(2)}, u32[]{:S(2)}) collective-permute-start(bf16[128,1,768]{2,0,1:T(8,128)(2,1)S(1)} %maximum_bitcast_fusion), channel_id=1, source_target_pairs={{0,64},{8,72},{16,80},{24,88},{32,96},{40,104},{48,112},{56,120},{... | collective-permute-start | bytes 589832 | tf_op jit(solution)/shard_map/ppermute | solution.py:51
  7.1 7.2 %collective-permute-done = bf16[128,1,768]{2,0,1:T(8,128)(2,1)S(1)} collective-permute-done((bf16[128,1,768]{2,0,1:T(8,128)(2,1)S(1)}, bf16[128,1,768]{2,0,1:T(8,128)(2,1)S(1)}, u32[]{:S(2)}, u32[]{:S(2)}) %collective-permute-start) | collective-permute-done | bytes 196640 | tf_op jit(solution)/shard_map/ppermute | solution.py:51
  14.4 4.6 %collective-permute-start.1 = (bf16[128,2,768]{2,0,1:T(8,128)(2,1)S(1)}, bf16[128,2,768]{2,0,1:T(8,128)(2,1)S(1)}, u32[]{:S(2)}, u32[]{:S(2)}) collective-permute-start(bf16[128,2,768]{2,0,1:T(8,128)(2,1)S(1)} %maximum_select_fusion.5), channel_id=1, source_target_pairs={{0,32},{8,40},{16,48},{24,56},{32,0},{40,8},{48,16},{56,24},{64,96... | collective-permute-start | bytes 1179656 | tf_op jit(solution)/shard_map/ppermute | solution.py:51
  19.0 7.9 %collective-permute-done.1 = bf16[128,2,768]{2,0,1:T(8,128)(2,1)S(1)} collective-permute-done((bf16[128,2,768]{2,0,1:T(8,128)(2,1)S(1)}, bf16[128,2,768]{2,0,1:T(8,128)(2,1)S(1)}, u32[]{:S(2)}, u32[]{:S(2)}) %collective-permute-start.1) | collective-permute-done | bytes 393248 | tf_op jit(solution)/shard_map/ppermute | solution.py:51
  27.2 4.4 %collective-permute-start.3 = (bf16[128,4,384]{2,0,1:T(8,128)(2,1)S(1)}, bf16[128,4,384]{2,0,1:T(8,128)(2,1)S(1)}, u32[]{:S(2)}, u32[]{:S(2)}) collective-permute-start(bf16[128,4,384]{2,0,1:T(8,128)(2,1)S(1)} %get-tuple-element.39), channel_id=1, source_target_pairs={{0,24},{8,16},{16,8},{24,0},{32,56},{40,48},{48,40},{56,32},{64,88... | collective-permute-start | bytes 1179656 | tf_op jit(solution)/shard_map/ppermute | solution.py:85
  31.6 1.9 %collective-permute-start.2 = (bf16[128,4,384]{2,0,1:T(8,128)(2,1)S(1)}, bf16[128,4,384]{2,0,1:T(8,128)(2,1)S(1)}, u32[]{:S(2)}, u32[]{:S(2)}) collective-permute-start(bf16[128,4,384]{2,0,1:T(8,128)(2,1)S(1)} %get-tuple-element.40), channel_id=1, source_target_pairs={{0,8},{8,0},{16,24},{24,16},{32,40},{40,32},{48,56},{56,48},{64,72... | collective-permute-start | bytes 1179656 | tf_op jit(solution)/shard_map/ppermute | solution.py:84
  33.6 5.4 %collective-permute-done.3 = bf16[128,4,384]{2,0,1:T(8,128)(2,1)S(1)} collective-permute-done((bf16[128,4,384]{2,0,1:T(8,128)(2,1)S(1)}, bf16[128,4,384]{2,0,1:T(8,128)(2,1)S(1)}, u32[]{:S(2)}, u32[]{:S(2)}) %collective-permute-start.3) | collective-permute-done | bytes 393248 | tf_op jit(solution)/shard_map/ppermute | solution.py:85
  39.0 2.7 %collective-permute-done.2 = bf16[128,4,384]{2,0,1:T(8,128)(2,1)S(1)} collective-permute-done((bf16[128,4,384]{2,0,1:T(8,128)(2,1)S(1)}, bf16[128,4,384]{2,0,1:T(8,128)(2,1)S(1)}, u32[]{:S(2)}, u32[]{:S(2)}) %collective-permute-start.2) | collective-permute-done | bytes 393248 | tf_op jit(solution)/shard_map/ppermute | solution.py:84
  41.9 2.2 %collective-permute-start.4 = (bf16[128,8,384]{2,0,1:T(8,128)(2,1)S(1)}, bf16[128,8,384]{2,0,1:T(8,128)(2,1)S(1)}, u32[]{:S(2)}, u32[]{:S(2)}) collective-permute-start(bf16[128,8,384]{2,0,1:T(8,128)(2,1)S(1)} %maximum_select_fusion.3), channel_id=1, source_target_pairs={{0,24},{8,16},{16,8},{24,0},{32,56},{40,48},{48,40},{56,32},{64,88... | collective-permute-start | bytes 2359304 | tf_op jit(solution)/shard_map/ppermute | solution.py:84
  44.1 1.9 %collective-permute-start.5 = (bf16[128,8,384]{2,0,1:T(8,128)(2,1)S(1)}, bf16[128,8,384]{2,0,1:T(8,128)(2,1)S(1)}, u32[]{:S(2)}, u32[]{:S(2)}) collective-permute-start(bf16[128,8,384]{2,0,1:T(8,128)(2,1)S(1)} %maximum_select_fusion.4), channel_id=1, source_target_pairs={{0,8},{8,0},{16,24},{24,16},{32,40},{40,32},{48,56},{56,48},{64,72... | collective-permute-start | bytes 2359304 | tf_op jit(solution)/shard_map/ppermute | solution.py:85
  46.4 0.6 gather_fusion
  47.0 13.8 %collective-permute-done.4 = bf16[128,8,384]{2,0,1:T(8,128)(2,1)S(1)} collective-permute-done((bf16[128,8,384]{2,0,1:T(8,128)(2,1)S(1)}, bf16[128,8,384]{2,0,1:T(8,128)(2,1)S(1)}, u32[]{:S(2)}, u32[]{:S(2)}) %collective-permute-start.4) | collective-permute-done | bytes 786464 | tf_op jit(solution)/shard_map/ppermute | solution.py:84
  62.0 0.5 slice_bitcast_fusion.2
  62.4 1.5 %fusion = (f32[512]{0:T(512)S(1)}, f32[512,2048]{1,0:T(8,128)S(1)}) fusion(s32[2048]{0:T(1024)S(1)} %bitcast.88, s32[512]{0:T(512)S(1)} %broadcast_bitcast_fusion, bf16[2048,384]{1,0:T(8,128)(2,1)S(1)} %bitcast.75, bf16[1,512,128]{2,1,0:T(8,128)(2,1)S(1)} %bitcast.86), kind=kOutput, calls=%fused_computation.3 | convolution fusion | flops 809500160 | bytes 5910528 | tf_op jit(solution)/shard_map/grd,kgd->grk/dot_general | solution.py:181
  64.0 1.5 %pad_maximum_fusion = bf16[256,16,256]{2,0,1:T(8,128)(2,1)} fusion(bf16[128,16,256]{2,0,1:T(8,128)(2,1)S(1)} %get-tuple-element.38, bf16[128,16,256]{2,0,1:T(8,128)(2,1)S(1)} %get-tuple-element.47), kind=kLoop, calls=%fused_computation.10 | loop fusion | flops 4194304 | bytes 4194304 | tf_op jit(solution)/shard_map/concatenate | solution.py:154
  65.4 6.3 %collective-permute-start.6 = (bf16[256,16,256]{2,0,1:T(8,128)(2,1)}, bf16[256,16,256]{2,0,1:T(8,128)(2,1)}, u32[]{:S(2)}, u32[]{:S(2)}) collective-permute-start(bf16[256,16,256]{2,0,1:T(8,128)(2,1)} %pad_maximum_fusion), channel_id=1, source_target_pairs={{0,128},{128,0},{256,384},{384,256},{1,129},{129,1},{257,385},{385... | collective-permute-start | bytes 6291464 | tf_op jit(solution)/shard_map/ppermute | solution.py:157
  71.7 1.2 fusion.1
  73.0 1.1 fusion.11
  75.9 0.4 fusion.24
  76.3 1.4 %fusion.38 = (f32[128,4,1,256]{3,0,2,1:T(8,128)}, f32[128,4,1,256]{3,0,2,1:T(8,128)}, f32[128,4,1,256]{3,0,2,1:T(8,128)}, f32[128,4,1,256]{3,0,2,1:T(8,128)}) fusion(f32[128,4,4,256]{3,0,2,1:T(8,128)S(1)} %fusion.24), kind=kLoop, calls=%fused_computation.58 | loop fusion | bytes 4194304 | tf_op jit(solution)/shard_map/slice | solution.py:77
  77.8 1.4 %fusion.40 = (f32[128,4,1,256]{3,0,2,1:T(8,128)}, f32[128,4,1,256]{3,0,2,1:T(8,128)}, f32[128,4,1,256]{3,0,2,1:T(8,128)}, f32[128,4,1,256]{3,0,2,1:T(8,128)}) fusion(f32[128,4,4,256]{3,0,2,1:T(8,128)S(1)} %pad_maximum_fusion.1), kind=kLoop, calls=%fused_computation.60 | loop fusion | bytes 4194304 | tf_op jit(solution)/shard_map/slice | solution.py:77
  79.1 2.7 %slice_bitcast_fusion.1 = (bf16[16,128,256]{2,1,0:T(8,128)(2,1)}, bf16[16,128,256]{2,1,0:T(8,128)(2,1)S(1)}) fusion(bf16[256,16,256]{2,0,1:T(8,128)(2,1)} %collective-permute-done.6), kind=kLoop, calls=%fused_computation.19 | loop fusion | bytes 4194304 | tf_op jit(solution)/shard_map/transpose | solution.py:205
  82.7 1.1 fusion.43
  83.8 0.6 copy-done.1
  85.7 1.0 slice-done
  87.5 0.8 copy-done.3
  89.4 0.5 fusion.14
  89.9 0.7 copy.23
  90.6 39.0 %all_to_all.5 = bf16[128,8,512]{0,2,1:T(8,128)(2,1)S(1)} all-to-all(bf16[128,8,512]{0,2,1:T(8,128)(2,1)S(1)} %bitcast.76), channel_id=1, replica_groups=mesh['dp'=4,'context'=16,'tensor'=8] {'tensor'}, dimensions={1} | all-to-all | bytes 2097152 | tf_op jit(solution)/shard_map/all_to_all | solution.py:218
  129.7 0.8 copy.24
  (68 shorter events, 8.1 us)
Async XLA Ops:
  0.0 46.3 %copy-start = (s32[2048]{0:T(1024)S(1)}, s32[2048]{0:T(1024)}, u32[]{:S(2)}) copy-start(s32[2048]{0:T(1024)} %param.9) | copy-start | bytes 24580
  2.0 12.3 %collective-permute-start = (bf16[128,1,768]{2,0,1:T(8,128)(2,1)S(1)}, bf16[128,1,768]{2,0,1:T(8,128)(2,1)S(1)}, u32[]{:S(2)}, u32[]{:S(2)}) collective-permute-start(bf16[128,1,768]{2,0,1:T(8,128)(2,1)S(1)} %maximum_bitcast_fusion), channel_id=1, source_target_pairs={{0,64},{8,72},{16,80},{24,88},{32,96},{40,104},{48,112},{56,120},{... | collective-permute-start | bytes 589832 | tf_op jit(solution)/shard_map/ppermute | solution.py:51
  14.4 12.6 %collective-permute-start.1 = (bf16[128,2,768]{2,0,1:T(8,128)(2,1)S(1)}, bf16[128,2,768]{2,0,1:T(8,128)(2,1)S(1)}, u32[]{:S(2)}, u32[]{:S(2)}) collective-permute-start(bf16[128,2,768]{2,0,1:T(8,128)(2,1)S(1)} %maximum_select_fusion.5), channel_id=1, source_target_pairs={{0,32},{8,40},{16,48},{24,56},{32,0},{40,8},{48,16},{56,24},{64,96... | collective-permute-start | bytes 1179656 | tf_op jit(solution)/shard_map/ppermute | solution.py:51
  27.1 18.9 %copy-start.13 = (bf16[128,512]{1,0:T(8,128)(2,1)S(1)}, bf16[128,512]{1,0:T(8,128)(2,1)}, u32[]{:S(2)}) copy-start(bf16[128,512]{1,0:T(8,128)(2,1)} %param.6) | copy-start | bytes 393220
  27.2 19.2 %copy-start.14 = (s32[16]{0:T(128)S(1)}, s32[16]{0:T(128)}, u32[]{:S(2)}) copy-start(s32[16]{0:T(128)} %constant.67) | copy-start | bytes 196
  27.2 11.7 %collective-permute-start.3 = (bf16[128,4,384]{2,0,1:T(8,128)(2,1)S(1)}, bf16[128,4,384]{2,0,1:T(8,128)(2,1)S(1)}, u32[]{:S(2)}, u32[]{:S(2)}) collective-permute-start(bf16[128,4,384]{2,0,1:T(8,128)(2,1)S(1)} %get-tuple-element.39), channel_id=1, source_target_pairs={{0,24},{8,16},{16,8},{24,0},{32,56},{40,48},{48,40},{56,32},{64,88... | collective-permute-start | bytes 1179656 | tf_op jit(solution)/shard_map/ppermute | solution.py:85
  31.6 10.1 %collective-permute-start.2 = (bf16[128,4,384]{2,0,1:T(8,128)(2,1)S(1)}, bf16[128,4,384]{2,0,1:T(8,128)(2,1)S(1)}, u32[]{:S(2)}, u32[]{:S(2)}) collective-permute-start(bf16[128,4,384]{2,0,1:T(8,128)(2,1)S(1)} %get-tuple-element.40), channel_id=1, source_target_pairs={{0,8},{8,0},{16,24},{24,16},{32,40},{40,32},{48,56},{56,48},{64,72... | collective-permute-start | bytes 1179656 | tf_op jit(solution)/shard_map/ppermute | solution.py:84
  41.9 18.9 %collective-permute-start.4 = (bf16[128,8,384]{2,0,1:T(8,128)(2,1)S(1)}, bf16[128,8,384]{2,0,1:T(8,128)(2,1)S(1)}, u32[]{:S(2)}, u32[]{:S(2)}) collective-permute-start(bf16[128,8,384]{2,0,1:T(8,128)(2,1)S(1)} %maximum_select_fusion.3), channel_id=1, source_target_pairs={{0,24},{8,16},{16,8},{24,0},{32,56},{40,48},{48,40},{56,32},{64,88... | collective-permute-start | bytes 2359304 | tf_op jit(solution)/shard_map/ppermute | solution.py:84
  44.1 17.5 %collective-permute-start.5 = (bf16[128,8,384]{2,0,1:T(8,128)(2,1)S(1)}, bf16[128,8,384]{2,0,1:T(8,128)(2,1)S(1)}, u32[]{:S(2)}, u32[]{:S(2)}) collective-permute-start(bf16[128,8,384]{2,0,1:T(8,128)(2,1)S(1)} %maximum_select_fusion.4), channel_id=1, source_target_pairs={{0,8},{8,0},{16,24},{24,16},{32,40},{40,32},{48,56},{56,48},{64,72... | collective-permute-start | bytes 2359304 | tf_op jit(solution)/shard_map/ppermute | solution.py:85
  65.4 13.7 %collective-permute-start.6 = (bf16[256,16,256]{2,0,1:T(8,128)(2,1)}, bf16[256,16,256]{2,0,1:T(8,128)(2,1)}, u32[]{:S(2)}, u32[]{:S(2)}) collective-permute-start(bf16[256,16,256]{2,0,1:T(8,128)(2,1)} %pad_maximum_fusion), channel_id=1, source_target_pairs={{0,128},{128,0},{256,384},{384,256},{1,129},{129,1},{257,385},{385... | collective-permute-start | bytes 6291464 | tf_op jit(solution)/shard_map/ppermute | solution.py:157
  82.7 1.7 %copy-start.1 = (f32[128,4,4,256]{3,0,2,1:T(8,128)}, f32[128,4,4,256]{3,0,2,1:T(8,128)S(1)}, u32[]{:S(2)}) copy-start(f32[128,4,4,256]{3,0,2,1:T(8,128)S(1)} %fusion.18) | copy-start | bytes 6291460
  82.7 2.0 %copy-start.2 = (bf16[16,128,256]{2,1,0:T(8,128)(2,1)S(1)}, bf16[16,128,256]{2,1,0:T(8,128)(2,1)}, u32[]{:S(2)}) copy-start(bf16[16,128,256]{2,1,0:T(8,128)(2,1)} %get-tuple-element.21) | copy-start | bytes 3145732
  85.5 1.2 slice-start
  85.5 1.3 %copy-start.11 = (f32[128,1,4,256]{3,0,2,1:T(8,128)S(1)}, f32[128,1,4,256]{3,0,2,1:T(8,128)}, u32[]{:S(2)}) copy-start(f32[128,1,4,256]{3,0,2,1:T(8,128)} %get-tuple-element.33) | copy-start | bytes 1572868
  85.5 1.5 %copy-start.12 = (f32[128,1,4,256]{3,0,2,1:T(8,128)S(1)}, f32[128,1,4,256]{3,0,2,1:T(8,128)}, u32[]{:S(2)}) copy-start(f32[128,1,4,256]{3,0,2,1:T(8,128)} %get-tuple-element.34) | copy-start | bytes 1572868
  87.2 1.0 copy-start.3
  87.2 1.2 copy-start.4
  87.2 1.3 %copy-start.5 = (f32[128,4,1,256]{3,0,2,1:T(8,128)S(1)}, f32[128,4,1,256]{3,0,2,1:T(8,128)}, u32[]{:S(2)}) copy-start(f32[128,4,1,256]{3,0,2,1:T(8,128)} %get-tuple-element.15) | copy-start | bytes 1572868
  87.2 1.5 %copy-start.6 = (f32[128,4,1,256]{3,0,2,1:T(8,128)S(1)}, f32[128,4,1,256]{3,0,2,1:T(8,128)}, u32[]{:S(2)}) copy-start(f32[128,4,1,256]{3,0,2,1:T(8,128)} %get-tuple-element.16) | copy-start | bytes 1572868
  87.2 1.6 %copy-start.7 = (f32[128,4,1,256]{3,0,2,1:T(8,128)S(1)}, f32[128,4,1,256]{3,0,2,1:T(8,128)}, u32[]{:S(2)}) copy-start(f32[128,4,1,256]{3,0,2,1:T(8,128)} %get-tuple-element.23) | copy-start | bytes 1572868
  87.3 1.8 %copy-start.8 = (f32[128,4,1,256]{3,0,2,1:T(8,128)S(1)}, f32[128,4,1,256]{3,0,2,1:T(8,128)}, u32[]{:S(2)}) copy-start(f32[128,4,1,256]{3,0,2,1:T(8,128)} %get-tuple-element.24) | copy-start | bytes 1572868
  87.3 1.9 %copy-start.9 = (f32[128,4,1,256]{3,0,2,1:T(8,128)S(1)}, f32[128,4,1,256]{3,0,2,1:T(8,128)}, u32[]{:S(2)}) copy-start(f32[128,4,1,256]{3,0,2,1:T(8,128)} %get-tuple-element.25) | copy-start | bytes 1572868
  87.3 2.1 %copy-start.10 = (f32[128,4,1,256]{3,0,2,1:T(8,128)S(1)}, f32[128,4,1,256]{3,0,2,1:T(8,128)}, u32[]{:S(2)}) copy-start(f32[128,4,1,256]{3,0,2,1:T(8,128)} %get-tuple-element.26) | copy-start | bytes 1572868

commit v19 on v18

--- a/solution.py
+++ b/solution.py
@@ -186,12 +186,31 @@
     new_max = jnp.maximum(running_max, jnp.max(scores, axis=2))
     weights = jnp.where(visible, jnp.exp(scores - new_max[..., None]), 0.0)
     new_sum = jnp.sum(weights, axis=2)
-    product = jnp.einsum(
-        "grk,kgd->grd",
-        weights.astype(jnp.bfloat16),
-        value_heads,
-        preferred_element_type=jnp.float32,
-    )
+    if whole_rows and x_size > 1:
+        y_count = context_size // x_size
+        group = y_count * row_count
+        x_a = [sources_a[ix * y_count] for ix in range(x_size)]
+        x_b = [sources_b[ix * y_count] for ix in range(x_size)]
+        value_rows = jnp.swapaxes(gathered_b, 0, 1).reshape(context_size * row_count, -1)
+        probs = weights.astype(jnp.bfloat16)
+        product = None
+        for ia, x in enumerate(x_a):
+            ib = x_b.index(x)
+            part = jnp.einsum(
+                "grk,kd->grd",
+                probs[:, :, ia * group : (ia + 1) * group],
+                value_rows[ib * group : (ib + 1) * group],
+                preferred_element_type=jnp.float32,
+            )
+            product = part if product is None else product + part
+        product = product[:, :, :HEAD_SIZE]
+    else:
+        product = jnp.einsum(
+            "grk,kgd->grd",
+            weights.astype(jnp.bfloat16),
+            value_heads,
+            preferred_element_type=jnp.float32,
+        )
     attended = (product / new_sum[..., None]).astype(jnp.bfloat16)
     attended = attended.reshape(local_groups, query_head_group, row_count, HEAD_SIZE).transpose(
         2, 0, 1, 3

time: 133 us -> 134 us (level)
  no operation moved by 1% of the time
where the time goes in v19:
time: 134 us; the launch traced here: 132 us
  blocking collectives  39 us (29%)
  waiting for transfers between devices  37.5 us (28%)
  starting transfers between devices  26.3 us (20%)
  local copies, waits for them, and re-layouts  17.2 us (13%)
  other arithmetic  6.06 us (5%)
  matrix products  5.06 us (4%)
    all_to_all x1, blocking collectives, per_device(): pieces = lax.all_to_all(pieces, 'tensor', 1, 1, tiled=True)  39 us
    ppermute x2, waiting for transfers between devices, exchange_gather_pair(): lax.ppermute(stack_a, axis_name, [(i, i ^ mask_a) for i in range(count)])  16.6 us
    ppermute x2, waiting for transfers between devices, exchange_gather(): lax.ppermute(stack, axis_name, [(i, i ^ mask) for i in range(count)])  15.2 us
    ppermute x2, starting transfers between devices, exchange_gather(): lax.ppermute(stack, axis_name, [(i, i ^ mask) for i in range(count)])  9.68 us
    ppermute x2, starting transfers between devices, exchange_gather_pair(): lax.ppermute(stack_b, axis_name, [(i, i ^ mask_b) for i in range(count)])  6.31 us
    ppermute x1, starting transfers between devices, per_device(): lax.ppermute(mine_weights, 'dp', [(i, i ^ 1) for i in range(dp_size)])  6.27 us
    ppermute x2, waiting for transfers between devices, exchange_gather_pair(): lax.ppermute(stack_b, axis_name, [(i, i ^ mask_b) for i in range(count)])  5.79 us
    ppermute x2, starting transfers between devices, exchange_gather_pair(): lax.ppermute(stack_a, axis_name, [(i, i ^ mask_a) for i in range(count)])  4.07 us
  transfers between devices with their start and end apart: 7, of which 6 were waited for; matrix products, arithmetic and copies ran while one was open for 7% of the time, Pallas kernels for 0%

profile of v19, /device:TPU:1, one launch (start us, length us, event | category | flops | bytes accessed | tf_op | source)
XLA Modules:
  0.0 131.7 jit_solution(15771237052183630227)
XLA Ops:
  0.0 0.9 dynamic-slice_bitcast_fusion.1
  1.2 0.8 maximum_bitcast_fusion
  2.0 5.0 %collective-permute-start = (bf16[128,1,768]{2,0,1:T(8,128)(2,1)S(1)}, bf16[128,1,768]{2,0,1:T(8,128)(2,1)S(1)}, u32[]{:S(2)}, u32[]{:S(2)}) collective-permute-start(bf16[128,1,768]{2,0,1:T(8,128)(2,1)S(1)} %maximum_bitcast_fusion), channel_id=1, source_target_pairs={{0,64},{8,72},{16,80},{24,88},{32,96},{40,104},{48,112},{56,120},{... | collective-permute-start | bytes 589832 | tf_op jit(solution)/shard_map/ppermute | solution.py:51
  7.1 7.2 %collective-permute-done = bf16[128,1,768]{2,0,1:T(8,128)(2,1)S(1)} collective-permute-done((bf16[128,1,768]{2,0,1:T(8,128)(2,1)S(1)}, bf16[128,1,768]{2,0,1:T(8,128)(2,1)S(1)}, u32[]{:S(2)}, u32[]{:S(2)}) %collective-permute-start) | collective-permute-done | bytes 196640 | tf_op jit(solution)/shard_map/ppermute | solution.py:51
  14.4 4.6 %collective-permute-start.1 = (bf16[128,2,768]{2,0,1:T(8,128)(2,1)S(1)}, bf16[128,2,768]{2,0,1:T(8,128)(2,1)S(1)}, u32[]{:S(2)}, u32[]{:S(2)}) collective-permute-start(bf16[128,2,768]{2,0,1:T(8,128)(2,1)S(1)} %maximum_select_fusion.5), channel_id=1, source_target_pairs={{0,32},{8,40},{16,48},{24,56},{32,0},{40,8},{48,16},{56,24},{64,96... | collective-permute-start | bytes 1179656 | tf_op jit(solution)/shard_map/ppermute | solution.py:51
  19.0 7.9 %collective-permute-done.1 = bf16[128,2,768]{2,0,1:T(8,128)(2,1)S(1)} collective-permute-done((bf16[128,2,768]{2,0,1:T(8,128)(2,1)S(1)}, bf16[128,2,768]{2,0,1:T(8,128)(2,1)S(1)}, u32[]{:S(2)}, u32[]{:S(2)}) %collective-permute-start.1) | collective-permute-done | bytes 393248 | tf_op jit(solution)/shard_map/ppermute | solution.py:51
  27.2 4.4 %collective-permute-start.3 = (bf16[128,4,384]{2,0,1:T(8,128)(2,1)S(1)}, bf16[128,4,384]{2,0,1:T(8,128)(2,1)S(1)}, u32[]{:S(2)}, u32[]{:S(2)}) collective-permute-start(bf16[128,4,384]{2,0,1:T(8,128)(2,1)S(1)} %get-tuple-element.45), channel_id=1, source_target_pairs={{0,24},{8,16},{16,8},{24,0},{32,56},{40,48},{48,40},{56,32},{64,88... | collective-permute-start | bytes 1179656 | tf_op jit(solution)/shard_map/ppermute | solution.py:85
  31.6 1.9 %collective-permute-start.2 = (bf16[128,4,384]{2,0,1:T(8,128)(2,1)S(1)}, bf16[128,4,384]{2,0,1:T(8,128)(2,1)S(1)}, u32[]{:S(2)}, u32[]{:S(2)}) collective-permute-start(bf16[128,4,384]{2,0,1:T(8,128)(2,1)S(1)} %get-tuple-element.46), channel_id=1, source_target_pairs={{0,8},{8,0},{16,24},{24,16},{32,40},{40,32},{48,56},{56,48},{64,72... | collective-permute-start | bytes 1179656 | tf_op jit(solution)/shard_map/ppermute | solution.py:84
  33.6 5.4 %collective-permute-done.3 = bf16[128,4,384]{2,0,1:T(8,128)(2,1)S(1)} collective-permute-done((bf16[128,4,384]{2,0,1:T(8,128)(2,1)S(1)}, bf16[128,4,384]{2,0,1:T(8,128)(2,1)S(1)}, u32[]{:S(2)}, u32[]{:S(2)}) %collective-permute-start.3) | collective-permute-done | bytes 393248 | tf_op jit(solution)/shard_map/ppermute | solution.py:85
  39.0 2.7 %collective-permute-done.2 = bf16[128,4,384]{2,0,1:T(8,128)(2,1)S(1)} collective-permute-done((bf16[128,4,384]{2,0,1:T(8,128)(2,1)S(1)}, bf16[128,4,384]{2,0,1:T(8,128)(2,1)S(1)}, u32[]{:S(2)}, u32[]{:S(2)}) %collective-permute-start.2) | collective-permute-done | bytes 393248 | tf_op jit(solution)/shard_map/ppermute | solution.py:84
  41.9 2.2 %collective-permute-start.4 = (bf16[128,8,384]{2,0,1:T(8,128)(2,1)S(1)}, bf16[128,8,384]{2,0,1:T(8,128)(2,1)S(1)}, u32[]{:S(2)}, u32[]{:S(2)}) collective-permute-start(bf16[128,8,384]{2,0,1:T(8,128)(2,1)S(1)} %maximum_select_fusion.3), channel_id=1, source_target_pairs={{0,24},{8,16},{16,8},{24,0},{32,56},{40,48},{48,40},{56,32},{64,88... | collective-permute-start | bytes 2359304 | tf_op jit(solution)/shard_map/ppermute | solution.py:84
  44.1 1.9 %collective-permute-start.5 = (bf16[128,8,384]{2,0,1:T(8,128)(2,1)S(1)}, bf16[128,8,384]{2,0,1:T(8,128)(2,1)S(1)}, u32[]{:S(2)}, u32[]{:S(2)}) collective-permute-start(bf16[128,8,384]{2,0,1:T(8,128)(2,1)S(1)} %maximum_select_fusion.4), channel_id=1, source_target_pairs={{0,8},{8,0},{16,24},{24,16},{32,40},{40,32},{48,56},{56,48},{64,72... | collective-permute-start | bytes 2359304 | tf_op jit(solution)/shard_map/ppermute | solution.py:85
  46.4 0.6 gather_fusion
  47.0 13.8 %collective-permute-done.4 = bf16[128,8,384]{2,0,1:T(8,128)(2,1)S(1)} collective-permute-done((bf16[128,8,384]{2,0,1:T(8,128)(2,1)S(1)}, bf16[128,8,384]{2,0,1:T(8,128)(2,1)S(1)}, u32[]{:S(2)}, u32[]{:S(2)}) %collective-permute-start.4) | collective-permute-done | bytes 786464 | tf_op jit(solution)/shard_map/ppermute | solution.py:84
  61.8 1.5 %fusion = (f32[512]{0:T(512)S(1)}, f32[512,2048]{1,0:T(8,128)S(1)}) fusion(s32[2048]{0:T(1024)S(1)} %bitcast.108, s32[512]{0:T(512)S(1)} %broadcast_bitcast_fusion, bf16[2048,384]{1,0:T(8,128)(2,1)S(1)} %bitcast.94, bf16[1,512,128]{2,1,0:T(8,128)(2,1)S(1)} %bitcast.107), kind=kOutput, calls=%fused_computation.3 | convolution fusion | flops 809500160 | bytes 5910528 | tf_op jit(solution)/shard_map/grd,kgd->grk/dot_general | solution.py:181
  63.3 0.5 slice_bitcast_fusion.10
  64.0 1.5 %pad_maximum_fusion = bf16[256,16,256]{2,0,1:T(8,128)(2,1)} fusion(bf16[128,16,256]{2,0,1:T(8,128)(2,1)S(1)} %get-tuple-element.40, bf16[128,16,256]{2,0,1:T(8,128)(2,1)S(1)} %get-tuple-element.51), kind=kLoop, calls=%fused_computation.11 | loop fusion | flops 4194304 | bytes 4194304 | tf_op jit(solution)/shard_map/concatenate | solution.py:154
  65.5 6.3 %collective-permute-start.6 = (bf16[256,16,256]{2,0,1:T(8,128)(2,1)}, bf16[256,16,256]{2,0,1:T(8,128)(2,1)}, u32[]{:S(2)}, u32[]{:S(2)}) collective-permute-start(bf16[256,16,256]{2,0,1:T(8,128)(2,1)} %pad_maximum_fusion), channel_id=1, source_target_pairs={{0,128},{128,0},{256,384},{384,256},{1,129},{129,1},{257,385},{385... | collective-permute-start | bytes 6291464 | tf_op jit(solution)/shard_map/ppermute | solution.py:157
  71.8 1.6 %fusion.1 = (f32[512]{0:T(512)S(1)}, bf16[1,512,2048]{2,1,0:T(8,128)(2,1)S(1)}) fusion(f32[512,2048]{1,0:T(8,128)S(1)} %get-tuple-element.50, f32[512]{0:T(512)S(1)} %broadcast_maximum_fusion, s32[2048]{0:T(1024)S(1)} %bitcast.109, s32[512]{0:T(512)S(1)} %broadcast_bitcast_fusion), kind=kLoop, calls=%fused_computation.4 | loop fusion | flops 7339520 | bytes 6305792 | tf_op jit(solution)/shard_map/reduce_sum | solution.py:188
  73.8 0.5 convolution_add_fusion.2
  74.7 0.4 fusion.7
  77.5 1.4 %fusion.31 = (f32[128,4,1,256]{3,0,2,1:T(8,128)}, f32[128,4,1,256]{3,0,2,1:T(8,128)}, f32[128,4,1,256]{3,0,2,1:T(8,128)}, f32[128,4,1,256]{3,0,2,1:T(8,128)}) fusion(f32[128,4,4,256]{3,0,2,1:T(8,128)S(1)} %fusion.20), kind=kLoop, calls=%fused_computation.63 | loop fusion | bytes 4194304 | tf_op jit(solution)/shard_map/slice | solution.py:77
  79.0 1.4 %fusion.33 = (f32[128,4,1,256]{3,0,2,1:T(8,128)}, f32[128,4,1,256]{3,0,2,1:T(8,128)}, f32[128,4,1,256]{3,0,2,1:T(8,128)}, f32[128,4,1,256]{3,0,2,1:T(8,128)}) fusion(f32[128,4,4,256]{3,0,2,1:T(8,128)S(1)} %pad_maximum_fusion.1), kind=kLoop, calls=%fused_computation.65 | loop fusion | bytes 4194304 | tf_op jit(solution)/shard_map/slice | solution.py:77
  80.3 2.7 %slice_bitcast_fusion.1 = (bf16[16,128,256]{2,1,0:T(8,128)(2,1)}, bf16[16,128,256]{2,1,0:T(8,128)(2,1)S(1)}) fusion(bf16[256,16,256]{2,0,1:T(8,128)(2,1)} %collective-permute-done.6), kind=kLoop, calls=%fused_computation.21 | loop fusion | bytes 4194304 | tf_op jit(solution)/shard_map/transpose | solution.py:224
  83.9 1.1 fusion.36
  85.0 0.6 copy-done.1
  86.9 1.0 slice-done
  88.7 0.8 copy-done.3
  90.6 0.5 fusion.8
  91.1 0.7 copy.23
  91.8 39.0 %all_to_all.5 = bf16[128,8,512]{0,2,1:T(8,128)(2,1)S(1)} all-to-all(bf16[128,8,512]{0,2,1:T(8,128)(2,1)S(1)} %bitcast.95), channel_id=1, replica_groups=mesh['dp'=4,'context'=16,'tensor'=8] {'tensor'}, dimensions={1} | all-to-all | bytes 2097152 | tf_op jit(solution)/shard_map/all_to_all | solution.py:237
  130.9 0.8 copy.24
  (69 shorter events, 9.6 us)
Async XLA Ops:
  0.0 46.3 %copy-start = (s32[2048]{0:T(1024)S(1)}, s32[2048]{0:T(1024)}, u32[]{:S(2)}) copy-start(s32[2048]{0:T(1024)} %param.9) | copy-start | bytes 24580
  2.0 12.3 %collective-permute-start = (bf16[128,1,768]{2,0,1:T(8,128)(2,1)S(1)}, bf16[128,1,768]{2,0,1:T(8,128)(2,1)S(1)}, u32[]{:S(2)}, u32[]{:S(2)}) collective-permute-start(bf16[128,1,768]{2,0,1:T(8,128)(2,1)S(1)} %maximum_bitcast_fusion), channel_id=1, source_target_pairs={{0,64},{8,72},{16,80},{24,88},{32,96},{40,104},{48,112},{56,120},{... | collective-permute-start | bytes 589832 | tf_op jit(solution)/shard_map/ppermute | solution.py:51
  14.4 12.6 %collective-permute-start.1 = (bf16[128,2,768]{2,0,1:T(8,128)(2,1)S(1)}, bf16[128,2,768]{2,0,1:T(8,128)(2,1)S(1)}, u32[]{:S(2)}, u32[]{:S(2)}) collective-permute-start(bf16[128,2,768]{2,0,1:T(8,128)(2,1)S(1)} %maximum_select_fusion.5), channel_id=1, source_target_pairs={{0,32},{8,40},{16,48},{24,56},{32,0},{40,8},{48,16},{56,24},{64,96... | collective-permute-start | bytes 1179656 | tf_op jit(solution)/shard_map/ppermute | solution.py:51
  27.1 18.9 %copy-start.13 = (bf16[128,512]{1,0:T(8,128)(2,1)S(1)}, bf16[128,512]{1,0:T(8,128)(2,1)}, u32[]{:S(2)}) copy-start(bf16[128,512]{1,0:T(8,128)(2,1)} %param.6) | copy-start | bytes 393220
  27.2 19.2 %copy-start.14 = (s32[16]{0:T(128)S(1)}, s32[16]{0:T(128)}, u32[]{:S(2)}) copy-start(s32[16]{0:T(128)} %constant.67) | copy-start | bytes 196
  27.2 11.7 %collective-permute-start.3 = (bf16[128,4,384]{2,0,1:T(8,128)(2,1)S(1)}, bf16[128,4,384]{2,0,1:T(8,128)(2,1)S(1)}, u32[]{:S(2)}, u32[]{:S(2)}) collective-permute-start(bf16[128,4,384]{2,0,1:T(8,128)(2,1)S(1)} %get-tuple-element.45), channel_id=1, source_target_pairs={{0,24},{8,16},{16,8},{24,0},{32,56},{40,48},{48,40},{56,32},{64,88... | collective-permute-start | bytes 1179656 | tf_op jit(solution)/shard_map/ppermute | solution.py:85
  31.6 10.1 %collective-permute-start.2 = (bf16[128,4,384]{2,0,1:T(8,128)(2,1)S(1)}, bf16[128,4,384]{2,0,1:T(8,128)(2,1)S(1)}, u32[]{:S(2)}, u32[]{:S(2)}) collective-permute-start(bf16[128,4,384]{2,0,1:T(8,128)(2,1)S(1)} %get-tuple-element.46), channel_id=1, source_target_pairs={{0,8},{8,0},{16,24},{24,16},{32,40},{40,32},{48,56},{56,48},{64,72... | collective-permute-start | bytes 1179656 | tf_op jit(solution)/shard_map/ppermute | solution.py:84
  41.9 18.9 %collective-permute-start.4 = (bf16[128,8,384]{2,0,1:T(8,128)(2,1)S(1)}, bf16[128,8,384]{2,0,1:T(8,128)(2,1)S(1)}, u32[]{:S(2)}, u32[]{:S(2)}) collective-permute-start(bf16[128,8,384]{2,0,1:T(8,128)(2,1)S(1)} %maximum_select_fusion.3), channel_id=1, source_target_pairs={{0,24},{8,16},{16,8},{24,0},{32,56},{40,48},{48,40},{56,32},{64,88... | collective-permute-start | bytes 2359304 | tf_op jit(solution)/shard_map/ppermute | solution.py:84
  44.1 17.5 %collective-permute-start.5 = (bf16[128,8,384]{2,0,1:T(8,128)(2,1)S(1)}, bf16[128,8,384]{2,0,1:T(8,128)(2,1)S(1)}, u32[]{:S(2)}, u32[]{:S(2)}) collective-permute-start(bf16[128,8,384]{2,0,1:T(8,128)(2,1)S(1)} %maximum_select_fusion.4), channel_id=1, source_target_pairs={{0,8},{8,0},{16,24},{24,16},{32,40},{40,32},{48,56},{56,48},{64,72... | collective-permute-start | bytes 2359304 | tf_op jit(solution)/shard_map/ppermute | solution.py:85
  65.5 14.8 %collective-permute-start.6 = (bf16[256,16,256]{2,0,1:T(8,128)(2,1)}, bf16[256,16,256]{2,0,1:T(8,128)(2,1)}, u32[]{:S(2)}, u32[]{:S(2)}) collective-permute-start(bf16[256,16,256]{2,0,1:T(8,128)(2,1)} %pad_maximum_fusion), channel_id=1, source_target_pairs={{0,128},{128,0},{256,384},{384,256},{1,129},{129,1},{257,385},{385... | collective-permute-start | bytes 6291464 | tf_op jit(solution)/shard_map/ppermute | solution.py:157
  83.9 1.7 %copy-start.1 = (f32[128,4,4,256]{3,0,2,1:T(8,128)}, f32[128,4,4,256]{3,0,2,1:T(8,128)S(1)}, u32[]{:S(2)}) copy-start(f32[128,4,4,256]{3,0,2,1:T(8,128)S(1)} %fusion.14) | copy-start | bytes 6291460
  83.9 2.0 %copy-start.2 = (bf16[16,128,256]{2,1,0:T(8,128)(2,1)S(1)}, bf16[16,128,256]{2,1,0:T(8,128)(2,1)}, u32[]{:S(2)}) copy-start(bf16[16,128,256]{2,1,0:T(8,128)(2,1)} %get-tuple-element.23) | copy-start | bytes 3145732
  86.7 1.2 slice-start
  86.7 1.3 %copy-start.11 = (f32[128,1,4,256]{3,0,2,1:T(8,128)S(1)}, f32[128,1,4,256]{3,0,2,1:T(8,128)}, u32[]{:S(2)}) copy-start(f32[128,1,4,256]{3,0,2,1:T(8,128)} %get-tuple-element.35) | copy-start | bytes 1572868
  86.7 1.5 %copy-start.12 = (f32[128,1,4,256]{3,0,2,1:T(8,128)S(1)}, f32[128,1,4,256]{3,0,2,1:T(8,128)}, u32[]{:S(2)}) copy-start(f32[128,1,4,256]{3,0,2,1:T(8,128)} %get-tuple-element.36) | copy-start | bytes 1572868
  88.4 1.0 copy-start.3
  88.4 1.2 copy-start.4
  88.4 1.3 %copy-start.5 = (f32[128,4,1,256]{3,0,2,1:T(8,128)S(1)}, f32[128,4,1,256]{3,0,2,1:T(8,128)}, u32[]{:S(2)}) copy-start(f32[128,4,1,256]{3,0,2,1:T(8,128)} %get-tuple-element.17) | copy-start | bytes 1572868
  88.4 1.5 %copy-start.6 = (f32[128,4,1,256]{3,0,2,1:T(8,128)S(1)}, f32[128,4,1,256]{3,0,2,1:T(8,128)}, u32[]{:S(2)}) copy-start(f32[128,4,1,256]{3,0,2,1:T(8,128)} %get-tuple-element.18) | copy-start | bytes 1572868
  88.4 1.6 %copy-start.7 = (f32[128,4,1,256]{3,0,2,1:T(8,128)S(1)}, f32[128,4,1,256]{3,0,2,1:T(8,128)}, u32[]{:S(2)}) copy-start(f32[128,4,1,256]{3,0,2,1:T(8,128)} %get-tuple-element.25) | copy-start | bytes 1572868
  88.5 1.8 %copy-start.8 = (f32[128,4,1,256]{3,0,2,1:T(8,128)S(1)}, f32[128,4,1,256]{3,0,2,1:T(8,128)}, u32[]{:S(2)}) copy-start(f32[128,4,1,256]{3,0,2,1:T(8,128)} %get-tuple-element.26) | copy-start | bytes 1572868
  88.5 1.9 %copy-start.9 = (f32[128,4,1,256]{3,0,2,1:T(8,128)S(1)}, f32[128,4,1,256]{3,0,2,1:T(8,128)}, u32[]{:S(2)}) copy-start(f32[128,4,1,256]{3,0,2,1:T(8,128)} %get-tuple-element.27) | copy-start | bytes 1572868
  88.5 2.1 %copy-start.10 = (f32[128,4,1,256]{3,0,2,1:T(8,128)S(1)}, f32[128,4,1,256]{3,0,2,1:T(8,128)}, u32[]{:S(2)}) copy-start(f32[128,4,1,256]{3,0,2,1:T(8,128)} %get-tuple-element.28) | copy-start | bytes 1572868

commit v20 on v18

--- a/solution.py
+++ b/solution.py
@@ -151,10 +151,11 @@
     sources_a = stacked_sources(context_size, steps_a)
     sources_b = stacked_sources(context_size, steps_b)
 
-    mine_weights = jnp.concatenate(
-        [gathered_a[:, :, key_width:], gathered_b[:, :, values.shape[1] :]], axis=0
-    )
-    other_weights = lax.ppermute(mine_weights, "dp", [(i, i ^ 1) for i in range(dp_size)])
+    other_a, other_b = lax.ppermute(
+        (gathered_a, gathered_b), "dp", [(i, i ^ 1) for i in range(dp_size)]
+    )
+    mine_weights = (gathered_a[:, :, key_width:], gathered_b[:, :, values.shape[1] :])
+    other_weights = (other_a[:, :, key_width:], other_b[:, :, values.shape[1] :])
 
     whole_rows = local_groups == 1
     key_stack = gathered_a if whole_rows else gathered_a[:, :, :key_width]
@@ -201,7 +202,7 @@
     total = None
     for piece, sources in ((0, sources_a), (1, sources_b)):
         for which, held in ((0, mine_weights), (1, other_weights)):
-            piece_t = held[piece * row_count : (piece + 1) * row_count]
+            piece_t = held[piece]
             piece_t = jnp.swapaxes(piece_t, 0, 1).reshape(context_size, weight_cols, quarter)
             owner = core if which == 0 else 1 - core
             piece_rows = lax.dynamic_slice_in_dim(

time: 133 us -> 140 us (1.053)
  the two profiles are of different devices: /device:TPU:1 before, /device:TPU:16 now
where the time goes in v20:
time: 140 us; the launch traced here: 139 us
  blocking collectives  39 us (28%)
  waiting for transfers between devices  37.1 us (26%)
  starting transfers between devices  30.9 us (22%)
  local copies, waits for them, and re-layouts  20.1 us (14%)
  matrix products  5.8 us (4%)
  other arithmetic  5.3 us (4%)
    all_to_all x1, blocking collectives, per_device(): pieces = lax.all_to_all(pieces, 'tensor', 1, 1, tiled=True)  39 us
    ppermute x2, waiting for transfers between devices, exchange_gather_pair(): lax.ppermute(stack_a, axis_name, [(i, i ^ mask_a) for i in range(count)])  18.8 us
    ppermute x2, starting transfers between devices, exchange_gather(): lax.ppermute(stack, axis_name, [(i, i ^ mask) for i in range(count)])  13.3 us
    ppermute x2, waiting for transfers between devices, exchange_gather(): lax.ppermute(stack, axis_name, [(i, i ^ mask) for i in range(count)])  13 us
    ppermute x2, starting transfers between devices, exchange_gather_pair(): lax.ppermute(stack_a, axis_name, [(i, i ^ mask_a) for i in range(count)])  7.4 us
    ppermute x2, starting transfers between devices, exchange_gather_pair(): lax.ppermute(stack_b, axis_name, [(i, i ^ mask_b) for i in range(count)])  5.92 us
    transpose x3, local copies, waits for them, and re-layouts, per_device(): jnp.swapaxes(piece_t, 0, 1).reshape(context_size, weight_cols, quarter)  5.45 us
    ppermute x2, waiting for transfers between devices, exchange_gather_pair(): lax.ppermute(stack_b, axis_name, [(i, i ^ mask_b) for i in range(count)])  5.3 us
  transfers between devices with their start and end apart: 8, of which 6 were waited for; matrix products, arithmetic and copies ran while one was open for 14% of the time, Pallas kernels for 0%

profile of v20, /device:TPU:16, one launch (start us, length us, event | category | flops | bytes accessed | tf_op | source)
XLA Modules:
  0.0 138.8 jit_solution(17108818006247034350)
XLA Ops:
  0.0 0.9 dynamic-slice_bitcast_fusion.1
  1.2 0.8 maximum_bitcast_fusion
  2.0 7.6 %collective-permute-start = (bf16[128,1,768]{2,0,1:T(8,128)(2,1)S(1)}, bf16[128,1,768]{2,0,1:T(8,128)(2,1)S(1)}, u32[]{:S(2)}, u32[]{:S(2)}) collective-permute-start(bf16[128,1,768]{2,0,1:T(8,128)(2,1)S(1)} %maximum_bitcast_fusion), channel_id=1, source_target_pairs={{0,64},{8,72},{16,80},{24,88},{32,96},{40,104},{48,112},{56,120},{... | collective-permute-start | bytes 589832 | tf_op jit(solution)/shard_map/ppermute | solution.py:51
  9.6 3.7 %collective-permute-done = bf16[128,1,768]{2,0,1:T(8,128)(2,1)S(1)} collective-permute-done((bf16[128,1,768]{2,0,1:T(8,128)(2,1)S(1)}, bf16[128,1,768]{2,0,1:T(8,128)(2,1)S(1)}, u32[]{:S(2)}, u32[]{:S(2)}) %collective-permute-start) | collective-permute-done | bytes 196640 | tf_op jit(solution)/shard_map/ppermute | solution.py:51
  13.4 5.7 %collective-permute-start.1 = (bf16[128,2,768]{2,0,1:T(8,128)(2,1)S(1)}, bf16[128,2,768]{2,0,1:T(8,128)(2,1)S(1)}, u32[]{:S(2)}, u32[]{:S(2)}) collective-permute-start(bf16[128,2,768]{2,0,1:T(8,128)(2,1)S(1)} %maximum_select_fusion.5), channel_id=1, source_target_pairs={{0,32},{8,40},{16,48},{24,56},{32,0},{40,8},{48,16},{56,24},{64,96... | collective-permute-start | bytes 1179656 | tf_op jit(solution)/shard_map/ppermute | solution.py:51
  19.1 9.3 %collective-permute-done.1 = bf16[128,2,768]{2,0,1:T(8,128)(2,1)S(1)} collective-permute-done((bf16[128,2,768]{2,0,1:T(8,128)(2,1)S(1)}, bf16[128,2,768]{2,0,1:T(8,128)(2,1)S(1)}, u32[]{:S(2)}, u32[]{:S(2)}) %collective-permute-start.1) | collective-permute-done | bytes 393248 | tf_op jit(solution)/shard_map/ppermute | solution.py:51
  28.6 3.4 %collective-permute-start.2 = (bf16[128,4,384]{2,0,1:T(8,128)(2,1)S(1)}, bf16[128,4,384]{2,0,1:T(8,128)(2,1)S(1)}, u32[]{:S(2)}, u32[]{:S(2)}) collective-permute-start(bf16[128,4,384]{2,0,1:T(8,128)(2,1)S(1)} %get-tuple-element.34), channel_id=1, source_target_pairs={{0,8},{8,0},{16,24},{24,16},{32,40},{40,32},{48,56},{56,48},{64,72... | collective-permute-start | bytes 1179656 | tf_op jit(solution)/shard_map/ppermute | solution.py:84
  32.0 4.0 %collective-permute-start.3 = (bf16[128,4,384]{2,0,1:T(8,128)(2,1)S(1)}, bf16[128,4,384]{2,0,1:T(8,128)(2,1)S(1)}, u32[]{:S(2)}, u32[]{:S(2)}) collective-permute-start(bf16[128,4,384]{2,0,1:T(8,128)(2,1)S(1)} %get-tuple-element.33), channel_id=1, source_target_pairs={{0,24},{8,16},{16,8},{24,0},{32,56},{40,48},{48,40},{56,32},{64,88... | collective-permute-start | bytes 1179656 | tf_op jit(solution)/shard_map/ppermute | solution.py:85
  36.0 4.9 %collective-permute-done.2 = bf16[128,4,384]{2,0,1:T(8,128)(2,1)S(1)} collective-permute-done((bf16[128,4,384]{2,0,1:T(8,128)(2,1)S(1)}, bf16[128,4,384]{2,0,1:T(8,128)(2,1)S(1)}, u32[]{:S(2)}, u32[]{:S(2)}) %collective-permute-start.2) | collective-permute-done | bytes 393248 | tf_op jit(solution)/shard_map/ppermute | solution.py:84
  41.1 4.2 %collective-permute-done.3 = bf16[128,4,384]{2,0,1:T(8,128)(2,1)S(1)} collective-permute-done((bf16[128,4,384]{2,0,1:T(8,128)(2,1)S(1)}, bf16[128,4,384]{2,0,1:T(8,128)(2,1)S(1)}, u32[]{:S(2)}, u32[]{:S(2)}) %collective-permute-start.3) | collective-permute-done | bytes 393248 | tf_op jit(solution)/shard_map/ppermute | solution.py:85
  45.5 4.0 %collective-permute-start.4 = (bf16[128,8,384]{2,0,1:T(8,128)(2,1)S(1)}, bf16[128,8,384]{2,0,1:T(8,128)(2,1)S(1)}, u32[]{:S(2)}, u32[]{:S(2)}) collective-permute-start(bf16[128,8,384]{2,0,1:T(8,128)(2,1)S(1)} %maximum_select_fusion.3), channel_id=1, source_target_pairs={{0,24},{8,16},{16,8},{24,0},{32,56},{40,48},{48,40},{56,32},{64,88... | collective-permute-start | bytes 2359304 | tf_op jit(solution)/shard_map/ppermute | solution.py:84
  49.5 1.9 %collective-permute-start.5 = (bf16[128,8,384]{2,0,1:T(8,128)(2,1)S(1)}, bf16[128,8,384]{2,0,1:T(8,128)(2,1)S(1)}, u32[]{:S(2)}, u32[]{:S(2)}) collective-permute-start(bf16[128,8,384]{2,0,1:T(8,128)(2,1)S(1)} %maximum_select_fusion.4), channel_id=1, source_target_pairs={{0,8},{8,0},{16,24},{24,16},{32,40},{40,32},{48,56},{56,48},{64,72... | collective-permute-start | bytes 2359304 | tf_op jit(solution)/shard_map/ppermute | solution.py:85
  52.4 13.9 %collective-permute-done.4 = bf16[128,8,384]{2,0,1:T(8,128)(2,1)S(1)} collective-permute-done((bf16[128,8,384]{2,0,1:T(8,128)(2,1)S(1)}, bf16[128,8,384]{2,0,1:T(8,128)(2,1)S(1)}, u32[]{:S(2)}, u32[]{:S(2)}) %collective-permute-start.4) | collective-permute-done | bytes 786464 | tf_op jit(solution)/shard_map/ppermute | solution.py:84
  66.3 1.4 %maximum_select_fusion = bf16[128,16,384]{2,0,1:T(8,128)(2,1)} fusion(bf16[128,8,384]{2,0,1:T(8,128)(2,1)S(1)} %maximum_select_fusion.3, bf16[128,8,384]{2,0,1:T(8,128)(2,1)S(1)} %collective-permute-done.4, pred[]{:T(512)S(6)} %ne.22), kind=kLoop, calls=%fused_computation.13 | loop fusion | flops 2359296 | bytes 3145729 | tf_op jit(solution)/shard_map/jit(_where)/select_n | solution.py:86
  67.7 1.1 collective-permute-done.5
  69.3 1.9 %collective-permute-start.7 = (bf16[128,16,384]{2,0,1:T(8,128)(2,1)S(1)}, bf16[128,16,384]{2,0,1:T(8,128)(2,1)}, u32[]{:S(2)}, u32[]{:S(2)}) collective-permute-start(bf16[128,16,384]{2,0,1:T(8,128)(2,1)S(1)} %maximum_select_fusion.1), channel_id=1, source_target_pairs={{0,128},{128,0},{256,384},{384,256},{1,129},{129,1},{257,385},{385... | collective-permute-start | bytes 4718600 | tf_op jit(solution)/shard_map/ppermute | solution.py:154
  71.2 2.4 %collective-permute-start.6 = (bf16[128,16,384]{2,0,1:T(8,128)(2,1)}, bf16[128,16,384]{2,0,1:T(8,128)(2,1)}, u32[]{:S(2)}, u32[]{:S(2)}) collective-permute-start(bf16[128,16,384]{2,0,1:T(8,128)(2,1)} %maximum_select_fusion), channel_id=1, source_target_pairs={{0,128},{128,0},{256,384},{384,256},{1,129},{129,1},{257,385},{385... | collective-permute-start | bytes 4718600 | tf_op jit(solution)/shard_map/ppermute | solution.py:154
  73.6 2.9 %slice_bitcast_fusion.2 = (bf16[16,128,256]{2,1,0:T(8,128)(2,1)}, bf16[16,128,256]{2,1,0:T(8,128)(2,1)}) fusion(bf16[128,16,384]{2,0,1:T(8,128)(2,1)S(1)} %maximum_select_fusion.1, bf16[128,16,384]{2,0,1:T(8,128)(2,1)} %maximum_select_fusion), kind=kLoop, calls=%fused_computation.19 | loop fusion | bytes 4194304 | tf_op jit(solution)/shard_map/transpose | solution.py:206
  76.5 2.9 %fusion = (f32[512]{0:T(512)S(1)}, f32[512,2048]{1,0:T(8,128)S(1)}) fusion(s32[2048]{0:T(1024)S(1)} %bitcast.87, s32[512]{0:T(512)S(1)} %broadcast_bitcast_fusion, bf16[2048,384]{1,0:T(8,128)(2,1)} %bitcast.11, bf16[1,512,128]{2,1,0:T(8,128)(2,1)S(1)} %bitcast.85), kind=kOutput, calls=%fused_computation.3 | convolution fusion | flops 809500160 | bytes 5910528 | tf_op jit(solution)/shard_map/grd,kgd->grk/dot_general | solution.py:182
  79.4 1.3 fusion.1
  80.7 1.1 fusion.11
  82.0 1.4 %dot_general.32 = bf16[4,4,256,128]{3,2,1,0:T(8,128)(2,1)S(1)} reshape(bf16[16,128,256]{2,1,0:T(8,128)(2,1)} %get-tuple-element.41) | data formatting | bytes 2097152 | tf_op jit(solution)/shard_map/rh,nkh->rnk/dot_general | solution.py:211
  84.2 1.4 %fusion.40 = (f32[128,4,1,256]{3,0,2,1:T(8,128)}, f32[128,4,1,256]{3,0,2,1:T(8,128)}, f32[128,4,1,256]{3,0,2,1:T(8,128)}, f32[128,4,1,256]{3,0,2,1:T(8,128)}) fusion(f32[128,4,4,256]{3,0,2,1:T(8,128)S(1)} %pad_maximum_fusion), kind=kLoop, calls=%fused_computation.59 | loop fusion | bytes 4194304 | tf_op jit(solution)/shard_map/slice | solution.py:77
  85.6 1.4 %dot_general.28 = bf16[4,4,256,128]{3,2,1,0:T(8,128)(2,1)S(1)} reshape(bf16[16,128,256]{2,1,0:T(8,128)(2,1)} %get-tuple-element.42) | data formatting | bytes 2097152 | tf_op jit(solution)/shard_map/rh,nkh->rnk/dot_general | solution.py:211
  87.5 1.4 %fusion.38 = (f32[128,4,1,256]{3,0,2,1:T(8,128)}, f32[128,4,1,256]{3,0,2,1:T(8,128)}, f32[128,4,1,256]{3,0,2,1:T(8,128)}, f32[128,4,1,256]{3,0,2,1:T(8,128)}) fusion(f32[128,4,4,256]{3,0,2,1:T(8,128)S(1)} %fusion.24), kind=kLoop, calls=%fused_computation.57 | loop fusion | bytes 4194304 | tf_op jit(solution)/shard_map/slice | solution.py:77
  88.9 1.3 slice_bitcast_fusion
  91.2 1.2 copy-done.1
  92.4 1.3 slice_bitcast_fusion.1
  94.6 0.8 slice-done
  98.2 0.7 copy.23
  98.9 39.0 %all_to_all.5 = bf16[128,8,512]{0,2,1:T(8,128)(2,1)S(1)} all-to-all(bf16[128,8,512]{0,2,1:T(8,128)(2,1)S(1)} %bitcast.75), channel_id=1, replica_groups=mesh['dp'=4,'context'=16,'tensor'=8] {'tensor'}, dimensions={1} | all-to-all | bytes 2097152 | tf_op jit(solution)/shard_map/all_to_all | solution.py:219
  138.1 0.8 copy.24
  (63 shorter events, 8.2 us)
Async XLA Ops:
  0.0 51.7 %copy-start = (s32[2048]{0:T(1024)S(1)}, s32[2048]{0:T(1024)}, u32[]{:S(2)}) copy-start(s32[2048]{0:T(1024)} %param.9) | copy-start | bytes 24580
  2.0 11.3 %collective-permute-start = (bf16[128,1,768]{2,0,1:T(8,128)(2,1)S(1)}, bf16[128,1,768]{2,0,1:T(8,128)(2,1)S(1)}, u32[]{:S(2)}, u32[]{:S(2)}) collective-permute-start(bf16[128,1,768]{2,0,1:T(8,128)(2,1)S(1)} %maximum_bitcast_fusion), channel_id=1, source_target_pairs={{0,64},{8,72},{16,80},{24,88},{32,96},{40,104},{48,112},{56,120},{... | collective-permute-start | bytes 589832 | tf_op jit(solution)/shard_map/ppermute | solution.py:51
  13.4 15.0 %collective-permute-start.1 = (bf16[128,2,768]{2,0,1:T(8,128)(2,1)S(1)}, bf16[128,2,768]{2,0,1:T(8,128)(2,1)S(1)}, u32[]{:S(2)}, u32[]{:S(2)}) collective-permute-start(bf16[128,2,768]{2,0,1:T(8,128)(2,1)S(1)} %maximum_select_fusion.5), channel_id=1, source_target_pairs={{0,32},{8,40},{16,48},{24,56},{32,0},{40,8},{48,16},{56,24},{64,96... | collective-permute-start | bytes 1179656 | tf_op jit(solution)/shard_map/ppermute | solution.py:51
  28.5 22.9 %copy-start.10 = (bf16[128,512]{1,0:T(8,128)(2,1)S(1)}, bf16[128,512]{1,0:T(8,128)(2,1)}, u32[]{:S(2)}) copy-start(bf16[128,512]{1,0:T(8,128)(2,1)} %param.6) | copy-start | bytes 393220
  28.6 23.2 %copy-start.11 = (s32[16]{0:T(128)S(1)}, s32[16]{0:T(128)}, u32[]{:S(2)}) copy-start(s32[16]{0:T(128)} %constant.67) | copy-start | bytes 196
  28.6 12.4 %collective-permute-start.2 = (bf16[128,4,384]{2,0,1:T(8,128)(2,1)S(1)}, bf16[128,4,384]{2,0,1:T(8,128)(2,1)S(1)}, u32[]{:S(2)}, u32[]{:S(2)}) collective-permute-start(bf16[128,4,384]{2,0,1:T(8,128)(2,1)S(1)} %get-tuple-element.34), channel_id=1, source_target_pairs={{0,8},{8,0},{16,24},{24,16},{32,40},{40,32},{48,56},{56,48},{64,72... | collective-permute-start | bytes 1179656 | tf_op jit(solution)/shard_map/ppermute | solution.py:84
  32.0 13.3 %collective-permute-start.3 = (bf16[128,4,384]{2,0,1:T(8,128)(2,1)S(1)}, bf16[128,4,384]{2,0,1:T(8,128)(2,1)S(1)}, u32[]{:S(2)}, u32[]{:S(2)}) collective-permute-start(bf16[128,4,384]{2,0,1:T(8,128)(2,1)S(1)} %get-tuple-element.33), channel_id=1, source_target_pairs={{0,24},{8,16},{16,8},{24,0},{32,56},{40,48},{48,40},{56,32},{64,88... | collective-permute-start | bytes 1179656 | tf_op jit(solution)/shard_map/ppermute | solution.py:85
  45.5 20.9 %collective-permute-start.4 = (bf16[128,8,384]{2,0,1:T(8,128)(2,1)S(1)}, bf16[128,8,384]{2,0,1:T(8,128)(2,1)S(1)}, u32[]{:S(2)}, u32[]{:S(2)}) collective-permute-start(bf16[128,8,384]{2,0,1:T(8,128)(2,1)S(1)} %maximum_select_fusion.3), channel_id=1, source_target_pairs={{0,24},{8,16},{16,8},{24,0},{32,56},{40,48},{48,40},{56,32},{64,88... | collective-permute-start | bytes 2359304 | tf_op jit(solution)/shard_map/ppermute | solution.py:84
  49.5 19.4 %collective-permute-start.5 = (bf16[128,8,384]{2,0,1:T(8,128)(2,1)S(1)}, bf16[128,8,384]{2,0,1:T(8,128)(2,1)S(1)}, u32[]{:S(2)}, u32[]{:S(2)}) collective-permute-start(bf16[128,8,384]{2,0,1:T(8,128)(2,1)S(1)} %maximum_select_fusion.4), channel_id=1, source_target_pairs={{0,8},{8,0},{16,24},{24,16},{32,40},{40,32},{48,56},{56,48},{64,72... | collective-permute-start | bytes 2359304 | tf_op jit(solution)/shard_map/ppermute | solution.py:85
  69.3 19.7 %collective-permute-start.7 = (bf16[128,16,384]{2,0,1:T(8,128)(2,1)S(1)}, bf16[128,16,384]{2,0,1:T(8,128)(2,1)}, u32[]{:S(2)}, u32[]{:S(2)}) collective-permute-start(bf16[128,16,384]{2,0,1:T(8,128)(2,1)S(1)} %maximum_select_fusion.1), channel_id=1, source_target_pairs={{0,128},{128,0},{256,384},{384,256},{1,129},{129,1},{257,385},{385... | collective-permute-start | bytes 4718600 | tf_op jit(solution)/shard_map/ppermute | solution.py:154
  71.2 21.2 %collective-permute-start.6 = (bf16[128,16,384]{2,0,1:T(8,128)(2,1)}, bf16[128,16,384]{2,0,1:T(8,128)(2,1)}, u32[]{:S(2)}, u32[]{:S(2)}) collective-permute-start(bf16[128,16,384]{2,0,1:T(8,128)(2,1)} %maximum_select_fusion), channel_id=1, source_target_pairs={{0,128},{128,0},{256,384},{384,256},{1,129},{129,1},{257,385},{385... | collective-permute-start | bytes 4718600 | tf_op jit(solution)/shard_map/ppermute | solution.py:154
  91.1 1.3 copy-start.1
  94.1 1.2 slice-start
  95.5 1.0 copy-start.2
  95.5 1.2 copy-start.3
  95.5 1.3 copy-start.4
  95.5 1.5 %copy-start.5 = (f32[128,4,1,256]{3,0,2,1:T(8,128)S(1)}, f32[128,4,1,256]{3,0,2,1:T(8,128)}, u32[]{:S(2)}) copy-start(f32[128,4,1,256]{3,0,2,1:T(8,128)} %get-tuple-element.24) | copy-start | bytes 1572868
  95.5 1.6 %copy-start.6 = (f32[128,4,1,256]{3,0,2,1:T(8,128)S(1)}, f32[128,4,1,256]{3,0,2,1:T(8,128)}, u32[]{:S(2)}) copy-start(f32[128,4,1,256]{3,0,2,1:T(8,128)} %get-tuple-element.13) | copy-start | bytes 1572868
  95.6 1.8 %copy-start.7 = (f32[128,4,1,256]{3,0,2,1:T(8,128)S(1)}, f32[128,4,1,256]{3,0,2,1:T(8,128)}, u32[]{:S(2)}) copy-start(f32[128,4,1,256]{3,0,2,1:T(8,128)} %get-tuple-element.14) | copy-start | bytes 1572868
  95.6 1.9 %copy-start.8 = (f32[128,4,1,256]{3,0,2,1:T(8,128)S(1)}, f32[128,4,1,256]{3,0,2,1:T(8,128)}, u32[]{:S(2)}) copy-start(f32[128,4,1,256]{3,0,2,1:T(8,128)} %get-tuple-element.15) | copy-start | bytes 1572868
  95.6 2.1 %copy-start.9 = (f32[128,4,1,256]{3,0,2,1:T(8,128)S(1)}, f32[128,4,1,256]{3,0,2,1:T(8,128)}, u32[]{:S(2)}) copy-start(f32[128,4,1,256]{3,0,2,1:T(8,128)} %get-tuple-element.16) | copy-start | bytes 1572868
